TPU v7x, 32 devices: a whole 2x2x4 slice. The times are simulated.
32 devices in a mesh: seq: 8 (over y, x, core), chan: 4 (over z).
Axes of the slice: x: 2, y: 2, z: 4, core: 2. Of those that a mesh axis runs over, the one named last changes fastest.
Arguments:
- query_proj: bfloat16 [1024, 8192], P('seq', 'chan'), may hold values from -8 to 8
- key_proj: bfloat16 [1024, 8192], P('seq', 'chan'), may hold values from -8 to 8
- value_proj: bfloat16 [1024, 8192], P('seq', 'chan'), may hold values from -6 to 6
- residual: bfloat16 [1024, 8192], P('seq', 'chan'), may hold values from -6 to 6
- out_weight: bfloat16 [8192, 8192], P('chan', 'seq'), may hold values from -0.0625 to 0.0625
Outputs:
- attn_out: bfloat16 [1024, 8192], P('seq', 'chan')
All inputs are finite; a program needn't handle non-finite values.
Results may differ from a plain program's by a relative error of at most 0.008.
Values may be sent and summed in bfloat16 or wider, within the bound.
No kernel may reach another device: no remote copies, remote signals or barrier semaphores. Data moves between devices by JAX's collectives and lax.ppermute only.
A program may use at most 64 MiB of HBM per device.

v0:
```python
import math

import jax
import jax.numpy as jnp
from jax import lax
from jax.sharding import PartitionSpec as P

HEAD_DIM = 128


def attend(state, query_rows, first_pos, key_block, value_block, block_start, score_scale):
    row_max, row_total, accum = state
    scores = (
        jnp.einsum("qhd,khd->hqk", query_rows, key_block, preferred_element_type=jnp.float32)
        * score_scale
    )
    row_pos = first_pos + jnp.arange(query_rows.shape[0], dtype=jnp.int32)
    col_pos = block_start + jnp.arange(key_block.shape[0], dtype=jnp.int32)
    allowed = (col_pos[None, :] <= row_pos[:, None])[None]
    scores = jnp.where(allowed, scores, -1e30)
    new_max = jnp.maximum(row_max, jnp.max(scores, axis=-1))
    weights = jnp.where(allowed, jnp.exp(scores - new_max[..., None]), 0.0)
    factor = jnp.exp(row_max - new_max)
    row_total = row_total * factor + jnp.sum(weights, axis=-1)
    accum = accum * factor[..., None] + jnp.einsum(
        "hqk,khd->hqd",
        weights.astype(jnp.bfloat16),
        value_block,
        preferred_element_type=jnp.float32,
    )
    return (new_max, row_total, accum)


def guarded(state, query_rows, first_pos, key_block, value_block, block_start, score_scale):
    last_pos = first_pos + query_rows.shape[0] - 1

    def do_update(inner):
        return attend(
            inner, query_rows, first_pos, key_block, value_block, block_start, score_scale
        )

    def keep_state(inner):
        return inner

    return lax.cond(block_start <= last_pos, do_update, keep_state, state)


def per_device(query_proj, key_proj, value_proj, residual, out_weight):
    seg_rows = query_proj.shape[0]
    feat_width = query_proj.shape[1]
    heads_here = feat_width // HEAD_DIM
    seq_count = lax.axis_size("seq")
    chan_count = lax.axis_size("chan")
    segment = lax.axis_index("seq")
    score_scale = 1.0 / math.sqrt(HEAD_DIM)
    groups = [(query_proj, segment * seg_rows)]
    shaped = [
        (rows.reshape(rows.shape[0], heads_here, HEAD_DIM), first_pos) for rows, first_pos in groups
    ]
    starting = tuple(
        (
            (
                jnp.full((heads_here, rows.shape[0]), -1e30, jnp.float32),
                jnp.zeros((heads_here, rows.shape[0]), jnp.float32),
                jnp.zeros((heads_here, rows.shape[0], HEAD_DIM), jnp.float32),
            )
            for rows, first_pos in shaped
        )
    )
    piece_keys = lax.all_gather(key_proj, "seq", axis=0, tiled=True)
    piece_values = lax.all_gather(value_proj, "seq", axis=0, tiled=True)
    piece_rows = piece_keys.shape[0]

    def one_block(block_index, states):
        offset = block_index * seg_rows
        key_block = lax.dynamic_slice_in_dim(piece_keys, offset, seg_rows, 0).reshape(
            seg_rows, heads_here, HEAD_DIM
        )
        value_block = lax.dynamic_slice_in_dim(piece_values, offset, seg_rows, 0).reshape(
            seg_rows, heads_here, HEAD_DIM
        )
        updated = []
        for (query_rows, first_pos), state in zip(shaped, states):
            updated.append(
                guarded(state, query_rows, first_pos, key_block, value_block, offset, score_scale)
            )
        return tuple(updated)

    finals = lax.fori_loop(0, piece_rows // seg_rows, one_block, starting)
    pieces_out = []
    for row_max, row_total, accum in finals:
        ratio = accum / row_total[..., None]
        pieces_out.append(
            ratio.transpose(1, 0, 2).reshape(ratio.shape[1], feat_width).astype(jnp.bfloat16)
        )
    local_context = pieces_out[0]
    gathered = lax.all_gather(local_context, "seq", axis=0, tiled=True)
    sub_rows = seg_rows // chan_count
    grid = gathered.reshape(seq_count, chan_count, sub_rows, feat_width)
    block_tokens = seq_count * sub_rows
    rows = grid.transpose(1, 0, 2, 3).reshape(block_tokens * lax.axis_size("chan"), feat_width)
    partial_sums = lax.psum_scatter(
        jnp.dot(rows, out_weight, preferred_element_type=jnp.float32).astype(jnp.bfloat16),
        "chan",
        scatter_dimension=0,
        tiled=True,
    ).astype(jnp.float32)
    relaid = lax.all_to_all(
        lax.all_to_all(
            partial_sums.astype(jnp.bfloat16), "seq", split_axis=0, concat_axis=1, tiled=True
        ),
        "chan",
        split_axis=1,
        concat_axis=0,
        tiled=True,
    ).astype(partial_sums.dtype)
    return (residual.astype(jnp.float32) + relaid).astype(jnp.bfloat16)


def solution(mesh):
    placed = (
        P("seq", "chan"),
        P("seq", "chan"),
        P("seq", "chan"),
        P("seq", "chan"),
        P("chan", "seq"),
    )
    return jax.shard_map(
        per_device, mesh=mesh, in_specs=placed, out_specs=P("seq", "chan"), check_vma=False
    )
```

profile of v0, /device:TPU:0, one launch (start us, length us, event | category | flops | bytes accessed | tf_op | source)
XLA Modules:
  0.0 250.2 jit_solution(13693621716920695424)
XLA Ops:
  6.5 2.0 copy.32
  8.7 2.1 copy.34
  10.8 1.3 copy.33
  12.4 37.0 %all-gather.4.cloned.1.call-done = bf16[1024,2048]{0,1:T(8,128)(2,1)} async-done(((bf16[128,2048]{0,1:T(8,128)(2,1)}), bf16[1024,2048]{0,1:T(8,128)(2,1)}) %all-gather.4.cloned.1.call-update) | async-done | bytes 4194320 | tf_op jit(solution)/shard_map/all_gather | solution.py:70
  49.4 39.3 %all-gather.6.cloned.1.call-done = bf16[1024,2048]{0,1:T(8,128)(2,1)} async-done(((bf16[128,2048]{0,1:T(8,128)(2,1)}), bf16[1024,2048]{0,1:T(8,128)(2,1)}) %all-gather.6.cloned.1.call-update) | async-done | bytes 4194320 | tf_op jit(solution)/shard_map/all_gather | solution.py:71
  88.9 3.3 %while.19 = (s32[]{:T(128)}, f32[16,128]{1,0:T(8,128)S(1)}, f32[16,128]{1,0:T(8,128)S(1)}, f32[16,128,128]{2,1,0:T(8,128)S(1)}, s32[]{:T(128)}, /*index=5*/s32[]...) while((s32[]{:T(128)}, f32[16,128]{1,0:T(8,128)S(1)}, ...), condition=%wide.region_5.6_spmd, body=%wide.region_0.5_spmd.sunk | while | flops 137122048 | bytes 9111853 | solution.py:89
  88.9 3.0 %conditional.2 = ((f32[16,128]{1,0:T(8,128)S(1)}, f32[16,128]{1,0:T(8,128)S(1)}, f32[16,128,128]{2,1,0:T(8,128)S(1)})) conditional(s32[]{:T(128)} %convert_element_type.63, (f32[16,128]{1,0:T(8,128)S(1)}, f32[16,128]{1,0:T(8,128)S(1)}, f32[16,128,128]{2,1,0:T(8,128)S(1)}) %tuple.61, (s32[]{:T(128)}, s32[]{:T(128)}, bf16[1024,2048]{0,1:T(8,128)(2,1)}, ...), branch_computations={%region_1.0_spmd, %region_2.4_spmd} | conditional | flops 137122048 | bytes 9111630 | solution.py:45
  88.9 1.3 constant_dynamic-slice_fusion
  90.3 0.5 fusion.10
  91.1 0.8 convolution_add_fusion
  92.2 0.3 copy.36
  92.5 0.9 divide_convert_fusion
  93.5 58.4 %all-gather.8.cloned.1.call-done = bf16[1024,2048]{0,1:T(8,128)(2,1)} async-done(((bf16[128,2048]{0,1:T(8,128)(2,1)}), bf16[1024,2048]{0,1:T(8,128)(2,1)}) %all-gather.8.cloned.1.call-update) | async-done | bytes 4194320 | tf_op jit(solution)/shard_map/all_gather | solution.py:97
  151.9 6.5 %copy.37 = bf16[1024,2048]{1,0:T(8,128)(2,1)} copy(bf16[1024,2048]{0,1:T(8,128)(2,1)} %all-gather.8.cloned.1.call-done) | data formatting | bytes 8388608 | tf_op jit(solution)/shard_map/all_gather | solution.py:97
  158.4 2.7 %copy.38 = bf16[4,8,32,2048]{3,2,1,0:T(8,128)(2,1)S(1)} copy(bf16[4,8,32,2048]{3,2,0,1:T(8,128)(2,1)} %bitcast.29) | data formatting | bytes 8388608 | tf_op jit(solution)/shard_map/transpose | solution.py:101
  161.1 0.8 copy-done.1
  161.9 5.7 %convolution_convert_fusion = bf16[1024,1024]{1,0:T(8,128)(2,1)} fusion(bf16[1024,2048]{1,0:T(8,128)(2,1)S(1)} %bitcast.30, bf16[2048,1024]{1,0:T(8,128)(2,1)S(1)} %copy-done.1), kind=kOutput, calls=%fused_computation.18 | convolution fusion | flops 4296015872 | bytes 10485760 | tf_op jit(solution)/shard_map/dot_general | solution.py:103
  167.7 44.0 %reduce-scatter.2.cloned.1.call-done = bf16[256,1024]{1,0:T(8,128)(2,1)} async-done(((bf16[1024,1024]{1,0:T(8,128)(2,1)}), bf16[256,1024]{1,0:T(8,128)(2,1)}) %reduce-scatter.2.cloned.1.call-update) | async-done | bytes 524304 | tf_op jit(solution)/shard_map/reduce_scatter | solution.py:102
  211.7 13.4 %all_to_all.29 = bf16[8,32,1024]{2,1,0:T(8,128)(2,1)S(1)} all-to-all(bf16[8,32,1024]{2,1,0:T(8,128)(2,1)} %bitcast.34), channel_id=1, replica_groups=mesh['seq'=8,'chan'=4] {'seq'}, dimensions={0} | all-to-all | bytes 1048576 | tf_op jit(solution)/shard_map/all_to_all | solution.py:109
  225.1 0.3 copy.39
  225.3 0.4 all_to_all.25
  225.7 0.3 copy.40
  226.0 16.7 %all_to_all.30 = bf16[32,4,2048]{2,0,1:T(8,128)(2,1)S(1)} all-to-all(bf16[32,4,2048]{2,0,1:T(8,128)(2,1)S(1)} %copy.40), channel_id=1, replica_groups=mesh['seq'=8,'chan'=4] {'chan'}, dimensions={1} | all-to-all | bytes 1048576 | tf_op jit(solution)/shard_map/all_to_all | solution.py:108
  242.7 0.9 fusion.9
  (28 shorter events, 1.0 us)
Async XLA Ops:
  6.5 42.9 %all-gather.4.cloned.1.call-start = ((), (), s32[]{:S(2)}) async-start(), calls=%async_computation.3 | async-start | bytes 4718592 | tf_op jit(solution)/shard_map/all_gather | solution.py:70
  8.6 80.1 %all-gather.6.cloned.1.call-start = ((), (), s32[]{:S(2)}) async-start(), calls=%async_computation.4 | async-start | bytes 4718592 | tf_op jit(solution)/shard_map/all_gather | solution.py:71
  10.8 141.2 %all-gather.8.cloned.1.call-start = ((), (), s32[]{:S(2)}) async-start(), calls=%async_computation.5 | async-start | bytes 4718592 | tf_op jit(solution)/shard_map/all_gather | solution.py:97
  93.5 118.2 %reduce-scatter.2.cloned.1.call-start = ((), (), s32[]{:S(2)}) async-start(), calls=%async_computation.6 | async-start | bytes 2621440 | tf_op jit(solution)/shard_map/reduce_scatter | solution.py:102
  158.4 3.4 %copy-start.1 = (bf16[2048,1024]{1,0:T(8,128)(2,1)S(1)}, bf16[2048,1024]{1,0:T(8,128)(2,1)}, u32[]{:S(2)}) copy-start(bf16[2048,1024]{1,0:T(8,128)(2,1)} %param.13) | copy-start | bytes 12582916
  167.6 75.1 %copy-start = (bf16[128,2048]{1,0:T(8,128)(2,1)S(1)}, bf16[128,2048]{1,0:T(8,128)(2,1)}, u32[]{:S(2)}) copy-start(bf16[128,2048]{1,0:T(8,128)(2,1)} %param.12) | copy-start | bytes 1572868
Sparse Core Ops, SparseCore 0:
  9.2 40.1 all-gather.3
  51.3 37.4 all-gather.5
  93.6 58.2 all-gather.7
  167.8 43.8 reduce-scatter.1
where the time goes:
time: 251 us; the launch traced here: 250 us
  waiting for transfers between devices  179 us (71%)
  blocking collectives  30.1 us (12%)
  local copies, waits for them, and re-layouts  18.4 us (7%)
  between operations  13.2 us (5%)
  matrix products  7.06 us (3%)
    all_gather x1, waiting for transfers between devices, per_device(): gathered = lax.all_gather(local_context, 'seq', axis=0, tiled=True)  58.4 us
    reduce_scatter x1, waiting for transfers between devices, per_device(): lax.psum_scatter(jnp.dot(rows, out_weight, preferred_element_type=jnp.flo...  44 us
    all_gather x1, waiting for transfers between devices, per_device(): piece_values = lax.all_gather(value_proj, 'seq', axis=0, tiled=True)  39.3 us
    all_gather x1, waiting for transfers between devices, per_device(): piece_keys = lax.all_gather(key_proj, 'seq', axis=0, tiled=True)  37 us
    all_to_all x1, blocking collectives, per_device(): lax.all_to_all(lax.all_to_all(partial_sums.astype(jnp.bfloat16), 'seq', s...  16.7 us
    all_to_all x1, blocking collectives, per_device(): lax.all_to_all(partial_sums.astype(jnp.bfloat16), 'seq', split_axis=0, co...  13.4 us
    all_gather x1, local copies, waits for them, and re-layouts, per_device(): gathered = lax.all_gather(local_context, 'seq', axis=0, tiled=True)  6.53 us
    unnamed x7, local copies, waits for them, and re-layouts  6.22 us
  transfers between devices with their start and end apart: 4, of which 4 were waited for; matrix products, arithmetic and copies ran while one was open for 1% of the time, Pallas kernels for 0%

commit v1 on v0

v1 whole, which is shorter than its diff:
```python
import math

import jax
import jax.numpy as jnp
import numpy as np
from jax import lax
from jax.sharding import Mesh
from jax.sharding import PartitionSpec as P

HEAD_DIM = 128
SEQ = ("hi", "lo")


def cores_per_chip_along_seq(mesh):
    column = mesh.devices[:, 0]
    first = tuple(column[0].coords)
    count = 1
    while count < len(column) and tuple(column[count].coords) == first:
        count += 1
    return count


def gather_seq(x):
    return lax.all_gather(lax.all_gather(x, "hi", axis=0, tiled=True), "lo", axis=0, tiled=True)


def per_device(query_proj, key_proj, value_proj, residual, out_weight):
    seg_rows = query_proj.shape[0]
    feat_width = query_proj.shape[1]
    heads_here = feat_width // HEAD_DIM
    n_hi = lax.axis_size("hi")
    n_lo = lax.axis_size("lo")
    seq_count = n_hi * n_lo
    chan_count = lax.axis_size("chan")
    segment = lax.axis_index("hi") * n_lo + lax.axis_index("lo")
    score_scale = 1.0 / math.sqrt(HEAD_DIM)

    both = gather_seq(jnp.concatenate([key_proj, value_proj], axis=1))
    total_rows = both.shape[0]
    keys = both[:, :feat_width].reshape(total_rows, heads_here, HEAD_DIM)
    values = both[:, feat_width:].reshape(total_rows, heads_here, HEAD_DIM)
    block = np.arange(seq_count)
    block_segment = (block % n_hi) * n_lo + block // n_hi
    key_pos = jnp.asarray(
        (block_segment[:, None] * seg_rows + np.arange(seg_rows)[None, :]).reshape(-1), jnp.int32
    )
    row_pos = segment * seg_rows + jnp.arange(seg_rows, dtype=jnp.int32)
    queries = query_proj.reshape(seg_rows, heads_here, HEAD_DIM)
    scores = (
        jnp.einsum("qhd,khd->hqk", queries, keys, preferred_element_type=jnp.float32) * score_scale
    )
    allowed = (key_pos[None, :] <= row_pos[:, None])[None]
    scores = jnp.where(allowed, scores, -1e30)
    row_max = jnp.max(scores, axis=-1)
    weights = jnp.where(allowed, jnp.exp(scores - row_max[..., None]), 0.0)
    row_total = jnp.sum(weights, axis=-1)
    numer = jnp.einsum(
        "hqk,khd->hqd", weights.astype(jnp.bfloat16), values, preferred_element_type=jnp.float32
    )
    ratio = numer / row_total[..., None]
    local_context = ratio.transpose(1, 0, 2).reshape(seg_rows, feat_width).astype(jnp.bfloat16)

    gathered = gather_seq(local_context)
    sub_rows = seg_rows // chan_count
    grid = gathered.reshape(n_lo, n_hi, chan_count, sub_rows, feat_width)
    block_tokens = seq_count * sub_rows
    rows = grid.transpose(2, 1, 0, 3, 4).reshape(block_tokens * chan_count, feat_width)
    partial_sums = lax.psum_scatter(
        jnp.dot(rows, out_weight, preferred_element_type=jnp.float32).astype(jnp.bfloat16),
        "chan",
        scatter_dimension=0,
        tiled=True,
    ).astype(jnp.float32)
    relaid = lax.all_to_all(
        lax.all_to_all(
            partial_sums.astype(jnp.bfloat16), SEQ, split_axis=0, concat_axis=1, tiled=True
        ),
        "chan",
        split_axis=1,
        concat_axis=0,
        tiled=True,
    ).astype(partial_sums.dtype)
    return (residual.astype(jnp.float32) + relaid).astype(jnp.bfloat16)


def solution(mesh):
    seq_size, chan_size = mesh.devices.shape
    n_lo = cores_per_chip_along_seq(mesh)
    split = Mesh(
        mesh.devices.reshape(seq_size // n_lo, n_lo, chan_size), ("hi", "lo", mesh.axis_names[1])
    )
    rows_cols = P(SEQ, "chan")
    placed = (rows_cols, rows_cols, rows_cols, rows_cols, P("chan", SEQ))
    return jax.shard_map(
        per_device, mesh=split, in_specs=placed, out_specs=rows_cols, check_vma=False
    )
```

time: 251 us -> 248 us (0.988)
  local copies, waits for them, and re-layouts: 18.4 us -> 12.1 us
  waiting for transfers between devices: 179 us -> 173 us
  other arithmetic: 2.15 us -> 8.02 us
  matrix products: 7.06 us -> 10.6 us
    all_gather x3 -> x4, waiting for transfers between devices: 135 us -> 128 us  [the longest x2 92 us: gather_seq(): lax.all_gather(x, 'hi', axis=0, tiled=True)]
    all_gather x1 -> x0, local copies, waits for them, and re-layouts: 6.53 us -> none  [per_device(): gathered = lax.all_gather(local_context, 'seq', axis=0, tiled=True)]
    sub x0 -> x1, other arithmetic: none -> 5.84 us  [per_device(): weights = jnp.where(allowed, jnp.exp(scores - row_max[..., None]), 0.0)]
    slice x0 -> x1, local copies, waits for them, and re-layouts: none -> 3.93 us  [per_device(): keys = both[:, :feat_width].reshape(total_rows, heads_here, HEAD_DIM)]
    dot_general x2, matrix products: 1.33 us -> 4.87 us  [the longest x1 3.5 us: per_device(): jnp.einsum('hqk,khd->hqd', weights.astype(jnp.bfloat16), values, preferre...]
    unnamed x7 -> x10, local copies, waits for them, and re-layouts: 6.22 us -> 3.49 us
  transfers between devices with their start and end apart: 4 -> 5, of which waited for: 4 -> 5; matrix products, arithmetic and copies ran while one was open for 1% -> 0% of each run, Pallas kernels for 0% -> 0%
where the time goes in v1:
time: 248 us
  waiting for transfers between devices  173 us (70%)
  blocking collectives  30 us (12%)
  between operations  13.2 us (5%)
  local copies, waits for them, and re-layouts  12.1 us (5%)
  matrix products  10.6 us (4%)
  other arithmetic  8.02 us (3%)
    all_gather x2, waiting for transfers between devices, gather_seq(): lax.all_gather(x, 'hi', axis=0, tiled=True)  92 us
    reduce_scatter x1, waiting for transfers between devices, per_device(): lax.psum_scatter(jnp.dot(rows, out_weight, preferred_element_type=jnp.flo...  45.2 us
    all_gather x2, waiting for transfers between devices, gather_seq(): lax.all_gather(lax.all_gather(x, 'hi', axis=0, tiled=True), 'lo', axis=0,...  36.2 us
    all_to_all x1, blocking collectives, per_device(): lax.all_to_all(lax.all_to_all(partial_sums.astype(jnp.bfloat16), SEQ, spl...  16.6 us
    all_to_all x1, blocking collectives, per_device(): lax.all_to_all(partial_sums.astype(jnp.bfloat16), SEQ, split_axis=0, conc...  13.4 us
    sub x1, other arithmetic, per_device(): weights = jnp.where(allowed, jnp.exp(scores - row_max[..., None]), 0.0)  5.84 us
    dot_general x1, matrix products, per_device(): jnp.dot(rows, out_weight, preferred_element_type=jnp.float32)  5.74 us
  transfers between devices with their start and end apart: 5, of which 5 were waited for; matrix products, arithmetic and copies ran while one was open for 0% of the time, Pallas kernels for 0%

profile of v1, /device:TPU:0, one launch (start us, length us, event | category | flops | bytes accessed | tf_op | source)
XLA Modules:
  0.0 247.5 jit_solution(12309192706006640301)
XLA Ops:
  6.5 1.4 copy.27
  7.9 1.3 copy.28
  9.2 1.0 pad_maximum_fusion
  10.3 0.0 all-gather.7.cloned.1.call-start
  10.4 55.4 %all-gather.5.cloned.1.call-done = bf16[512,4096]{0,1:T(8,128)(2,1)} async-done(((bf16[128,4096]{0,1:T(8,128)(2,1)}), bf16[512,4096]{0,1:T(8,128)(2,1)}) %all-gather.5.cloned.1.call-update) | async-done | bytes 4194320 | tf_op jit(solution)/shard_map/all_gather | solution.py:24
  65.8 0.2 broadcast_compare_fusion
  66.1 21.1 %all-gather.7.cloned.1.call-done = bf16[1024,4096]{0,1:T(8,128)(2,1)} async-done(((bf16[512,4096]{0,1:T(8,128)(2,1)}), bf16[1024,4096]{0,1:T(8,128)(2,1)}) %all-gather.7.cloned.1.call-update) | async-done | bytes 8388624 | tf_op jit(solution)/shard_map/all_gather | solution.py:24
  87.2 3.9 %fusion.22 = (bf16[1024,2048]{0,1:T(8,128)(2,1)S(1)}, bf16[1024,2048]{0,1:T(8,128)(2,1)S(1)}) fusion(bf16[1024,4096]{0,1:T(8,128)(2,1)} %all-gather.7.cloned.1.call-done), kind=kLoop, calls=%fused_computation.23 | loop fusion | bytes 16777216 | tf_op jit(solution)/shard_map/slice | solution.py:40
  91.1 1.4 fusion.17
  92.5 5.8 %fusion.23 = (f32[16,128]{1,0:T(8,128)S(1)}, bf16[16,128,1024]{1,2,0:T(8,128)(2,1)}) fusion(f32[16,1024,128]{2,1,0:T(8,128)S(1)} %fusion.17, pred[128,1024]{0,1:T(8,128)(4,1)S(1)} %broadcast_compare_fusion), kind=kOutput, calls=%fused_computation.24 | output fusion | flops 16778240 | bytes 12722176 | tf_op jit(solution)/shard_map/sub | solution.py:55
  98.3 3.5 %fusion.13 = bf16[128,16,128]{0,2,1:T(8,128)(2,1)S(1)} fusion(bf16[1024,16,128]{0,2,1:T(8,128)(2,1)S(1)} %bitcast.48, bf16[16,128,1024]{1,2,0:T(8,128)(2,1)} %get-tuple-element.8, f32[128,16]{0,1:T(8,128)S(1)} %bitcast.52), kind=kOutput, calls=%fused_computation.12 | convolution fusion | flops 537395200 | bytes 8921088 | tf_op jit(solution)/shard_map/hqk,khd->hqd/dot_general | solution.py:57
  101.8 1.0 copy.32
  102.9 36.6 %all-gather.9.cloned.1.call-done = bf16[512,2048]{1,0:T(8,128)(2,1)} async-done(((bf16[128,2048]{1,0:T(8,128)(2,1)}), bf16[512,2048]{1,0:T(8,128)(2,1)}) %all-gather.9.cloned.1.call-update) | async-done | bytes 2097168 | tf_op jit(solution)/shard_map/all_gather | solution.py:24
  139.6 15.0 %all-gather.11.cloned.1.call-done = bf16[1024,2048]{1,0:T(8,128)(2,1)} async-done(((bf16[512,2048]{1,0:T(8,128)(2,1)}), bf16[1024,2048]{1,0:T(8,128)(2,1)}) %all-gather.11.cloned.1.call-update) | async-done | bytes 4194320 | tf_op jit(solution)/shard_map/all_gather | solution.py:24
  154.6 2.7 %copy.33 = bf16[4,4,2,32,2048]{4,3,2,1,0:T(8,128)(2,1)S(1)} copy(bf16[4,4,2,32,2048]{4,3,0,1,2:T(8,128)(2,1)} %bitcast.46) | data formatting | bytes 8388608 | tf_op jit(solution)/shard_map/transpose | solution.py:67
  157.3 0.8 copy-done.3
  158.1 5.7 %convolution_convert_fusion = bf16[1024,1024]{1,0:T(8,128)(2,1)} fusion(bf16[1024,2048]{1,0:T(8,128)(2,1)S(1)} %bitcast.47, bf16[2048,1024]{1,0:T(8,128)(2,1)S(1)} %copy-done.3), kind=kOutput, calls=%fused_computation.9 | convolution fusion | flops 4296015872 | bytes 10485760 | tf_op jit(solution)/shard_map/dot_general | solution.py:69
  163.8 45.2 %reduce-scatter.2.cloned.1.call-done = bf16[256,1024]{1,0:T(8,128)(2,1)} async-done(((bf16[1024,1024]{1,0:T(8,128)(2,1)}), bf16[256,1024]{1,0:T(8,128)(2,1)}) %reduce-scatter.2.cloned.1.call-update) | async-done | bytes 524304 | tf_op jit(solution)/shard_map/reduce_scatter | solution.py:68
  209.0 13.4 %all_to_all.29 = bf16[8,32,1024]{2,1,0:T(8,128)(2,1)S(1)} all-to-all(bf16[8,32,1024]{2,1,0:T(8,128)(2,1)} %bitcast.50), channel_id=1, replica_groups=mesh['hi'=4,'lo'=2,'chan'=4] {'hi','lo'}, dimensions={0} | all-to-all | bytes 1048576 | tf_op jit(solution)/shard_map/all_to_all | solution.py:75
  222.4 0.3 copy.34
  222.7 0.4 all_to_all.25
  223.1 0.3 copy.35
  223.4 16.6 %all_to_all.30 = bf16[32,4,2048]{2,0,1:T(8,128)(2,1)S(1)} all-to-all(bf16[32,4,2048]{2,0,1:T(8,128)(2,1)S(1)} %copy.35), channel_id=1, replica_groups=mesh['hi'=4,'lo'=2,'chan'=4] {'chan'}, dimensions={1} | all-to-all | bytes 1048576 | tf_op jit(solution)/shard_map/all_to_all | solution.py:74
  240.1 0.9 fusion.16
  (17 shorter events, 0.2 us)
Async XLA Ops:
  6.5 84.6 %copy-start = (bf16[128,2048]{1,0:T(8,128)(2,1)S(1)}, bf16[128,2048]{1,0:T(8,128)(2,1)}, u32[]{:S(2)}) copy-start(bf16[128,2048]{1,0:T(8,128)(2,1)} %param.6) | copy-start | bytes 1572868
  6.5 59.2 %all-gather.5.cloned.1.call-start = ((), (), s32[]{:S(2)}) async-start(), calls=%async_computation.3 | async-start | bytes 5242880 | tf_op jit(solution)/shard_map/all_gather | solution.py:24
  7.9 57.9 %copy-start.2 = (s32[1024]{0:T(1024)S(1)}, s32[1024]{0:T(1024)}, u32[]{:S(2)}) copy-start(s32[1024]{0:T(1024)} %constant.24.clone) | copy-start | bytes 12292
  10.3 76.9 %all-gather.7.cloned.1.call-start = ((), (), s32[]{:S(2)}) async-start(), calls=%async_computation.4 | async-start | bytes 12582912 | tf_op jit(solution)/shard_map/all_gather | solution.py:24
  65.8 73.8 %all-gather.9.cloned.1.call-start = ((), (), s32[]{:S(2)}) async-start(), calls=%async_computation.5 | async-start | bytes 2621440 | tf_op jit(solution)/shard_map/all_gather | solution.py:24
  102.9 51.7 %all-gather.11.cloned.1.call-start = ((), (), s32[]{:S(2)}) async-start(), calls=%async_computation.6 | async-start | bytes 6291456 | tf_op jit(solution)/shard_map/all_gather | solution.py:24
  139.5 69.5 %reduce-scatter.2.cloned.1.call-start = ((), (), s32[]{:S(2)}) async-start(), calls=%async_computation.7 | async-start | bytes 2621440 | tf_op jit(solution)/shard_map/reduce_scatter | solution.py:68
  154.6 3.4 %copy-start.3 = (bf16[2048,1024]{1,0:T(8,128)(2,1)S(1)}, bf16[2048,1024]{1,0:T(8,128)(2,1)}, u32[]{:S(2)}) copy-start(bf16[2048,1024]{1,0:T(8,128)(2,1)} %param.10) | copy-start | bytes 12582916
  163.8 76.3 %copy-start.1 = (bf16[128,2048]{1,0:T(8,128)(2,1)S(1)}, bf16[128,2048]{1,0:T(8,128)(2,1)}, u32[]{:S(2)}) copy-start(bf16[128,2048]{1,0:T(8,128)(2,1)} %param.9) | copy-start | bytes 1572868
Sparse Core Ops, SparseCore 0:
  10.4 55.2 all-gather.4
  67.3 19.8 all-gather.6
  103.0 36.4 all-gather.8
  140.9 13.6 all-gather.10
  164.0 45.0 reduce-scatter.1

commit v2 on v1

v2 whole, which is shorter than its diff:
```python
import math

import jax
import jax.numpy as jnp
import numpy as np
from jax import lax
from jax.sharding import Mesh
from jax.sharding import PartitionSpec as P

HEAD_DIM = 128
SEQ = ("hi", "lo")


def cores_per_chip_along_seq(mesh):
    column = mesh.devices[:, 0]
    first = tuple(column[0].coords)
    count = 1
    while count < len(column) and tuple(column[count].coords) == first:
        count += 1
    return count


def is_square_of_chips(mesh, n_lo):
    column = mesh.devices[::n_lo, 0]
    if n_lo != 2 or len(column) != 4:
        return False
    coords = [np.array(d.coords) for d in column]
    for i in range(4):
        for flip in (1, 2):
            if np.abs(coords[i] - coords[i ^ flip]).sum() != 1:
                return False
    return True


def swap(axis, flip, n):
    return [(i, i ^ flip) for i in range(n)]


def assemble(pieces, rows, width, dtype):
    out = jnp.zeros((len(pieces) * rows, width), dtype)
    for piece, slot in pieces:
        out = lax.dynamic_update_slice(out, piece, (slot * rows, 0))
    return out


def gather_seq_square(x):
    rows, width = x.shape
    half = rows // 2
    chip = lax.axis_index("hi")
    core = lax.axis_index("lo")
    from_x = lax.ppermute(x, "hi", swap("hi", 1, 4))
    from_y = lax.ppermute(x, "hi", swap("hi", 2, 4))
    diag = jnp.concatenate(
        [
            lax.ppermute(from_y[:half], "hi", swap("hi", 1, 4)),
            lax.ppermute(from_x[half:], "hi", swap("hi", 2, 4)),
        ],
        axis=0,
    )
    mine = [(x, chip), (from_x, chip ^ 1), (from_y, chip ^ 2), (diag, chip ^ 3)]
    pieces = []
    for block, source in mine:
        pieces.append((block, source * 2 + core))
        pieces.append((lax.ppermute(block, "lo", [(0, 1), (1, 0)]), source * 2 + (1 - core)))
    return assemble(pieces, rows, width, x.dtype)


def make_per_device(square):
    def gather_seq(x):
        if square:
            return gather_seq_square(x)
        return lax.all_gather(x, SEQ, axis=0, tiled=True)

    def per_device(query_proj, key_proj, value_proj, residual, out_weight):
        seg_rows = query_proj.shape[0]
        feat_width = query_proj.shape[1]
        heads_here = feat_width // HEAD_DIM
        seq_count = lax.axis_size("hi") * lax.axis_size("lo")
        chan_count = lax.axis_size("chan")
        segment = lax.axis_index("hi") * lax.axis_size("lo") + lax.axis_index("lo")
        score_scale = 1.0 / math.sqrt(HEAD_DIM)

        both = gather_seq(jnp.concatenate([key_proj, value_proj], axis=1))
        total_rows = both.shape[0]
        keys = both[:, :feat_width].reshape(total_rows, heads_here, HEAD_DIM)
        values = both[:, feat_width:].reshape(total_rows, heads_here, HEAD_DIM)
        key_pos = jnp.arange(total_rows, dtype=jnp.int32)
        row_pos = segment * seg_rows + jnp.arange(seg_rows, dtype=jnp.int32)
        queries = query_proj.reshape(seg_rows, heads_here, HEAD_DIM)
        scores = (
            jnp.einsum("qhd,khd->hqk", queries, keys, preferred_element_type=jnp.float32)
            * score_scale
        )
        allowed = (key_pos[None, :] <= row_pos[:, None])[None]
        scores = jnp.where(allowed, scores, -1e30)
        row_max = jnp.max(scores, axis=-1)
        weights = jnp.where(allowed, jnp.exp(scores - row_max[..., None]), 0.0)
        row_total = jnp.sum(weights, axis=-1)
        numer = jnp.einsum(
            "hqk,khd->hqd", weights.astype(jnp.bfloat16), values, preferred_element_type=jnp.float32
        )
        ratio = numer / row_total[..., None]
        local_context = ratio.transpose(1, 0, 2).reshape(seg_rows, feat_width).astype(jnp.bfloat16)

        gathered = gather_seq(local_context)
        sub_rows = seg_rows // chan_count
        grid = gathered.reshape(seq_count, chan_count, sub_rows, feat_width)
        block_tokens = seq_count * sub_rows
        rows = grid.transpose(1, 0, 2, 3).reshape(block_tokens * chan_count, feat_width)
        partial_sums = lax.psum_scatter(
            jnp.dot(rows, out_weight, preferred_element_type=jnp.float32).astype(jnp.bfloat16),
            "chan",
            scatter_dimension=0,
            tiled=True,
        ).astype(jnp.float32)
        relaid = lax.all_to_all(
            lax.all_to_all(
                partial_sums.astype(jnp.bfloat16), SEQ, split_axis=0, concat_axis=1, tiled=True
            ),
            "chan",
            split_axis=1,
            concat_axis=0,
            tiled=True,
        ).astype(partial_sums.dtype)
        return (residual.astype(jnp.float32) + relaid).astype(jnp.bfloat16)

    return per_device


def solution(mesh):
    seq_size, chan_size = mesh.devices.shape
    n_lo = cores_per_chip_along_seq(mesh)
    split = Mesh(
        mesh.devices.reshape(seq_size // n_lo, n_lo, chan_size), ("hi", "lo", mesh.axis_names[1])
    )
    rows_cols = P(SEQ, "chan")
    placed = (rows_cols, rows_cols, rows_cols, rows_cols, P("chan", SEQ))
    return jax.shard_map(
        make_per_device(is_square_of_chips(mesh, n_lo)),
        mesh=split,
        in_specs=placed,
        out_specs=rows_cols,
        check_vma=False,
    )
```

time: 248 us -> 206 us (0.83)
  waiting for transfers between devices: 173 us -> 93.8 us
  local copies, waits for them, and re-layouts: 12.1 us -> 34.1 us
  starting transfers between devices: 0.16 us -> 12.8 us
    all_gather x4 -> x0, waiting for transfers between devices: 128 us -> none  [the longest x2 92 us: gather_seq(): lax.all_gather(x, 'hi', axis=0, tiled=True)]
    ppermute x0 -> x16, waiting for transfers between devices: none -> 49.9 us  [the longest x2 22 us: gather_seq_square(): from_x = lax.ppermute(x, 'hi', swap('hi', 1, 4))]
    ppermute x0 -> x16, starting transfers between devices: none -> 12.8 us  [the longest x2 4.46 us: gather_seq_square(): from_x = lax.ppermute(x, 'hi', swap('hi', 1, 4))]
    dynamic_update_slice x0 -> x14, local copies, waits for them, and re-layouts: none -> 12.2 us  [assemble(): out = lax.dynamic_update_slice(out, piece, (slot * rows, 0))]
    broadcast_in_dim x0 -> x2, local copies, waits for them, and re-layouts: none -> 4.83 us  [assemble(): out = jnp.zeros((len(pieces) * rows, width), dtype)]
    ppermute x0 -> x2, local copies, waits for them, and re-layouts: none -> 3.91 us  [the longest x1 2.4 us: gather_seq_square(): lax.ppermute(from_y[:half], 'hi', swap('hi', 1, 4))]
    slice x0 -> x5, local copies, waits for them, and re-layouts: none -> 3.07 us  [the longest x3 1.93 us: gather_seq_square(): from_x[half:]]
  transfers between devices with their start and end apart: 5 -> 17, of which waited for: 5 -> 9; matrix products, arithmetic and copies ran while one was open for 0% -> 8% of each run, Pallas kernels for 0% -> 0%
where the time goes in v2:
time: 206 us; the launch traced here: 205 us
  waiting for transfers between devices  93.8 us (46%)
  local copies, waits for them, and re-layouts  34.1 us (17%)
  blocking collectives  30.1 us (15%)
  between operations  13.6 us (7%)
  starting transfers between devices  12.8 us (6%)
  matrix products  10.6 us (5%)
  other arithmetic  10 us (5%)
    reduce_scatter x1, waiting for transfers between devices, per_device(): lax.psum_scatter(jnp.dot(rows, out_weight, preferred_element_type=jnp.flo...  43.9 us
    ppermute x2, waiting for transfers between devices, gather_seq_square(): from_x = lax.ppermute(x, 'hi', swap('hi', 1, 4))  22 us
    all_to_all x1, blocking collectives, per_device(): lax.all_to_all(lax.all_to_all(partial_sums.astype(jnp.bfloat16), SEQ, spl...  16.7 us
    all_to_all x1, blocking collectives, per_device(): lax.all_to_all(partial_sums.astype(jnp.bfloat16), SEQ, split_axis=0, conc...  13.4 us
    dynamic_update_slice x14, local copies, waits for them, and re-layouts, assemble(): out = lax.dynamic_update_slice(out, piece, (slot * rows, 0))  12.2 us
    ppermute x2, waiting for transfers between devices, gather_seq_square(): from_y = lax.ppermute(x, 'hi', swap('hi', 2, 4))  11.3 us
    ppermute x2, waiting for transfers between devices, gather_seq_square(): lax.ppermute(from_x[half:], 'hi', swap('hi', 2, 4))  6.62 us
    ppermute x2, waiting for transfers between devices, gather_seq_square(): lax.ppermute(from_y[:half], 'hi', swap('hi', 1, 4))  5.88 us
  transfers between devices with their start and end apart: 17, of which 9 were waited for; matrix products, arithmetic and copies ran while one was open for 8% of the time, Pallas kernels for 0%

profile of v2, /device:TPU:0, one launch (start us, length us, event | category | flops | bytes accessed | tf_op | source)
XLA Modules:
  0.0 204.9 jit_solution(9363554237750222493)
XLA Ops:
  9.2 4.3 %broadcast_in_dim.31 = bf16[1024,4096]{0,1:T(8,128)(2,1)} broadcast(bf16[]{:T(256)} %constant.14.clone.1), dimensions={} | broadcast | bytes 8388610 | tf_op jit(solution)/shard_map/broadcast_in_dim | solution.py:40
  15.1 2.9 %collective-permute-start.1 = (bf16[128,4096]{0,1:T(8,128)(2,1)}, bf16[128,4096]{0,1:T(8,128)(2,1)}, u32[]{:S(2)}, u32[]{:S(2)}) collective-permute-start(bf16[128,4096]{0,1:T(8,128)(2,1)} %get-tuple-element.9), channel_id=1, source_target_pairs={{0,8},{8,0},{16,24},{24,16},{1,9},{9,1},{17,25},{25,17},{2,10},{10... | collective-permute-start | bytes 3145736 | tf_op jit(solution)/shard_map/ppermute | solution.py:51
  19.5 22.0 %collective-permute-done.1 = bf16[128,4096]{0,1:T(8,128)(2,1)} collective-permute-done((bf16[128,4096]{0,1:T(8,128)(2,1)}, bf16[128,4096]{0,1:T(8,128)(2,1)}, u32[]{:S(2)}, u32[]{:S(2)}) %collective-permute-start.1) | collective-permute-done | bytes 1048608 | tf_op jit(solution)/shard_map/ppermute | solution.py:51
  41.5 1.6 slice.25
  43.4 1.9 collective-permute-start.6
  47.9 2.4 %constant_dynamic-update-slice_fusion.16 = bf16[1024,4096]{0,1:T(8,128)(2,1)} fusion(bf16[1024,4096]{0,1:T(8,128)(2,1)} %get-tuple-element.10, bf16[128,4096]{0,1:T(8,128)(2,1)} %collective-permute-done, s32[]{:T(128)S(6)} %select_n.40), kind=kLoop, calls=%fused_computation.37 | loop fusion | bytes 2097156 | tf_op jit(solution)/shard_map/dynamic_update_slice | solution.py:42
  50.2 2.4 %constant_dynamic-update-slice_fusion.15 = bf16[1024,4096]{0,1:T(8,128)(2,1)} fusion(bf16[1024,4096]{0,1:T(8,128)(2,1)} %constant_dynamic-update-slice_fusion.16, bf16[128,4096]{0,1:T(8,128)(2,1)} %collective-permute-done.1, s32[]{:T(128)S(6)} %select_n.41), kind=kLoop, calls=%fused_computation.36 | loop fusion | bytes 2097156 | tf_op jit(solution)/shard_map/dynamic_update_slice | solution.py:42
  52.6 5.4 %collective-permute-done.6 = bf16[64,4096]{1,0:T(8,128)(2,1)} collective-permute-done((bf16[64,4096]{1,0:T(8,128)(2,1)S(1)}, bf16[64,4096]{1,0:T(8,128)(2,1)}, u32[]{:S(2)}, u32[]{:S(2)}) %collective-permute-start.6) | collective-permute-done | bytes 524320 | tf_op jit(solution)/shard_map/ppermute | solution.py:56
  60.8 2.4 %copy.43 = bf16[64,4096]{0,1:T(8,128)(2,1)} copy(bf16[64,4096]{1,0:T(8,128)(2,1)} %collective-permute-done.5) | data formatting | bytes 1048576 | tf_op jit(solution)/shard_map/ppermute | solution.py:55
  63.2 2.4 %constant_dynamic-update-slice_fusion.14 = bf16[1024,4096]{0,1:T(8,128)(2,1)} fusion(bf16[1024,4096]{0,1:T(8,128)(2,1)} %constant_dynamic-update-slice_fusion.15, bf16[128,4096]{0,1:T(8,128)(2,1)} %collective-permute-done.2, s32[]{:T(128)S(6)} %select_n.42), kind=kLoop, calls=%fused_computation.35 | loop fusion | bytes 2097156 | tf_op jit(solution)/shard_map/dynamic_update_slice | solution.py:42
  66.7 2.4 %constant_dynamic-update-slice_fusion.12 = bf16[1024,4096]{0,1:T(8,128)(2,1)} fusion(bf16[1024,4096]{0,1:T(8,128)(2,1)} %constant_dynamic-update-slice_fusion.13, bf16[128,4096]{0,1:T(8,128)(2,1)} %collective-permute-done.4, s32[]{:T(128)S(6)} %select_n.44), kind=kLoop, calls=%fused_computation.33 | loop fusion | bytes 2097156 | tf_op jit(solution)/shard_map/dynamic_update_slice | solution.py:42
  69.1 1.6 constant_dynamic-update-slice_fusion.11
  70.8 2.6 %collective-permute-done.7 = bf16[128,4096]{0,1:T(8,128)(2,1)S(1)} collective-permute-done((bf16[128,4096]{0,1:T(8,128)(2,1)S(1)}, bf16[128,4096]{0,1:T(8,128)(2,1)S(1)}, u32[]{:S(2)}, u32[]{:S(2)}) %collective-permute-start.7) | collective-permute-done | bytes 1048608 | tf_op jit(solution)/shard_map/ppermute | solution.py:64
  74.5 3.9 %fusion.22 = (bf16[1024,2048]{0,1:T(8,128)(2,1)S(1)}, bf16[1024,2048]{0,1:T(8,128)(2,1)S(1)}) fusion(bf16[1024,4096]{0,1:T(8,128)(2,1)} %constant_dynamic-update-slice_fusion.10), kind=kLoop, calls=%fused_computation.42 | loop fusion | bytes 16777216 | tf_op jit(solution)/shard_map/slice | solution.py:85
  79.8 5.8 %fusion.23 = (f32[16,128]{1,0:T(8,128)S(1)}, bf16[16,128,1024]{1,2,0:T(8,128)(2,1)}) fusion(f32[16,1024,128]{2,1,0:T(8,128)S(1)} %fusion.17, pred[128,1024]{0,1:T(8,128)(4,1)S(1)} %iota_compare_fusion), kind=kOutput, calls=%fused_computation.43 | output fusion | flops 16778240 | bytes 12722176 | tf_op jit(solution)/shard_map/sub | solution.py:97
  85.6 3.5 %fusion.13 = bf16[128,16,128]{0,2,1:T(8,128)(2,1)S(1)} fusion(bf16[1024,16,128]{0,2,1:T(8,128)(2,1)S(1)} %bitcast.50, bf16[16,128,1024]{1,2,0:T(8,128)(2,1)} %get-tuple-element.12, f32[128,16]{0,1:T(8,128)S(1)} %bitcast.54), kind=kOutput, calls=%fused_computation.12 | convolution fusion | flops 537395200 | bytes 8921088 | tf_op jit(solution)/shard_map/hqk,khd->hqd/dot_general | solution.py:99
  92.1 11.2 %collective-permute-done.11 = bf16[128,2048]{1,0:T(8,128)(2,1)S(1)} collective-permute-done((bf16[128,2048]{1,0:T(8,128)(2,1)S(1)}, bf16[128,2048]{1,0:T(8,128)(2,1)S(1)}, u32[]{:S(2)}, u32[]{:S(2)}) %collective-permute-start.11) | collective-permute-done | bytes 524320 | tf_op jit(solution)/shard_map/ppermute | solution.py:52
  106.3 4.6 %collective-permute-done.13 = bf16[64,2048]{1,0:T(8,128)(2,1)S(1)} collective-permute-done((bf16[64,2048]{1,0:T(8,128)(2,1)S(1)}, bf16[64,2048]{1,0:T(8,128)(2,1)S(1)}, u32[]{:S(2)}, u32[]{:S(2)}) %collective-permute-start.13) | collective-permute-done | bytes 262176 | tf_op jit(solution)/shard_map/ppermute | solution.py:55
  112.6 1.6 collective-permute-done.15
  114.9 1.6 copy-done.4
  116.5 5.7 %convolution_convert_fusion = bf16[1024,1024]{1,0:T(8,128)(2,1)} fusion(bf16[1024,2048]{1,0:T(8,128)(2,1)S(1)} %bitcast.49, bf16[2048,1024]{1,0:T(8,128)(2,1)S(1)} %copy-done.4), kind=kOutput, calls=%fused_computation.9 | convolution fusion | flops 4296015872 | bytes 10485760 | tf_op jit(solution)/shard_map/dot_general | solution.py:111
  122.2 43.9 %reduce-scatter.2.cloned.1.call-done = bf16[256,1024]{1,0:T(8,128)(2,1)} async-done(((bf16[1024,1024]{1,0:T(8,128)(2,1)}), bf16[256,1024]{1,0:T(8,128)(2,1)}) %reduce-scatter.2.cloned.1.call-update) | async-done | bytes 524304 | tf_op jit(solution)/shard_map/reduce_scatter | solution.py:110
  166.1 13.4 %all_to_all.29 = bf16[8,32,1024]{2,1,0:T(8,128)(2,1)S(1)} all-to-all(bf16[8,32,1024]{2,1,0:T(8,128)(2,1)} %bitcast.52), channel_id=1, replica_groups=mesh['hi'=4,'lo'=2,'chan'=4] {'hi','lo'}, dimensions={0} | all-to-all | bytes 1048576 | tf_op jit(solution)/shard_map/all_to_all | solution.py:117
  180.5 16.7 %all_to_all.30 = bf16[32,4,2048]{2,0,1:T(8,128)(2,1)S(1)} all-to-all(bf16[32,4,2048]{2,0,1:T(8,128)(2,1)S(1)} %copy.54), channel_id=1, replica_groups=mesh['hi'=4,'lo'=2,'chan'=4] {'chan'}, dimensions={1} | all-to-all | bytes 1048576 | tf_op jit(solution)/shard_map/all_to_all | solution.py:116
  (65 shorter events, 25.2 us)
Async XLA Ops:
  6.5 71.9 %copy-start = (bf16[128,2048]{1,0:T(8,128)(2,1)S(1)}, bf16[128,2048]{1,0:T(8,128)(2,1)}, u32[]{:S(2)}) copy-start(bf16[128,2048]{1,0:T(8,128)(2,1)} %param.5) | copy-start | bytes 1572868
  6.5 159.6 %reduce-scatter.2.cloned.1.call-start = ((), (), s32[]{:S(2)}) async-start(), calls=%async_computation.3 | async-start | bytes 2621440 | tf_op jit(solution)/shard_map/reduce_scatter | solution.py:110
  15.1 26.4 %collective-permute-start.1 = (bf16[128,4096]{0,1:T(8,128)(2,1)}, bf16[128,4096]{0,1:T(8,128)(2,1)}, u32[]{:S(2)}, u32[]{:S(2)}) collective-permute-start(bf16[128,4096]{0,1:T(8,128)(2,1)} %get-tuple-element.9), channel_id=1, source_target_pairs={{0,8},{8,0},{16,24},{24,16},{1,9},{9,1},{17,25},{25,17},{2,10},{10... | collective-permute-start | bytes 3145736 | tf_op jit(solution)/shard_map/ppermute | solution.py:51
  18.0 27.2 %collective-permute-start.3 = (bf16[128,4096]{0,1:T(8,128)(2,1)}, bf16[128,4096]{0,1:T(8,128)(2,1)S(1)}, u32[]{:S(2)}, u32[]{:S(2)}) collective-permute-start(bf16[128,4096]{0,1:T(8,128)(2,1)} %get-tuple-element.9), channel_id=1, source_target_pairs={{0,16},{8,24},{16,0},{24,8},{1,17},{9,25},{17,1},{25,9},{2,18},{10... | collective-permute-start | bytes 3145736 | tf_op jit(solution)/shard_map/ppermute | solution.py:52
  19.5 28.3 %collective-permute-start = (bf16[128,4096]{0,1:T(8,128)(2,1)}, bf16[128,4096]{0,1:T(8,128)(2,1)}, u32[]{:S(2)}, u32[]{:S(2)}) collective-permute-start(bf16[128,4096]{0,1:T(8,128)(2,1)} %get-tuple-element.9), channel_id=1, source_target_pairs={{0,4},{4,0},{1,5},{5,1},{2,6},{6,2},{3,7},{7,3},{8,12},{12,8},{9,1... | collective-permute-start | bytes 3145736 | tf_op jit(solution)/shard_map/ppermute | solution.py:64
  41.5 21.7 %collective-permute-start.2 = (bf16[128,4096]{0,1:T(8,128)(2,1)}, bf16[128,4096]{0,1:T(8,128)(2,1)}, u32[]{:S(2)}, u32[]{:S(2)}) collective-permute-start(bf16[128,4096]{0,1:T(8,128)(2,1)} %collective-permute-done.1), channel_id=1, source_target_pairs={{0,4},{4,0},{1,5},{5,1},{2,6},{6,2},{3,7},{7,3},{8,12},{12,8},{9,1... | collective-permute-start | bytes 3145736 | tf_op jit(solution)/shard_map/ppermute | solution.py:64
  43.4 14.6 %collective-permute-start.6 = (bf16[64,4096]{1,0:T(8,128)(2,1)S(1)}, bf16[64,4096]{1,0:T(8,128)(2,1)}, u32[]{:S(2)}, u32[]{:S(2)}) collective-permute-start(bf16[64,4096]{1,0:T(8,128)(2,1)S(1)} %copy.42), channel_id=1, source_target_pairs={{0,16},{8,24},{16,0},{24,8},{1,17},{9,25},{17,1},{25,9},{2,18},{10... | collective-permute-start | bytes 1572872 | tf_op jit(solution)/shard_map/ppermute | solution.py:56
  46.4 14.4 %collective-permute-start.5 = (bf16[64,4096]{1,0:T(8,128)(2,1)}, bf16[64,4096]{1,0:T(8,128)(2,1)}, u32[]{:S(2)}, u32[]{:S(2)}) collective-permute-start(bf16[64,4096]{1,0:T(8,128)(2,1)} %copy.41), channel_id=1, source_target_pairs={{0,8},{8,0},{16,24},{24,16},{1,9},{9,1},{17,25},{25,17},{2,10},{10... | collective-permute-start | bytes 1572872 | tf_op jit(solution)/shard_map/ppermute | solution.py:55
  47.9 18.8 %collective-permute-start.4 = (bf16[128,4096]{0,1:T(8,128)(2,1)S(1)}, bf16[128,4096]{0,1:T(8,128)(2,1)}, u32[]{:S(2)}, u32[]{:S(2)}) collective-permute-start(bf16[128,4096]{0,1:T(8,128)(2,1)S(1)} %collective-permute-done.3), channel_id=1, source_target_pairs={{0,4},{4,0},{1,5},{5,1},{2,6},{6,2},{3,7},{7,3},{8,12},{12,8},{9,1... | collective-permute-start | bytes 3145736 | tf_op jit(solution)/shard_map/ppermute | solution.py:64
  63.2 5.9 %copy-start.2 = (bf16[64,4096]{0,1:T(8,128)(2,1)S(1)}, bf16[64,4096]{0,1:T(8,128)(2,1)}, u32[]{:S(2)}) copy-start(bf16[64,4096]{0,1:T(8,128)(2,1)} %copy.43) | copy-start | bytes 1572868
  70.7 2.7 %collective-permute-start.7 = (bf16[128,4096]{0,1:T(8,128)(2,1)S(1)}, bf16[128,4096]{0,1:T(8,128)(2,1)S(1)}, u32[]{:S(2)}, u32[]{:S(2)}) collective-permute-start(bf16[128,4096]{0,1:T(8,128)(2,1)S(1)} %get-tuple-element.6), channel_id=1, source_target_pairs={{0,4},{4,0},{1,5},{5,1},{2,6},{6,2},{3,7},{7,3},{8,12},{12,8},{9,1... | collective-permute-start | bytes 3145736 | tf_op jit(solution)/shard_map/ppermute | solution.py:64
  89.3 14.0 %collective-permute-start.11 = (bf16[128,2048]{1,0:T(8,128)(2,1)S(1)}, bf16[128,2048]{1,0:T(8,128)(2,1)S(1)}, u32[]{:S(2)}, u32[]{:S(2)}) collective-permute-start(bf16[128,2048]{1,0:T(8,128)(2,1)S(1)} %copy.48), channel_id=1, source_target_pairs={{0,16},{8,24},{16,0},{24,8},{1,17},{9,25},{17,1},{25,9},{2,18},{10... | collective-permute-start | bytes 1572872 | tf_op jit(solution)/shard_map/ppermute | solution.py:52
  90.0 15.0 %collective-permute-start.9 = (bf16[128,2048]{1,0:T(8,128)(2,1)S(1)}, bf16[128,2048]{1,0:T(8,128)(2,1)S(1)}, u32[]{:S(2)}, u32[]{:S(2)}) collective-permute-start(bf16[128,2048]{1,0:T(8,128)(2,1)S(1)} %copy.48), channel_id=1, source_target_pairs={{0,8},{8,0},{16,24},{24,16},{1,9},{9,1},{17,25},{25,17},{2,10},{10... | collective-permute-start | bytes 1572872 | tf_op jit(solution)/shard_map/ppermute | solution.py:51
  91.5 14.7 %collective-permute-start.8 = (bf16[128,2048]{1,0:T(8,128)(2,1)S(1)}, bf16[128,2048]{1,0:T(8,128)(2,1)S(1)}, u32[]{:S(2)}, u32[]{:S(2)}) collective-permute-start(bf16[128,2048]{1,0:T(8,128)(2,1)S(1)} %copy.48), channel_id=1, source_target_pairs={{0,4},{4,0},{1,5},{5,1},{2,6},{6,2},{3,7},{7,3},{8,12},{12,8},{9,1... | collective-permute-start | bytes 1572872 | tf_op jit(solution)/shard_map/ppermute | solution.py:64
  103.4 7.6 %collective-permute-start.13 = (bf16[64,2048]{1,0:T(8,128)(2,1)S(1)}, bf16[64,2048]{1,0:T(8,128)(2,1)S(1)}, u32[]{:S(2)}, u32[]{:S(2)}) collective-permute-start(bf16[64,2048]{1,0:T(8,128)(2,1)S(1)} %slice.28), channel_id=1, source_target_pairs={{0,8},{8,0},{16,24},{24,16},{1,9},{9,1},{17,25},{25,17},{2,10},{10... | collective-permute-start | bytes 786440 | tf_op jit(solution)/shard_map/ppermute | solution.py:55
  105.0 7.2 %collective-permute-start.14 = (bf16[64,2048]{1,0:T(8,128)(2,1)S(1)}, bf16[64,2048]{1,0:T(8,128)(2,1)S(1)}, u32[]{:S(2)}, u32[]{:S(2)}) collective-permute-start(bf16[64,2048]{1,0:T(8,128)(2,1)S(1)} %slice.29), channel_id=1, source_target_pairs={{0,16},{8,24},{16,0},{24,8},{1,17},{9,25},{17,1},{25,9},{2,18},{10... | collective-permute-start | bytes 786440 | tf_op jit(solution)/shard_map/ppermute | solution.py:56
  105.7 6.6 %collective-permute-start.10 = (bf16[128,2048]{1,0:T(8,128)(2,1)S(1)}, bf16[128,2048]{1,0:T(8,128)(2,1)S(1)}, u32[]{:S(2)}, u32[]{:S(2)}) collective-permute-start(bf16[128,2048]{1,0:T(8,128)(2,1)S(1)} %collective-permute-done.9), channel_id=1, source_target_pairs={{0,4},{4,0},{1,5},{5,1},{2,6},{6,2},{3,7},{7,3},{8,12},{12,8},{9,1... | collective-permute-start | bytes 1572872 | tf_op jit(solution)/shard_map/ppermute | solution.py:64
  105.7 6.8 %collective-permute-start.12 = (bf16[128,2048]{1,0:T(8,128)(2,1)S(1)}, bf16[128,2048]{1,0:T(8,128)(2,1)S(1)}, u32[]{:S(2)}, u32[]{:S(2)}) collective-permute-start(bf16[128,2048]{1,0:T(8,128)(2,1)S(1)} %collective-permute-done.11), channel_id=1, source_target_pairs={{0,4},{4,0},{1,5},{5,1},{2,6},{6,2},{3,7},{7,3},{8,12},{12,8},{9,1... | collective-permute-start | bytes 1572872 | tf_op jit(solution)/shard_map/ppermute | solution.py:64
  112.2 2.0 collective-permute-start.15
  114.3 2.2 %copy-start.4 = (bf16[2048,1024]{1,0:T(8,128)(2,1)S(1)}, bf16[2048,1024]{1,0:T(8,128)(2,1)}, u32[]{:S(2)}) copy-start(bf16[2048,1024]{1,0:T(8,128)(2,1)} %param.9) | copy-start | bytes 12582916
  122.2 75.0 %copy-start.3 = (bf16[128,2048]{1,0:T(8,128)(2,1)S(1)}, bf16[128,2048]{1,0:T(8,128)(2,1)}, u32[]{:S(2)}) copy-start(bf16[128,2048]{1,0:T(8,128)(2,1)} %param.8) | copy-start | bytes 1572868
  122.2 75.9 %copy-start.1 = (bf16[128,2048]{1,0:T(8,128)(2,1)S(1)}, bf16[128,2048]{1,0:T(8,128)(2,1)}, u32[]{:S(2)}) copy-start(bf16[128,2048]{1,0:T(8,128)(2,1)} %param.5) | copy-start | bytes 1572868
Sparse Core Ops, SparseCore 0:
  122.4 43.7 reduce-scatter.1

commit v3 on v1

v3 whole, which is shorter than its diff:
```python
import math

import jax
import jax.numpy as jnp
import numpy as np
from jax import lax
from jax.sharding import Mesh
from jax.sharding import PartitionSpec as P

HEAD_DIM = 128
SEQ = ("hi", "lo")


def cores_per_chip_along_seq(mesh):
    column = mesh.devices[:, 0]
    first = tuple(column[0].coords)
    count = 1
    while count < len(column) and tuple(column[count].coords) == first:
        count += 1
    return count


def is_square_of_chips(mesh, n_lo):
    column = mesh.devices[::n_lo, 0]
    if n_lo != 2 or len(column) != 4:
        return False
    coords = [np.array(d.coords) for d in column]
    for i in range(4):
        for flip in (1, 2):
            if np.abs(coords[i] - coords[i ^ flip]).sum() != 1:
                return False
    return True


def swap(axis, flip, n):
    return [(i, i ^ flip) for i in range(n)]


def gather_seq_square(x):
    half = x.shape[0] // 2
    from_x = lax.ppermute(x, "hi", swap("hi", 1, 4))
    from_y = lax.ppermute(x, "hi", swap("hi", 2, 4))
    diag = jnp.concatenate(
        [
            lax.ppermute(from_y[:half], "hi", swap("hi", 1, 4)),
            lax.ppermute(from_x[half:], "hi", swap("hi", 2, 4)),
        ],
        axis=0,
    )
    pieces = []
    for block in (x, from_x, from_y, diag):
        pieces.append(block)
        pieces.append(lax.ppermute(block, "lo", [(0, 1), (1, 0)]))
    return jnp.concatenate(pieces, axis=0)


def relative_segments(count):
    block = jnp.arange(count, dtype=jnp.int32)
    chip = lax.axis_index("hi") ^ (block // 2)
    core = lax.axis_index("lo") ^ (block % 2)
    return chip * 2 + core


def attention(query_proj, keys_values, segment, key_segment):
    seg_rows, feat_width = query_proj.shape
    heads_here = feat_width // HEAD_DIM
    total_rows = keys_values.shape[0]
    score_scale = 1.0 / math.sqrt(HEAD_DIM)
    keys = keys_values[:, :feat_width].reshape(total_rows, heads_here, HEAD_DIM)
    values = keys_values[:, feat_width:].reshape(total_rows, heads_here, HEAD_DIM)
    key_pos = (
        key_segment[:, None] * seg_rows + jnp.arange(seg_rows, dtype=jnp.int32)[None, :]
    ).reshape(-1)
    row_pos = segment * seg_rows + jnp.arange(seg_rows, dtype=jnp.int32)
    queries = query_proj.reshape(seg_rows, heads_here, HEAD_DIM)
    scores = (
        jnp.einsum("qhd,khd->hqk", queries, keys, preferred_element_type=jnp.float32) * score_scale
    )
    allowed = (key_pos[None, :] <= row_pos[:, None])[None]
    scores = jnp.where(allowed, scores, -1e30)
    row_max = jnp.max(scores, axis=-1)
    weights = jnp.where(allowed, jnp.exp(scores - row_max[..., None]), 0.0)
    row_total = jnp.sum(weights, axis=-1)
    numer = jnp.einsum(
        "hqk,khd->hqd", weights.astype(jnp.bfloat16), values, preferred_element_type=jnp.float32
    )
    ratio = numer / row_total[..., None]
    return ratio.transpose(1, 0, 2).reshape(seg_rows, feat_width).astype(jnp.bfloat16)


def per_device_square(query_proj, key_proj, value_proj, residual, out_weight):
    seg_rows = query_proj.shape[0]
    chips = lax.axis_size("hi")
    chip = lax.axis_index("hi")
    core = lax.axis_index("lo")
    segment = chip * 2 + core
    both = gather_seq_square(jnp.concatenate([key_proj, value_proj], axis=1))
    local_context = attention(query_proj, both, segment, relative_segments(2 * chips))
    rows = gather_seq_square(local_context)
    reduced = lax.psum_scatter(
        jnp.dot(rows, out_weight, preferred_element_type=jnp.float32).astype(jnp.bfloat16),
        "chan",
        scatter_dimension=0,
        tiled=True,
    )
    chans = lax.axis_size("chan")
    received = []
    for t in range(2):
        pairs = []
        for hi in range(chips):
            for lo in range(2):
                for c in range(chans):
                    pairs.append((((hi * 2) + lo) * chans + c, (((hi ^ c) * 2) + (lo ^ t)) * chans + hi))
        received.append(
            lax.ppermute(reduced[t * seg_rows : (t + 1) * seg_rows], ("hi", "lo", "chan"), pairs)
        )
    ordered = jnp.where(
        core == 0,
        jnp.concatenate(received, axis=1),
        jnp.concatenate(received[::-1], axis=1),
    )
    return (residual.astype(jnp.float32) + ordered.astype(jnp.float32)).astype(jnp.bfloat16)


def per_device_general(query_proj, key_proj, value_proj, residual, out_weight):
    seg_rows = query_proj.shape[0]
    feat_width = query_proj.shape[1]
    seq_count = lax.axis_size("hi") * lax.axis_size("lo")
    chan_count = lax.axis_size("chan")
    segment = lax.axis_index("hi") * lax.axis_size("lo") + lax.axis_index("lo")
    both = lax.all_gather(jnp.concatenate([key_proj, value_proj], axis=1), SEQ, axis=0, tiled=True)
    local_context = attention(
        query_proj, both, segment, jnp.arange(seq_count, dtype=jnp.int32)
    )
    gathered = lax.all_gather(local_context, SEQ, axis=0, tiled=True)
    sub_rows = seg_rows // chan_count
    grid = gathered.reshape(seq_count, chan_count, sub_rows, feat_width)
    rows = grid.transpose(1, 0, 2, 3).reshape(seq_count * sub_rows * chan_count, feat_width)
    partial_sums = lax.psum_scatter(
        jnp.dot(rows, out_weight, preferred_element_type=jnp.float32).astype(jnp.bfloat16),
        "chan",
        scatter_dimension=0,
        tiled=True,
    )
    relaid = lax.all_to_all(
        lax.all_to_all(partial_sums, SEQ, split_axis=0, concat_axis=1, tiled=True),
        "chan",
        split_axis=1,
        concat_axis=0,
        tiled=True,
    )
    return (residual.astype(jnp.float32) + relaid.astype(jnp.float32)).astype(jnp.bfloat16)


def solution(mesh):
    seq_size, chan_size = mesh.devices.shape
    n_lo = cores_per_chip_along_seq(mesh)
    split = Mesh(
        mesh.devices.reshape(seq_size // n_lo, n_lo, chan_size), ("hi", "lo", mesh.axis_names[1])
    )
    rows_cols = P(SEQ, "chan")
    placed = (rows_cols, rows_cols, rows_cols, rows_cols, P("chan", SEQ))
    return jax.shard_map(
        per_device_square
        if is_square_of_chips(mesh, n_lo) and chan_size == 4
        else per_device_general,
        mesh=split,
        in_specs=placed,
        out_specs=rows_cols,
        check_vma=False,
    )
```

time: 248 us -> 228 us (0.919)
  the two profiles are of different devices: /device:TPU:0 before, /device:TPU:3 now
where the time goes in v3:
time: 228 us; the launch traced here: 227 us
  waiting for transfers between devices  137 us (60%)
  local copies, waits for them, and re-layouts  35.1 us (15%)
  starting transfers between devices  16.9 us (7%)
  matrix products  14.3 us (6%)
  between operations  13.5 us (6%)
  other arithmetic  10.2 us (4%)
    reduce_scatter x1, waiting for transfers between devices, per_device_square(): lax.psum_scatter(jnp.dot(rows, out_weight, preferred_element_type=jnp.flo...  44.7 us
    ppermute x2, waiting for transfers between devices, per_device_square(): lax.ppermute(reduced[t * seg_rows:(t + 1) * seg_rows], ('hi', 'lo', 'chan...  36.7 us
    ppermute x2, waiting for transfers between devices, gather_seq_square(): from_x = lax.ppermute(x, 'hi', swap('hi', 1, 4))  35.4 us
    concatenate x2, local copies, waits for them, and re-layouts, gather_seq_square(): return jnp.concatenate(pieces, axis=0)  20.3 us
    ppermute x2, waiting for transfers between devices, gather_seq_square(): lax.ppermute(from_x[half:], 'hi', swap('hi', 2, 4))  14.4 us
    ppermute x8, starting transfers between devices, gather_seq_square(): pieces.append(lax.ppermute(block, 'lo', [(0, 1), (1, 0)]))  10.1 us
    dot_general x1, matrix products, per_device_square(): jnp.dot(rows, out_weight, preferred_element_type=jnp.float32)  9.44 us
    sub x1, other arithmetic, attention(): weights = jnp.where(allowed, jnp.exp(scores - row_max[..., None]), 0.0)  5.84 us
  transfers between devices with their start and end apart: 19, of which 9 were waited for; matrix products, arithmetic and copies ran while one was open for 3% of the time, Pallas kernels for 0%

profile of v3, /device:TPU:3, one launch (start us, length us, event | category | flops | bytes accessed | tf_op | source)
XLA Modules:
  0.0 226.7 jit_solution(17158158425412672395)
XLA Ops:
  10.4 1.5 collective-permute-start.3
  11.9 22.8 %collective-permute-done.1 = bf16[128,4096]{0,1:T(8,128)(2,1)} collective-permute-done((bf16[128,4096]{0,1:T(8,128)(2,1)}, bf16[128,4096]{0,1:T(8,128)(2,1)}, u32[]{:S(2)}, u32[]{:S(2)}) %collective-permute-start.1) | collective-permute-done | bytes 1048608 | tf_op jit(solution)/shard_map/ppermute | solution.py:41
  34.7 1.6 slice.33
  38.0 2.3 %copy.16 = bf16[64,4096]{1,0:T(8,128)(2,1)} copy(bf16[64,4096]{0,1:T(8,128)(2,1)} %bitcast.35) | data formatting | bytes 1048576 | tf_op jit(solution)/shard_map/slice | solution.py:45
  40.6 2.1 collective-permute-start
  43.2 5.4 %collective-permute-done.6 = bf16[64,4096]{1,0:T(8,128)(2,1)S(1)} collective-permute-done((bf16[64,4096]{1,0:T(8,128)(2,1)S(1)}, bf16[64,4096]{1,0:T(8,128)(2,1)S(1)}, u32[]{:S(2)}, u32[]{:S(2)}) %collective-permute-start.6) | collective-permute-done | bytes 524320 | tf_op jit(solution)/shard_map/ppermute | solution.py:46
  49.1 3.0 %collective-permute-done.5 = bf16[64,4096]{1,0:T(8,128)(2,1)S(1)} collective-permute-done((bf16[64,4096]{1,0:T(8,128)(2,1)}, bf16[64,4096]{1,0:T(8,128)(2,1)S(1)}, u32[]{:S(2)}, u32[]{:S(2)}) %collective-permute-start.5) | collective-permute-done | bytes 524320 | tf_op jit(solution)/shard_map/ppermute | solution.py:45
  52.6 1.6 pad_maximum_fusion.1
  54.2 2.7 %collective-permute-start.7 = (bf16[128,4096]{0,1:T(8,128)(2,1)}, bf16[128,4096]{0,1:T(8,128)(2,1)}, u32[]{:S(2)}, u32[]{:S(2)}) collective-permute-start(bf16[128,4096]{0,1:T(8,128)(2,1)} %pad_maximum_fusion.1), channel_id=1, source_target_pairs={{0,4},{4,0},{1,5},{5,1},{2,6},{6,2},{3,7},{7,3},{8,12},{12,8},{9,1... | collective-permute-start | bytes 3145736 | tf_op jit(solution)/shard_map/ppermute | solution.py:53
  57.2 2.3 %collective-permute-done.7 = bf16[128,4096]{0,1:T(8,128)(2,1)} collective-permute-done((bf16[128,4096]{0,1:T(8,128)(2,1)}, bf16[128,4096]{0,1:T(8,128)(2,1)}, u32[]{:S(2)}, u32[]{:S(2)}) %collective-permute-start.7) | collective-permute-done | bytes 1048608 | tf_op jit(solution)/shard_map/ppermute | solution.py:53
  59.5 12.9 %concatenate.25 = bf16[1024,4096]{0,1:T(8,128)(2,1)} concatenate(bf16[128,4096]{0,1:T(8,128)(2,1)} %pad_maximum_fusion, bf16[128,4096]{0,1:T(8,128)(2,1)} %collective-permute-done, bf16[128,4096]{0,1:T(8,128)(2,1)} %collective-permute-done.1, bf16[128,4096]{0,1:T(8,128)(2,1)} %collective-permute-done.2, bf16[128,4096]{0,1:T(8,128)(2,1)} %collective-permute-done.3, ...), dimensions={0} | concatenate | bytes 16777216 | tf_op jit(solution)/shard_map/concatenate | solution.py:54
  72.4 3.9 %fusion.26 = (bf16[1024,2048]{0,1:T(8,128)(2,1)S(1)}, bf16[1024,2048]{0,1:T(8,128)(2,1)S(1)}) fusion(bf16[1024,4096]{0,1:T(8,128)(2,1)} %concatenate.25), kind=kLoop, calls=%fused_computation.36 | loop fusion | bytes 16777216 | tf_op jit(solution)/shard_map/slice | solution.py:69
  77.7 5.8 %fusion.28 = (f32[16,128]{1,0:T(8,128)S(1)}, bf16[16,128,1024]{1,2,0:T(8,128)(2,1)}) fusion(f32[16,1024,128]{2,1,0:T(8,128)S(1)} %fusion.16, pred[128,1024]{0,1:T(8,128)(4,1)S(1)} %broadcast_compare_fusion), kind=kOutput, calls=%fused_computation.38 | output fusion | flops 16778240 | bytes 12722176 | tf_op jit(solution)/shard_map/sub | solution.py:82
  83.6 3.5 %fusion.13 = bf16[128,16,128]{0,2,1:T(8,128)(2,1)S(1)} fusion(bf16[1024,16,128]{0,2,1:T(8,128)(2,1)S(1)} %bitcast.38, bf16[16,128,1024]{1,2,0:T(8,128)(2,1)} %get-tuple-element.10, f32[128,16]{0,1:T(8,128)S(1)} %bitcast.44), kind=kOutput, calls=%fused_computation.12 | convolution fusion | flops 537395200 | bytes 8921088 | tf_op jit(solution)/shard_map/hqk,khd->hqd/dot_general | solution.py:84
  87.7 12.6 %collective-permute-done.9 = bf16[128,2048]{0,1:T(8,128)(2,1)S(1)} collective-permute-done((bf16[128,2048]{0,1:T(8,128)(2,1)S(1)}, bf16[128,2048]{0,1:T(8,128)(2,1)S(1)}, u32[]{:S(2)}, u32[]{:S(2)}) %collective-permute-start.9) | collective-permute-done | bytes 524320 | tf_op jit(solution)/shard_map/ppermute | solution.py:41
  101.4 1.8 collective-permute-start.8
  103.7 9.0 %collective-permute-done.14 = bf16[64,2048]{0,1:T(8,128)(2,1)S(1)} collective-permute-done((bf16[64,2048]{0,1:T(8,128)(2,1)S(1)}, bf16[64,2048]{0,1:T(8,128)(2,1)S(1)}, u32[]{:S(2)}, u32[]{:S(2)}) %collective-permute-start.14) | collective-permute-done | bytes 262176 | tf_op jit(solution)/shard_map/ppermute | solution.py:46
  113.1 2.4 %collective-permute-start.15 = (bf16[128,2048]{0,1:T(8,128)(2,1)S(1)}, bf16[128,2048]{0,1:T(8,128)(2,1)}, u32[]{:S(2)}, u32[]{:S(2)}) collective-permute-start(bf16[128,2048]{0,1:T(8,128)(2,1)S(1)} %pad_maximum_fusion.2), channel_id=1, source_target_pairs={{0,4},{4,0},{1,5},{5,1},{2,6},{6,2},{3,7},{7,3},{8,12},{12,8},{9,1... | collective-permute-start | bytes 1572872 | tf_op jit(solution)/shard_map/ppermute | solution.py:53
  117.3 7.4 %concatenate.27 = bf16[1024,2048]{0,1:T(8,128)(2,1)} concatenate(bf16[128,2048]{0,1:T(8,128)(2,1)S(1)} %bitcast.42, bf16[128,2048]{0,1:T(8,128)(2,1)} %copy-done.1, bf16[128,2048]{0,1:T(8,128)(2,1)S(1)} %collective-permute-done.9, bf16[128,2048]{0,1:T(8,128)(2,1)} %copy-done.2, bf16[128,2048]{0,1:T(8,128)(2,1)S(1)} %collective-permute-done.11, bf16[128,2048]{0,1:T(8,128)(2,1)} %copy-done.3, ...), dimensions={0} | concatenate | bytes 8388608 | tf_op jit(solution)/shard_map/concatenate | solution.py:54
  124.7 9.4 %convolution_convert_fusion = bf16[1024,1024]{1,0:T(8,128)(2,1)} fusion(bf16[1024,2048]{0,1:T(8,128)(2,1)} %concatenate.27, bf16[2048,1024]{1,0:T(8,128)(2,1)} %param.9), kind=kOutput, calls=%fused_computation.9 | convolution fusion | flops 4296015872 | bytes 10485760 | tf_op jit(solution)/shard_map/dot_general | solution.py:101
  134.1 44.7 %reduce-scatter.2.cloned.1.call-done = bf16[256,1024]{1,0:T(8,128)(2,1)} async-done(((bf16[1024,1024]{1,0:T(8,128)(2,1)}), bf16[256,1024]{1,0:T(8,128)(2,1)}) %reduce-scatter.2.cloned.1.call-update) | async-done | bytes 524304 | tf_op jit(solution)/shard_map/reduce_scatter | solution.py:100
  179.9 1.9 collective-permute-start.16
  182.1 30.3 %collective-permute-done.16 = bf16[128,1024]{1,0:T(8,128)(2,1)S(1)} collective-permute-done((bf16[128,1024]{1,0:T(8,128)(2,1)S(1)}, bf16[128,1024]{1,0:T(8,128)(2,1)S(1)}, u32[]{:S(2)}, u32[]{:S(2)}) %collective-permute-start.16) | collective-permute-done | bytes 262176 | tf_op jit(solution)/shard_map/ppermute | solution.py:115
  212.4 6.4 %collective-permute-done.17 = bf16[128,1024]{1,0:T(8,128)(2,1)S(1)} collective-permute-done((bf16[128,1024]{1,0:T(8,128)(2,1)S(1)}, bf16[128,1024]{1,0:T(8,128)(2,1)S(1)}, u32[]{:S(2)}, u32[]{:S(2)}) %collective-permute-start.17) | collective-permute-done | bytes 262176 | tf_op jit(solution)/shard_map/ppermute | solution.py:115
  (49 shorter events, 15.6 us)
Async XLA Ops:
  6.5 69.8 %copy-start = (bf16[128,2048]{1,0:T(8,128)(2,1)S(1)}, bf16[128,2048]{1,0:T(8,128)(2,1)}, u32[]{:S(2)}) copy-start(bf16[128,2048]{1,0:T(8,128)(2,1)} %param.5) | copy-start | bytes 1572868
  6.5 172.3 %reduce-scatter.2.cloned.1.call-start = ((), (), s32[]{:S(2)}) async-start(), calls=%async_computation.1 | async-start | bytes 2621440 | tf_op jit(solution)/shard_map/reduce_scatter | solution.py:100
  10.4 24.3 %collective-permute-start.1 = (bf16[128,4096]{0,1:T(8,128)(2,1)}, bf16[128,4096]{0,1:T(8,128)(2,1)}, u32[]{:S(2)}, u32[]{:S(2)}) collective-permute-start(bf16[128,4096]{0,1:T(8,128)(2,1)} %pad_maximum_fusion), channel_id=1, source_target_pairs={{0,8},{8,0},{16,24},{24,16},{1,9},{9,1},{17,25},{25,17},{2,10},{10... | collective-permute-start | bytes 3145736 | tf_op jit(solution)/shard_map/ppermute | solution.py:41
  10.4 27.6 %collective-permute-start.3 = (bf16[128,4096]{0,1:T(8,128)(2,1)}, bf16[128,4096]{0,1:T(8,128)(2,1)}, u32[]{:S(2)}, u32[]{:S(2)}) collective-permute-start(bf16[128,4096]{0,1:T(8,128)(2,1)} %pad_maximum_fusion), channel_id=1, source_target_pairs={{0,16},{8,24},{16,0},{24,8},{1,17},{9,25},{17,1},{25,9},{2,18},{10... | collective-permute-start | bytes 3145736 | tf_op jit(solution)/shard_map/ppermute | solution.py:42
  36.6 11.9 %collective-permute-start.6 = (bf16[64,4096]{1,0:T(8,128)(2,1)S(1)}, bf16[64,4096]{1,0:T(8,128)(2,1)S(1)}, u32[]{:S(2)}, u32[]{:S(2)}) collective-permute-start(bf16[64,4096]{1,0:T(8,128)(2,1)S(1)} %copy.17), channel_id=1, source_target_pairs={{0,16},{8,24},{16,0},{24,8},{1,17},{9,25},{17,1},{25,9},{2,18},{10... | collective-permute-start | bytes 1572872 | tf_op jit(solution)/shard_map/ppermute | solution.py:46
  40.3 11.8 %collective-permute-start.5 = (bf16[64,4096]{1,0:T(8,128)(2,1)}, bf16[64,4096]{1,0:T(8,128)(2,1)S(1)}, u32[]{:S(2)}, u32[]{:S(2)}) collective-permute-start(bf16[64,4096]{1,0:T(8,128)(2,1)} %copy.16), channel_id=1, source_target_pairs={{0,8},{8,0},{16,24},{24,16},{1,9},{9,1},{17,25},{25,17},{2,10},{10... | collective-permute-start | bytes 1572872 | tf_op jit(solution)/shard_map/ppermute | solution.py:45
  40.6 16.6 %collective-permute-start = (bf16[128,4096]{0,1:T(8,128)(2,1)}, bf16[128,4096]{0,1:T(8,128)(2,1)}, u32[]{:S(2)}, u32[]{:S(2)}) collective-permute-start(bf16[128,4096]{0,1:T(8,128)(2,1)} %pad_maximum_fusion), channel_id=1, source_target_pairs={{0,4},{4,0},{1,5},{5,1},{2,6},{6,2},{3,7},{7,3},{8,12},{12,8},{9,1... | collective-permute-start | bytes 3145736 | tf_op jit(solution)/shard_map/ppermute | solution.py:53
  42.7 14.6 %collective-permute-start.2 = (bf16[128,4096]{0,1:T(8,128)(2,1)}, bf16[128,4096]{0,1:T(8,128)(2,1)}, u32[]{:S(2)}, u32[]{:S(2)}) collective-permute-start(bf16[128,4096]{0,1:T(8,128)(2,1)} %collective-permute-done.1), channel_id=1, source_target_pairs={{0,4},{4,0},{1,5},{5,1},{2,6},{6,2},{3,7},{7,3},{8,12},{12,8},{9,1... | collective-permute-start | bytes 3145736 | tf_op jit(solution)/shard_map/ppermute | solution.py:53
  42.7 14.6 %collective-permute-start.4 = (bf16[128,4096]{0,1:T(8,128)(2,1)}, bf16[128,4096]{0,1:T(8,128)(2,1)}, u32[]{:S(2)}, u32[]{:S(2)}) collective-permute-start(bf16[128,4096]{0,1:T(8,128)(2,1)} %collective-permute-done.3), channel_id=1, source_target_pairs={{0,4},{4,0},{1,5},{5,1},{2,6},{6,2},{3,7},{7,3},{8,12},{12,8},{9,1... | collective-permute-start | bytes 3145736 | tf_op jit(solution)/shard_map/ppermute | solution.py:53
  54.2 5.4 %collective-permute-start.7 = (bf16[128,4096]{0,1:T(8,128)(2,1)}, bf16[128,4096]{0,1:T(8,128)(2,1)}, u32[]{:S(2)}, u32[]{:S(2)}) collective-permute-start(bf16[128,4096]{0,1:T(8,128)(2,1)} %pad_maximum_fusion.1), channel_id=1, source_target_pairs={{0,4},{4,0},{1,5},{5,1},{2,6},{6,2},{3,7},{7,3},{8,12},{12,8},{9,1... | collective-permute-start | bytes 3145736 | tf_op jit(solution)/shard_map/ppermute | solution.py:53
  87.1 13.2 %collective-permute-start.9 = (bf16[128,2048]{0,1:T(8,128)(2,1)S(1)}, bf16[128,2048]{0,1:T(8,128)(2,1)S(1)}, u32[]{:S(2)}, u32[]{:S(2)}) collective-permute-start(bf16[128,2048]{0,1:T(8,128)(2,1)S(1)} %bitcast.39), channel_id=1, source_target_pairs={{0,8},{8,0},{16,24},{24,16},{1,9},{9,1},{17,25},{25,17},{2,10},{10... | collective-permute-start | bytes 1572872 | tf_op jit(solution)/shard_map/ppermute | solution.py:41
  87.4 13.4 %collective-permute-start.11 = (bf16[128,2048]{0,1:T(8,128)(2,1)S(1)}, bf16[128,2048]{0,1:T(8,128)(2,1)S(1)}, u32[]{:S(2)}, u32[]{:S(2)}) collective-permute-start(bf16[128,2048]{0,1:T(8,128)(2,1)S(1)} %bitcast.40), channel_id=1, source_target_pairs={{0,16},{8,24},{16,0},{24,8},{1,17},{9,25},{17,1},{25,9},{2,18},{10... | collective-permute-start | bytes 1572872 | tf_op jit(solution)/shard_map/ppermute | solution.py:42
  100.5 12.3 %collective-permute-start.14 = (bf16[64,2048]{0,1:T(8,128)(2,1)S(1)}, bf16[64,2048]{0,1:T(8,128)(2,1)S(1)}, u32[]{:S(2)}, u32[]{:S(2)}) collective-permute-start(bf16[64,2048]{0,1:T(8,128)(2,1)S(1)} %slice.37), channel_id=1, source_target_pairs={{0,16},{8,24},{16,0},{24,8},{1,17},{9,25},{17,1},{25,9},{2,18},{10... | collective-permute-start | bytes 786440 | tf_op jit(solution)/shard_map/ppermute | solution.py:46
  100.8 12.0 %collective-permute-start.13 = (bf16[64,2048]{0,1:T(8,128)(2,1)S(1)}, bf16[64,2048]{0,1:T(8,128)(2,1)S(1)}, u32[]{:S(2)}, u32[]{:S(2)}) collective-permute-start(bf16[64,2048]{0,1:T(8,128)(2,1)S(1)} %bitcast.43), channel_id=1, source_target_pairs={{0,8},{8,0},{16,24},{24,16},{1,9},{9,1},{17,25},{25,17},{2,10},{10... | collective-permute-start | bytes 786440 | tf_op jit(solution)/shard_map/ppermute | solution.py:45
  101.4 14.1 %collective-permute-start.8 = (bf16[128,2048]{0,1:T(8,128)(2,1)S(1)}, bf16[128,2048]{0,1:T(8,128)(2,1)S(1)}, u32[]{:S(2)}, u32[]{:S(2)}) collective-permute-start(bf16[128,2048]{0,1:T(8,128)(2,1)S(1)} %bitcast.41), channel_id=1, source_target_pairs={{0,4},{4,0},{1,5},{5,1},{2,6},{6,2},{3,7},{7,3},{8,12},{12,8},{9,1... | collective-permute-start | bytes 1572872 | tf_op jit(solution)/shard_map/ppermute | solution.py:53
  103.2 12.3 %collective-permute-start.10 = (bf16[128,2048]{0,1:T(8,128)(2,1)S(1)}, bf16[128,2048]{0,1:T(8,128)(2,1)S(1)}, u32[]{:S(2)}, u32[]{:S(2)}) collective-permute-start(bf16[128,2048]{0,1:T(8,128)(2,1)S(1)} %collective-permute-done.9), channel_id=1, source_target_pairs={{0,4},{4,0},{1,5},{5,1},{2,6},{6,2},{3,7},{7,3},{8,12},{12,8},{9,1... | collective-permute-start | bytes 1572872 | tf_op jit(solution)/shard_map/ppermute | solution.py:53
  103.2 12.3 %collective-permute-start.12 = (bf16[128,2048]{0,1:T(8,128)(2,1)S(1)}, bf16[128,2048]{0,1:T(8,128)(2,1)S(1)}, u32[]{:S(2)}, u32[]{:S(2)}) collective-permute-start(bf16[128,2048]{0,1:T(8,128)(2,1)S(1)} %collective-permute-done.11), channel_id=1, source_target_pairs={{0,4},{4,0},{1,5},{5,1},{2,6},{6,2},{3,7},{7,3},{8,12},{12,8},{9,1... | collective-permute-start | bytes 1572872 | tf_op jit(solution)/shard_map/ppermute | solution.py:53
  113.1 4.2 %collective-permute-start.15 = (bf16[128,2048]{0,1:T(8,128)(2,1)S(1)}, bf16[128,2048]{0,1:T(8,128)(2,1)}, u32[]{:S(2)}, u32[]{:S(2)}) collective-permute-start(bf16[128,2048]{0,1:T(8,128)(2,1)S(1)} %pad_maximum_fusion.2), channel_id=1, source_target_pairs={{0,4},{4,0},{1,5},{5,1},{2,6},{6,2},{3,7},{7,3},{8,12},{12,8},{9,1... | collective-permute-start | bytes 1572872 | tf_op jit(solution)/shard_map/ppermute | solution.py:53
  115.5 0.8 copy-start.1
  115.5 1.0 copy-start.2
  116.5 0.8 copy-start.3
  124.7 94.1 %copy-start.4 = (bf16[128,2048]{1,0:T(8,128)(2,1)S(1)}, bf16[128,2048]{1,0:T(8,128)(2,1)}, u32[]{:S(2)}) copy-start(bf16[128,2048]{1,0:T(8,128)(2,1)} %param.8) | copy-start | bytes 1572868
  179.9 32.5 %collective-permute-start.16 = (bf16[128,1024]{1,0:T(8,128)(2,1)S(1)}, bf16[128,1024]{1,0:T(8,128)(2,1)S(1)}, u32[]{:S(2)}, u32[]{:S(2)}) collective-permute-start(bf16[128,1024]{1,0:T(8,128)(2,1)S(1)} %get-tuple-element.7), channel_id=1, source_target_pairs={{0,0},{1,8},{2,16},{3,24},{4,4},{5,12},{6,20},{7,28},{8,9},{9,1},{... | collective-permute-start | bytes 786440 | tf_op jit(solution)/shard_map/ppermute | solution.py:115
  181.8 37.0 %collective-permute-start.17 = (bf16[128,1024]{1,0:T(8,128)(2,1)S(1)}, bf16[128,1024]{1,0:T(8,128)(2,1)S(1)}, u32[]{:S(2)}, u32[]{:S(2)}) collective-permute-start(bf16[128,1024]{1,0:T(8,128)(2,1)S(1)} %get-tuple-element.8), channel_id=1, source_target_pairs={{0,4},{1,12},{2,20},{3,28},{4,0},{5,8},{6,16},{7,24},{8,13},{9,5},... | collective-permute-start | bytes 786440 | tf_op jit(solution)/shard_map/ppermute | solution.py:115
Sparse Core Ops, SparseCore 0:
  134.3 44.4 reduce-scatter.1

commit v4 on v3

--- a/solution.py
+++ b/solution.py
@@ -51,75 +51,95 @@
     for block in (x, from_x, from_y, diag):
         pieces.append(block)
         pieces.append(lax.ppermute(block, "lo", [(0, 1), (1, 0)]))
-    return jnp.concatenate(pieces, axis=0)
+    return pieces
 
 
-def relative_segments(count):
-    block = jnp.arange(count, dtype=jnp.int32)
-    chip = lax.axis_index("hi") ^ (block // 2)
-    core = lax.axis_index("lo") ^ (block % 2)
-    return chip * 2 + core
+def relative_segment(block):
+    return (lax.axis_index("hi") ^ (block // 2)) * 2 + (lax.axis_index("lo") ^ (block % 2))
+
+
+def attention_blocks(query_proj, key_blocks, value_blocks, segment, key_segments):
+    seg_rows, feat_width = query_proj.shape
+    heads_here = feat_width // HEAD_DIM
+    score_scale = 1.0 / math.sqrt(HEAD_DIM)
+    queries = query_proj.reshape(seg_rows, heads_here, HEAD_DIM)
+    row_pos = segment * seg_rows + jnp.arange(seg_rows, dtype=jnp.int32)
+    scores = []
+    masks = []
+    for keys, key_segment in zip(key_blocks, key_segments):
+        keys = keys.reshape(keys.shape[0], heads_here, HEAD_DIM)
+        part = (
+            jnp.einsum("qhd,khd->hqk", queries, keys, preferred_element_type=jnp.float32)
+            * score_scale
+        )
+        key_pos = key_segment * seg_rows + jnp.arange(keys.shape[0], dtype=jnp.int32)
+        allowed = (key_pos[None, :] <= row_pos[:, None])[None]
+        scores.append(jnp.where(allowed, part, -1e30))
+        masks.append(allowed)
+    row_max = jnp.max(jnp.stack([jnp.max(s, axis=-1) for s in scores]), axis=0)
+    row_total = jnp.zeros_like(row_max)
+    numer = jnp.zeros((heads_here, seg_rows, HEAD_DIM), jnp.float32)
+    for part, allowed, values in zip(scores, masks, value_blocks):
+        weights = jnp.where(allowed, jnp.exp(part - row_max[..., None]), 0.0)
+        row_total = row_total + jnp.sum(weights, axis=-1)
+        values = values.reshape(values.shape[0], heads_here, HEAD_DIM)
+        numer = numer + jnp.einsum(
+            "hqk,khd->hqd", weights.astype(jnp.bfloat16), values, preferred_element_type=jnp.float32
+        )
+    ratio = numer / row_total[..., None]
+    return ratio.transpose(1, 0, 2).reshape(seg_rows, feat_width).astype(jnp.bfloat16)
 
 
 def attention(query_proj, keys_values, segment, key_segment):
-    seg_rows, feat_width = query_proj.shape
-    heads_here = feat_width // HEAD_DIM
-    total_rows = keys_values.shape[0]
-    score_scale = 1.0 / math.sqrt(HEAD_DIM)
-    keys = keys_values[:, :feat_width].reshape(total_rows, heads_here, HEAD_DIM)
-    values = keys_values[:, feat_width:].reshape(total_rows, heads_here, HEAD_DIM)
-    key_pos = (
-        key_segment[:, None] * seg_rows + jnp.arange(seg_rows, dtype=jnp.int32)[None, :]
-    ).reshape(-1)
-    row_pos = segment * seg_rows + jnp.arange(seg_rows, dtype=jnp.int32)
-    queries = query_proj.reshape(seg_rows, heads_here, HEAD_DIM)
-    scores = (
-        jnp.einsum("qhd,khd->hqk", queries, keys, preferred_element_type=jnp.float32) * score_scale
+    feat_width = query_proj.shape[1]
+    seg_rows = query_proj.shape[0]
+    count = keys_values.shape[0] // seg_rows
+    key_blocks = [keys_values[i * seg_rows : (i + 1) * seg_rows, :feat_width] for i in range(count)]
+    value_blocks = [keys_values[i * seg_rows : (i + 1) * seg_rows, feat_width:] for i in range(count)]
+    return attention_blocks(
+        query_proj, key_blocks, value_blocks, segment, [key_segment[i] for i in range(count)]
     )
-    allowed = (key_pos[None, :] <= row_pos[:, None])[None]
-    scores = jnp.where(allowed, scores, -1e30)
-    row_max = jnp.max(scores, axis=-1)
-    weights = jnp.where(allowed, jnp.exp(scores - row_max[..., None]), 0.0)
-    row_total = jnp.sum(weights, axis=-1)
-    numer = jnp.einsum(
-        "hqk,khd->hqd", weights.astype(jnp.bfloat16), values, preferred_element_type=jnp.float32
-    )
-    ratio = numer / row_total[..., None]
-    return ratio.transpose(1, 0, 2).reshape(seg_rows, feat_width).astype(jnp.bfloat16)
 
 
 def per_device_square(query_proj, key_proj, value_proj, residual, out_weight):
     seg_rows = query_proj.shape[0]
     chips = lax.axis_size("hi")
+    chans = lax.axis_size("chan")
     chip = lax.axis_index("hi")
     core = lax.axis_index("lo")
-    segment = chip * 2 + core
-    both = gather_seq_square(jnp.concatenate([key_proj, value_proj], axis=1))
-    local_context = attention(query_proj, both, segment, relative_segments(2 * chips))
-    rows = gather_seq_square(local_context)
-    reduced = lax.psum_scatter(
-        jnp.dot(rows, out_weight, preferred_element_type=jnp.float32).astype(jnp.bfloat16),
-        "chan",
-        scatter_dimension=0,
-        tiled=True,
+    chan = lax.axis_index("chan")
+    key_blocks = gather_seq_square(key_proj)
+    value_blocks = gather_seq_square(value_proj)
+    key_segments = [relative_segment(b) for b in range(len(key_blocks))]
+    local_context = attention_blocks(
+        query_proj, key_blocks, value_blocks, chip * 2 + core, key_segments
     )
-    chans = lax.axis_size("chan")
-    received = []
+    context_blocks = gather_seq_square(local_context)
+    partial = jnp.stack(
+        [
+            jnp.dot(block, out_weight, preferred_element_type=jnp.float32).astype(jnp.bfloat16)
+            for block in context_blocks
+        ]
+    )
+    halves = [None, None]
     for t in range(2):
-        pairs = []
-        for hi in range(chips):
-            for lo in range(2):
-                for c in range(chans):
-                    pairs.append((((hi * 2) + lo) * chans + c, (((hi ^ c) * 2) + (lo ^ t)) * chans + hi))
-        received.append(
-            lax.ppermute(reduced[t * seg_rows : (t + 1) * seg_rows], ("hi", "lo", "chan"), pairs)
-        )
+        for u in range(chans):
+            pairs = []
+            for hi in range(chips):
+                for lo in range(2):
+                    for c in range(chans):
+                        pairs.append(
+                            ((hi * 2 + lo) * chans + c, (((c ^ u) * 2) + (lo ^ t)) * chans + hi)
+                        )
+            piece = partial[2 * (chip ^ chan ^ u) + t]
+            got = lax.ppermute(piece, ("hi", "lo", "chan"), pairs).astype(jnp.float32)
+            halves[t] = got if halves[t] is None else halves[t] + got
     ordered = jnp.where(
         core == 0,
-        jnp.concatenate(received, axis=1),
-        jnp.concatenate(received[::-1], axis=1),
+        jnp.concatenate(halves, axis=1),
+        jnp.concatenate(halves[::-1], axis=1),
     )
-    return (residual.astype(jnp.float32) + ordered.astype(jnp.float32)).astype(jnp.bfloat16)
+    return (residual.astype(jnp.float32) + ordered).astype(jnp.bfloat16)
 
 
 def per_device_general(query_proj, key_proj, value_proj, residual, out_weight):

time: 228 us -> 255 us (1.12)
  the two profiles are of different devices: /device:TPU:3 before, /device:TPU:27 now
where the time goes in v4:
time: 255 us; the launch traced here: 254 us
  starting transfers between devices  101 us (40%)
  waiting for transfers between devices  89 us (35%)
  matrix products  36.6 us (14%)
  local copies, waits for them, and re-layouts  21.4 us (8%)
  other arithmetic  5.93 us (2%)
    ppermute x8, starting transfers between devices, per_device_square(): got = lax.ppermute(piece, ('hi', 'lo', 'chan'), pairs).astype(jnp.float32)  76.3 us
    ppermute x8, waiting for transfers between devices, per_device_square(): got = lax.ppermute(piece, ('hi', 'lo', 'chan'), pairs).astype(jnp.float32)  63.1 us
    dot_general x8, matrix products, attention_blocks(): jnp.einsum('qhd,khd->hqk', queries, keys, preferred_element_type=jnp.floa...  18.5 us
    ppermute x12, starting transfers between devices, gather_seq_square(): pieces.append(lax.ppermute(block, 'lo', [(0, 1), (1, 0)]))  14.7 us
    ppermute x3, waiting for transfers between devices, gather_seq_square(): from_x = lax.ppermute(x, 'hi', swap('hi', 1, 4))  11.6 us
    dot_general x8, matrix products, attention_blocks(): jnp.einsum('hqk,khd->hqd', weights.astype(jnp.bfloat16), values, preferre...  9.85 us
    ppermute x4, local copies, waits for them, and re-layouts, gather_seq_square(): pieces.append(lax.ppermute(block, 'lo', [(0, 1), (1, 0)]))  8.3 us
    dot_general x8, matrix products, per_device_square(): jnp.dot(block, out_weight, preferred_element_type=jnp.float32)  8.28 us
  transfers between devices with their start and end apart: 32, of which 9 were waited for; matrix products, arithmetic and copies ran while one was open for 19% of the time, Pallas kernels for 0%

profile of v4, /device:TPU:27, one launch (start us, length us, event | category | flops | bytes accessed | tf_op | source)
XLA Modules:
  0.0 254.2 jit_solution(5027523403726129073)
XLA Ops:
  8.5 2.5 fusion.118
  11.0 4.1 %collective-permute-done.1 = bf16[128,2048]{0,1:T(8,128)(2,1)S(1)} collective-permute-done((bf16[128,2048]{0,1:T(8,128)(2,1)}, bf16[128,2048]{0,1:T(8,128)(2,1)S(1)}, u32[]{:S(2)}, u32[]{:S(2)}) %collective-permute-start.1) | collective-permute-done | bytes 524320 | tf_op jit(solution)/shard_map/ppermute | solution.py:41
  15.1 2.7 %collective-permute-start.8 = (bf16[128,2048]{1,0:T(8,128)(2,1)S(1)}, bf16[128,2048]{1,0:T(8,128)(2,1)}, u32[]{:S(2)}, u32[]{:S(2)}) collective-permute-start(bf16[128,2048]{1,0:T(8,128)(2,1)S(1)} %copy-done.17), channel_id=1, source_target_pairs={{0,4},{4,0},{1,5},{5,1},{2,6},{6,2},{3,7},{7,3},{8,12},{12,8},{9,1... | collective-permute-start | bytes 1572872 | tf_op jit(solution)/shard_map/ppermute | solution.py:53
  20.2 6.3 %collective-permute-done.11 = bf16[128,2048]{1,0:T(8,128)(2,1)S(1)} collective-permute-done((bf16[128,2048]{1,0:T(8,128)(2,1)}, bf16[128,2048]{1,0:T(8,128)(2,1)S(1)}, u32[]{:S(2)}, u32[]{:S(2)}) %collective-permute-start.11) | collective-permute-done | bytes 524320 | tf_op jit(solution)/shard_map/ppermute | solution.py:42
  30.3 3.0 %fusion.115 = (f32[16,128]{1,0:T(8,128)}, f32[16,128,128]{2,1,0:T(8,128)}) fusion(bf16[128,16,128]{0,2,1:T(8,128)(2,1)} %bitcast.196, pred[128,128]{1,0:T(8,128)(4,1)S(1)} %copy.72, bf16[128,2048]{1,0:T(8,128)(2,1)S(1)} %copy-done), kind=kOutput, calls=%fused_computation.168 | convolution fusion | flops 67893248 | bytes 2121728 | tf_op jit(solution)/shard_map/qhd,khd->hqk/dot_general | solution.py:72
  33.3 3.0 %fusion.117 = (f32[16,128]{1,0:T(8,128)}, f32[16,128,128]{2,1,0:T(8,128)}) fusion(bf16[128,16,128]{0,2,1:T(8,128)(2,1)} %bitcast.193, pred[128,128]{1,0:T(8,128)(4,1)S(1)} %copy.61, bf16[128,2048]{1,0:T(8,128)(2,1)S(1)} %copy-done), kind=kOutput, calls=%fused_computation.170 | convolution fusion | flops 67893248 | bytes 2121728 | tf_op jit(solution)/shard_map/qhd,khd->hqk/dot_general | solution.py:72
  37.5 3.0 %fusion.119 = (f32[16,128]{1,0:T(8,128)}, f32[16,128,128]{2,1,0:T(8,128)}) fusion(bf16[128,16,128]{0,2,1:T(8,128)(2,1)} %bitcast, pred[128,128]{1,0:T(8,128)(4,1)S(1)} %copy.55, bf16[128,2048]{1,0:T(8,128)(2,1)S(1)} %copy-done), kind=kOutput, calls=%fused_computation.172 | convolution fusion | flops 67893248 | bytes 2121728 | tf_op jit(solution)/shard_map/qhd,khd->hqk/dot_general | solution.py:72
  43.6 4.1 %collective-permute-start.4 = (bf16[128,2048]{0,1:T(8,128)(2,1)}, bf16[128,2048]{0,1:T(8,128)(2,1)}, u32[]{:S(2)}, u32[]{:S(2)}) collective-permute-start(bf16[128,2048]{0,1:T(8,128)(2,1)} %copy-done.23), channel_id=1, source_target_pairs={{0,4},{4,0},{1,5},{5,1},{2,6},{6,2},{3,7},{7,3},{8,12},{12,8},{9,1... | collective-permute-start | bytes 1572872 | tf_op jit(solution)/shard_map/ppermute | solution.py:53
  58.0 2.5 fusion.114
  60.5 2.4 fusion.116
  64.6 2.5 fusion.60
  82.1 3.1 %fusion.17 = bf16[8,128,1024]{2,1,0:T(8,128)(2,1)S(1)} fusion(bf16[128,2048]{0,1:T(8,128)(2,1)S(1)} %bitcast.192, bf16[2048,1024]{1,0:T(8,128)(2,1)} %param.9), kind=kOutput, calls=%fused_computation.37 | convolution fusion | flops 537001984 | bytes 4980736 | tf_op jit(solution)/shard_map/dot_general | solution.py:120
  85.2 7.5 %collective-permute-done.17 = bf16[128,2048]{0,1:T(8,128)(2,1)S(1)} collective-permute-done((bf16[128,2048]{0,1:T(8,128)(2,1)S(1)}, bf16[128,2048]{0,1:T(8,128)(2,1)S(1)}, u32[]{:S(2)}, u32[]{:S(2)}) %collective-permute-start.17) | collective-permute-done | bytes 524320 | tf_op jit(solution)/shard_map/ppermute | solution.py:41
  97.8 7.3 %collective-permute-done.22 = bf16[64,2048]{0,1:T(8,128)(2,1)S(1)} collective-permute-done((bf16[64,2048]{0,1:T(8,128)(2,1)S(1)}, bf16[64,2048]{0,1:T(8,128)(2,1)S(1)}, u32[]{:S(2)}, u32[]{:S(2)}) %collective-permute-start.22) | collective-permute-done | bytes 262176 | tf_op jit(solution)/shard_map/ppermute | solution.py:46
  105.7 2.6 %collective-permute-start.23 = (bf16[128,2048]{0,1:T(8,128)(2,1)S(1)}, bf16[128,2048]{0,1:T(8,128)(2,1)S(1)}, u32[]{:S(2)}, u32[]{:S(2)}) collective-permute-start(bf16[128,2048]{0,1:T(8,128)(2,1)S(1)} %pad_maximum_fusion.1), channel_id=1, source_target_pairs={{0,4},{4,0},{1,5},{5,1},{2,6},{6,2},{3,7},{7,3},{8,12},{12,8},{9,1... | collective-permute-start | bytes 1572872 | tf_op jit(solution)/shard_map/ppermute | solution.py:53
  112.3 2.5 collective-permute-start.24
  114.8 2.6 %collective-permute-start.25 = (bf16[128,1024]{1,0:T(8,128)(2,1)S(1)}, bf16[128,1024]{1,0:T(8,128)(2,1)}, u32[]{:S(2)}, u32[]{:S(2)}) collective-permute-start(bf16[128,1024]{1,0:T(8,128)(2,1)S(1)} %get-tuple-element.20), channel_id=1, source_target_pairs={{0,8},{1,0},{2,24},{3,16},{4,12},{5,4},{6,28},{7,20},{8,9},{9,1},{... | collective-permute-start | bytes 786440 | tf_op jit(solution)/shard_map/ppermute | solution.py:135
  117.4 2.8 %collective-permute-start.27 = (bf16[128,1024]{1,0:T(8,128)(2,1)S(1)}, bf16[128,1024]{1,0:T(8,128)(2,1)}, u32[]{:S(2)}, u32[]{:S(2)}) collective-permute-start(bf16[128,1024]{1,0:T(8,128)(2,1)S(1)} %get-tuple-element.18), channel_id=1, source_target_pairs={{0,24},{1,16},{2,8},{3,0},{4,28},{5,20},{6,12},{7,4},{8,25},{9,17}... | collective-permute-start | bytes 786440 | tf_op jit(solution)/shard_map/ppermute | solution.py:135
  120.2 2.8 %collective-permute-start.28 = (bf16[128,1024]{1,0:T(8,128)(2,1)S(1)}, bf16[128,1024]{1,0:T(8,128)(2,1)S(1)}, u32[]{:S(2)}, u32[]{:S(2)}) collective-permute-start(bf16[128,1024]{1,0:T(8,128)(2,1)S(1)} %get-tuple-element.17), channel_id=1, source_target_pairs={{0,4},{1,12},{2,20},{3,28},{4,0},{5,8},{6,16},{7,24},{8,5},{9,13},... | collective-permute-start | bytes 786440 | tf_op jit(solution)/shard_map/ppermute | solution.py:135
  123.0 29.1 %collective-permute-done.24 = bf16[128,1024]{1,0:T(8,128)(2,1)S(1)} collective-permute-done((bf16[128,1024]{1,0:T(8,128)(2,1)S(1)}, bf16[128,1024]{1,0:T(8,128)(2,1)S(1)}, u32[]{:S(2)}, u32[]{:S(2)}) %collective-permute-start.24) | collective-permute-done | bytes 262176 | tf_op jit(solution)/shard_map/ppermute | solution.py:135
  154.3 34.8 %collective-permute-start.30 = (bf16[128,1024]{1,0:T(8,128)(2,1)S(1)}, bf16[128,1024]{1,0:T(8,128)(2,1)S(1)}, u32[]{:S(2)}, u32[]{:S(2)}) collective-permute-start(bf16[128,1024]{1,0:T(8,128)(2,1)S(1)} %get-tuple-element.15), channel_id=1, source_target_pairs={{0,20},{1,28},{2,4},{3,12},{4,16},{5,24},{6,0},{7,8},{8,21},{9,29}... | collective-permute-start | bytes 786440 | tf_op jit(solution)/shard_map/ppermute | solution.py:135
  189.0 28.6 %collective-permute-start.31 = (bf16[128,1024]{1,0:T(8,128)(2,1)S(1)}, bf16[128,1024]{1,0:T(8,128)(2,1)S(1)}, u32[]{:S(2)}, u32[]{:S(2)}) collective-permute-start(bf16[128,1024]{1,0:T(8,128)(2,1)S(1)} %get-tuple-element.14), channel_id=1, source_target_pairs={{0,28},{1,20},{2,12},{3,4},{4,24},{5,16},{6,8},{7,0},{8,29},{9,21}... | collective-permute-start | bytes 786440 | tf_op jit(solution)/shard_map/ppermute | solution.py:135
  217.7 12.9 %collective-permute-done.27 = bf16[128,1024]{1,0:T(8,128)(2,1)} collective-permute-done((bf16[128,1024]{1,0:T(8,128)(2,1)S(1)}, bf16[128,1024]{1,0:T(8,128)(2,1)}, u32[]{:S(2)}, u32[]{:S(2)}) %collective-permute-start.27) | collective-permute-done | bytes 262176 | tf_op jit(solution)/shard_map/ppermute | solution.py:135
  231.9 21.1 %collective-permute-done.31 = bf16[128,1024]{1,0:T(8,128)(2,1)S(1)} collective-permute-done((bf16[128,1024]{1,0:T(8,128)(2,1)S(1)}, bf16[128,1024]{1,0:T(8,128)(2,1)S(1)}, u32[]{:S(2)}, u32[]{:S(2)}) %collective-permute-start.31) | collective-permute-done | bytes 262176 | tf_op jit(solution)/shard_map/ppermute | solution.py:135
  (147 shorter events, 59.9 us)
Async XLA Ops:
  2.1 13.0 %collective-permute-start.1 = (bf16[128,2048]{0,1:T(8,128)(2,1)}, bf16[128,2048]{0,1:T(8,128)(2,1)S(1)}, u32[]{:S(2)}, u32[]{:S(2)}) collective-permute-start(bf16[128,2048]{0,1:T(8,128)(2,1)} %copy.56), channel_id=1, source_target_pairs={{0,8},{8,0},{16,24},{24,16},{1,9},{9,1},{17,25},{25,17},{2,10},{10... | collective-permute-start | bytes 1572872 | tf_op jit(solution)/shard_map/ppermute | solution.py:41
  2.4 16.5 %collective-permute-start.3 = (bf16[128,2048]{0,1:T(8,128)(2,1)}, bf16[128,2048]{0,1:T(8,128)(2,1)S(1)}, u32[]{:S(2)}, u32[]{:S(2)}) collective-permute-start(bf16[128,2048]{0,1:T(8,128)(2,1)} %copy.56), channel_id=1, source_target_pairs={{0,16},{8,24},{16,0},{24,8},{1,17},{9,25},{17,1},{25,9},{2,18},{10... | collective-permute-start | bytes 1572872 | tf_op jit(solution)/shard_map/ppermute | solution.py:42
  3.6 32.6 %collective-permute-start = (bf16[128,2048]{0,1:T(8,128)(2,1)}, bf16[128,2048]{0,1:T(8,128)(2,1)}, u32[]{:S(2)}, u32[]{:S(2)}) collective-permute-start(bf16[128,2048]{0,1:T(8,128)(2,1)} %copy.56), channel_id=1, source_target_pairs={{0,4},{4,0},{1,5},{5,1},{2,6},{6,2},{3,7},{7,3},{8,12},{12,8},{9,1... | collective-permute-start | bytes 1572872 | tf_op jit(solution)/shard_map/ppermute | solution.py:53
  4.9 23.5 %collective-permute-start.9 = (bf16[128,2048]{1,0:T(8,128)(2,1)}, bf16[128,2048]{1,0:T(8,128)(2,1)}, u32[]{:S(2)}, u32[]{:S(2)}) collective-permute-start(bf16[128,2048]{1,0:T(8,128)(2,1)} %param.7), channel_id=1, source_target_pairs={{0,8},{8,0},{16,24},{24,16},{1,9},{9,1},{17,25},{25,17},{2,10},{10... | collective-permute-start | bytes 1572872 | tf_op jit(solution)/shard_map/ppermute | solution.py:41
  6.1 20.3 %collective-permute-start.11 = (bf16[128,2048]{1,0:T(8,128)(2,1)}, bf16[128,2048]{1,0:T(8,128)(2,1)S(1)}, u32[]{:S(2)}, u32[]{:S(2)}) collective-permute-start(bf16[128,2048]{1,0:T(8,128)(2,1)} %param.7), channel_id=1, source_target_pairs={{0,16},{8,24},{16,0},{24,8},{1,17},{9,25},{17,1},{25,9},{2,18},{10... | collective-permute-start | bytes 1572872 | tf_op jit(solution)/shard_map/ppermute | solution.py:42
  15.1 28.4 %collective-permute-start.8 = (bf16[128,2048]{1,0:T(8,128)(2,1)S(1)}, bf16[128,2048]{1,0:T(8,128)(2,1)}, u32[]{:S(2)}, u32[]{:S(2)}) collective-permute-start(bf16[128,2048]{1,0:T(8,128)(2,1)S(1)} %copy-done.17), channel_id=1, source_target_pairs={{0,4},{4,0},{1,5},{5,1},{2,6},{6,2},{3,7},{7,3},{8,12},{12,8},{9,1... | collective-permute-start | bytes 1572872 | tf_op jit(solution)/shard_map/ppermute | solution.py:53
  18.9 30.9 %collective-permute-start.6 = (bf16[64,2048]{0,1:T(8,128)(2,1)}, bf16[64,2048]{0,1:T(8,128)(2,1)S(1)}, u32[]{:S(2)}, u32[]{:S(2)}) collective-permute-start(bf16[64,2048]{0,1:T(8,128)(2,1)} %slice.25), channel_id=1, source_target_pairs={{0,16},{8,24},{16,0},{24,8},{1,17},{9,25},{17,1},{25,9},{2,18},{10... | collective-permute-start | bytes 786440 | tf_op jit(solution)/shard_map/ppermute | solution.py:46
  26.4 23.3 %collective-permute-start.5 = (bf16[64,2048]{0,1:T(8,128)(2,1)}, bf16[64,2048]{0,1:T(8,128)(2,1)S(1)}, u32[]{:S(2)}, u32[]{:S(2)}) collective-permute-start(bf16[64,2048]{0,1:T(8,128)(2,1)} %bitcast.195), channel_id=1, source_target_pairs={{0,8},{8,0},{16,24},{24,16},{1,9},{9,1},{17,25},{25,17},{2,10},{10... | collective-permute-start | bytes 786440 | tf_op jit(solution)/shard_map/ppermute | solution.py:45
  28.3 22.2 %collective-permute-start.13 = (bf16[64,2048]{1,0:T(8,128)(2,1)}, bf16[64,2048]{1,0:T(8,128)(2,1)S(1)}, u32[]{:S(2)}, u32[]{:S(2)}) collective-permute-start(bf16[64,2048]{1,0:T(8,128)(2,1)} %slice.26), channel_id=1, source_target_pairs={{0,8},{8,0},{16,24},{24,16},{1,9},{9,1},{17,25},{25,17},{2,10},{10... | collective-permute-start | bytes 786440 | tf_op jit(solution)/shard_map/ppermute | solution.py:45
  36.3 14.5 %collective-permute-start.14 = (bf16[64,2048]{1,0:T(8,128)(2,1)}, bf16[64,2048]{1,0:T(8,128)(2,1)}, u32[]{:S(2)}, u32[]{:S(2)}) collective-permute-start(bf16[64,2048]{1,0:T(8,128)(2,1)} %slice.27), channel_id=1, source_target_pairs={{0,16},{8,24},{16,0},{24,8},{1,17},{9,25},{17,1},{25,9},{2,18},{10... | collective-permute-start | bytes 786440 | tf_op jit(solution)/shard_map/ppermute | solution.py:46
  43.6 14.4 %collective-permute-start.4 = (bf16[128,2048]{0,1:T(8,128)(2,1)}, bf16[128,2048]{0,1:T(8,128)(2,1)}, u32[]{:S(2)}, u32[]{:S(2)}) collective-permute-start(bf16[128,2048]{0,1:T(8,128)(2,1)} %copy-done.23), channel_id=1, source_target_pairs={{0,4},{4,0},{1,5},{5,1},{2,6},{6,2},{3,7},{7,3},{8,12},{12,8},{9,1... | collective-permute-start | bytes 1572872 | tf_op jit(solution)/shard_map/ppermute | solution.py:53
  53.8 15.3 %collective-permute-start.15 = (bf16[128,2048]{1,0:T(8,128)(2,1)}, bf16[128,2048]{1,0:T(8,128)(2,1)}, u32[]{:S(2)}, u32[]{:S(2)}) collective-permute-start(bf16[128,2048]{1,0:T(8,128)(2,1)} %copy-done.13), channel_id=1, source_target_pairs={{0,4},{4,0},{1,5},{5,1},{2,6},{6,2},{3,7},{7,3},{8,12},{12,8},{9,1... | collective-permute-start | bytes 1572872 | tf_op jit(solution)/shard_map/ppermute | solution.py:53
  79.6 13.1 %collective-permute-start.17 = (bf16[128,2048]{0,1:T(8,128)(2,1)S(1)}, bf16[128,2048]{0,1:T(8,128)(2,1)S(1)}, u32[]{:S(2)}, u32[]{:S(2)}) collective-permute-start(bf16[128,2048]{0,1:T(8,128)(2,1)S(1)} %bitcast.189), channel_id=1, source_target_pairs={{0,8},{8,0},{16,24},{24,16},{1,9},{9,1},{17,25},{25,17},{2,10},{10... | collective-permute-start | bytes 1572872 | tf_op jit(solution)/shard_map/ppermute | solution.py:41
  81.1 15.2 %collective-permute-start.16 = (bf16[128,2048]{0,1:T(8,128)(2,1)S(1)}, bf16[128,2048]{0,1:T(8,128)(2,1)S(1)}, u32[]{:S(2)}, u32[]{:S(2)}) collective-permute-start(bf16[128,2048]{0,1:T(8,128)(2,1)S(1)} %bitcast.191), channel_id=1, source_target_pairs={{0,4},{4,0},{1,5},{5,1},{2,6},{6,2},{3,7},{7,3},{8,12},{12,8},{9,1... | collective-permute-start | bytes 1572872 | tf_op jit(solution)/shard_map/ppermute | solution.py:53
  94.4 13.9 %collective-permute-start.18 = (bf16[128,2048]{0,1:T(8,128)(2,1)S(1)}, bf16[128,2048]{0,1:T(8,128)(2,1)S(1)}, u32[]{:S(2)}, u32[]{:S(2)}) collective-permute-start(bf16[128,2048]{0,1:T(8,128)(2,1)S(1)} %collective-permute-done.17), channel_id=1, source_target_pairs={{0,4},{4,0},{1,5},{5,1},{2,6},{6,2},{3,7},{7,3},{8,12},{12,8},{9,1... | collective-permute-start | bytes 1572872 | tf_op jit(solution)/shard_map/ppermute | solution.py:53
  96.2 13.5 %collective-permute-start.20 = (bf16[128,2048]{0,1:T(8,128)(2,1)S(1)}, bf16[128,2048]{0,1:T(8,128)(2,1)S(1)}, u32[]{:S(2)}, u32[]{:S(2)}) collective-permute-start(bf16[128,2048]{0,1:T(8,128)(2,1)S(1)} %collective-permute-done.19), channel_id=1, source_target_pairs={{0,4},{4,0},{1,5},{5,1},{2,6},{6,2},{3,7},{7,3},{8,12},{12,8},{9,1... | collective-permute-start | bytes 1572872 | tf_op jit(solution)/shard_map/ppermute | solution.py:53
  112.3 39.8 %collective-permute-start.24 = (bf16[128,1024]{1,0:T(8,128)(2,1)S(1)}, bf16[128,1024]{1,0:T(8,128)(2,1)S(1)}, u32[]{:S(2)}, u32[]{:S(2)}) collective-permute-start(bf16[128,1024]{1,0:T(8,128)(2,1)S(1)} %get-tuple-element.13), channel_id=1, source_target_pairs={{0,0},{1,8},{2,16},{3,24},{4,4},{5,12},{6,20},{7,28},{8,1},{9,9},{... | collective-permute-start | bytes 786440 | tf_op jit(solution)/shard_map/ppermute | solution.py:135
  114.8 39.4 %collective-permute-start.25 = (bf16[128,1024]{1,0:T(8,128)(2,1)S(1)}, bf16[128,1024]{1,0:T(8,128)(2,1)}, u32[]{:S(2)}, u32[]{:S(2)}) collective-permute-start(bf16[128,1024]{1,0:T(8,128)(2,1)S(1)} %get-tuple-element.20), channel_id=1, source_target_pairs={{0,8},{1,0},{2,24},{3,16},{4,12},{5,4},{6,28},{7,20},{8,9},{9,1},{... | collective-permute-start | bytes 786440 | tf_op jit(solution)/shard_map/ppermute | solution.py:135
  117.4 71.6 %collective-permute-start.26 = (bf16[128,1024]{1,0:T(8,128)(2,1)S(1)}, bf16[128,1024]{1,0:T(8,128)(2,1)}, u32[]{:S(2)}, u32[]{:S(2)}) collective-permute-start(bf16[128,1024]{1,0:T(8,128)(2,1)S(1)} %get-tuple-element.19), channel_id=1, source_target_pairs={{0,16},{1,24},{2,0},{3,8},{4,20},{5,28},{6,4},{7,12},{8,17},{9,25}... | collective-permute-start | bytes 786440 | tf_op jit(solution)/shard_map/ppermute | solution.py:135
  117.4 113.2 %collective-permute-start.27 = (bf16[128,1024]{1,0:T(8,128)(2,1)S(1)}, bf16[128,1024]{1,0:T(8,128)(2,1)}, u32[]{:S(2)}, u32[]{:S(2)}) collective-permute-start(bf16[128,1024]{1,0:T(8,128)(2,1)S(1)} %get-tuple-element.18), channel_id=1, source_target_pairs={{0,24},{1,16},{2,8},{3,0},{4,28},{5,20},{6,12},{7,4},{8,25},{9,17}... | collective-permute-start | bytes 786440 | tf_op jit(solution)/shard_map/ppermute | solution.py:135
  120.2 111.6 %collective-permute-start.28 = (bf16[128,1024]{1,0:T(8,128)(2,1)S(1)}, bf16[128,1024]{1,0:T(8,128)(2,1)S(1)}, u32[]{:S(2)}, u32[]{:S(2)}) collective-permute-start(bf16[128,1024]{1,0:T(8,128)(2,1)S(1)} %get-tuple-element.17), channel_id=1, source_target_pairs={{0,4},{1,12},{2,20},{3,28},{4,0},{5,8},{6,16},{7,24},{8,5},{9,13},... | collective-permute-start | bytes 786440 | tf_op jit(solution)/shard_map/ppermute | solution.py:135
  152.1 79.8 %collective-permute-start.29 = (bf16[128,1024]{1,0:T(8,128)(2,1)S(1)}, bf16[128,1024]{1,0:T(8,128)(2,1)S(1)}, u32[]{:S(2)}, u32[]{:S(2)}) collective-permute-start(bf16[128,1024]{1,0:T(8,128)(2,1)S(1)} %get-tuple-element.16), channel_id=1, source_target_pairs={{0,12},{1,4},{2,28},{3,20},{4,8},{5,0},{6,24},{7,16},{8,13},{9,5},... | collective-permute-start | bytes 786440 | tf_op jit(solution)/shard_map/ppermute | solution.py:135
  154.3 77.6 %collective-permute-start.30 = (bf16[128,1024]{1,0:T(8,128)(2,1)S(1)}, bf16[128,1024]{1,0:T(8,128)(2,1)S(1)}, u32[]{:S(2)}, u32[]{:S(2)}) collective-permute-start(bf16[128,1024]{1,0:T(8,128)(2,1)S(1)} %get-tuple-element.15), channel_id=1, source_target_pairs={{0,20},{1,28},{2,4},{3,12},{4,16},{5,24},{6,0},{7,8},{8,21},{9,29}... | collective-permute-start | bytes 786440 | tf_op jit(solution)/shard_map/ppermute | solution.py:135
  189.0 63.9 %collective-permute-start.31 = (bf16[128,1024]{1,0:T(8,128)(2,1)S(1)}, bf16[128,1024]{1,0:T(8,128)(2,1)S(1)}, u32[]{:S(2)}, u32[]{:S(2)}) collective-permute-start(bf16[128,1024]{1,0:T(8,128)(2,1)S(1)} %get-tuple-element.14), channel_id=1, source_target_pairs={{0,28},{1,20},{2,12},{3,4},{4,24},{5,16},{6,8},{7,0},{8,29},{9,21}... | collective-permute-start | bytes 786440 | tf_op jit(solution)/shard_map/ppermute | solution.py:135
  (32 other events, 356.6 us)

commit v5 on v2

--- a/solution.py
+++ b/solution.py
@@ -103,26 +103,22 @@
         local_context = ratio.transpose(1, 0, 2).reshape(seg_rows, feat_width).astype(jnp.bfloat16)
 
         gathered = gather_seq(local_context)
-        sub_rows = seg_rows // chan_count
-        grid = gathered.reshape(seq_count, chan_count, sub_rows, feat_width)
-        block_tokens = seq_count * sub_rows
-        rows = grid.transpose(1, 0, 2, 3).reshape(block_tokens * chan_count, feat_width)
-        partial_sums = lax.psum_scatter(
-            jnp.dot(rows, out_weight, preferred_element_type=jnp.float32).astype(jnp.bfloat16),
-            "chan",
-            scatter_dimension=0,
-            tiled=True,
-        ).astype(jnp.float32)
-        relaid = lax.all_to_all(
-            lax.all_to_all(
-                partial_sums.astype(jnp.bfloat16), SEQ, split_axis=0, concat_axis=1, tiled=True
-            ),
-            "chan",
-            split_axis=1,
-            concat_axis=0,
-            tiled=True,
-        ).astype(partial_sums.dtype)
-        return (residual.astype(jnp.float32) + relaid).astype(jnp.bfloat16)
+        group = seq_count // chan_count
+        chunks = 2
+        width = out_weight.shape[1] // chunks
+        reduced = []
+        for j in range(chunks):
+            partial = jnp.dot(
+                gathered, out_weight[:, j * width : (j + 1) * width], preferred_element_type=jnp.float32
+            ).astype(jnp.bfloat16)
+            by_row = lax.all_to_all(partial, SEQ, split_axis=0, concat_axis=1, tiled=True)
+            reduced.append(
+                lax.psum_scatter(by_row, "chan", scatter_dimension=1, tiled=True)
+            )
+        ordered = jnp.concatenate(
+            [part[:, b * width : (b + 1) * width] for b in range(group) for part in reduced], axis=1
+        )
+        return (residual.astype(jnp.float32) + ordered.astype(jnp.float32)).astype(jnp.bfloat16)
 
     return per_device
 

time: 206 us -> 204 us (level)
  waiting for transfers between devices: 93.8 us -> 86.1 us
  blocking collectives: 30.1 us -> 36.6 us
    reduce_scatter x1 -> x2, waiting for transfers between devices: 43.9 us -> 29.5 us  [per_device(): lax.psum_scatter(by_row, 'chan', scatter_dimension=1, tiled=True)]
    ppermute x2, waiting for transfers between devices: 22 us -> 33.8 us  [gather_seq_square(): from_x = lax.ppermute(x, 'hi', swap('hi', 1, 4))]
    ppermute x2, waiting for transfers between devices: 11.3 us -> 0.01 us  [gather_seq_square(): from_y = lax.ppermute(x, 'hi', swap('hi', 2, 4))]
    ppermute x2, waiting for transfers between devices: 6.62 us -> 15.4 us  [gather_seq_square(): lax.ppermute(from_x[half:], 'hi', swap('hi', 2, 4))]
    all_to_all x2, blocking collectives: 30.1 us -> 36.6 us  [per_device(): lax.all_to_all(partial, SEQ, split_axis=0, concat_axis=1, tiled=True)]
    ppermute x2, waiting for transfers between devices: 5.88 us -> 1.68 us  [gather_seq_square(): lax.ppermute(from_y[:half], 'hi', swap('hi', 1, 4))]
    dot_general x1, matrix products: 3.5 us -> 1.25 us  [per_device(): jnp.einsum('hqk,khd->hqd', weights.astype(jnp.bfloat16), values, preferre...]
    dot_general x1 -> x2, matrix products: 5.75 us -> 7.63 us  [per_device(): jnp.dot(gathered, out_weight[:, j * width:(j + 1) * width], preferred_ele...]
  transfers between devices with their start and end apart: 17 -> 18, of which waited for: 9 -> 11; matrix products, arithmetic and copies ran while one was open for 8% -> 12% of each run, Pallas kernels for 0% -> 0%
where the time goes in v5:
time: 204 us
  waiting for transfers between devices  86.1 us (42%)
  blocking collectives  36.6 us (18%)
  local copies, waits for them, and re-layouts  35.8 us (18%)
  between operations  13.7 us (7%)
  starting transfers between devices  12.2 us (6%)
  matrix products  10.3 us (5%)
  other arithmetic  9.15 us (4%)
    all_to_all x2, blocking collectives, per_device(): lax.all_to_all(partial, SEQ, split_axis=0, concat_axis=1, tiled=True)  36.6 us
    ppermute x2, waiting for transfers between devices, gather_seq_square(): from_x = lax.ppermute(x, 'hi', swap('hi', 1, 4))  33.8 us
    reduce_scatter x2, waiting for transfers between devices, per_device(): lax.psum_scatter(by_row, 'chan', scatter_dimension=1, tiled=True)  29.5 us
    ppermute x2, waiting for transfers between devices, gather_seq_square(): lax.ppermute(from_x[half:], 'hi', swap('hi', 2, 4))  15.4 us
    dynamic_update_slice x13, local copies, waits for them, and re-layouts, assemble(): out = lax.dynamic_update_slice(out, piece, (slot * rows, 0))  13 us
    dot_general x2, matrix products, per_device(): jnp.dot(gathered, out_weight[:, j * width:(j + 1) * width], preferred_ele...  7.63 us
    ppermute x8, waiting for transfers between devices, gather_seq_square(): lax.ppermute(block, 'lo', [(0, 1), (1, 0)])  5.61 us
    broadcast_in_dim x2, local copies, waits for them, and re-layouts, assemble(): out = jnp.zeros((len(pieces) * rows, width), dtype)  4.85 us
  transfers between devices with their start and end apart: 18, of which 11 were waited for; matrix products, arithmetic and copies ran while one was open for 12% of the time, Pallas kernels for 0%

profile of v5, /device:TPU:0, one launch (start us, length us, event | category | flops | bytes accessed | tf_op | source)
XLA Modules:
  0.0 203.8 jit_solution(1813360767020501486)
XLA Ops:
  9.2 4.3 %broadcast_in_dim.31 = bf16[1024,4096]{0,1:T(8,128)(2,1)} broadcast(bf16[]{:T(256)} %constant.14.clone.1), dimensions={} | broadcast | bytes 8388610 | tf_op jit(solution)/shard_map/broadcast_in_dim | solution.py:40
  15.1 2.9 %collective-permute-start.1 = (bf16[128,4096]{0,1:T(8,128)(2,1)}, bf16[128,4096]{0,1:T(8,128)(2,1)}, u32[]{:S(2)}, u32[]{:S(2)}) collective-permute-start(bf16[128,4096]{0,1:T(8,128)(2,1)} %get-tuple-element.11), channel_id=1, source_target_pairs={{0,8},{8,0},{16,24},{24,16},{1,9},{9,1},{17,25},{25,17},{2,10},{10... | collective-permute-start | bytes 3145736 | tf_op jit(solution)/shard_map/ppermute | solution.py:51
  19.5 22.0 %collective-permute-done.1 = bf16[128,4096]{0,1:T(8,128)(2,1)} collective-permute-done((bf16[128,4096]{0,1:T(8,128)(2,1)}, bf16[128,4096]{0,1:T(8,128)(2,1)}, u32[]{:S(2)}, u32[]{:S(2)}) %collective-permute-start.1) | collective-permute-done | bytes 1048608 | tf_op jit(solution)/shard_map/ppermute | solution.py:51
  41.5 1.6 slice.49
  43.4 1.9 collective-permute-start.6
  47.9 2.4 %constant_dynamic-update-slice_fusion.14 = bf16[1024,4096]{0,1:T(8,128)(2,1)} fusion(bf16[1024,4096]{0,1:T(8,128)(2,1)} %get-tuple-element.12, bf16[128,4096]{0,1:T(8,128)(2,1)} %collective-permute-done, s32[]{:T(128)S(6)} %select_n.40), kind=kLoop, calls=%fused_computation.40 | loop fusion | bytes 2097156 | tf_op jit(solution)/shard_map/dynamic_update_slice | solution.py:42
  50.2 2.4 %constant_dynamic-update-slice_fusion.13 = bf16[1024,4096]{0,1:T(8,128)(2,1)} fusion(bf16[1024,4096]{0,1:T(8,128)(2,1)} %constant_dynamic-update-slice_fusion.14, bf16[128,4096]{0,1:T(8,128)(2,1)} %collective-permute-done.1, s32[]{:T(128)S(6)} %select_n.41), kind=kLoop, calls=%fused_computation.39 | loop fusion | bytes 2097156 | tf_op jit(solution)/shard_map/dynamic_update_slice | solution.py:42
  52.6 5.4 %collective-permute-done.6 = bf16[64,4096]{1,0:T(8,128)(2,1)} collective-permute-done((bf16[64,4096]{1,0:T(8,128)(2,1)S(1)}, bf16[64,4096]{1,0:T(8,128)(2,1)}, u32[]{:S(2)}, u32[]{:S(2)}) %collective-permute-start.6) | collective-permute-done | bytes 524320 | tf_op jit(solution)/shard_map/ppermute | solution.py:56
  60.8 2.4 %copy.29 = bf16[64,4096]{0,1:T(8,128)(2,1)} copy(bf16[64,4096]{1,0:T(8,128)(2,1)} %collective-permute-done.5) | data formatting | bytes 1048576 | tf_op jit(solution)/shard_map/ppermute | solution.py:55
  63.2 2.4 %constant_dynamic-update-slice_fusion.12 = bf16[1024,4096]{0,1:T(8,128)(2,1)} fusion(bf16[1024,4096]{0,1:T(8,128)(2,1)} %constant_dynamic-update-slice_fusion.13, bf16[128,4096]{0,1:T(8,128)(2,1)} %collective-permute-done.2, s32[]{:T(128)S(6)} %select_n.42), kind=kLoop, calls=%fused_computation.38 | loop fusion | bytes 2097156 | tf_op jit(solution)/shard_map/dynamic_update_slice | solution.py:42
  66.7 2.4 %constant_dynamic-update-slice_fusion.10 = bf16[1024,4096]{0,1:T(8,128)(2,1)} fusion(bf16[1024,4096]{0,1:T(8,128)(2,1)} %constant_dynamic-update-slice_fusion.11, bf16[128,4096]{0,1:T(8,128)(2,1)} %collective-permute-done.4, s32[]{:T(128)S(6)} %select_n.44), kind=kLoop, calls=%fused_computation.36 | loop fusion | bytes 2097156 | tf_op jit(solution)/shard_map/dynamic_update_slice | solution.py:42
  69.0 1.6 constant_dynamic-update-slice_fusion.9
  70.8 2.6 %collective-permute-done.7 = bf16[128,4096]{0,1:T(8,128)(2,1)S(1)} collective-permute-done((bf16[128,4096]{0,1:T(8,128)(2,1)S(1)}, bf16[128,4096]{0,1:T(8,128)(2,1)S(1)}, u32[]{:S(2)}, u32[]{:S(2)}) %collective-permute-start.7) | collective-permute-done | bytes 1048608 | tf_op jit(solution)/shard_map/ppermute | solution.py:64
  74.4 3.9 %fusion.31 = (bf16[1024,2048]{0,1:T(8,128)(2,1)S(1)}, bf16[1024,2048]{0,1:T(8,128)(2,1)S(1)}) fusion(bf16[1024,4096]{0,1:T(8,128)(2,1)} %constant_dynamic-update-slice_fusion.8), kind=kLoop, calls=%fused_computation.45 | loop fusion | bytes 16777216 | tf_op jit(solution)/shard_map/slice | solution.py:85
  79.8 4.6 %fusion.34 = (f32[16,128]{1,0:T(8,128)S(1)}, bf16[16,128,1024]{1,2,0:T(8,128)(2,1)S(1)}) fusion(f32[16,1024,128]{2,1,0:T(8,128)S(1)} %fusion.26, pred[128,1024]{0,1:T(8,128)(4,1)S(1)} %iota_compare_fusion), kind=kOutput, calls=%fused_computation.48 | output fusion | flops 16778240 | bytes 12722176 | tf_op jit(solution)/shard_map/sub | solution.py:97
  87.7 11.8 %collective-permute-done.9 = bf16[128,2048]{0,1:T(8,128)(2,1)S(1)} collective-permute-done((bf16[128,2048]{0,1:T(8,128)(2,1)S(1)}, bf16[128,2048]{0,1:T(8,128)(2,1)S(1)}, u32[]{:S(2)}, u32[]{:S(2)}) %collective-permute-start.9) | collective-permute-done | bytes 524320 | tf_op jit(solution)/shard_map/ppermute | solution.py:51
  104.8 10.1 %collective-permute-done.14 = bf16[64,2048]{0,1:T(8,128)(2,1)S(1)} collective-permute-done((bf16[64,2048]{0,1:T(8,128)(2,1)S(1)}, bf16[64,2048]{0,1:T(8,128)(2,1)S(1)}, u32[]{:S(2)}, u32[]{:S(2)}) %collective-permute-start.14) | collective-permute-done | bytes 262176 | tf_op jit(solution)/shard_map/ppermute | solution.py:56
  115.8 1.9 collective-permute-done.15
  117.9 2.4 %fusion.11 = bf16[1024,512]{1,0:T(8,128)(2,1)S(1)} fusion(bf16[1024,2048]{0,1:T(8,128)(2,1)S(1)} %constant_dynamic-update-slice_fusion, bf16[2048,1024]{1,0:T(8,128)(2,1)S(1)} %copy-done.5), kind=kOutput, calls=%fused_computation.13 | convolution fusion | flops 2148007936 | bytes 7340032 | tf_op jit(solution)/shard_map/dot_general | solution.py:111
  120.3 18.7 %all_to_all.38 = bf16[8,128,512]{2,1,0:T(8,128)(2,1)S(1)} all-to-all(bf16[8,128,512]{2,1,0:T(8,128)(2,1)S(1)} %bitcast.51), channel_id=1, replica_groups=mesh['hi'=4,'lo'=2,'chan'=4] {'hi','lo'}, dimensions={0} | all-to-all | bytes 2097152 | tf_op jit(solution)/shard_map/all_to_all | solution.py:114
  140.2 5.3 %fusion.14 = bf16[1024,512]{1,0:T(8,128)(2,1)S(1)} fusion(bf16[1024,2048]{0,1:T(8,128)(2,1)} %copy-done.3, bf16[2048,1024]{1,0:T(8,128)(2,1)} %param.9), kind=kOutput, calls=%fused_computation.14 | convolution fusion | flops 2148007936 | bytes 7340032 | tf_op jit(solution)/shard_map/dot_general | solution.py:111
  145.5 17.9 %all_to_all.39 = bf16[8,128,512]{2,1,0:T(8,128)(2,1)S(1)} all-to-all(bf16[8,128,512]{2,1,0:T(8,128)(2,1)S(1)} %bitcast.50), channel_id=1, replica_groups=mesh['hi'=4,'lo'=2,'chan'=4] {'hi','lo'}, dimensions={0} | all-to-all | bytes 2097152 | tf_op jit(solution)/shard_map/all_to_all | solution.py:114
  164.6 2.2 %reduce-scatter.3.cloned.1.call-done = bf16[128,1024]{1,0:T(8,128)(2,1)} async-done(((bf16[128,4096]{1,0:T(8,128)(2,1)}), bf16[128,1024]{1,0:T(8,128)(2,1)}) %reduce-scatter.3.cloned.1.call-update) | async-done | bytes 262160 | tf_op jit(solution)/shard_map/reduce_scatter | solution.py:116
  167.8 27.2 %reduce-scatter.5.cloned.1.call-done = bf16[128,1024]{1,0:T(8,128)(2,1)} async-done(((bf16[128,4096]{1,0:T(8,128)(2,1)}), bf16[128,1024]{1,0:T(8,128)(2,1)}) %reduce-scatter.5.cloned.1.call-update) | async-done | bytes 262160 | tf_op jit(solution)/shard_map/reduce_scatter | solution.py:116
  (67 shorter events, 30.0 us)
Async XLA Ops:
  6.5 71.8 %copy-start = (bf16[128,2048]{1,0:T(8,128)(2,1)S(1)}, bf16[128,2048]{1,0:T(8,128)(2,1)}, u32[]{:S(2)}) copy-start(bf16[128,2048]{1,0:T(8,128)(2,1)} %param.5) | copy-start | bytes 1572868
  6.5 160.3 %reduce-scatter.3.cloned.1.call-start = ((), (), s32[]{:S(2)}) async-start(), calls=%async_computation.4 | async-start | bytes 1310720 | tf_op jit(solution)/shard_map/reduce_scatter | solution.py:116
  15.1 26.4 %collective-permute-start.1 = (bf16[128,4096]{0,1:T(8,128)(2,1)}, bf16[128,4096]{0,1:T(8,128)(2,1)}, u32[]{:S(2)}, u32[]{:S(2)}) collective-permute-start(bf16[128,4096]{0,1:T(8,128)(2,1)} %get-tuple-element.11), channel_id=1, source_target_pairs={{0,8},{8,0},{16,24},{24,16},{1,9},{9,1},{17,25},{25,17},{2,10},{10... | collective-permute-start | bytes 3145736 | tf_op jit(solution)/shard_map/ppermute | solution.py:51
  18.1 27.2 %collective-permute-start.3 = (bf16[128,4096]{0,1:T(8,128)(2,1)}, bf16[128,4096]{0,1:T(8,128)(2,1)S(1)}, u32[]{:S(2)}, u32[]{:S(2)}) collective-permute-start(bf16[128,4096]{0,1:T(8,128)(2,1)} %get-tuple-element.11), channel_id=1, source_target_pairs={{0,16},{8,24},{16,0},{24,8},{1,17},{9,25},{17,1},{25,9},{2,18},{10... | collective-permute-start | bytes 3145736 | tf_op jit(solution)/shard_map/ppermute | solution.py:52
  19.5 28.3 %collective-permute-start = (bf16[128,4096]{0,1:T(8,128)(2,1)}, bf16[128,4096]{0,1:T(8,128)(2,1)}, u32[]{:S(2)}, u32[]{:S(2)}) collective-permute-start(bf16[128,4096]{0,1:T(8,128)(2,1)} %get-tuple-element.11), channel_id=1, source_target_pairs={{0,4},{4,0},{1,5},{5,1},{2,6},{6,2},{3,7},{7,3},{8,12},{12,8},{9,1... | collective-permute-start | bytes 3145736 | tf_op jit(solution)/shard_map/ppermute | solution.py:64
  41.5 21.7 %collective-permute-start.2 = (bf16[128,4096]{0,1:T(8,128)(2,1)}, bf16[128,4096]{0,1:T(8,128)(2,1)}, u32[]{:S(2)}, u32[]{:S(2)}) collective-permute-start(bf16[128,4096]{0,1:T(8,128)(2,1)} %collective-permute-done.1), channel_id=1, source_target_pairs={{0,4},{4,0},{1,5},{5,1},{2,6},{6,2},{3,7},{7,3},{8,12},{12,8},{9,1... | collective-permute-start | bytes 3145736 | tf_op jit(solution)/shard_map/ppermute | solution.py:64
  43.4 14.6 %collective-permute-start.6 = (bf16[64,4096]{1,0:T(8,128)(2,1)S(1)}, bf16[64,4096]{1,0:T(8,128)(2,1)}, u32[]{:S(2)}, u32[]{:S(2)}) collective-permute-start(bf16[64,4096]{1,0:T(8,128)(2,1)S(1)} %copy.28), channel_id=1, source_target_pairs={{0,16},{8,24},{16,0},{24,8},{1,17},{9,25},{17,1},{25,9},{2,18},{10... | collective-permute-start | bytes 1572872 | tf_op jit(solution)/shard_map/ppermute | solution.py:56
  46.4 14.4 %collective-permute-start.5 = (bf16[64,4096]{1,0:T(8,128)(2,1)}, bf16[64,4096]{1,0:T(8,128)(2,1)}, u32[]{:S(2)}, u32[]{:S(2)}) collective-permute-start(bf16[64,4096]{1,0:T(8,128)(2,1)} %copy.27), channel_id=1, source_target_pairs={{0,8},{8,0},{16,24},{24,16},{1,9},{9,1},{17,25},{25,17},{2,10},{10... | collective-permute-start | bytes 1572872 | tf_op jit(solution)/shard_map/ppermute | solution.py:55
  47.9 18.8 %collective-permute-start.4 = (bf16[128,4096]{0,1:T(8,128)(2,1)S(1)}, bf16[128,4096]{0,1:T(8,128)(2,1)}, u32[]{:S(2)}, u32[]{:S(2)}) collective-permute-start(bf16[128,4096]{0,1:T(8,128)(2,1)S(1)} %collective-permute-done.3), channel_id=1, source_target_pairs={{0,4},{4,0},{1,5},{5,1},{2,6},{6,2},{3,7},{7,3},{8,12},{12,8},{9,1... | collective-permute-start | bytes 3145736 | tf_op jit(solution)/shard_map/ppermute | solution.py:64
  63.2 5.9 %copy-start.2 = (bf16[64,4096]{0,1:T(8,128)(2,1)S(1)}, bf16[64,4096]{0,1:T(8,128)(2,1)}, u32[]{:S(2)}) copy-start(bf16[64,4096]{0,1:T(8,128)(2,1)} %copy.29) | copy-start | bytes 1572868
  70.7 2.7 %collective-permute-start.7 = (bf16[128,4096]{0,1:T(8,128)(2,1)S(1)}, bf16[128,4096]{0,1:T(8,128)(2,1)S(1)}, u32[]{:S(2)}, u32[]{:S(2)}) collective-permute-start(bf16[128,4096]{0,1:T(8,128)(2,1)S(1)} %get-tuple-element.8), channel_id=1, source_target_pairs={{0,4},{4,0},{1,5},{5,1},{2,6},{6,2},{3,7},{7,3},{8,12},{12,8},{9,1... | collective-permute-start | bytes 3145736 | tf_op jit(solution)/shard_map/ppermute | solution.py:64
  85.6 14.0 %collective-permute-start.9 = (bf16[128,2048]{0,1:T(8,128)(2,1)S(1)}, bf16[128,2048]{0,1:T(8,128)(2,1)S(1)}, u32[]{:S(2)}, u32[]{:S(2)}) collective-permute-start(bf16[128,2048]{0,1:T(8,128)(2,1)S(1)} %bitcast.53), channel_id=1, source_target_pairs={{0,8},{8,0},{16,24},{24,16},{1,9},{9,1},{17,25},{25,17},{2,10},{10... | collective-permute-start | bytes 1572872 | tf_op jit(solution)/shard_map/ppermute | solution.py:51
  87.2 14.1 %collective-permute-start.11 = (bf16[128,2048]{0,1:T(8,128)(2,1)S(1)}, bf16[128,2048]{0,1:T(8,128)(2,1)S(1)}, u32[]{:S(2)}, u32[]{:S(2)}) collective-permute-start(bf16[128,2048]{0,1:T(8,128)(2,1)S(1)} %bitcast.54), channel_id=1, source_target_pairs={{0,16},{8,24},{16,0},{24,8},{1,17},{9,25},{17,1},{25,9},{2,18},{10... | collective-permute-start | bytes 1572872 | tf_op jit(solution)/shard_map/ppermute | solution.py:52
  87.7 15.0 %collective-permute-start.8 = (bf16[128,2048]{0,1:T(8,128)(2,1)S(1)}, bf16[128,2048]{0,1:T(8,128)(2,1)S(1)}, u32[]{:S(2)}, u32[]{:S(2)}) collective-permute-start(bf16[128,2048]{0,1:T(8,128)(2,1)S(1)} %bitcast.55), channel_id=1, source_target_pairs={{0,4},{4,0},{1,5},{5,1},{2,6},{6,2},{3,7},{7,3},{8,12},{12,8},{9,1... | collective-permute-start | bytes 1572872 | tf_op jit(solution)/shard_map/ppermute | solution.py:64
  99.6 3.5 %collective-permute-start.10 = (bf16[128,2048]{0,1:T(8,128)(2,1)S(1)}, bf16[128,2048]{0,1:T(8,128)(2,1)S(1)}, u32[]{:S(2)}, u32[]{:S(2)}) collective-permute-start(bf16[128,2048]{0,1:T(8,128)(2,1)S(1)} %collective-permute-done.9), channel_id=1, source_target_pairs={{0,4},{4,0},{1,5},{5,1},{2,6},{6,2},{3,7},{7,3},{8,12},{12,8},{9,1... | collective-permute-start | bytes 1572872 | tf_op jit(solution)/shard_map/ppermute | solution.py:64
  100.5 14.4 %collective-permute-start.14 = (bf16[64,2048]{0,1:T(8,128)(2,1)S(1)}, bf16[64,2048]{0,1:T(8,128)(2,1)S(1)}, u32[]{:S(2)}, u32[]{:S(2)}) collective-permute-start(bf16[64,2048]{0,1:T(8,128)(2,1)S(1)} %slice.53), channel_id=1, source_target_pairs={{0,16},{8,24},{16,0},{24,8},{1,17},{9,25},{17,1},{25,9},{2,18},{10... | collective-permute-start | bytes 786440 | tf_op jit(solution)/shard_map/ppermute | solution.py:56
  101.3 16.7 %copy-start.5 = (bf16[2048,1024]{1,0:T(8,128)(2,1)S(1)}, bf16[2048,1024]{1,0:T(8,128)(2,1)}, u32[]{:S(2)}) copy-start(bf16[2048,1024]{1,0:T(8,128)(2,1)} %param.9) | copy-start | bytes 12582916
  101.3 14.1 %collective-permute-start.13 = (bf16[64,2048]{0,1:T(8,128)(2,1)S(1)}, bf16[64,2048]{0,1:T(8,128)(2,1)S(1)}, u32[]{:S(2)}, u32[]{:S(2)}) collective-permute-start(bf16[64,2048]{0,1:T(8,128)(2,1)S(1)} %bitcast.52), channel_id=1, source_target_pairs={{0,8},{8,0},{16,24},{24,16},{1,9},{9,1},{17,25},{25,17},{2,10},{10... | collective-permute-start | bytes 786440 | tf_op jit(solution)/shard_map/ppermute | solution.py:55
  102.7 1.9 collective-permute-start.12
  115.8 2.0 collective-permute-start.15
  117.9 2.4 %copy-start.3 = (bf16[1024,2048]{0,1:T(8,128)(2,1)}, bf16[1024,2048]{0,1:T(8,128)(2,1)S(1)}, u32[]{:S(2)}) copy-start(bf16[1024,2048]{0,1:T(8,128)(2,1)S(1)} %constant_dynamic-update-slice_fusion) | copy-start | bytes 12582916
  140.2 54.9 %reduce-scatter.5.cloned.1.call-start = ((), (), s32[]{:S(2)}) async-start(), calls=%async_computation.5 | async-start | bytes 1310720 | tf_op jit(solution)/shard_map/reduce_scatter | solution.py:116
  140.2 56.7 %copy-start.1 = (bf16[128,2048]{1,0:T(8,128)(2,1)S(1)}, bf16[128,2048]{1,0:T(8,128)(2,1)}, u32[]{:S(2)}) copy-start(bf16[128,2048]{1,0:T(8,128)(2,1)} %param.5) | copy-start | bytes 1572868
  145.5 50.5 %copy-start.4 = (bf16[128,2048]{1,0:T(8,128)(2,1)S(1)}, bf16[128,2048]{1,0:T(8,128)(2,1)}, u32[]{:S(2)}) copy-start(bf16[128,2048]{1,0:T(8,128)(2,1)} %param.8) | copy-start | bytes 1572868
Sparse Core Ops, SparseCore 0:
  140.3 26.4 reduce-scatter.2
  169.2 25.7 reduce-scatter.4

commit v6 on v5

--- a/solution.py
+++ b/solution.py
@@ -65,6 +65,25 @@
     return assemble(pieces, rows, width, x.dtype)
 
 
+def a2a_seq_square(x):
+    rows = x.shape[0] // 8
+    width = x.shape[1]
+    chip = lax.axis_index("hi")
+    core = lax.axis_index("lo")
+    own = chip * 2 + core
+    out = jnp.zeros((rows, 8 * width), x.dtype)
+    out = lax.dynamic_update_slice(out, lax.dynamic_slice_in_dim(x, own * rows, rows, 0), (0, own * width))
+    for r in range(4):
+        for t in range(2):
+            if r == 0 and t == 0:
+                continue
+            other = (chip ^ r) * 2 + (core ^ t)
+            pairs = [(h * 2 + l, (h ^ r) * 2 + (l ^ t)) for h in range(4) for l in range(2)]
+            got = lax.ppermute(lax.dynamic_slice_in_dim(x, other * rows, rows, 0), SEQ, pairs)
+            out = lax.dynamic_update_slice(out, got, (0, other * width))
+    return out
+
+
 def make_per_device(square):
     def gather_seq(x):
         if square:
@@ -111,7 +130,10 @@
             partial = jnp.dot(
                 gathered, out_weight[:, j * width : (j + 1) * width], preferred_element_type=jnp.float32
             ).astype(jnp.bfloat16)
-            by_row = lax.all_to_all(partial, SEQ, split_axis=0, concat_axis=1, tiled=True)
+            if square:
+                by_row = a2a_seq_square(partial)
+            else:
+                by_row = lax.all_to_all(partial, SEQ, split_axis=0, concat_axis=1, tiled=True)
             reduced.append(
                 lax.psum_scatter(by_row, "chan", scatter_dimension=1, tiled=True)
             )

time: 204 us -> 210 us (1.029)
  blocking collectives: 36.6 us -> 0 us
  waiting for transfers between devices: 86.1 us -> 104 us
  starting transfers between devices: 12.2 us -> 26.2 us
  local copies, waits for them, and re-layouts: 35.8 us -> 43.2 us
  matrix products: 10.3 us -> 13.1 us
    all_to_all x2 -> x0, blocking collectives: 36.6 us -> none  [per_device(): lax.all_to_all(partial, SEQ, split_axis=0, concat_axis=1, tiled=True)]
    ppermute x0 -> x14, waiting for transfers between devices: none -> 17.7 us  [a2a_seq_square(): lax.ppermute(lax.dynamic_slice_in_dim(x, other * rows, rows, 0), SEQ, pairs)]
    ppermute x0 -> x14, starting transfers between devices: none -> 13.8 us  [a2a_seq_square(): lax.ppermute(lax.dynamic_slice_in_dim(x, other * rows, rows, 0), SEQ, pairs)]
    dynamic_update_slice x13, local copies, waits for them, and re-layouts: 13 us -> 17.9 us  [assemble(): out = lax.dynamic_update_slice(out, piece, (slot * rows, 0))]
    reduce_scatter x2, waiting for transfers between devices: 29.5 us -> 32.8 us  [per_device(): lax.psum_scatter(by_row, 'chan', scatter_dimension=1, tiled=True)]
    dot_general x2, matrix products: 7.63 us -> 10.5 us  [per_device(): jnp.dot(gathered, out_weight[:, j * width:(j + 1) * width], preferred_ele...]
    ppermute x2, waiting for transfers between devices: 15.4 us -> 13.1 us  [gather_seq_square(): lax.ppermute(from_x[half:], 'hi', swap('hi', 2, 4))]
    all_to_all x2 -> x0, local copies, waits for them, and re-layouts: 2.21 us -> none  [per_device(): lax.all_to_all(partial, SEQ, split_axis=0, concat_axis=1, tiled=True)]
  transfers between devices with their start and end apart: 18 -> 32, of which waited for: 11 -> 16; matrix products, arithmetic and copies ran while one was open for 12% -> 14% of each run, Pallas kernels for 0% -> 0%
where the time goes in v6:
time: 210 us
  waiting for transfers between devices  104 us (50%)
  local copies, waits for them, and re-layouts  43.2 us (21%)
  starting transfers between devices  26.2 us (12%)
  between operations  13.7 us (7%)
  matrix products  13.1 us (6%)
  other arithmetic  9.83 us (5%)
    ppermute x2, waiting for transfers between devices, gather_seq_square(): from_x = lax.ppermute(x, 'hi', swap('hi', 1, 4))  33.8 us
    reduce_scatter x2, waiting for transfers between devices, per_device(): lax.psum_scatter(by_row, 'chan', scatter_dimension=1, tiled=True)  32.8 us
    dynamic_update_slice x13, local copies, waits for them, and re-layouts, assemble(): out = lax.dynamic_update_slice(out, piece, (slot * rows, 0))  17.9 us
    ppermute x14, waiting for transfers between devices, a2a_seq_square(): lax.ppermute(lax.dynamic_slice_in_dim(x, other * rows, rows, 0), SEQ, pairs)  17.7 us
    ppermute x14, starting transfers between devices, a2a_seq_square(): lax.ppermute(lax.dynamic_slice_in_dim(x, other * rows, rows, 0), SEQ, pairs)  13.8 us
    ppermute x2, waiting for transfers between devices, gather_seq_square(): lax.ppermute(from_x[half:], 'hi', swap('hi', 2, 4))  13.1 us
    dot_general x2, matrix products, per_device(): jnp.dot(gathered, out_weight[:, j * width:(j + 1) * width], preferred_ele...  10.5 us
    broadcast_in_dim x2, local copies, waits for them, and re-layouts, assemble(): out = jnp.zeros((len(pieces) * rows, width), dtype)  6.88 us
  transfers between devices with their start and end apart: 32, of which 16 were waited for; matrix products, arithmetic and copies ran while one was open for 14% of the time, Pallas kernels for 0%

profile of v6, /device:TPU:0, one launch (start us, length us, event | category | flops | bytes accessed | tf_op | source)
XLA Modules:
  0.0 209.7 jit_solution(14550090161396019164)
XLA Ops:
  9.2 4.4 %broadcast_in_dim.31 = bf16[1024,4096]{0,1:T(8,128)(2,1)} broadcast(bf16[]{:T(256)} %constant.16.clone.1), dimensions={} | broadcast | bytes 8388610 | tf_op jit(solution)/shard_map/broadcast_in_dim | solution.py:40
  15.1 2.9 %collective-permute-start.1 = (bf16[128,4096]{0,1:T(8,128)(2,1)}, bf16[128,4096]{0,1:T(8,128)(2,1)}, u32[]{:S(2)}, u32[]{:S(2)}) collective-permute-start(bf16[128,4096]{0,1:T(8,128)(2,1)} %get-tuple-element.27), channel_id=1, source_target_pairs={{0,8},{8,0},{16,24},{24,16},{1,9},{9,1},{17,25},{25,17},{2,10},{10... | collective-permute-start | bytes 3145736 | tf_op jit(solution)/shard_map/ppermute | solution.py:51
  19.6 22.0 %collective-permute-done.1 = bf16[128,4096]{0,1:T(8,128)(2,1)} collective-permute-done((bf16[128,4096]{0,1:T(8,128)(2,1)}, bf16[128,4096]{0,1:T(8,128)(2,1)}, u32[]{:S(2)}, u32[]{:S(2)}) %collective-permute-start.1) | collective-permute-done | bytes 1048608 | tf_op jit(solution)/shard_map/ppermute | solution.py:51
  47.9 2.4 %constant_dynamic-update-slice_fusion.28 = bf16[1024,4096]{0,1:T(8,128)(2,1)} fusion(bf16[1024,4096]{0,1:T(8,128)(2,1)} %get-tuple-element.28, bf16[128,4096]{0,1:T(8,128)(2,1)} %collective-permute-done, s32[]{:T(128)S(6)} %select_n.48), kind=kLoop, calls=%fused_computation.70 | loop fusion | bytes 2097156 | tf_op jit(solution)/shard_map/dynamic_update_slice | solution.py:42
  50.3 2.4 %constant_dynamic-update-slice_fusion.27 = bf16[1024,4096]{0,1:T(8,128)(2,1)} fusion(bf16[1024,4096]{0,1:T(8,128)(2,1)} %constant_dynamic-update-slice_fusion.28, bf16[128,4096]{0,1:T(8,128)(2,1)} %collective-permute-done.1, s32[]{:T(128)S(6)} %select_n.49), kind=kLoop, calls=%fused_computation.69 | loop fusion | bytes 2097156 | tf_op jit(solution)/shard_map/dynamic_update_slice | solution.py:42
  52.7 5.4 %collective-permute-done.6 = bf16[64,4096]{1,0:T(8,128)(2,1)} collective-permute-done((bf16[64,4096]{1,0:T(8,128)(2,1)S(1)}, bf16[64,4096]{1,0:T(8,128)(2,1)}, u32[]{:S(2)}, u32[]{:S(2)}) %collective-permute-start.6) | collective-permute-done | bytes 524320 | tf_op jit(solution)/shard_map/ppermute | solution.py:56
  60.8 2.4 %copy.25 = bf16[64,4096]{0,1:T(8,128)(2,1)} copy(bf16[64,4096]{1,0:T(8,128)(2,1)} %collective-permute-done.5) | data formatting | bytes 1048576 | tf_op jit(solution)/shard_map/ppermute | solution.py:55
  63.2 2.4 %constant_dynamic-update-slice_fusion.26 = bf16[1024,4096]{0,1:T(8,128)(2,1)} fusion(bf16[1024,4096]{0,1:T(8,128)(2,1)} %constant_dynamic-update-slice_fusion.27, bf16[128,4096]{0,1:T(8,128)(2,1)} %collective-permute-done.2, s32[]{:T(128)S(6)} %select_n.98), kind=kLoop, calls=%fused_computation.68 | loop fusion | bytes 2097156 | tf_op jit(solution)/shard_map/dynamic_update_slice | solution.py:42
  66.8 2.4 %constant_dynamic-update-slice_fusion.24 = bf16[1024,4096]{0,1:T(8,128)(2,1)} fusion(bf16[1024,4096]{0,1:T(8,128)(2,1)} %constant_dynamic-update-slice_fusion.25, bf16[128,4096]{0,1:T(8,128)(2,1)} %collective-permute-done.4, s32[]{:T(128)S(6)} %select_n.100), kind=kLoop, calls=%fused_computation.66 | loop fusion | bytes 2097156 | tf_op jit(solution)/shard_map/dynamic_update_slice | solution.py:42
  70.9 2.6 %collective-permute-done.7 = bf16[128,4096]{0,1:T(8,128)(2,1)S(1)} collective-permute-done((bf16[128,4096]{0,1:T(8,128)(2,1)S(1)}, bf16[128,4096]{0,1:T(8,128)(2,1)S(1)}, u32[]{:S(2)}, u32[]{:S(2)}) %collective-permute-start.7) | collective-permute-done | bytes 1048608 | tf_op jit(solution)/shard_map/ppermute | solution.py:64
  74.5 3.9 %fusion.31 = (bf16[1024,2048]{0,1:T(8,128)(2,1)S(1)}, bf16[1024,2048]{0,1:T(8,128)(2,1)S(1)}) fusion(bf16[1024,4096]{0,1:T(8,128)(2,1)} %constant_dynamic-update-slice_fusion.22), kind=kLoop, calls=%fused_computation.75 | loop fusion | bytes 16777216 | tf_op jit(solution)/shard_map/slice | solution.py:104
  79.9 4.6 %fusion.34 = (f32[16,128]{1,0:T(8,128)S(1)}, bf16[16,128,1024]{1,2,0:T(8,128)(2,1)S(1)}) fusion(f32[16,1024,128]{2,1,0:T(8,128)S(1)} %fusion.26, pred[128,1024]{0,1:T(8,128)(4,1)S(1)} %iota_compare_fusion), kind=kOutput, calls=%fused_computation.78 | output fusion | flops 16778240 | bytes 12722176 | tf_op jit(solution)/shard_map/sub | solution.py:116
  87.8 11.8 %collective-permute-done.9 = bf16[128,2048]{0,1:T(8,128)(2,1)S(1)} collective-permute-done((bf16[128,2048]{0,1:T(8,128)(2,1)S(1)}, bf16[128,2048]{0,1:T(8,128)(2,1)S(1)}, u32[]{:S(2)}, u32[]{:S(2)}) %collective-permute-start.9) | collective-permute-done | bytes 524320 | tf_op jit(solution)/shard_map/ppermute | solution.py:51
  99.7 2.5 %broadcast_in_dim.29 = bf16[1024,2048]{0,1:T(8,128)(2,1)} broadcast(bf16[]{:T(256)} %constant.16.clone.1), dimensions={} | broadcast | bytes 4194306 | tf_op jit(solution)/shard_map/broadcast_in_dim | solution.py:40
  109.9 7.8 %collective-permute-done.14 = bf16[64,2048]{0,1:T(8,128)(2,1)S(1)} collective-permute-done((bf16[64,2048]{0,1:T(8,128)(2,1)S(1)}, bf16[64,2048]{0,1:T(8,128)(2,1)S(1)}, u32[]{:S(2)}, u32[]{:S(2)}) %collective-permute-start.14) | collective-permute-done | bytes 262176 | tf_op jit(solution)/shard_map/ppermute | solution.py:56
  119.2 1.9 collective-permute-done.15
  121.9 5.2 %fusion.11 = bf16[1024,512]{1,0:T(8,128)(2,1)S(1)} fusion(bf16[1024,2048]{0,1:T(8,128)(2,1)} %constant_dynamic-update-slice_fusion.14, bf16[2048,1024]{1,0:T(8,128)(2,1)} %param.9), kind=kOutput, calls=%fused_computation.13 | convolution fusion | flops 2148007936 | bytes 7340032 | tf_op jit(solution)/shard_map/dot_general | solution.py:130
  131.1 2.3 %collective-permute-start.21 = (bf16[128,512]{1,0:T(8,128)(2,1)S(1)}, bf16[128,512]{1,0:T(8,128)(2,1)S(1)}, u32[]{:S(2)}, u32[]{:S(2)}) collective-permute-start(bf16[128,512]{1,0:T(8,128)(2,1)S(1)} %get-tuple-element.12), channel_id=1, source_target_pairs={{0,24},{4,28},{8,16},{12,20},{16,8},{20,12},{24,0},{28,4},{1,25},{... | collective-permute-start | bytes 393224 | tf_op jit(solution)/shard_map/ppermute | solution.py:82
  135.8 7.3 %collective-permute-done.20 = bf16[128,512]{1,0:T(8,128)(2,1)S(1)} collective-permute-done((bf16[128,512]{1,0:T(8,128)(2,1)S(1)}, bf16[128,512]{1,0:T(8,128)(2,1)S(1)}, u32[]{:S(2)}, u32[]{:S(2)}) %collective-permute-start.20) | collective-permute-done | bytes 131104 | tf_op jit(solution)/shard_map/ppermute | solution.py:82
  144.5 5.3 %fusion.14 = bf16[1024,512]{1,0:T(8,128)(2,1)S(1)} fusion(bf16[1024,2048]{0,1:T(8,128)(2,1)} %constant_dynamic-update-slice_fusion.14, bf16[2048,1024]{1,0:T(8,128)(2,1)} %param.9), kind=kOutput, calls=%fused_computation.14 | convolution fusion | flops 2148007936 | bytes 7340032 | tf_op jit(solution)/shard_map/dot_general | solution.py:130
  153.9 2.3 %collective-permute-start.28 = (bf16[128,512]{1,0:T(8,128)(2,1)S(1)}, bf16[128,512]{1,0:T(8,128)(2,1)S(1)}, u32[]{:S(2)}, u32[]{:S(2)}) collective-permute-start(bf16[128,512]{1,0:T(8,128)(2,1)S(1)} %get-tuple-element.20), channel_id=1, source_target_pairs={{0,24},{4,28},{8,16},{12,20},{16,8},{20,12},{24,0},{28,4},{1,25},{... | collective-permute-start | bytes 393224 | tf_op jit(solution)/shard_map/ppermute | solution.py:82
  158.7 7.4 %collective-permute-done.27 = bf16[128,512]{1,0:T(8,128)(2,1)S(1)} collective-permute-done((bf16[128,512]{1,0:T(8,128)(2,1)S(1)}, bf16[128,512]{1,0:T(8,128)(2,1)S(1)}, u32[]{:S(2)}, u32[]{:S(2)}) %collective-permute-start.27) | collective-permute-done | bytes 131104 | tf_op jit(solution)/shard_map/ppermute | solution.py:82
  167.1 5.6 %reduce-scatter.3.cloned.1.call-done = bf16[128,1024]{1,0:T(8,128)(2,1)} async-done(((bf16[128,4096]{1,0:T(8,128)(2,1)}), bf16[128,1024]{1,0:T(8,128)(2,1)}) %reduce-scatter.3.cloned.1.call-update) | async-done | bytes 262160 | tf_op jit(solution)/shard_map/reduce_scatter | solution.py:138
  173.7 27.2 %reduce-scatter.5.cloned.1.call-done = bf16[128,1024]{1,0:T(8,128)(2,1)} async-done(((bf16[128,4096]{1,0:T(8,128)(2,1)}), bf16[128,1024]{1,0:T(8,128)(2,1)}) %reduce-scatter.5.cloned.1.call-update) | async-done | bytes 262160 | tf_op jit(solution)/shard_map/reduce_scatter | solution.py:138
  (109 shorter events, 51.7 us)
Async XLA Ops:
  6.5 166.1 %reduce-scatter.3.cloned.1.call-start = ((), (), s32[]{:S(2)}) async-start(), calls=%async_computation.2 | async-start | bytes 1310720 | tf_op jit(solution)/shard_map/reduce_scatter | solution.py:138
  15.1 26.4 %collective-permute-start.1 = (bf16[128,4096]{0,1:T(8,128)(2,1)}, bf16[128,4096]{0,1:T(8,128)(2,1)}, u32[]{:S(2)}, u32[]{:S(2)}) collective-permute-start(bf16[128,4096]{0,1:T(8,128)(2,1)} %get-tuple-element.27), channel_id=1, source_target_pairs={{0,8},{8,0},{16,24},{24,16},{1,9},{9,1},{17,25},{25,17},{2,10},{10... | collective-permute-start | bytes 3145736 | tf_op jit(solution)/shard_map/ppermute | solution.py:51
  18.1 27.2 %collective-permute-start.3 = (bf16[128,4096]{0,1:T(8,128)(2,1)}, bf16[128,4096]{0,1:T(8,128)(2,1)S(1)}, u32[]{:S(2)}, u32[]{:S(2)}) collective-permute-start(bf16[128,4096]{0,1:T(8,128)(2,1)} %get-tuple-element.27), channel_id=1, source_target_pairs={{0,16},{8,24},{16,0},{24,8},{1,17},{9,25},{17,1},{25,9},{2,18},{10... | collective-permute-start | bytes 3145736 | tf_op jit(solution)/shard_map/ppermute | solution.py:52
  19.6 28.4 %collective-permute-start = (bf16[128,4096]{0,1:T(8,128)(2,1)}, bf16[128,4096]{0,1:T(8,128)(2,1)}, u32[]{:S(2)}, u32[]{:S(2)}) collective-permute-start(bf16[128,4096]{0,1:T(8,128)(2,1)} %get-tuple-element.27), channel_id=1, source_target_pairs={{0,4},{4,0},{1,5},{5,1},{2,6},{6,2},{3,7},{7,3},{8,12},{12,8},{9,1... | collective-permute-start | bytes 3145736 | tf_op jit(solution)/shard_map/ppermute | solution.py:64
  41.6 21.7 %collective-permute-start.2 = (bf16[128,4096]{0,1:T(8,128)(2,1)}, bf16[128,4096]{0,1:T(8,128)(2,1)}, u32[]{:S(2)}, u32[]{:S(2)}) collective-permute-start(bf16[128,4096]{0,1:T(8,128)(2,1)} %collective-permute-done.1), channel_id=1, source_target_pairs={{0,4},{4,0},{1,5},{5,1},{2,6},{6,2},{3,7},{7,3},{8,12},{12,8},{9,1... | collective-permute-start | bytes 3145736 | tf_op jit(solution)/shard_map/ppermute | solution.py:64
  43.5 14.5 %collective-permute-start.6 = (bf16[64,4096]{1,0:T(8,128)(2,1)S(1)}, bf16[64,4096]{1,0:T(8,128)(2,1)}, u32[]{:S(2)}, u32[]{:S(2)}) collective-permute-start(bf16[64,4096]{1,0:T(8,128)(2,1)S(1)} %copy.24), channel_id=1, source_target_pairs={{0,16},{8,24},{16,0},{24,8},{1,17},{9,25},{17,1},{25,9},{2,18},{10... | collective-permute-start | bytes 1572872 | tf_op jit(solution)/shard_map/ppermute | solution.py:56
  46.4 14.4 %collective-permute-start.5 = (bf16[64,4096]{1,0:T(8,128)(2,1)}, bf16[64,4096]{1,0:T(8,128)(2,1)}, u32[]{:S(2)}, u32[]{:S(2)}) collective-permute-start(bf16[64,4096]{1,0:T(8,128)(2,1)} %copy.23), channel_id=1, source_target_pairs={{0,8},{8,0},{16,24},{24,16},{1,9},{9,1},{17,25},{25,17},{2,10},{10... | collective-permute-start | bytes 1572872 | tf_op jit(solution)/shard_map/ppermute | solution.py:55
  47.9 18.9 %collective-permute-start.4 = (bf16[128,4096]{0,1:T(8,128)(2,1)S(1)}, bf16[128,4096]{0,1:T(8,128)(2,1)}, u32[]{:S(2)}, u32[]{:S(2)}) collective-permute-start(bf16[128,4096]{0,1:T(8,128)(2,1)S(1)} %collective-permute-done.3), channel_id=1, source_target_pairs={{0,4},{4,0},{1,5},{5,1},{2,6},{6,2},{3,7},{7,3},{8,12},{12,8},{9,1... | collective-permute-start | bytes 3145736 | tf_op jit(solution)/shard_map/ppermute | solution.py:64
  85.7 14.0 %collective-permute-start.9 = (bf16[128,2048]{0,1:T(8,128)(2,1)S(1)}, bf16[128,2048]{0,1:T(8,128)(2,1)S(1)}, u32[]{:S(2)}, u32[]{:S(2)}) collective-permute-start(bf16[128,2048]{0,1:T(8,128)(2,1)S(1)} %bitcast.39), channel_id=1, source_target_pairs={{0,8},{8,0},{16,24},{24,16},{1,9},{9,1},{17,25},{25,17},{2,10},{10... | collective-permute-start | bytes 1572872 | tf_op jit(solution)/shard_map/ppermute | solution.py:51
  87.2 16.8 %collective-permute-start.11 = (bf16[128,2048]{0,1:T(8,128)(2,1)S(1)}, bf16[128,2048]{0,1:T(8,128)(2,1)S(1)}, u32[]{:S(2)}, u32[]{:S(2)}) collective-permute-start(bf16[128,2048]{0,1:T(8,128)(2,1)S(1)} %bitcast.40), channel_id=1, source_target_pairs={{0,16},{8,24},{16,0},{24,8},{1,17},{9,25},{17,1},{25,9},{2,18},{10... | collective-permute-start | bytes 1572872 | tf_op jit(solution)/shard_map/ppermute | solution.py:52
  87.8 17.7 %collective-permute-start.8 = (bf16[128,2048]{0,1:T(8,128)(2,1)S(1)}, bf16[128,2048]{0,1:T(8,128)(2,1)S(1)}, u32[]{:S(2)}, u32[]{:S(2)}) collective-permute-start(bf16[128,2048]{0,1:T(8,128)(2,1)S(1)} %bitcast.41), channel_id=1, source_target_pairs={{0,4},{4,0},{1,5},{5,1},{2,6},{6,2},{3,7},{7,3},{8,12},{12,8},{9,1... | collective-permute-start | bytes 1572872 | tf_op jit(solution)/shard_map/ppermute | solution.py:64
  99.7 7.6 %collective-permute-start.10 = (bf16[128,2048]{0,1:T(8,128)(2,1)S(1)}, bf16[128,2048]{0,1:T(8,128)(2,1)S(1)}, u32[]{:S(2)}, u32[]{:S(2)}) collective-permute-start(bf16[128,2048]{0,1:T(8,128)(2,1)S(1)} %collective-permute-done.9), channel_id=1, source_target_pairs={{0,4},{4,0},{1,5},{5,1},{2,6},{6,2},{3,7},{7,3},{8,12},{12,8},{9,1... | collective-permute-start | bytes 1572872 | tf_op jit(solution)/shard_map/ppermute | solution.py:64
  103.3 14.4 %collective-permute-start.14 = (bf16[64,2048]{0,1:T(8,128)(2,1)S(1)}, bf16[64,2048]{0,1:T(8,128)(2,1)S(1)}, u32[]{:S(2)}, u32[]{:S(2)}) collective-permute-start(bf16[64,2048]{0,1:T(8,128)(2,1)S(1)} %slice.53), channel_id=1, source_target_pairs={{0,16},{8,24},{16,0},{24,8},{1,17},{9,25},{17,1},{25,9},{2,18},{10... | collective-permute-start | bytes 786440 | tf_op jit(solution)/shard_map/ppermute | solution.py:56
  104.0 14.0 %collective-permute-start.13 = (bf16[64,2048]{0,1:T(8,128)(2,1)S(1)}, bf16[64,2048]{0,1:T(8,128)(2,1)S(1)}, u32[]{:S(2)}, u32[]{:S(2)}) collective-permute-start(bf16[64,2048]{0,1:T(8,128)(2,1)S(1)} %bitcast.38), channel_id=1, source_target_pairs={{0,8},{8,0},{16,24},{24,16},{1,9},{9,1},{17,25},{25,17},{2,10},{10... | collective-permute-start | bytes 786440 | tf_op jit(solution)/shard_map/ppermute | solution.py:55
  129.2 6.6 %collective-permute-start.18 = (bf16[128,512]{1,0:T(8,128)(2,1)S(1)}, bf16[128,512]{1,0:T(8,128)(2,1)S(1)}, u32[]{:S(2)}, u32[]{:S(2)}) collective-permute-start(bf16[128,512]{1,0:T(8,128)(2,1)S(1)} %get-tuple-element.15), channel_id=1, source_target_pairs={{0,12},{4,8},{8,4},{12,0},{16,28},{20,24},{24,20},{28,16},{1,13},{... | collective-permute-start | bytes 393224 | tf_op jit(solution)/shard_map/ppermute | solution.py:82
  130.8 12.3 %collective-permute-start.20 = (bf16[128,512]{1,0:T(8,128)(2,1)S(1)}, bf16[128,512]{1,0:T(8,128)(2,1)S(1)}, u32[]{:S(2)}, u32[]{:S(2)}) collective-permute-start(bf16[128,512]{1,0:T(8,128)(2,1)S(1)} %get-tuple-element.13), channel_id=1, source_target_pairs={{0,20},{4,16},{8,28},{12,24},{16,4},{20,0},{24,12},{28,8},{1,21},{... | collective-permute-start | bytes 393224 | tf_op jit(solution)/shard_map/ppermute | solution.py:82
  131.1 12.0 %collective-permute-start.21 = (bf16[128,512]{1,0:T(8,128)(2,1)S(1)}, bf16[128,512]{1,0:T(8,128)(2,1)S(1)}, u32[]{:S(2)}, u32[]{:S(2)}) collective-permute-start(bf16[128,512]{1,0:T(8,128)(2,1)S(1)} %get-tuple-element.12), channel_id=1, source_target_pairs={{0,24},{4,28},{8,16},{12,20},{16,8},{20,12},{24,0},{28,4},{1,25},{... | collective-permute-start | bytes 393224 | tf_op jit(solution)/shard_map/ppermute | solution.py:82
  133.9 9.3 %collective-permute-start.22 = (bf16[128,512]{1,0:T(8,128)(2,1)S(1)}, bf16[128,512]{1,0:T(8,128)(2,1)S(1)}, u32[]{:S(2)}, u32[]{:S(2)}) collective-permute-start(bf16[128,512]{1,0:T(8,128)(2,1)S(1)} %get-tuple-element.11), channel_id=1, source_target_pairs={{0,28},{4,24},{8,20},{12,16},{16,12},{20,8},{24,4},{28,0},{1,29},{... | collective-permute-start | bytes 393224 | tf_op jit(solution)/shard_map/ppermute | solution.py:82
  144.3 56.6 %reduce-scatter.5.cloned.1.call-start = ((), (), s32[]{:S(2)}) async-start(), calls=%async_computation.3 | async-start | bytes 1310720 | tf_op jit(solution)/shard_map/reduce_scatter | solution.py:138
  151.9 6.7 %collective-permute-start.25 = (bf16[128,512]{1,0:T(8,128)(2,1)S(1)}, bf16[128,512]{1,0:T(8,128)(2,1)S(1)}, u32[]{:S(2)}, u32[]{:S(2)}) collective-permute-start(bf16[128,512]{1,0:T(8,128)(2,1)S(1)} %get-tuple-element.23), channel_id=1, source_target_pairs={{0,12},{4,8},{8,4},{12,0},{16,28},{20,24},{24,20},{28,16},{1,13},{... | collective-permute-start | bytes 393224 | tf_op jit(solution)/shard_map/ppermute | solution.py:82
  152.0 6.6 %collective-permute-start.26 = (bf16[128,512]{1,0:T(8,128)(2,1)S(1)}, bf16[128,512]{1,0:T(8,128)(2,1)S(1)}, u32[]{:S(2)}, u32[]{:S(2)}) collective-permute-start(bf16[128,512]{1,0:T(8,128)(2,1)S(1)} %get-tuple-element.22), channel_id=1, source_target_pairs={{0,16},{4,20},{8,24},{12,28},{16,0},{20,4},{24,8},{28,12},{1,17},{... | collective-permute-start | bytes 393224 | tf_op jit(solution)/shard_map/ppermute | solution.py:82
  153.6 12.5 %collective-permute-start.27 = (bf16[128,512]{1,0:T(8,128)(2,1)S(1)}, bf16[128,512]{1,0:T(8,128)(2,1)S(1)}, u32[]{:S(2)}, u32[]{:S(2)}) collective-permute-start(bf16[128,512]{1,0:T(8,128)(2,1)S(1)} %get-tuple-element.21), channel_id=1, source_target_pairs={{0,20},{4,16},{8,28},{12,24},{16,4},{20,0},{24,12},{28,8},{1,21},{... | collective-permute-start | bytes 393224 | tf_op jit(solution)/shard_map/ppermute | solution.py:82
  153.9 12.1 %collective-permute-start.28 = (bf16[128,512]{1,0:T(8,128)(2,1)S(1)}, bf16[128,512]{1,0:T(8,128)(2,1)S(1)}, u32[]{:S(2)}, u32[]{:S(2)}) collective-permute-start(bf16[128,512]{1,0:T(8,128)(2,1)S(1)} %get-tuple-element.20), channel_id=1, source_target_pairs={{0,24},{4,28},{8,16},{12,20},{16,8},{20,12},{24,0},{28,4},{1,25},{... | collective-permute-start | bytes 393224 | tf_op jit(solution)/shard_map/ppermute | solution.py:82
  156.7 9.3 %collective-permute-start.29 = (bf16[128,512]{1,0:T(8,128)(2,1)S(1)}, bf16[128,512]{1,0:T(8,128)(2,1)S(1)}, u32[]{:S(2)}, u32[]{:S(2)}) collective-permute-start(bf16[128,512]{1,0:T(8,128)(2,1)S(1)} %get-tuple-element.19), channel_id=1, source_target_pairs={{0,28},{4,24},{8,20},{12,16},{16,12},{20,8},{24,4},{28,0},{1,29},{... | collective-permute-start | bytes 393224 | tf_op jit(solution)/shard_map/ppermute | solution.py:82
  (14 other events, 225.0 us)
Sparse Core Ops, SparseCore 0:
  144.4 28.2 reduce-scatter.2
  175.1 25.7 reduce-scatter.4

commit v7 on v5

--- a/solution.py
+++ b/solution.py
@@ -65,6 +65,53 @@
     return assemble(pieces, rows, width, x.dtype)
 
 
+def gather_blocks_square(x):
+    half = x.shape[0] // 2
+    from_x = lax.ppermute(x, "hi", swap("hi", 1, 4))
+    from_y = lax.ppermute(x, "hi", swap("hi", 2, 4))
+    diag = jnp.concatenate(
+        [
+            lax.ppermute(from_y[:half], "hi", swap("hi", 1, 4)),
+            lax.ppermute(from_x[half:], "hi", swap("hi", 2, 4)),
+        ],
+        axis=0,
+    )
+    blocks = []
+    for block in (x, from_x, from_y, diag):
+        blocks.append(block)
+        blocks.append(lax.ppermute(block, "lo", [(0, 1), (1, 0)]))
+    return blocks
+
+
+def attention_by_head(queries, key_blocks, value_blocks, row_pos, key_starts):
+    score_scale = 1.0 / math.sqrt(HEAD_DIM)
+    scores = []
+    masks = []
+    for keys, start in zip(key_blocks, key_starts):
+        part = (
+            jnp.einsum("hqd,hkd->hqk", queries, keys, preferred_element_type=jnp.float32)
+            * score_scale
+        )
+        key_pos = start + jnp.arange(keys.shape[1], dtype=jnp.int32)
+        allowed = (key_pos[None, :] <= row_pos[:, None])[None]
+        scores.append(jnp.where(allowed, part, -1e30))
+        masks.append(allowed)
+    row_max = scores[0].max(axis=-1)
+    for part in scores[1:]:
+        row_max = jnp.maximum(row_max, part.max(axis=-1))
+    row_total = None
+    numer = None
+    for part, allowed, values in zip(scores, masks, value_blocks):
+        weights = jnp.where(allowed, jnp.exp(part - row_max[..., None]), 0.0)
+        total = jnp.sum(weights, axis=-1)
+        term = jnp.einsum(
+            "hqk,hkd->hqd", weights.astype(jnp.bfloat16), values, preferred_element_type=jnp.float32
+        )
+        row_total = total if row_total is None else row_total + total
+        numer = term if numer is None else numer + term
+    return numer / row_total[..., None]
+
+
 def make_per_device(square):
     def gather_seq(x):
         if square:
@@ -80,26 +127,39 @@
         segment = lax.axis_index("hi") * lax.axis_size("lo") + lax.axis_index("lo")
         score_scale = 1.0 / math.sqrt(HEAD_DIM)
 
-        both = gather_seq(jnp.concatenate([key_proj, value_proj], axis=1))
-        total_rows = both.shape[0]
-        keys = both[:, :feat_width].reshape(total_rows, heads_here, HEAD_DIM)
-        values = both[:, feat_width:].reshape(total_rows, heads_here, HEAD_DIM)
-        key_pos = jnp.arange(total_rows, dtype=jnp.int32)
         row_pos = segment * seg_rows + jnp.arange(seg_rows, dtype=jnp.int32)
-        queries = query_proj.reshape(seg_rows, heads_here, HEAD_DIM)
-        scores = (
-            jnp.einsum("qhd,khd->hqk", queries, keys, preferred_element_type=jnp.float32)
-            * score_scale
-        )
-        allowed = (key_pos[None, :] <= row_pos[:, None])[None]
-        scores = jnp.where(allowed, scores, -1e30)
-        row_max = jnp.max(scores, axis=-1)
-        weights = jnp.where(allowed, jnp.exp(scores - row_max[..., None]), 0.0)
-        row_total = jnp.sum(weights, axis=-1)
-        numer = jnp.einsum(
-            "hqk,khd->hqd", weights.astype(jnp.bfloat16), values, preferred_element_type=jnp.float32
-        )
-        ratio = numer / row_total[..., None]
+        if square:
+            def by_head(x):
+                return x.reshape(seg_rows, heads_here, HEAD_DIM).transpose(1, 0, 2)
+
+            key_blocks = gather_blocks_square(by_head(key_proj))
+            value_blocks = gather_blocks_square(by_head(value_proj))
+            chip = lax.axis_index("hi")
+            core = lax.axis_index("lo")
+            key_starts = [
+                ((chip ^ (b // 2)) * 2 + (core ^ (b % 2))) * seg_rows for b in range(len(key_blocks))
+            ]
+            ratio = attention_by_head(by_head(query_proj), key_blocks, value_blocks, row_pos, key_starts)
+        else:
+            both = gather_seq(jnp.concatenate([key_proj, value_proj], axis=1))
+            total_rows = both.shape[0]
+            keys = both[:, :feat_width].reshape(total_rows, heads_here, HEAD_DIM)
+            values = both[:, feat_width:].reshape(total_rows, heads_here, HEAD_DIM)
+            key_pos = jnp.arange(total_rows, dtype=jnp.int32)
+            queries = query_proj.reshape(seg_rows, heads_here, HEAD_DIM)
+            scores = (
+                jnp.einsum("qhd,khd->hqk", queries, keys, preferred_element_type=jnp.float32)
+                * score_scale
+            )
+            allowed = (key_pos[None, :] <= row_pos[:, None])[None]
+            scores = jnp.where(allowed, scores, -1e30)
+            row_max = jnp.max(scores, axis=-1)
+            weights = jnp.where(allowed, jnp.exp(scores - row_max[..., None]), 0.0)
+            row_total = jnp.sum(weights, axis=-1)
+            numer = jnp.einsum(
+                "hqk,khd->hqd", weights.astype(jnp.bfloat16), values, preferred_element_type=jnp.float32
+            )
+            ratio = numer / row_total[..., None]
         local_context = ratio.transpose(1, 0, 2).reshape(seg_rows, feat_width).astype(jnp.bfloat16)
 
         gathered = gather_seq(local_context)

time: 204 us -> 184 us (0.902)
  local copies, waits for them, and re-layouts: 35.8 us -> 17.9 us
  waiting for transfers between devices: 86.1 us -> 73.4 us
  matrix products: 10.3 us -> 20.7 us
  other arithmetic: 9.15 us -> 4.93 us
  starting transfers between devices: 12.2 us -> 16 us
    ppermute x2 -> x1, waiting for transfers between devices: 33.8 us -> 12 us  [gather_seq_square(): from_x = lax.ppermute(x, 'hi', swap('hi', 1, 4))]
    ppermute x0 -> x16, waiting for transfers between devices: none -> 21.8 us  [the longest x2 14.8 us: gather_blocks_square(): from_y = lax.ppermute(x, 'hi', swap('hi', 2, 4))]
    ppermute x0 -> x16, starting transfers between devices: none -> 11.9 us  [the longest x2 3.11 us: gather_blocks_square(): from_y = lax.ppermute(x, 'hi', swap('hi', 2, 4))]
    dot_general x2 -> x16, matrix products: 2.62 us -> 10.3 us  [the longest x8 6.49 us: attention_by_head(): jnp.einsum('hqd,hkd->hqk', queries, keys, preferred_element_type=jnp.floa...]
    ppermute x2 -> x1, waiting for transfers between devices: 15.4 us -> 7.87 us  [gather_seq_square(): lax.ppermute(from_x[half:], 'hi', swap('hi', 2, 4))]
    dynamic_update_slice x13 -> x7, local copies, waits for them, and re-layouts: 13 us -> 6.23 us  [assemble(): out = lax.dynamic_update_slice(out, piece, (slot * rows, 0))]
    sub x1 -> x0, other arithmetic: 4.55 us -> none  [per_device(): weights = jnp.where(allowed, jnp.exp(scores - row_max[..., None]), 0.0)]
    slice x2 -> x4, local copies, waits for them, and re-layouts: 5.05 us -> 1.02 us  [the longest x2 0.99 us: gather_blocks_square(): from_y[:half]]
  transfers between devices with their start and end apart: 18 -> 26, of which waited for: 11 -> 12; matrix products, arithmetic and copies ran while one was open for 12% -> 17% of each run, Pallas kernels for 0% -> 0%
where the time goes in v7:
time: 184 us
  waiting for transfers between devices  73.4 us (40%)
  blocking collectives  36.8 us (20%)
  matrix products  20.7 us (11%)
  local copies, waits for them, and re-layouts  17.9 us (10%)
  starting transfers between devices  16 us (9%)
  between operations  13.8 us (8%)
  other arithmetic  4.93 us (3%)
    all_to_all x2, blocking collectives, per_device(): lax.all_to_all(partial, SEQ, split_axis=0, concat_axis=1, tiled=True)  36.8 us
    reduce_scatter x2, waiting for transfers between devices, per_device(): lax.psum_scatter(by_row, 'chan', scatter_dimension=1, tiled=True)  29.5 us
    ppermute x2, waiting for transfers between devices, gather_blocks_square(): from_y = lax.ppermute(x, 'hi', swap('hi', 2, 4))  14.8 us
    ppermute x1, waiting for transfers between devices, gather_seq_square(): from_x = lax.ppermute(x, 'hi', swap('hi', 1, 4))  12 us
    dot_general x2, matrix products, per_device(): jnp.dot(gathered, out_weight[:, j * width:(j + 1) * width], preferred_ele...  10.5 us
    ppermute x1, waiting for transfers between devices, gather_seq_square(): lax.ppermute(from_x[half:], 'hi', swap('hi', 2, 4))  7.87 us
    dot_general x8, matrix products, attention_by_head(): jnp.einsum('hqd,hkd->hqk', queries, keys, preferred_element_type=jnp.floa...  6.49 us
    dynamic_update_slice x7, local copies, waits for them, and re-layouts, assemble(): out = lax.dynamic_update_slice(out, piece, (slot * rows, 0))  6.23 us
  transfers between devices with their start and end apart: 26, of which 12 were waited for; matrix products, arithmetic and copies ran while one was open for 17% of the time, Pallas kernels for 0%

profile of v7, /device:TPU:0, one launch (start us, length us, event | category | flops | bytes accessed | tf_op | source)
XLA Modules:
  0.0 183.6 jit_solution(6268995229322505213)
XLA Ops:
  6.5 1.4 copy.40
  8.2 3.0 %collective-permute-start.3 = (bf16[16,128,128]{2,1,0:T(8,128)(2,1)S(1)}, bf16[16,128,128]{2,1,0:T(8,128)(2,1)}, u32[]{:S(2)}, u32[]{:S(2)}) collective-permute-start(bf16[16,128,128]{2,1,0:T(8,128)(2,1)S(1)} %bitcast.140), channel_id=1, source_target_pairs={{0,16},{8,24},{16,0},{24,8},{1,17},{9,25},{17,1},{25,9},{2,18},{10... | collective-permute-start | bytes 1572872 | tf_op jit(solution)/shard_map/ppermute | solution.py:71
  11.2 1.5 collective-permute-start.1
  16.1 8.0 %collective-permute-done.3 = bf16[16,128,128]{2,1,0:T(8,128)(2,1)} collective-permute-done((bf16[16,128,128]{2,1,0:T(8,128)(2,1)S(1)}, bf16[16,128,128]{2,1,0:T(8,128)(2,1)}, u32[]{:S(2)}, u32[]{:S(2)}) %collective-permute-start.3) | collective-permute-done | bytes 524320 | tf_op jit(solution)/shard_map/ppermute | solution.py:71
  26.1 1.5 collective-permute-start.5
  27.6 6.8 %collective-permute-done.11 = bf16[16,128,128]{1,2,0:T(8,128)(2,1)S(1)} collective-permute-done((bf16[16,128,128]{1,2,0:T(8,128)(2,1)S(1)}, bf16[16,128,128]{1,2,0:T(8,128)(2,1)S(1)}, u32[]{:S(2)}, u32[]{:S(2)}) %collective-permute-start.11) | collective-permute-done | bytes 524320 | tf_op jit(solution)/shard_map/ppermute | solution.py:71
  34.4 1.7 collective-permute-start.6
  37.3 1.5 collective-permute-start.13
  38.8 1.6 fusion.100
  41.6 1.6 fusion.104
  43.4 3.7 %collective-permute-done.13 = bf16[8,128,128]{1,2,0:T(8,128)(2,1)S(1)} collective-permute-done((bf16[8,128,128]{1,2,0:T(8,128)(2,1)S(1)}, bf16[8,128,128]{1,2,0:T(8,128)(2,1)S(1)}, u32[]{:S(2)}, u32[]{:S(2)}) %collective-permute-start.13) | collective-permute-done | bytes 262176 | tf_op jit(solution)/shard_map/ppermute | solution.py:74
  52.4 2.1 %fusion.28 = (f32[16,128]{1,0:T(8,128)S(1)}, f32[16,128]{1,0:T(8,128)S(1)}, f32[16,128]{1,0:T(8,128)S(1)}, f32[16,128]{1,0:T(8,128)S(1)}, f32[16,128]{1,0:T(8,128)S(1)}) fusion(f32[16,128,128]{2,1,0:T(8,128)S(1)} %get-tuple-element.42, f32[16,128]{1,0:T(8,128)S(1)} %maximum_maximum_fusion, pred[128,128]{1,0:T(8,128)(4,1)S(1)} %copy.43, ...), kind=kLoop, calls=%fused_computation.45 | loop fusion | flops 3921920 | bytes 5373952 | tf_op jit(solution)/shard_map/reduce_sum | solution.py:106
  58.4 1.5 collective-permute-start.17
  60.4 12.0 %collective-permute-done.17 = bf16[128,2048]{0,1:T(8,128)(2,1)S(1)} collective-permute-done((bf16[128,2048]{0,1:T(8,128)(2,1)S(1)}, bf16[128,2048]{0,1:T(8,128)(2,1)S(1)}, u32[]{:S(2)}, u32[]{:S(2)}) %collective-permute-start.17) | collective-permute-done | bytes 524320 | tf_op jit(solution)/shard_map/ppermute | solution.py:51
  72.4 2.6 %broadcast_in_dim.124 = bf16[1024,2048]{0,1:T(8,128)(2,1)} broadcast(bf16[]{:T(256)} %constant.4.clone.1), dimensions={} | broadcast | bytes 4194306 | tf_op jit(solution)/shard_map/broadcast_in_dim | solution.py:40
  76.8 1.4 collective-permute-start.21
  82.7 7.9 %collective-permute-done.22 = bf16[64,2048]{0,1:T(8,128)(2,1)S(1)} collective-permute-done((bf16[64,2048]{0,1:T(8,128)(2,1)S(1)}, bf16[64,2048]{0,1:T(8,128)(2,1)S(1)}, u32[]{:S(2)}, u32[]{:S(2)}) %collective-permute-start.22) | collective-permute-done | bytes 262176 | tf_op jit(solution)/shard_map/ppermute | solution.py:56
  91.9 1.9 %collective-permute-done.23 = bf16[128,2048]{0,1:T(8,128)(2,1)S(1)} collective-permute-done((bf16[128,2048]{0,1:T(8,128)(2,1)S(1)}, bf16[128,2048]{0,1:T(8,128)(2,1)S(1)}, u32[]{:S(2)}, u32[]{:S(2)}) %collective-permute-start.23) | collective-permute-done | bytes 524320 | tf_op jit(solution)/shard_map/ppermute | solution.py:64
  94.7 5.2 %fusion.4 = bf16[1024,512]{1,0:T(8,128)(2,1)S(1)} fusion(bf16[1024,2048]{0,1:T(8,128)(2,1)} %constant_dynamic-update-slice_fusion.4, bf16[2048,1024]{1,0:T(8,128)(2,1)} %param.9), kind=kOutput, calls=%fused_computation.4 | convolution fusion | flops 2148007936 | bytes 7340032 | tf_op jit(solution)/shard_map/dot_general | solution.py:171
  100.0 18.9 %all_to_all.38 = bf16[8,128,512]{2,1,0:T(8,128)(2,1)S(1)} all-to-all(bf16[8,128,512]{2,1,0:T(8,128)(2,1)S(1)} %bitcast.139), channel_id=1, replica_groups=mesh['hi'=4,'lo'=2,'chan'=4] {'hi','lo'}, dimensions={0} | all-to-all | bytes 2097152 | tf_op jit(solution)/shard_map/all_to_all | solution.py:174
  120.0 5.2 %fusion.7 = bf16[1024,512]{1,0:T(8,128)(2,1)S(1)} fusion(bf16[1024,2048]{0,1:T(8,128)(2,1)} %constant_dynamic-update-slice_fusion.4, bf16[2048,1024]{1,0:T(8,128)(2,1)} %param.9), kind=kOutput, calls=%fused_computation.5 | convolution fusion | flops 2148007936 | bytes 7340032 | tf_op jit(solution)/shard_map/dot_general | solution.py:171
  125.2 17.9 %all_to_all.39 = bf16[8,128,512]{2,1,0:T(8,128)(2,1)S(1)} all-to-all(bf16[8,128,512]{2,1,0:T(8,128)(2,1)S(1)} %bitcast.138), channel_id=1, replica_groups=mesh['hi'=4,'lo'=2,'chan'=4] {'hi','lo'}, dimensions={0} | all-to-all | bytes 2097152 | tf_op jit(solution)/shard_map/all_to_all | solution.py:174
  144.3 2.3 %reduce-scatter.3.cloned.1.call-done = bf16[128,1024]{1,0:T(8,128)(2,1)} async-done(((bf16[128,4096]{1,0:T(8,128)(2,1)}), bf16[128,1024]{1,0:T(8,128)(2,1)}) %reduce-scatter.3.cloned.1.call-update) | async-done | bytes 262160 | tf_op jit(solution)/shard_map/reduce_scatter | solution.py:176
  147.6 27.2 %reduce-scatter.5.cloned.1.call-done = bf16[128,1024]{1,0:T(8,128)(2,1)} async-done(((bf16[128,4096]{1,0:T(8,128)(2,1)}), bf16[128,1024]{1,0:T(8,128)(2,1)}) %reduce-scatter.5.cloned.1.call-update) | async-done | bytes 262160 | tf_op jit(solution)/shard_map/reduce_scatter | solution.py:176
  (94 shorter events, 31.2 us)
Async XLA Ops:
  6.5 140.1 %reduce-scatter.3.cloned.1.call-start = ((), (), s32[]{:S(2)}) async-start(), calls=%async_computation.4 | async-start | bytes 1310720 | tf_op jit(solution)/shard_map/reduce_scatter | solution.py:176
  8.2 15.9 %collective-permute-start.3 = (bf16[16,128,128]{2,1,0:T(8,128)(2,1)S(1)}, bf16[16,128,128]{2,1,0:T(8,128)(2,1)}, u32[]{:S(2)}, u32[]{:S(2)}) collective-permute-start(bf16[16,128,128]{2,1,0:T(8,128)(2,1)S(1)} %bitcast.140), channel_id=1, source_target_pairs={{0,16},{8,24},{16,0},{24,8},{1,17},{9,25},{17,1},{25,9},{2,18},{10... | collective-permute-start | bytes 1572872 | tf_op jit(solution)/shard_map/ppermute | solution.py:71
  11.2 14.8 %collective-permute-start.1 = (bf16[16,128,128]{2,1,0:T(8,128)(2,1)S(1)}, bf16[16,128,128]{2,1,0:T(8,128)(2,1)S(1)}, u32[]{:S(2)}, u32[]{:S(2)}) collective-permute-start(bf16[16,128,128]{2,1,0:T(8,128)(2,1)S(1)} %bitcast.141), channel_id=1, source_target_pairs={{0,8},{8,0},{16,24},{24,16},{1,9},{9,1},{17,25},{25,17},{2,10},{10... | collective-permute-start | bytes 1572872 | tf_op jit(solution)/shard_map/ppermute | solution.py:70
  12.7 28.3 %collective-permute-start = (bf16[16,128,128]{2,1,0:T(8,128)(2,1)S(1)}, bf16[16,128,128]{2,1,0:T(8,128)(2,1)}, u32[]{:S(2)}, u32[]{:S(2)}) collective-permute-start(bf16[16,128,128]{2,1,0:T(8,128)(2,1)S(1)} %bitcast.142), channel_id=1, source_target_pairs={{0,4},{4,0},{1,5},{5,1},{2,6},{6,2},{3,7},{7,3},{8,12},{12,8},{9,1... | collective-permute-start | bytes 1572872 | tf_op jit(solution)/shard_map/ppermute | solution.py:82
  14.0 23.3 %collective-permute-start.9 = (bf16[16,128,128]{1,2,0:T(8,128)(2,1)S(1)}, bf16[16,128,128]{1,2,0:T(8,128)(2,1)S(1)}, u32[]{:S(2)}, u32[]{:S(2)}) collective-permute-start(bf16[16,128,128]{1,2,0:T(8,128)(2,1)S(1)} %bitcast.133), channel_id=1, source_target_pairs={{0,8},{8,0},{16,24},{24,16},{1,9},{9,1},{17,25},{25,17},{2,10},{10... | collective-permute-start | bytes 1572872 | tf_op jit(solution)/shard_map/ppermute | solution.py:70
  14.6 19.7 %collective-permute-start.11 = (bf16[16,128,128]{1,2,0:T(8,128)(2,1)S(1)}, bf16[16,128,128]{1,2,0:T(8,128)(2,1)S(1)}, u32[]{:S(2)}, u32[]{:S(2)}) collective-permute-start(bf16[16,128,128]{1,2,0:T(8,128)(2,1)S(1)} %bitcast.134), channel_id=1, source_target_pairs={{0,16},{8,24},{16,0},{24,8},{1,17},{9,25},{17,1},{25,9},{2,18},{10... | collective-permute-start | bytes 1572872 | tf_op jit(solution)/shard_map/ppermute | solution.py:71
  24.1 30.4 %collective-permute-start.8 = (bf16[16,128,128]{1,2,0:T(8,128)(2,1)S(1)}, bf16[16,128,128]{1,2,0:T(8,128)(2,1)S(1)}, u32[]{:S(2)}, u32[]{:S(2)}) collective-permute-start(bf16[16,128,128]{1,2,0:T(8,128)(2,1)S(1)} %bitcast.135), channel_id=1, source_target_pairs={{0,4},{4,0},{1,5},{5,1},{2,6},{6,2},{3,7},{7,3},{8,12},{12,8},{9,1... | collective-permute-start | bytes 1572872 | tf_op jit(solution)/shard_map/ppermute | solution.py:82
  26.1 17.2 %collective-permute-start.5 = (bf16[8,128,128]{2,1,0:T(8,128)(2,1)S(1)}, bf16[8,128,128]{2,1,0:T(8,128)(2,1)S(1)}, u32[]{:S(2)}, u32[]{:S(2)}) collective-permute-start(bf16[8,128,128]{2,1,0:T(8,128)(2,1)S(1)} %slice.48), channel_id=1, source_target_pairs={{0,8},{8,0},{16,24},{24,16},{1,9},{9,1},{17,25},{25,17},{2,10},{10... | collective-permute-start | bytes 786440 | tf_op jit(solution)/shard_map/ppermute | solution.py:74
  34.4 12.7 %collective-permute-start.6 = (bf16[8,128,128]{2,1,0:T(8,128)(2,1)S(1)}, bf16[8,128,128]{2,1,0:T(8,128)(2,1)S(1)}, u32[]{:S(2)}, u32[]{:S(2)}) collective-permute-start(bf16[8,128,128]{2,1,0:T(8,128)(2,1)S(1)} %slice.49), channel_id=1, source_target_pairs={{0,16},{8,24},{16,0},{24,8},{1,17},{9,25},{17,1},{25,9},{2,18},{10... | collective-permute-start | bytes 786440 | tf_op jit(solution)/shard_map/ppermute | solution.py:75
  37.3 9.8 %collective-permute-start.13 = (bf16[8,128,128]{1,2,0:T(8,128)(2,1)S(1)}, bf16[8,128,128]{1,2,0:T(8,128)(2,1)S(1)}, u32[]{:S(2)}, u32[]{:S(2)}) collective-permute-start(bf16[8,128,128]{1,2,0:T(8,128)(2,1)S(1)} %slice.50), channel_id=1, source_target_pairs={{0,8},{8,0},{16,24},{24,16},{1,9},{9,1},{17,25},{25,17},{2,10},{10... | collective-permute-start | bytes 786440 | tf_op jit(solution)/shard_map/ppermute | solution.py:74
  41.0 6.7 %collective-permute-start.14 = (bf16[8,128,128]{1,2,0:T(8,128)(2,1)S(1)}, bf16[8,128,128]{1,2,0:T(8,128)(2,1)S(1)}, u32[]{:S(2)}, u32[]{:S(2)}) collective-permute-start(bf16[8,128,128]{1,2,0:T(8,128)(2,1)S(1)} %slice.51), channel_id=1, source_target_pairs={{0,16},{8,24},{16,0},{24,8},{1,17},{9,25},{17,1},{25,9},{2,18},{10... | collective-permute-start | bytes 786440 | tf_op jit(solution)/shard_map/ppermute | solution.py:75
  43.3 5.1 %collective-permute-start.4 = (bf16[16,128,128]{2,1,0:T(8,128)(2,1)}, bf16[16,128,128]{2,1,0:T(8,128)(2,1)S(1)}, u32[]{:S(2)}, u32[]{:S(2)}) collective-permute-start(bf16[16,128,128]{2,1,0:T(8,128)(2,1)} %collective-permute-done.3), channel_id=1, source_target_pairs={{0,4},{4,0},{1,5},{5,1},{2,6},{6,2},{3,7},{7,3},{8,12},{12,8},{9,1... | collective-permute-start | bytes 1572872 | tf_op jit(solution)/shard_map/ppermute | solution.py:82
  47.1 10.0 %collective-permute-start.10 = (bf16[16,128,128]{1,2,0:T(8,128)(2,1)S(1)}, bf16[16,128,128]{1,2,0:T(8,128)(2,1)S(1)}, u32[]{:S(2)}, u32[]{:S(2)}) collective-permute-start(bf16[16,128,128]{1,2,0:T(8,128)(2,1)S(1)} %collective-permute-done.9), channel_id=1, source_target_pairs={{0,4},{4,0},{1,5},{5,1},{2,6},{6,2},{3,7},{7,3},{8,12},{12,8},{9,1... | collective-permute-start | bytes 1572872 | tf_op jit(solution)/shard_map/ppermute | solution.py:82
  47.7 10.0 %collective-permute-start.12 = (bf16[16,128,128]{1,2,0:T(8,128)(2,1)S(1)}, bf16[16,128,128]{1,2,0:T(8,128)(2,1)S(1)}, u32[]{:S(2)}, u32[]{:S(2)}) collective-permute-start(bf16[16,128,128]{1,2,0:T(8,128)(2,1)S(1)} %collective-permute-done.11), channel_id=1, source_target_pairs={{0,4},{4,0},{1,5},{5,1},{2,6},{6,2},{3,7},{7,3},{8,12},{12,8},{9,1... | collective-permute-start | bytes 1572872 | tf_op jit(solution)/shard_map/ppermute | solution.py:82
  48.4 2.9 %collective-permute-start.7 = (bf16[16,128,128]{2,1,0:T(8,128)(2,1)S(1)}, bf16[16,128,128]{2,1,0:T(8,128)(2,1)S(1)}, u32[]{:S(2)}, u32[]{:S(2)}) collective-permute-start(bf16[16,128,128]{2,1,0:T(8,128)(2,1)S(1)} %constant_dynamic-update-slice_fusion), channel_id=1, source_target_pairs={{0,4},{4,0},{1,5},{5,1},{2,6},{6,2},{3,7},{7,3},{8,12},{12,8},{9,1... | collective-permute-start | bytes 1572872 | tf_op jit(solution)/shard_map/ppermute | solution.py:82
  49.5 7.3 %collective-permute-start.15 = (bf16[16,128,128]{1,2,0:T(8,128)(2,1)S(1)}, bf16[16,128,128]{1,2,0:T(8,128)(2,1)S(1)}, u32[]{:S(2)}, u32[]{:S(2)}) collective-permute-start(bf16[16,128,128]{1,2,0:T(8,128)(2,1)S(1)} %constant_dynamic-update-slice_fusion.2), channel_id=1, source_target_pairs={{0,4},{4,0},{1,5},{5,1},{2,6},{6,2},{3,7},{7,3},{8,12},{12,8},{9,1... | collective-permute-start | bytes 1572872 | tf_op jit(solution)/shard_map/ppermute | solution.py:82
  58.4 14.0 %collective-permute-start.17 = (bf16[128,2048]{0,1:T(8,128)(2,1)S(1)}, bf16[128,2048]{0,1:T(8,128)(2,1)S(1)}, u32[]{:S(2)}, u32[]{:S(2)}) collective-permute-start(bf16[128,2048]{0,1:T(8,128)(2,1)S(1)} %bitcast.144), channel_id=1, source_target_pairs={{0,8},{8,0},{16,24},{24,16},{1,9},{9,1},{17,25},{25,17},{2,10},{10... | collective-permute-start | bytes 1572872 | tf_op jit(solution)/shard_map/ppermute | solution.py:51
  59.9 16.9 %collective-permute-start.19 = (bf16[128,2048]{0,1:T(8,128)(2,1)S(1)}, bf16[128,2048]{0,1:T(8,128)(2,1)S(1)}, u32[]{:S(2)}, u32[]{:S(2)}) collective-permute-start(bf16[128,2048]{0,1:T(8,128)(2,1)S(1)} %bitcast.145), channel_id=1, source_target_pairs={{0,16},{8,24},{16,0},{24,8},{1,17},{9,25},{17,1},{25,9},{2,18},{10... | collective-permute-start | bytes 1572872 | tf_op jit(solution)/shard_map/ppermute | solution.py:52
  60.4 17.8 %collective-permute-start.16 = (bf16[128,2048]{0,1:T(8,128)(2,1)S(1)}, bf16[128,2048]{0,1:T(8,128)(2,1)S(1)}, u32[]{:S(2)}, u32[]{:S(2)}) collective-permute-start(bf16[128,2048]{0,1:T(8,128)(2,1)S(1)} %bitcast.146), channel_id=1, source_target_pairs={{0,4},{4,0},{1,5},{5,1},{2,6},{6,2},{3,7},{7,3},{8,12},{12,8},{9,1... | collective-permute-start | bytes 1572872 | tf_op jit(solution)/shard_map/ppermute | solution.py:64
  72.4 7.6 %collective-permute-start.18 = (bf16[128,2048]{0,1:T(8,128)(2,1)S(1)}, bf16[128,2048]{0,1:T(8,128)(2,1)S(1)}, u32[]{:S(2)}, u32[]{:S(2)}) collective-permute-start(bf16[128,2048]{0,1:T(8,128)(2,1)S(1)} %collective-permute-done.17), channel_id=1, source_target_pairs={{0,4},{4,0},{1,5},{5,1},{2,6},{6,2},{3,7},{7,3},{8,12},{12,8},{9,1... | collective-permute-start | bytes 1572872 | tf_op jit(solution)/shard_map/ppermute | solution.py:64
  76.1 14.4 %collective-permute-start.22 = (bf16[64,2048]{0,1:T(8,128)(2,1)S(1)}, bf16[64,2048]{0,1:T(8,128)(2,1)S(1)}, u32[]{:S(2)}, u32[]{:S(2)}) collective-permute-start(bf16[64,2048]{0,1:T(8,128)(2,1)S(1)} %slice.53), channel_id=1, source_target_pairs={{0,16},{8,24},{16,0},{24,8},{1,17},{9,25},{17,1},{25,9},{2,18},{10... | collective-permute-start | bytes 786440 | tf_op jit(solution)/shard_map/ppermute | solution.py:56
  76.8 14.1 %collective-permute-start.21 = (bf16[64,2048]{0,1:T(8,128)(2,1)S(1)}, bf16[64,2048]{0,1:T(8,128)(2,1)S(1)}, u32[]{:S(2)}, u32[]{:S(2)}) collective-permute-start(bf16[64,2048]{0,1:T(8,128)(2,1)S(1)} %bitcast.143), channel_id=1, source_target_pairs={{0,8},{8,0},{16,24},{24,16},{1,9},{9,1},{17,25},{25,17},{2,10},{10... | collective-permute-start | bytes 786440 | tf_op jit(solution)/shard_map/ppermute | solution.py:55
  78.2 3.6 %collective-permute-start.20 = (bf16[128,2048]{0,1:T(8,128)(2,1)S(1)}, bf16[128,2048]{0,1:T(8,128)(2,1)S(1)}, u32[]{:S(2)}, u32[]{:S(2)}) collective-permute-start(bf16[128,2048]{0,1:T(8,128)(2,1)S(1)} %collective-permute-done.19), channel_id=1, source_target_pairs={{0,4},{4,0},{1,5},{5,1},{2,6},{6,2},{3,7},{7,3},{8,12},{12,8},{9,1... | collective-permute-start | bytes 1572872 | tf_op jit(solution)/shard_map/ppermute | solution.py:64
  119.9 54.9 %reduce-scatter.5.cloned.1.call-start = ((), (), s32[]{:S(2)}) async-start(), calls=%async_computation.5 | async-start | bytes 1310720 | tf_op jit(solution)/shard_map/reduce_scatter | solution.py:176
  (4 other events, 64.0 us)
Sparse Core Ops, SparseCore 0:
  120.1 26.4 reduce-scatter.2
  149.0 25.7 reduce-scatter.4

commit v8 on v7

--- a/solution.py
+++ b/solution.py
@@ -164,19 +164,26 @@
 
         gathered = gather_seq(local_context)
         group = seq_count // chan_count
-        chunks = 2
-        width = out_weight.shape[1] // chunks
+        total = out_weight.shape[1]
+        widths = [total // 4, total - total // 4]
         reduced = []
-        for j in range(chunks):
+        offset = 0
+        for width in widths:
             partial = jnp.dot(
-                gathered, out_weight[:, j * width : (j + 1) * width], preferred_element_type=jnp.float32
+                gathered, out_weight[:, offset : offset + width], preferred_element_type=jnp.float32
             ).astype(jnp.bfloat16)
+            offset += width
             by_row = lax.all_to_all(partial, SEQ, split_axis=0, concat_axis=1, tiled=True)
             reduced.append(
                 lax.psum_scatter(by_row, "chan", scatter_dimension=1, tiled=True)
             )
         ordered = jnp.concatenate(
-            [part[:, b * width : (b + 1) * width] for b in range(group) for part in reduced], axis=1
+            [
+                part[:, b * width : (b + 1) * width]
+                for b in range(group)
+                for part, width in zip(reduced, widths)
+            ],
+            axis=1,
         )
         return (residual.astype(jnp.float32) + ordered.astype(jnp.float32)).astype(jnp.bfloat16)
 

time: 184 us -> 188 us (1.022)
  blocking collectives: 36.8 us -> 0 us
  waiting for transfers between devices: 73.4 us -> 105 us
  starting transfers between devices: 16 us -> 23.4 us
  matrix products: 20.7 us -> 22.7 us
    all_to_all x2 -> x0, blocking collectives: 36.8 us -> none  [per_device(): lax.all_to_all(partial, SEQ, split_axis=0, concat_axis=1, tiled=True)]
    all_to_all x0 -> x2, waiting for transfers between devices: none -> 21.9 us  [per_device(): lax.all_to_all(partial, SEQ, split_axis=0, concat_axis=1, tiled=True)]
    reduce_scatter x2, waiting for transfers between devices: 29.5 us -> 39.1 us  [per_device(): lax.psum_scatter(by_row, 'chan', scatter_dimension=1, tiled=True)]
    all_to_all x0 -> x2, starting transfers between devices: none -> 7.33 us  [per_device(): lax.all_to_all(partial, SEQ, split_axis=0, concat_axis=1, tiled=True)]
    dot_general x2, matrix products: 10.5 us -> 12.4 us  [per_device(): jnp.dot(gathered, out_weight[:, offset:offset + width], preferred_element...]
  transfers between devices with their start and end apart: 26 -> 28, of which waited for: 12 -> 14; matrix products, arithmetic and copies ran while one was open for 17% -> 19% of each run, Pallas kernels for 0% -> 0%
where the time goes in v8:
time: 188 us; the launch traced here: 187 us
  waiting for transfers between devices  105 us (56%)
  starting transfers between devices  23.4 us (12%)
  matrix products  22.7 us (12%)
  local copies, waits for them, and re-layouts  17.9 us (10%)
  between operations  13.8 us (7%)
  other arithmetic  4.94 us (3%)
    reduce_scatter x2, waiting for transfers between devices, per_device(): lax.psum_scatter(by_row, 'chan', scatter_dimension=1, tiled=True)  39.1 us
    all_to_all x2, waiting for transfers between devices, per_device(): lax.all_to_all(partial, SEQ, split_axis=0, concat_axis=1, tiled=True)  21.9 us
    ppermute x2, waiting for transfers between devices, gather_blocks_square(): from_y = lax.ppermute(x, 'hi', swap('hi', 2, 4))  14.8 us
    dot_general x2, matrix products, per_device(): jnp.dot(gathered, out_weight[:, offset:offset + width], preferred_element...  12.4 us
    ppermute x1, waiting for transfers between devices, gather_seq_square(): from_x = lax.ppermute(x, 'hi', swap('hi', 1, 4))  12 us
    ppermute x1, waiting for transfers between devices, gather_seq_square(): lax.ppermute(from_x[half:], 'hi', swap('hi', 2, 4))  7.88 us
    all_to_all x2, starting transfers between devices, per_device(): lax.all_to_all(partial, SEQ, split_axis=0, concat_axis=1, tiled=True)  7.33 us
    dot_general x8, matrix products, attention_by_head(): jnp.einsum('hqd,hkd->hqk', queries, keys, preferred_element_type=jnp.floa...  6.48 us
  transfers between devices with their start and end apart: 28, of which 14 were waited for; matrix products, arithmetic and copies ran while one was open for 19% of the time, Pallas kernels for 0%

profile of v8, /device:TPU:0, one launch (start us, length us, event | category | flops | bytes accessed | tf_op | source)
XLA Modules:
  0.0 187.5 jit_solution(16094348183771492194)
XLA Ops:
  8.2 3.0 %collective-permute-start.3 = (bf16[16,128,128]{2,1,0:T(8,128)(2,1)S(1)}, bf16[16,128,128]{2,1,0:T(8,128)(2,1)}, u32[]{:S(2)}, u32[]{:S(2)}) collective-permute-start(bf16[16,128,128]{2,1,0:T(8,128)(2,1)S(1)} %bitcast.139), channel_id=1, source_target_pairs={{0,16},{8,24},{16,0},{24,8},{1,17},{9,25},{17,1},{25,9},{2,18},{10... | collective-permute-start | bytes 1572872 | tf_op jit(solution)/shard_map/ppermute | solution.py:71
  11.2 1.5 collective-permute-start.1
  16.1 8.0 %collective-permute-done.3 = bf16[16,128,128]{2,1,0:T(8,128)(2,1)} collective-permute-done((bf16[16,128,128]{2,1,0:T(8,128)(2,1)S(1)}, bf16[16,128,128]{2,1,0:T(8,128)(2,1)}, u32[]{:S(2)}, u32[]{:S(2)}) %collective-permute-start.3) | collective-permute-done | bytes 524320 | tf_op jit(solution)/shard_map/ppermute | solution.py:71
  26.1 1.5 collective-permute-start.5
  27.6 6.8 %collective-permute-done.11 = bf16[16,128,128]{1,2,0:T(8,128)(2,1)S(1)} collective-permute-done((bf16[16,128,128]{1,2,0:T(8,128)(2,1)S(1)}, bf16[16,128,128]{1,2,0:T(8,128)(2,1)S(1)}, u32[]{:S(2)}, u32[]{:S(2)}) %collective-permute-start.11) | collective-permute-done | bytes 524320 | tf_op jit(solution)/shard_map/ppermute | solution.py:71
  34.4 1.7 collective-permute-start.6
  37.3 1.5 collective-permute-start.13
  38.8 1.6 fusion.96
  41.6 1.6 fusion.100
  43.4 3.7 %collective-permute-done.13 = bf16[8,128,128]{1,2,0:T(8,128)(2,1)S(1)} collective-permute-done((bf16[8,128,128]{1,2,0:T(8,128)(2,1)S(1)}, bf16[8,128,128]{1,2,0:T(8,128)(2,1)S(1)}, u32[]{:S(2)}, u32[]{:S(2)}) %collective-permute-start.13) | collective-permute-done | bytes 262176 | tf_op jit(solution)/shard_map/ppermute | solution.py:74
  52.4 2.1 %fusion.24 = (f32[16,128]{1,0:T(8,128)S(1)}, f32[16,128]{1,0:T(8,128)S(1)}, f32[16,128]{1,0:T(8,128)S(1)}, f32[16,128]{1,0:T(8,128)S(1)}, f32[16,128]{1,0:T(8,128)S(1)}) fusion(f32[16,128,128]{2,1,0:T(8,128)S(1)} %get-tuple-element.42, f32[16,128]{1,0:T(8,128)S(1)} %maximum_maximum_fusion, pred[128,128]{1,0:T(8,128)(4,1)S(1)} %copy.43, ...), kind=kLoop, calls=%fused_computation.44 | loop fusion | flops 3921920 | bytes 5373952 | tf_op jit(solution)/shard_map/reduce_sum | solution.py:106
  58.4 1.6 collective-permute-start.17
  60.4 12.0 %collective-permute-done.17 = bf16[128,2048]{0,1:T(8,128)(2,1)S(1)} collective-permute-done((bf16[128,2048]{0,1:T(8,128)(2,1)S(1)}, bf16[128,2048]{0,1:T(8,128)(2,1)S(1)}, u32[]{:S(2)}, u32[]{:S(2)}) %collective-permute-start.17) | collective-permute-done | bytes 524320 | tf_op jit(solution)/shard_map/ppermute | solution.py:51
  72.4 2.6 %broadcast_in_dim.124 = bf16[1024,2048]{0,1:T(8,128)(2,1)} broadcast(bf16[]{:T(256)} %constant.4.clone.1), dimensions={} | broadcast | bytes 4194306 | tf_op jit(solution)/shard_map/broadcast_in_dim | solution.py:40
  82.7 7.9 %collective-permute-done.22 = bf16[64,2048]{0,1:T(8,128)(2,1)S(1)} collective-permute-done((bf16[64,2048]{0,1:T(8,128)(2,1)S(1)}, bf16[64,2048]{0,1:T(8,128)(2,1)S(1)}, u32[]{:S(2)}, u32[]{:S(2)}) %collective-permute-start.22) | collective-permute-done | bytes 262176 | tf_op jit(solution)/shard_map/ppermute | solution.py:56
  91.9 1.9 %collective-permute-done.23 = bf16[128,2048]{0,1:T(8,128)(2,1)S(1)} collective-permute-done((bf16[128,2048]{0,1:T(8,128)(2,1)S(1)}, bf16[128,2048]{0,1:T(8,128)(2,1)S(1)}, u32[]{:S(2)}, u32[]{:S(2)}) %collective-permute-start.23) | collective-permute-done | bytes 524320 | tf_op jit(solution)/shard_map/ppermute | solution.py:64
  94.7 4.6 %convolution_convert_fusion = bf16[1024,256]{1,0:T(8,128)(2,1)} fusion(bf16[1024,2048]{0,1:T(8,128)(2,1)} %constant_dynamic-update-slice_fusion.4, bf16[2048,1024]{1,0:T(8,128)(2,1)} %param.9), kind=kOutput, calls=%fused_computation.31 | convolution fusion | flops 1074003968 | bytes 5767168 | tf_op jit(solution)/shard_map/dot_general | solution.py:172
  99.3 3.7 %all-to-all-start = ((bf16[8,128,256]{2,1,0:T(8,128)(2,1)}), bf16[8,128,256]{2,1,0:T(8,128)(2,1)S(1)}, u32[]{:S(2)}, u32[]{:S(2)}) async-start(bf16[8,128,256]{2,1,0:T(8,128)(2,1)} %bitcast.11), calls=%async_computation | async-start | bytes 1048576 | tf_op jit(solution)/shard_map/all_to_all | solution.py:176
  103.0 7.9 %fusion.2 = bf16[1024,768]{1,0:T(8,128)(2,1)} fusion(bf16[1024,2048]{0,1:T(8,128)(2,1)} %constant_dynamic-update-slice_fusion.4, bf16[2048,1024]{1,0:T(8,128)(2,1)} %param.9), kind=kOutput, calls=%fused_computation.2 | convolution fusion | flops 3222011904 | bytes 8912896 | tf_op jit(solution)/shard_map/dot_general | solution.py:172
  110.9 1.9 %all-to-all-done = bf16[8,128,256]{2,1,0:T(8,128)(2,1)S(1)} async-done(((bf16[8,128,256]{2,1,0:T(8,128)(2,1)}), bf16[8,128,256]{2,1,0:T(8,128)(2,1)S(1)}, u32[]{:S(2)}, u32[]{:S(2)}) %all-to-all-start) | async-done | bytes 524320 | tf_op jit(solution)/shard_map/all_to_all | solution.py:176
  112.8 3.6 %all-to-all-start.1 = ((bf16[8,128,768]{2,1,0:T(8,128)(2,1)}), bf16[8,128,768]{2,1,0:T(8,128)(2,1)S(1)}, u32[]{:S(2)}, u32[]{:S(2)}) async-start(bf16[8,128,768]{2,1,0:T(8,128)(2,1)} %bitcast.138), calls=%async_computation.2 | async-start | bytes 3145728 | tf_op jit(solution)/shard_map/all_to_all | solution.py:176
  117.4 20.0 %all-to-all-done.1 = bf16[8,128,768]{2,1,0:T(8,128)(2,1)S(1)} async-done(((bf16[8,128,768]{2,1,0:T(8,128)(2,1)}), bf16[8,128,768]{2,1,0:T(8,128)(2,1)S(1)}, u32[]{:S(2)}, u32[]{:S(2)}) %all-to-all-start.1) | async-done | bytes 1572896 | tf_op jit(solution)/shard_map/all_to_all | solution.py:176
  138.7 4.1 %reduce-scatter.3.cloned.1.call-done = bf16[128,512]{1,0:T(8,128)(2,1)} async-done(((bf16[128,2048]{1,0:T(8,128)(2,1)}), bf16[128,512]{1,0:T(8,128)(2,1)}) %reduce-scatter.3.cloned.1.call-update) | async-done | bytes 131088 | tf_op jit(solution)/shard_map/reduce_scatter | solution.py:178
  143.6 35.0 %reduce-scatter.5.cloned.1.call-done = bf16[128,1536]{1,0:T(8,128)(2,1)} async-done(((bf16[128,6144]{1,0:T(8,128)(2,1)}), bf16[128,1536]{1,0:T(8,128)(2,1)}) %reduce-scatter.5.cloned.1.call-update) | async-done | bytes 393232 | tf_op jit(solution)/shard_map/reduce_scatter | solution.py:178
  (96 shorter events, 34.0 us)
Async XLA Ops:
  8.2 15.9 %collective-permute-start.3 = (bf16[16,128,128]{2,1,0:T(8,128)(2,1)S(1)}, bf16[16,128,128]{2,1,0:T(8,128)(2,1)}, u32[]{:S(2)}, u32[]{:S(2)}) collective-permute-start(bf16[16,128,128]{2,1,0:T(8,128)(2,1)S(1)} %bitcast.139), channel_id=1, source_target_pairs={{0,16},{8,24},{16,0},{24,8},{1,17},{9,25},{17,1},{25,9},{2,18},{10... | collective-permute-start | bytes 1572872 | tf_op jit(solution)/shard_map/ppermute | solution.py:71
  11.2 14.8 %collective-permute-start.1 = (bf16[16,128,128]{2,1,0:T(8,128)(2,1)S(1)}, bf16[16,128,128]{2,1,0:T(8,128)(2,1)S(1)}, u32[]{:S(2)}, u32[]{:S(2)}) collective-permute-start(bf16[16,128,128]{2,1,0:T(8,128)(2,1)S(1)} %bitcast.140), channel_id=1, source_target_pairs={{0,8},{8,0},{16,24},{24,16},{1,9},{9,1},{17,25},{25,17},{2,10},{10... | collective-permute-start | bytes 1572872 | tf_op jit(solution)/shard_map/ppermute | solution.py:70
  12.7 28.3 %collective-permute-start = (bf16[16,128,128]{2,1,0:T(8,128)(2,1)S(1)}, bf16[16,128,128]{2,1,0:T(8,128)(2,1)}, u32[]{:S(2)}, u32[]{:S(2)}) collective-permute-start(bf16[16,128,128]{2,1,0:T(8,128)(2,1)S(1)} %bitcast.141), channel_id=1, source_target_pairs={{0,4},{4,0},{1,5},{5,1},{2,6},{6,2},{3,7},{7,3},{8,12},{12,8},{9,1... | collective-permute-start | bytes 1572872 | tf_op jit(solution)/shard_map/ppermute | solution.py:82
  14.0 23.3 %collective-permute-start.9 = (bf16[16,128,128]{1,2,0:T(8,128)(2,1)S(1)}, bf16[16,128,128]{1,2,0:T(8,128)(2,1)S(1)}, u32[]{:S(2)}, u32[]{:S(2)}) collective-permute-start(bf16[16,128,128]{1,2,0:T(8,128)(2,1)S(1)} %bitcast.131), channel_id=1, source_target_pairs={{0,8},{8,0},{16,24},{24,16},{1,9},{9,1},{17,25},{25,17},{2,10},{10... | collective-permute-start | bytes 1572872 | tf_op jit(solution)/shard_map/ppermute | solution.py:70
  14.6 19.7 %collective-permute-start.11 = (bf16[16,128,128]{1,2,0:T(8,128)(2,1)S(1)}, bf16[16,128,128]{1,2,0:T(8,128)(2,1)S(1)}, u32[]{:S(2)}, u32[]{:S(2)}) collective-permute-start(bf16[16,128,128]{1,2,0:T(8,128)(2,1)S(1)} %bitcast.132), channel_id=1, source_target_pairs={{0,16},{8,24},{16,0},{24,8},{1,17},{9,25},{17,1},{25,9},{2,18},{10... | collective-permute-start | bytes 1572872 | tf_op jit(solution)/shard_map/ppermute | solution.py:71
  24.1 30.4 %collective-permute-start.8 = (bf16[16,128,128]{1,2,0:T(8,128)(2,1)S(1)}, bf16[16,128,128]{1,2,0:T(8,128)(2,1)S(1)}, u32[]{:S(2)}, u32[]{:S(2)}) collective-permute-start(bf16[16,128,128]{1,2,0:T(8,128)(2,1)S(1)} %bitcast.133), channel_id=1, source_target_pairs={{0,4},{4,0},{1,5},{5,1},{2,6},{6,2},{3,7},{7,3},{8,12},{12,8},{9,1... | collective-permute-start | bytes 1572872 | tf_op jit(solution)/shard_map/ppermute | solution.py:82
  26.1 17.2 %collective-permute-start.5 = (bf16[8,128,128]{2,1,0:T(8,128)(2,1)S(1)}, bf16[8,128,128]{2,1,0:T(8,128)(2,1)S(1)}, u32[]{:S(2)}, u32[]{:S(2)}) collective-permute-start(bf16[8,128,128]{2,1,0:T(8,128)(2,1)S(1)} %slice.48), channel_id=1, source_target_pairs={{0,8},{8,0},{16,24},{24,16},{1,9},{9,1},{17,25},{25,17},{2,10},{10... | collective-permute-start | bytes 786440 | tf_op jit(solution)/shard_map/ppermute | solution.py:74
  34.4 12.7 %collective-permute-start.6 = (bf16[8,128,128]{2,1,0:T(8,128)(2,1)S(1)}, bf16[8,128,128]{2,1,0:T(8,128)(2,1)S(1)}, u32[]{:S(2)}, u32[]{:S(2)}) collective-permute-start(bf16[8,128,128]{2,1,0:T(8,128)(2,1)S(1)} %slice.49), channel_id=1, source_target_pairs={{0,16},{8,24},{16,0},{24,8},{1,17},{9,25},{17,1},{25,9},{2,18},{10... | collective-permute-start | bytes 786440 | tf_op jit(solution)/shard_map/ppermute | solution.py:75
  37.3 9.8 %collective-permute-start.13 = (bf16[8,128,128]{1,2,0:T(8,128)(2,1)S(1)}, bf16[8,128,128]{1,2,0:T(8,128)(2,1)S(1)}, u32[]{:S(2)}, u32[]{:S(2)}) collective-permute-start(bf16[8,128,128]{1,2,0:T(8,128)(2,1)S(1)} %slice.50), channel_id=1, source_target_pairs={{0,8},{8,0},{16,24},{24,16},{1,9},{9,1},{17,25},{25,17},{2,10},{10... | collective-permute-start | bytes 786440 | tf_op jit(solution)/shard_map/ppermute | solution.py:74
  41.0 6.7 %collective-permute-start.14 = (bf16[8,128,128]{1,2,0:T(8,128)(2,1)S(1)}, bf16[8,128,128]{1,2,0:T(8,128)(2,1)S(1)}, u32[]{:S(2)}, u32[]{:S(2)}) collective-permute-start(bf16[8,128,128]{1,2,0:T(8,128)(2,1)S(1)} %slice.51), channel_id=1, source_target_pairs={{0,16},{8,24},{16,0},{24,8},{1,17},{9,25},{17,1},{25,9},{2,18},{10... | collective-permute-start | bytes 786440 | tf_op jit(solution)/shard_map/ppermute | solution.py:75
  43.2 5.1 %collective-permute-start.4 = (bf16[16,128,128]{2,1,0:T(8,128)(2,1)}, bf16[16,128,128]{2,1,0:T(8,128)(2,1)S(1)}, u32[]{:S(2)}, u32[]{:S(2)}) collective-permute-start(bf16[16,128,128]{2,1,0:T(8,128)(2,1)} %collective-permute-done.3), channel_id=1, source_target_pairs={{0,4},{4,0},{1,5},{5,1},{2,6},{6,2},{3,7},{7,3},{8,12},{12,8},{9,1... | collective-permute-start | bytes 1572872 | tf_op jit(solution)/shard_map/ppermute | solution.py:82
  47.1 10.0 %collective-permute-start.10 = (bf16[16,128,128]{1,2,0:T(8,128)(2,1)S(1)}, bf16[16,128,128]{1,2,0:T(8,128)(2,1)S(1)}, u32[]{:S(2)}, u32[]{:S(2)}) collective-permute-start(bf16[16,128,128]{1,2,0:T(8,128)(2,1)S(1)} %collective-permute-done.9), channel_id=1, source_target_pairs={{0,4},{4,0},{1,5},{5,1},{2,6},{6,2},{3,7},{7,3},{8,12},{12,8},{9,1... | collective-permute-start | bytes 1572872 | tf_op jit(solution)/shard_map/ppermute | solution.py:82
  47.7 10.0 %collective-permute-start.12 = (bf16[16,128,128]{1,2,0:T(8,128)(2,1)S(1)}, bf16[16,128,128]{1,2,0:T(8,128)(2,1)S(1)}, u32[]{:S(2)}, u32[]{:S(2)}) collective-permute-start(bf16[16,128,128]{1,2,0:T(8,128)(2,1)S(1)} %collective-permute-done.11), channel_id=1, source_target_pairs={{0,4},{4,0},{1,5},{5,1},{2,6},{6,2},{3,7},{7,3},{8,12},{12,8},{9,1... | collective-permute-start | bytes 1572872 | tf_op jit(solution)/shard_map/ppermute | solution.py:82
  49.5 7.3 %collective-permute-start.15 = (bf16[16,128,128]{1,2,0:T(8,128)(2,1)S(1)}, bf16[16,128,128]{1,2,0:T(8,128)(2,1)S(1)}, u32[]{:S(2)}, u32[]{:S(2)}) collective-permute-start(bf16[16,128,128]{1,2,0:T(8,128)(2,1)S(1)} %constant_dynamic-update-slice_fusion.2), channel_id=1, source_target_pairs={{0,4},{4,0},{1,5},{5,1},{2,6},{6,2},{3,7},{7,3},{8,12},{12,8},{9,1... | collective-permute-start | bytes 1572872 | tf_op jit(solution)/shard_map/ppermute | solution.py:82
  58.4 14.0 %collective-permute-start.17 = (bf16[128,2048]{0,1:T(8,128)(2,1)S(1)}, bf16[128,2048]{0,1:T(8,128)(2,1)S(1)}, u32[]{:S(2)}, u32[]{:S(2)}) collective-permute-start(bf16[128,2048]{0,1:T(8,128)(2,1)S(1)} %bitcast.143), channel_id=1, source_target_pairs={{0,8},{8,0},{16,24},{24,16},{1,9},{9,1},{17,25},{25,17},{2,10},{10... | collective-permute-start | bytes 1572872 | tf_op jit(solution)/shard_map/ppermute | solution.py:51
  59.9 16.8 %collective-permute-start.19 = (bf16[128,2048]{0,1:T(8,128)(2,1)S(1)}, bf16[128,2048]{0,1:T(8,128)(2,1)S(1)}, u32[]{:S(2)}, u32[]{:S(2)}) collective-permute-start(bf16[128,2048]{0,1:T(8,128)(2,1)S(1)} %bitcast.144), channel_id=1, source_target_pairs={{0,16},{8,24},{16,0},{24,8},{1,17},{9,25},{17,1},{25,9},{2,18},{10... | collective-permute-start | bytes 1572872 | tf_op jit(solution)/shard_map/ppermute | solution.py:52
  60.4 17.8 %collective-permute-start.16 = (bf16[128,2048]{0,1:T(8,128)(2,1)S(1)}, bf16[128,2048]{0,1:T(8,128)(2,1)S(1)}, u32[]{:S(2)}, u32[]{:S(2)}) collective-permute-start(bf16[128,2048]{0,1:T(8,128)(2,1)S(1)} %bitcast.145), channel_id=1, source_target_pairs={{0,4},{4,0},{1,5},{5,1},{2,6},{6,2},{3,7},{7,3},{8,12},{12,8},{9,1... | collective-permute-start | bytes 1572872 | tf_op jit(solution)/shard_map/ppermute | solution.py:64
  72.4 7.7 %collective-permute-start.18 = (bf16[128,2048]{0,1:T(8,128)(2,1)S(1)}, bf16[128,2048]{0,1:T(8,128)(2,1)S(1)}, u32[]{:S(2)}, u32[]{:S(2)}) collective-permute-start(bf16[128,2048]{0,1:T(8,128)(2,1)S(1)} %collective-permute-done.17), channel_id=1, source_target_pairs={{0,4},{4,0},{1,5},{5,1},{2,6},{6,2},{3,7},{7,3},{8,12},{12,8},{9,1... | collective-permute-start | bytes 1572872 | tf_op jit(solution)/shard_map/ppermute | solution.py:64
  76.1 14.4 %collective-permute-start.22 = (bf16[64,2048]{0,1:T(8,128)(2,1)S(1)}, bf16[64,2048]{0,1:T(8,128)(2,1)S(1)}, u32[]{:S(2)}, u32[]{:S(2)}) collective-permute-start(bf16[64,2048]{0,1:T(8,128)(2,1)S(1)} %slice.53), channel_id=1, source_target_pairs={{0,16},{8,24},{16,0},{24,8},{1,17},{9,25},{17,1},{25,9},{2,18},{10... | collective-permute-start | bytes 786440 | tf_op jit(solution)/shard_map/ppermute | solution.py:56
  76.8 14.1 %collective-permute-start.21 = (bf16[64,2048]{0,1:T(8,128)(2,1)S(1)}, bf16[64,2048]{0,1:T(8,128)(2,1)S(1)}, u32[]{:S(2)}, u32[]{:S(2)}) collective-permute-start(bf16[64,2048]{0,1:T(8,128)(2,1)S(1)} %bitcast.142), channel_id=1, source_target_pairs={{0,8},{8,0},{16,24},{24,16},{1,9},{9,1},{17,25},{25,17},{2,10},{10... | collective-permute-start | bytes 786440 | tf_op jit(solution)/shard_map/ppermute | solution.py:55
  99.3 13.5 %all-to-all-start = ((bf16[8,128,256]{2,1,0:T(8,128)(2,1)}), bf16[8,128,256]{2,1,0:T(8,128)(2,1)S(1)}, u32[]{:S(2)}, u32[]{:S(2)}) async-start(bf16[8,128,256]{2,1,0:T(8,128)(2,1)} %bitcast.11), calls=%async_computation | async-start | bytes 1048576 | tf_op jit(solution)/shard_map/all_to_all | solution.py:176
  112.8 24.5 %all-to-all-start.1 = ((bf16[8,128,768]{2,1,0:T(8,128)(2,1)}), bf16[8,128,768]{2,1,0:T(8,128)(2,1)S(1)}, u32[]{:S(2)}, u32[]{:S(2)}) async-start(bf16[8,128,768]{2,1,0:T(8,128)(2,1)} %bitcast.138), calls=%async_computation.2 | async-start | bytes 3145728 | tf_op jit(solution)/shard_map/all_to_all | solution.py:176
  116.4 26.4 %reduce-scatter.3.cloned.1.call-start = ((), (), s32[]{:S(2)}) async-start(), calls=%async_computation.4 | async-start | bytes 655360 | tf_op jit(solution)/shard_map/reduce_scatter | solution.py:178
  117.3 61.3 %reduce-scatter.5.cloned.1.call-start = ((), (), s32[]{:S(2)}) async-start(), calls=%async_computation.5 | async-start | bytes 1966080 | tf_op jit(solution)/shard_map/reduce_scatter | solution.py:178
  (6 other events, 83.1 us)
Sparse Core Ops, SparseCore 0:
  119.5 23.2 reduce-scatter.2
  145.0 33.5 reduce-scatter.4

commit v9 on v7

--- a/solution.py
+++ b/solution.py
@@ -110,6 +110,34 @@
         row_total = total if row_total is None else row_total + total
         numer = term if numer is None else numer + term
     return numer / row_total[..., None]
+
+
+def reduce_scatter_line(x, axis):
+    count = lax.axis_size(axis)
+    width = x.shape[1] // count
+    here = lax.axis_index(axis)
+
+    def chunk(k):
+        return x[:, k * width : (k + 1) * width].astype(jnp.float32)
+
+    total = lax.dynamic_slice_in_dim(x, here * width, width, 1).astype(jnp.float32)
+    from_below = {}
+    from_above = {}
+    for k in range(count - 1, 0, -1):
+        carried = None
+        for p in range(1, k + 1):
+            send = chunk(k) if carried is None else chunk(k) + carried
+            carried = lax.ppermute(send.astype(jnp.bfloat16), axis, [(p - 1, p)]).astype(jnp.float32)
+        from_below[k] = carried
+    for k in range(count - 1):
+        carried = None
+        for p in range(count - 2, k - 1, -1):
+            send = chunk(k) if carried is None else chunk(k) + carried
+            carried = lax.ppermute(send.astype(jnp.bfloat16), axis, [(p + 1, p)]).astype(jnp.float32)
+        from_above[k] = carried
+    for part in list(from_below.values()) + list(from_above.values()):
+        total = total + part
+    return total
 
 
 def make_per_device(square):
@@ -172,9 +200,14 @@
                 gathered, out_weight[:, j * width : (j + 1) * width], preferred_element_type=jnp.float32
             ).astype(jnp.bfloat16)
             by_row = lax.all_to_all(partial, SEQ, split_axis=0, concat_axis=1, tiled=True)
-            reduced.append(
-                lax.psum_scatter(by_row, "chan", scatter_dimension=1, tiled=True)
-            )
+            if square:
+                reduced.append(reduce_scatter_line(by_row, "chan"))
+            else:
+                reduced.append(
+                    lax.psum_scatter(by_row, "chan", scatter_dimension=1, tiled=True).astype(
+                        jnp.float32
+                    )
+                )
         ordered = jnp.concatenate(
             [part[:, b * width : (b + 1) * width] for b in range(group) for part in reduced], axis=1
         )

time: 184 us -> 202 us (1.098)
  starting transfers between devices: 16 us -> 62.3 us
  blocking collectives: 36.8 us -> 0 us
  between operations: 13.8 us -> 0.69 us
  waiting for transfers between devices: 73.4 us -> 84 us
  other arithmetic: 4.93 us -> 12 us
  matrix products: 20.7 us -> 22.8 us
    ppermute x0 -> x24, starting transfers between devices: none -> 39 us  [the longest x12 28.1 us: reduce_scatter_line(): lax.ppermute(send.astype(jnp.bfloat16), axis, [(p - 1, p)])]
    all_to_all x2 -> x0, blocking collectives: 36.8 us -> none  [per_device(): lax.all_to_all(partial, SEQ, split_axis=0, concat_axis=1, tiled=True)]
    reduce_scatter x2 -> x0, waiting for transfers between devices: 29.5 us -> none  [per_device(): lax.psum_scatter(by_row, 'chan', scatter_dimension=1, tiled=True)]
    ppermute x0 -> x24, waiting for transfers between devices: none -> 21.5 us  [the longest x12 16.6 us: reduce_scatter_line(): lax.ppermute(send.astype(jnp.bfloat16), axis, [(p + 1, p)])]
    all_to_all x0 -> x2, waiting for transfers between devices: none -> 18.8 us  [per_device(): lax.all_to_all(partial, SEQ, split_axis=0, concat_axis=1, tiled=True)]
    all_to_all x0 -> x2, starting transfers between devices: none -> 7.22 us  [per_device(): lax.all_to_all(partial, SEQ, split_axis=0, concat_axis=1, tiled=True)]
    convert_element_type x0 -> x6, other arithmetic: none -> 4.22 us  [reduce_scatter_line(): send.astype(jnp.bfloat16)]
    add x0 -> x2, other arithmetic: none -> 2.8 us  [reduce_scatter_line(): total = total + part]
  transfers between devices with their start and end apart: 26 -> 50, of which waited for: 12 -> 17; matrix products, arithmetic and copies ran while one was open for 17% -> 20% of each run, Pallas kernels for 0% -> 0%
where the time goes in v9:
time: 202 us; the launch traced here: 201 us
  waiting for transfers between devices  84 us (42%)
  starting transfers between devices  62.3 us (31%)
  matrix products  22.8 us (11%)
  local copies, waits for them, and re-layouts  19.2 us (10%)
  other arithmetic  12 us (6%)
    ppermute x12, starting transfers between devices, reduce_scatter_line(): lax.ppermute(send.astype(jnp.bfloat16), axis, [(p - 1, p)])  28.1 us
    all_to_all x2, waiting for transfers between devices, per_device(): lax.all_to_all(partial, SEQ, split_axis=0, concat_axis=1, tiled=True)  18.8 us
    ppermute x12, waiting for transfers between devices, reduce_scatter_line(): lax.ppermute(send.astype(jnp.bfloat16), axis, [(p + 1, p)])  16.6 us
    ppermute x2, waiting for transfers between devices, gather_blocks_square(): from_y = lax.ppermute(x, 'hi', swap('hi', 2, 4))  14.8 us
    dot_general x2, matrix products, per_device(): jnp.dot(gathered, out_weight[:, j * width:(j + 1) * width], preferred_ele...  12.5 us
    ppermute x1, waiting for transfers between devices, gather_seq_square(): from_x = lax.ppermute(x, 'hi', swap('hi', 1, 4))  12 us
    ppermute x12, starting transfers between devices, reduce_scatter_line(): lax.ppermute(send.astype(jnp.bfloat16), axis, [(p + 1, p)])  10.8 us
    ppermute x1, waiting for transfers between devices, gather_seq_square(): lax.ppermute(from_x[half:], 'hi', swap('hi', 2, 4))  7.82 us
  transfers between devices with their start and end apart: 50, of which 17 were waited for; matrix products, arithmetic and copies ran while one was open for 20% of the time, Pallas kernels for 0%

profile of v9, /device:TPU:0, one launch (start us, length us, event | category | flops | bytes accessed | tf_op | source)
XLA Modules:
  0.0 200.9 jit_solution(70124543835501435)
XLA Ops:
  1.7 3.0 %collective-permute-start.3 = (bf16[16,128,128]{2,1,0:T(8,128)(2,1)S(1)}, bf16[16,128,128]{2,1,0:T(8,128)(2,1)}, u32[]{:S(2)}, u32[]{:S(2)}) collective-permute-start(bf16[16,128,128]{2,1,0:T(8,128)(2,1)S(1)} %bitcast.147), channel_id=1, source_target_pairs={{0,16},{8,24},{16,0},{24,8},{1,17},{9,25},{17,1},{25,9},{2,18},{10... | collective-permute-start | bytes 1572872 | tf_op jit(solution)/shard_map/ppermute | solution.py:71
  9.6 8.0 %collective-permute-done.3 = bf16[16,128,128]{2,1,0:T(8,128)(2,1)} collective-permute-done((bf16[16,128,128]{2,1,0:T(8,128)(2,1)S(1)}, bf16[16,128,128]{2,1,0:T(8,128)(2,1)}, u32[]{:S(2)}, u32[]{:S(2)}) %collective-permute-start.3) | collective-permute-done | bytes 524320 | tf_op jit(solution)/shard_map/ppermute | solution.py:71
  21.1 6.8 %collective-permute-done.11 = bf16[16,128,128]{1,2,0:T(8,128)(2,1)S(1)} collective-permute-done((bf16[16,128,128]{1,2,0:T(8,128)(2,1)S(1)}, bf16[16,128,128]{1,2,0:T(8,128)(2,1)S(1)}, u32[]{:S(2)}, u32[]{:S(2)}) %collective-permute-start.11) | collective-permute-done | bytes 524320 | tf_op jit(solution)/shard_map/ppermute | solution.py:71
  27.9 1.7 collective-permute-start.6
  36.8 3.7 %collective-permute-done.13 = bf16[8,128,128]{1,2,0:T(8,128)(2,1)S(1)} collective-permute-done((bf16[8,128,128]{1,2,0:T(8,128)(2,1)S(1)}, bf16[8,128,128]{1,2,0:T(8,128)(2,1)S(1)}, u32[]{:S(2)}, u32[]{:S(2)}) %collective-permute-start.13) | collective-permute-done | bytes 262176 | tf_op jit(solution)/shard_map/ppermute | solution.py:74
  45.9 2.1 %fusion.29 = (f32[16,128]{1,0:T(8,128)S(1)}, f32[16,128]{1,0:T(8,128)S(1)}, f32[16,128]{1,0:T(8,128)S(1)}, f32[16,128]{1,0:T(8,128)S(1)}, f32[16,128]{1,0:T(8,128)S(1)}) fusion(f32[16,128,128]{2,1,0:T(8,128)S(1)} %get-tuple-element.58, f32[16,128]{1,0:T(8,128)S(1)} %maximum_maximum_fusion, pred[128,128]{1,0:T(8,128)(4,1)S(1)} %copy.43, ...), kind=kLoop, calls=%fused_computation.46 | loop fusion | flops 3921920 | bytes 5373952 | tf_op jit(solution)/shard_map/reduce_sum | solution.py:106
  53.9 12.0 %collective-permute-done.17 = bf16[128,2048]{0,1:T(8,128)(2,1)S(1)} collective-permute-done((bf16[128,2048]{0,1:T(8,128)(2,1)S(1)}, bf16[128,2048]{0,1:T(8,128)(2,1)S(1)}, u32[]{:S(2)}, u32[]{:S(2)}) %collective-permute-start.17) | collective-permute-done | bytes 524320 | tf_op jit(solution)/shard_map/ppermute | solution.py:51
  65.9 2.7 %broadcast_in_dim.124 = bf16[1024,2048]{0,1:T(8,128)(2,1)} broadcast(bf16[]{:T(256)} %constant.15.clone.1), dimensions={} | broadcast | bytes 4194306 | tf_op jit(solution)/shard_map/broadcast_in_dim | solution.py:40
  76.2 7.8 %collective-permute-done.22 = bf16[64,2048]{0,1:T(8,128)(2,1)S(1)} collective-permute-done((bf16[64,2048]{0,1:T(8,128)(2,1)S(1)}, bf16[64,2048]{0,1:T(8,128)(2,1)S(1)}, u32[]{:S(2)}, u32[]{:S(2)}) %collective-permute-start.22) | collective-permute-done | bytes 262176 | tf_op jit(solution)/shard_map/ppermute | solution.py:56
  85.4 1.9 collective-permute-done.23
  88.2 6.2 %fusion.4 = bf16[1024,512]{1,0:T(8,128)(2,1)} fusion(bf16[1024,2048]{0,1:T(8,128)(2,1)} %constant_dynamic-update-slice_fusion.4, bf16[2048,1024]{1,0:T(8,128)(2,1)} %param.9), kind=kOutput, calls=%fused_computation.4 | convolution fusion | flops 2148007936 | bytes 7340032 | tf_op jit(solution)/shard_map/dot_general | solution.py:199
  94.5 3.7 %all-to-all-start = ((bf16[8,128,512]{2,1,0:T(8,128)(2,1)}), bf16[8,128,512]{2,1,0:T(8,128)(2,1)S(1)}, u32[]{:S(2)}, u32[]{:S(2)}) async-start(bf16[8,128,512]{2,1,0:T(8,128)(2,1)} %bitcast.11), calls=%async_computation | async-start | bytes 2097152 | tf_op jit(solution)/shard_map/all_to_all | solution.py:202
  98.1 6.3 %fusion.7 = bf16[1024,512]{1,0:T(8,128)(2,1)} fusion(bf16[1024,2048]{0,1:T(8,128)(2,1)} %constant_dynamic-update-slice_fusion.4, bf16[2048,1024]{1,0:T(8,128)(2,1)} %param.9), kind=kOutput, calls=%fused_computation.5 | convolution fusion | flops 2148007936 | bytes 7340032 | tf_op jit(solution)/shard_map/dot_general | solution.py:199
  104.4 9.2 %all-to-all-done = bf16[8,128,512]{2,1,0:T(8,128)(2,1)S(1)} async-done(((bf16[8,128,512]{2,1,0:T(8,128)(2,1)}), bf16[8,128,512]{2,1,0:T(8,128)(2,1)S(1)}, u32[]{:S(2)}, u32[]{:S(2)}) %all-to-all-start) | async-done | bytes 1048608 | tf_op jit(solution)/shard_map/all_to_all | solution.py:202
  113.5 3.6 %all-to-all-start.1 = ((bf16[8,128,512]{2,1,0:T(8,128)(2,1)}), bf16[8,128,512]{2,1,0:T(8,128)(2,1)S(1)}, u32[]{:S(2)}, u32[]{:S(2)}) async-start(bf16[8,128,512]{2,1,0:T(8,128)(2,1)} %bitcast.146), calls=%async_computation.1 | async-start | bytes 2097152 | tf_op jit(solution)/shard_map/all_to_all | solution.py:202
  119.3 3.5 %collective-permute-start.24 = (bf16[128,1024]{1,0:T(8,128)(2,1)}, bf16[128,1024]{1,0:T(8,128)(2,1)S(1)}, u32[]{:S(2)}, u32[]{:S(2)}) collective-permute-start(bf16[128,1024]{1,0:T(8,128)(2,1)} %get-tuple-element.19), channel_id=1, source_target_pairs={{0,1},{4,5},{8,9},{12,13},{16,17},{20,21},{24,25},{28,29}} | collective-permute-start | bytes 786440 | tf_op jit(solution)/shard_map/ppermute | solution.py:130
  122.8 9.6 %all-to-all-done.1 = bf16[8,128,512]{2,1,0:T(8,128)(2,1)S(1)} async-done(((bf16[8,128,512]{2,1,0:T(8,128)(2,1)}), bf16[8,128,512]{2,1,0:T(8,128)(2,1)S(1)}, u32[]{:S(2)}, u32[]{:S(2)}) %all-to-all-start.1) | async-done | bytes 1048608 | tf_op jit(solution)/shard_map/all_to_all | solution.py:202
  135.6 3.5 %collective-permute-start.36 = (bf16[128,1024]{1,0:T(8,128)(2,1)S(1)}, bf16[128,1024]{1,0:T(8,128)(2,1)S(1)}, u32[]{:S(2)}, u32[]{:S(2)}) collective-permute-start(bf16[128,1024]{1,0:T(8,128)(2,1)S(1)} %get-tuple-element.27), channel_id=1, source_target_pairs={{0,1},{4,5},{8,9},{12,13},{16,17},{20,21},{24,25},{28,29}} | collective-permute-start | bytes 786440 | tf_op jit(solution)/shard_map/ppermute | solution.py:130
  142.5 3.1 %collective-permute-done.36 = bf16[128,1024]{1,0:T(8,128)(2,1)S(1)} collective-permute-done((bf16[128,1024]{1,0:T(8,128)(2,1)S(1)}, bf16[128,1024]{1,0:T(8,128)(2,1)S(1)}, u32[]{:S(2)}, u32[]{:S(2)}) %collective-permute-start.36) | collective-permute-done | bytes 262176 | tf_op jit(solution)/shard_map/ppermute | solution.py:130
  145.6 4.4 %collective-permute-start.29 = (bf16[128,1024]{1,0:T(8,128)(2,1)S(1)}, bf16[128,1024]{1,0:T(8,128)(2,1)S(1)}, u32[]{:S(2)}, u32[]{:S(2)}) collective-permute-start(bf16[128,1024]{1,0:T(8,128)(2,1)S(1)} %get-tuple-element.21), channel_id=1, source_target_pairs={{0,1},{4,5},{8,9},{12,13},{16,17},{20,21},{24,25},{28,29}} | collective-permute-start | bytes 786440 | tf_op jit(solution)/shard_map/ppermute | solution.py:130
  151.2 4.4 %collective-permute-start.39 = (bf16[128,1024]{1,0:T(8,128)(2,1)S(1)}, bf16[128,1024]{1,0:T(8,128)(2,1)S(1)}, u32[]{:S(2)}, u32[]{:S(2)}) collective-permute-start(bf16[128,1024]{1,0:T(8,128)(2,1)S(1)} %get-tuple-element.30), channel_id=1, source_target_pairs={{0,1},{4,5},{8,9},{12,13},{16,17},{20,21},{24,25},{28,29}} | collective-permute-start | bytes 786440 | tf_op jit(solution)/shard_map/ppermute | solution.py:130
  163.4 5.6 %collective-permute-start.41 = (bf16[128,1024]{1,0:T(8,128)(2,1)}, bf16[128,1024]{1,0:T(8,128)(2,1)}, u32[]{:S(2)}, u32[]{:S(2)}) collective-permute-start(bf16[128,1024]{1,0:T(8,128)(2,1)} %get-tuple-element.29), channel_id=1, source_target_pairs={{0,1},{4,5},{8,9},{12,13},{16,17},{20,21},{24,25},{28,29}} | collective-permute-start | bytes 786440 | tf_op jit(solution)/shard_map/ppermute | solution.py:130
  179.2 4.9 %collective-permute-done.32 = bf16[128,1024]{1,0:T(8,128)(2,1)} collective-permute-done((bf16[128,1024]{1,0:T(8,128)(2,1)}, bf16[128,1024]{1,0:T(8,128)(2,1)}, u32[]{:S(2)}, u32[]{:S(2)}) %collective-permute-start.32) | collective-permute-done | bytes 262176 | tf_op jit(solution)/shard_map/ppermute | solution.py:136
  187.0 11.6 %collective-permute-done.44 = bf16[128,1024]{1,0:T(8,128)(2,1)S(1)} collective-permute-done((bf16[128,1024]{1,0:T(8,128)(2,1)S(1)}, bf16[128,1024]{1,0:T(8,128)(2,1)S(1)}, u32[]{:S(2)}, u32[]{:S(2)}) %collective-permute-start.44) | collective-permute-done | bytes 262176 | tf_op jit(solution)/shard_map/ppermute | solution.py:136
  (158 shorter events, 71.0 us)
Async XLA Ops:
  1.7 15.9 %collective-permute-start.3 = (bf16[16,128,128]{2,1,0:T(8,128)(2,1)S(1)}, bf16[16,128,128]{2,1,0:T(8,128)(2,1)}, u32[]{:S(2)}, u32[]{:S(2)}) collective-permute-start(bf16[16,128,128]{2,1,0:T(8,128)(2,1)S(1)} %bitcast.147), channel_id=1, source_target_pairs={{0,16},{8,24},{16,0},{24,8},{1,17},{9,25},{17,1},{25,9},{2,18},{10... | collective-permute-start | bytes 1572872 | tf_op jit(solution)/shard_map/ppermute | solution.py:71
  4.7 14.8 %collective-permute-start.1 = (bf16[16,128,128]{2,1,0:T(8,128)(2,1)S(1)}, bf16[16,128,128]{2,1,0:T(8,128)(2,1)S(1)}, u32[]{:S(2)}, u32[]{:S(2)}) collective-permute-start(bf16[16,128,128]{2,1,0:T(8,128)(2,1)S(1)} %bitcast.148), channel_id=1, source_target_pairs={{0,8},{8,0},{16,24},{24,16},{1,9},{9,1},{17,25},{25,17},{2,10},{10... | collective-permute-start | bytes 1572872 | tf_op jit(solution)/shard_map/ppermute | solution.py:70
  6.2 28.3 %collective-permute-start = (bf16[16,128,128]{2,1,0:T(8,128)(2,1)S(1)}, bf16[16,128,128]{2,1,0:T(8,128)(2,1)}, u32[]{:S(2)}, u32[]{:S(2)}) collective-permute-start(bf16[16,128,128]{2,1,0:T(8,128)(2,1)S(1)} %bitcast.149), channel_id=1, source_target_pairs={{0,4},{4,0},{1,5},{5,1},{2,6},{6,2},{3,7},{7,3},{8,12},{12,8},{9,1... | collective-permute-start | bytes 1572872 | tf_op jit(solution)/shard_map/ppermute | solution.py:82
  7.5 23.3 %collective-permute-start.9 = (bf16[16,128,128]{1,2,0:T(8,128)(2,1)S(1)}, bf16[16,128,128]{1,2,0:T(8,128)(2,1)S(1)}, u32[]{:S(2)}, u32[]{:S(2)}) collective-permute-start(bf16[16,128,128]{1,2,0:T(8,128)(2,1)S(1)} %bitcast.141), channel_id=1, source_target_pairs={{0,8},{8,0},{16,24},{24,16},{1,9},{9,1},{17,25},{25,17},{2,10},{10... | collective-permute-start | bytes 1572872 | tf_op jit(solution)/shard_map/ppermute | solution.py:70
  8.1 19.7 %collective-permute-start.11 = (bf16[16,128,128]{1,2,0:T(8,128)(2,1)S(1)}, bf16[16,128,128]{1,2,0:T(8,128)(2,1)S(1)}, u32[]{:S(2)}, u32[]{:S(2)}) collective-permute-start(bf16[16,128,128]{1,2,0:T(8,128)(2,1)S(1)} %bitcast.142), channel_id=1, source_target_pairs={{0,16},{8,24},{16,0},{24,8},{1,17},{9,25},{17,1},{25,9},{2,18},{10... | collective-permute-start | bytes 1572872 | tf_op jit(solution)/shard_map/ppermute | solution.py:71
  17.6 30.4 %collective-permute-start.8 = (bf16[16,128,128]{1,2,0:T(8,128)(2,1)S(1)}, bf16[16,128,128]{1,2,0:T(8,128)(2,1)S(1)}, u32[]{:S(2)}, u32[]{:S(2)}) collective-permute-start(bf16[16,128,128]{1,2,0:T(8,128)(2,1)S(1)} %bitcast.143), channel_id=1, source_target_pairs={{0,4},{4,0},{1,5},{5,1},{2,6},{6,2},{3,7},{7,3},{8,12},{12,8},{9,1... | collective-permute-start | bytes 1572872 | tf_op jit(solution)/shard_map/ppermute | solution.py:82
  19.5 17.2 %collective-permute-start.5 = (bf16[8,128,128]{2,1,0:T(8,128)(2,1)S(1)}, bf16[8,128,128]{2,1,0:T(8,128)(2,1)S(1)}, u32[]{:S(2)}, u32[]{:S(2)}) collective-permute-start(bf16[8,128,128]{2,1,0:T(8,128)(2,1)S(1)} %slice.96), channel_id=1, source_target_pairs={{0,8},{8,0},{16,24},{24,16},{1,9},{9,1},{17,25},{25,17},{2,10},{10... | collective-permute-start | bytes 786440 | tf_op jit(solution)/shard_map/ppermute | solution.py:74
  27.9 12.7 %collective-permute-start.6 = (bf16[8,128,128]{2,1,0:T(8,128)(2,1)S(1)}, bf16[8,128,128]{2,1,0:T(8,128)(2,1)S(1)}, u32[]{:S(2)}, u32[]{:S(2)}) collective-permute-start(bf16[8,128,128]{2,1,0:T(8,128)(2,1)S(1)} %slice.97), channel_id=1, source_target_pairs={{0,16},{8,24},{16,0},{24,8},{1,17},{9,25},{17,1},{25,9},{2,18},{10... | collective-permute-start | bytes 786440 | tf_op jit(solution)/shard_map/ppermute | solution.py:75
  51.8 14.0 %collective-permute-start.17 = (bf16[128,2048]{0,1:T(8,128)(2,1)S(1)}, bf16[128,2048]{0,1:T(8,128)(2,1)S(1)}, u32[]{:S(2)}, u32[]{:S(2)}) collective-permute-start(bf16[128,2048]{0,1:T(8,128)(2,1)S(1)} %bitcast.151), channel_id=1, source_target_pairs={{0,8},{8,0},{16,24},{24,16},{1,9},{9,1},{17,25},{25,17},{2,10},{10... | collective-permute-start | bytes 1572872 | tf_op jit(solution)/shard_map/ppermute | solution.py:51
  53.4 16.9 %collective-permute-start.19 = (bf16[128,2048]{0,1:T(8,128)(2,1)S(1)}, bf16[128,2048]{0,1:T(8,128)(2,1)S(1)}, u32[]{:S(2)}, u32[]{:S(2)}) collective-permute-start(bf16[128,2048]{0,1:T(8,128)(2,1)S(1)} %bitcast.152), channel_id=1, source_target_pairs={{0,16},{8,24},{16,0},{24,8},{1,17},{9,25},{17,1},{25,9},{2,18},{10... | collective-permute-start | bytes 1572872 | tf_op jit(solution)/shard_map/ppermute | solution.py:52
  53.9 17.9 %collective-permute-start.16 = (bf16[128,2048]{0,1:T(8,128)(2,1)S(1)}, bf16[128,2048]{0,1:T(8,128)(2,1)S(1)}, u32[]{:S(2)}, u32[]{:S(2)}) collective-permute-start(bf16[128,2048]{0,1:T(8,128)(2,1)S(1)} %bitcast.153), channel_id=1, source_target_pairs={{0,4},{4,0},{1,5},{5,1},{2,6},{6,2},{3,7},{7,3},{8,12},{12,8},{9,1... | collective-permute-start | bytes 1572872 | tf_op jit(solution)/shard_map/ppermute | solution.py:64
  69.6 14.4 %collective-permute-start.22 = (bf16[64,2048]{0,1:T(8,128)(2,1)S(1)}, bf16[64,2048]{0,1:T(8,128)(2,1)S(1)}, u32[]{:S(2)}, u32[]{:S(2)}) collective-permute-start(bf16[64,2048]{0,1:T(8,128)(2,1)S(1)} %slice.101), channel_id=1, source_target_pairs={{0,16},{8,24},{16,0},{24,8},{1,17},{9,25},{17,1},{25,9},{2,18},{10... | collective-permute-start | bytes 786440 | tf_op jit(solution)/shard_map/ppermute | solution.py:56
  70.2 14.1 %collective-permute-start.21 = (bf16[64,2048]{0,1:T(8,128)(2,1)S(1)}, bf16[64,2048]{0,1:T(8,128)(2,1)S(1)}, u32[]{:S(2)}, u32[]{:S(2)}) collective-permute-start(bf16[64,2048]{0,1:T(8,128)(2,1)S(1)} %bitcast.150), channel_id=1, source_target_pairs={{0,8},{8,0},{16,24},{24,16},{1,9},{9,1},{17,25},{25,17},{2,10},{10... | collective-permute-start | bytes 786440 | tf_op jit(solution)/shard_map/ppermute | solution.py:55
  94.5 19.1 %all-to-all-start = ((bf16[8,128,512]{2,1,0:T(8,128)(2,1)}), bf16[8,128,512]{2,1,0:T(8,128)(2,1)S(1)}, u32[]{:S(2)}, u32[]{:S(2)}) async-start(bf16[8,128,512]{2,1,0:T(8,128)(2,1)} %bitcast.11), calls=%async_computation | async-start | bytes 2097152 | tf_op jit(solution)/shard_map/all_to_all | solution.py:202
  113.5 18.9 %all-to-all-start.1 = ((bf16[8,128,512]{2,1,0:T(8,128)(2,1)}), bf16[8,128,512]{2,1,0:T(8,128)(2,1)S(1)}, u32[]{:S(2)}, u32[]{:S(2)}) async-start(bf16[8,128,512]{2,1,0:T(8,128)(2,1)} %bitcast.146), calls=%async_computation.1 | async-start | bytes 2097152 | tf_op jit(solution)/shard_map/all_to_all | solution.py:202
  119.3 22.4 %collective-permute-start.24 = (bf16[128,1024]{1,0:T(8,128)(2,1)}, bf16[128,1024]{1,0:T(8,128)(2,1)S(1)}, u32[]{:S(2)}, u32[]{:S(2)}) collective-permute-start(bf16[128,1024]{1,0:T(8,128)(2,1)} %get-tuple-element.19), channel_id=1, source_target_pairs={{0,1},{4,5},{8,9},{12,13},{16,17},{20,21},{24,25},{28,29}} | collective-permute-start | bytes 786440 | tf_op jit(solution)/shard_map/ppermute | solution.py:130
  139.1 12.2 %collective-permute-start.27 = (bf16[128,1024]{1,0:T(8,128)(2,1)S(1)}, bf16[128,1024]{1,0:T(8,128)(2,1)S(1)}, u32[]{:S(2)}, u32[]{:S(2)}) collective-permute-start(bf16[128,1024]{1,0:T(8,128)(2,1)S(1)} %get-tuple-element.22), channel_id=1, source_target_pairs={{0,1},{4,5},{8,9},{12,13},{16,17},{20,21},{24,25},{28,29}} | collective-permute-start | bytes 786440 | tf_op jit(solution)/shard_map/ppermute | solution.py:130
  140.4 15.2 %collective-permute-start.30 = (bf16[128,1024]{1,0:T(8,128)(2,1)S(1)}, bf16[128,1024]{1,0:T(8,128)(2,1)S(1)}, u32[]{:S(2)}, u32[]{:S(2)}) collective-permute-start(bf16[128,1024]{1,0:T(8,128)(2,1)S(1)} %copy-done.6), channel_id=1, source_target_pairs={{3,2},{7,6},{11,10},{15,14},{19,18},{23,22},{27,26},{31,30}} | collective-permute-start | bytes 786440 | tf_op jit(solution)/shard_map/ppermute | solution.py:136
  141.1 15.2 %collective-permute-start.33 = (bf16[128,1024]{1,0:T(8,128)(2,1)S(1)}, bf16[128,1024]{1,0:T(8,128)(2,1)S(1)}, u32[]{:S(2)}, u32[]{:S(2)}) collective-permute-start(bf16[128,1024]{1,0:T(8,128)(2,1)S(1)} %get-tuple-element.21), channel_id=1, source_target_pairs={{3,2},{7,6},{11,10},{15,14},{19,18},{23,22},{27,26},{31,30}} | collective-permute-start | bytes 786440 | tf_op jit(solution)/shard_map/ppermute | solution.py:136
  141.9 15.2 %collective-permute-start.25 = (bf16[128,1024]{1,0:T(8,128)(2,1)S(1)}, bf16[128,1024]{1,0:T(8,128)(2,1)S(1)}, u32[]{:S(2)}, u32[]{:S(2)}) collective-permute-start(bf16[128,1024]{1,0:T(8,128)(2,1)S(1)} %fusion.43), channel_id=1, source_target_pairs={{1,2},{5,6},{9,10},{13,14},{17,18},{21,22},{25,26},{29,30}} | collective-permute-start | bytes 786440 | tf_op jit(solution)/shard_map/ppermute | solution.py:130
  145.6 23.4 %collective-permute-start.29 = (bf16[128,1024]{1,0:T(8,128)(2,1)S(1)}, bf16[128,1024]{1,0:T(8,128)(2,1)S(1)}, u32[]{:S(2)}, u32[]{:S(2)}) collective-permute-start(bf16[128,1024]{1,0:T(8,128)(2,1)S(1)} %get-tuple-element.21), channel_id=1, source_target_pairs={{0,1},{4,5},{8,9},{12,13},{16,17},{20,21},{24,25},{28,29}} | collective-permute-start | bytes 786440 | tf_op jit(solution)/shard_map/ppermute | solution.py:130
  162.1 12.0 %collective-permute-start.43 = (bf16[128,1024]{1,0:T(8,128)(2,1)S(1)}, bf16[128,1024]{1,0:T(8,128)(2,1)}, u32[]{:S(2)}, u32[]{:S(2)}) collective-permute-start(bf16[128,1024]{1,0:T(8,128)(2,1)S(1)} %get-tuple-element.24), channel_id=1, source_target_pairs={{2,1},{6,5},{10,9},{14,13},{18,17},{22,21},{26,25},{30,29}} | collective-permute-start | bytes 786440 | tf_op jit(solution)/shard_map/ppermute | solution.py:136
  163.4 13.0 %collective-permute-start.41 = (bf16[128,1024]{1,0:T(8,128)(2,1)}, bf16[128,1024]{1,0:T(8,128)(2,1)}, u32[]{:S(2)}, u32[]{:S(2)}) collective-permute-start(bf16[128,1024]{1,0:T(8,128)(2,1)} %get-tuple-element.29), channel_id=1, source_target_pairs={{0,1},{4,5},{8,9},{12,13},{16,17},{20,21},{24,25},{28,29}} | collective-permute-start | bytes 786440 | tf_op jit(solution)/shard_map/ppermute | solution.py:130
  184.1 14.6 %collective-permute-start.44 = (bf16[128,1024]{1,0:T(8,128)(2,1)S(1)}, bf16[128,1024]{1,0:T(8,128)(2,1)S(1)}, u32[]{:S(2)}, u32[]{:S(2)}) collective-permute-start(bf16[128,1024]{1,0:T(8,128)(2,1)S(1)} %fusion.50), channel_id=1, source_target_pairs={{1,0},{5,4},{9,8},{13,12},{17,16},{21,20},{25,24},{29,28}} | collective-permute-start | bytes 786440 | tf_op jit(solution)/shard_map/ppermute | solution.py:136
  (33 other events, 280.0 us)

commit v10 on v7

--- a/solution.py
+++ b/solution.py
@@ -162,6 +162,24 @@
             ratio = numer / row_total[..., None]
         local_context = ratio.transpose(1, 0, 2).reshape(seg_rows, feat_width).astype(jnp.bfloat16)
 
+        if square:
+            chip = lax.axis_index("hi")
+            core = lax.axis_index("lo")
+            blocks = gather_blocks_square(local_context)
+            width = out_weight.shape[1]
+            by_row = jnp.zeros((seg_rows, seq_count * width), jnp.bfloat16)
+            for b, block in enumerate(blocks):
+                r, t = b // 2, b % 2
+                partial = jnp.dot(block, out_weight, preferred_element_type=jnp.float32).astype(
+                    jnp.bfloat16
+                )
+                if b:
+                    pairs = [(h * 2 + l, (h ^ r) * 2 + (l ^ t)) for h in range(4) for l in range(2)]
+                    partial = lax.ppermute(partial, SEQ, pairs)
+                source = (chip ^ r) * 2 + (core ^ t)
+                by_row = lax.dynamic_update_slice(by_row, partial, (0, source * width))
+            ordered = lax.psum_scatter(by_row, "chan", scatter_dimension=1, tiled=True)
+            return (residual.astype(jnp.float32) + ordered.astype(jnp.float32)).astype(jnp.bfloat16)
         gathered = gather_seq(local_context)
         group = seq_count // chan_count
         chunks = 2

time: 184 us -> 168 us (0.913)
  blocking collectives: 36.8 us -> 0 us
  waiting for transfers between devices: 73.4 us -> 93.8 us
  local copies, waits for them, and re-layouts: 17.9 us -> 8.27 us
  starting transfers between devices: 16 us -> 22.6 us
  matrix products: 20.7 us -> 23.9 us
    all_to_all x2 -> x0, blocking collectives: 36.8 us -> none  [per_device(): lax.all_to_all(partial, SEQ, split_axis=0, concat_axis=1, tiled=True)]
    reduce_scatter x2 -> x1, waiting for transfers between devices: 29.5 us -> 45.9 us  [per_device(): ordered = lax.psum_scatter(by_row, 'chan', scatter_dimension=1, tiled=True)]
    ppermute x8 -> x7, waiting for transfers between devices: 22 us -> 12.5 us  [per_device(): partial = lax.ppermute(partial, SEQ, pairs)]
    ppermute x2 -> x3, waiting for transfers between devices: 2.18 us -> 11 us  [gather_blocks_square(): from_x = lax.ppermute(x, 'hi', swap('hi', 1, 4))]
    ppermute x2 -> x3, waiting for transfers between devices: 0.01 us -> 6.97 us  [gather_blocks_square(): lax.ppermute(from_x[half:], 'hi', swap('hi', 2, 4))]
    dynamic_update_slice x7, local copies, waits for them, and re-layouts: 6.23 us -> 0.15 us  [per_device(): by_row = lax.dynamic_update_slice(by_row, partial, (0, source * width))]
    ppermute x8 -> x7, starting transfers between devices: 4.13 us -> 6.69 us  [per_device(): partial = lax.ppermute(partial, SEQ, pairs)]
    broadcast_in_dim x1, local copies, waits for them, and re-layouts: 2.62 us -> 0.2 us  [per_device(): by_row = jnp.zeros((seg_rows, seq_count * width), jnp.bfloat16)]
  transfers between devices with their start and end apart: 26 -> 32, of which waited for: 12 -> 16; matrix products, arithmetic and copies ran while one was open for 17% -> 18% of each run, Pallas kernels for 0% -> 0%
where the time goes in v10:
time: 168 us
  waiting for transfers between devices  93.8 us (56%)
  matrix products  23.9 us (14%)
  starting transfers between devices  22.6 us (13%)
  between operations  13.9 us (8%)
  local copies, waits for them, and re-layouts  8.27 us (5%)
  other arithmetic  5.17 us (3%)
    reduce_scatter x1, waiting for transfers between devices, per_device(): ordered = lax.psum_scatter(by_row, 'chan', scatter_dimension=1, tiled=True)  45.9 us
    ppermute x3, waiting for transfers between devices, gather_blocks_square(): from_y = lax.ppermute(x, 'hi', swap('hi', 2, 4))  13.3 us
    ppermute x7, waiting for transfers between devices, per_device(): partial = lax.ppermute(partial, SEQ, pairs)  12.5 us
    ppermute x3, waiting for transfers between devices, gather_blocks_square(): from_x = lax.ppermute(x, 'hi', swap('hi', 1, 4))  11 us
    dot_general x8, matrix products, per_device(): jnp.dot(block, out_weight, preferred_element_type=jnp.float32)  10.8 us
    dot_general x8, matrix products, attention_by_head(): jnp.einsum('hqd,hkd->hqk', queries, keys, preferred_element_type=jnp.floa...  8.56 us
    ppermute x3, waiting for transfers between devices, gather_blocks_square(): lax.ppermute(from_x[half:], 'hi', swap('hi', 2, 4))  6.97 us
    ppermute x7, starting transfers between devices, per_device(): partial = lax.ppermute(partial, SEQ, pairs)  6.69 us
  transfers between devices with their start and end apart: 32, of which 16 were waited for; matrix products, arithmetic and copies ran while one was open for 18% of the time, Pallas kernels for 0%

profile of v10, /device:TPU:0, one launch (start us, length us, event | category | flops | bytes accessed | tf_op | source)
XLA Modules:
  0.0 167.6 jit_solution(15445071581417486169)
XLA Ops:
  8.9 3.0 %collective-permute-start.3 = (bf16[16,128,128]{2,1,0:T(8,128)(2,1)}, bf16[16,128,128]{2,1,0:T(8,128)(2,1)}, u32[]{:S(2)}, u32[]{:S(2)}) collective-permute-start(bf16[16,128,128]{2,1,0:T(8,128)(2,1)} %bitcast.2), channel_id=1, source_target_pairs={{0,16},{8,24},{16,0},{24,8},{1,17},{9,25},{17,1},{25,9},{2,18},{10... | collective-permute-start | bytes 1572872 | tf_op jit(solution)/shard_map/ppermute | solution.py:71
  11.9 1.5 collective-permute-start.1
  16.2 1.5 fusion.92
  17.8 7.2 %collective-permute-done.3 = bf16[16,128,128]{2,1,0:T(8,128)(2,1)} collective-permute-done((bf16[16,128,128]{2,1,0:T(8,128)(2,1)}, bf16[16,128,128]{2,1,0:T(8,128)(2,1)}, u32[]{:S(2)}, u32[]{:S(2)}) %collective-permute-start.3) | collective-permute-done | bytes 524320 | tf_op jit(solution)/shard_map/ppermute | solution.py:71
  27.1 1.5 collective-permute-start.5
  29.5 5.7 %collective-permute-done.11 = bf16[16,128,128]{1,2,0:T(8,128)(2,1)S(1)} collective-permute-done((bf16[16,128,128]{1,2,0:T(8,128)(2,1)S(1)}, bf16[16,128,128]{1,2,0:T(8,128)(2,1)S(1)}, u32[]{:S(2)}, u32[]{:S(2)}) %collective-permute-start.11) | collective-permute-done | bytes 524320 | tf_op jit(solution)/shard_map/ppermute | solution.py:71
  35.3 1.7 %collective-permute-start.6 = (bf16[8,128,128]{2,1,0:T(8,128)(2,1)S(1)}, bf16[8,128,128]{2,1,0:T(8,128)(2,1)S(1)}, u32[]{:S(2)}, u32[]{:S(2)}) collective-permute-start(bf16[8,128,128]{2,1,0:T(8,128)(2,1)S(1)} %slice.25), channel_id=1, source_target_pairs={{0,16},{8,24},{16,0},{24,8},{1,17},{9,25},{17,1},{25,9},{2,18},{10... | collective-permute-start | bytes 786440 | tf_op jit(solution)/shard_map/ppermute | solution.py:75
  39.7 1.6 fusion.89
  41.3 1.6 fusion.91
  43.5 1.6 fusion.93
  45.3 2.7 %collective-permute-done.13 = bf16[8,128,128]{1,2,0:T(8,128)(2,1)S(1)} collective-permute-done((bf16[8,128,128]{1,2,0:T(8,128)(2,1)S(1)}, bf16[8,128,128]{1,2,0:T(8,128)(2,1)S(1)}, u32[]{:S(2)}, u32[]{:S(2)}) %collective-permute-start.13) | collective-permute-done | bytes 262176 | tf_op jit(solution)/shard_map/ppermute | solution.py:74
  53.3 2.1 %fusion.19 = (f32[16,128]{1,0:T(8,128)S(1)}, f32[16,128]{1,0:T(8,128)S(1)}, f32[16,128]{1,0:T(8,128)S(1)}, f32[16,128]{1,0:T(8,128)S(1)}, f32[16,128]{1,0:T(8,128)S(1)}) fusion(f32[16,128,128]{2,1,0:T(8,128)S(1)} %get-tuple-element.36, f32[16,128]{1,0:T(8,128)S(1)} %maximum_maximum_fusion, pred[128,128]{1,0:T(8,128)(4,1)S(1)} %copy.41, ...), kind=kLoop, calls=%fused_computation.48 | loop fusion | flops 3921920 | bytes 5373952 | tf_op jit(solution)/shard_map/reduce_sum | solution.py:106
  60.0 1.5 collective-permute-start.18
  62.2 3.5 %fusion.16 = bf16[128,8192]{1,0:T(8,128)(2,1)S(1)} fusion(bf16[128,8192]{1,0:T(8,128)(2,1)S(1)} %broadcast_in_dim.124, s32[]{:T(128)S(6)} %select_n.89, bf16[128,2048]{0,1:T(8,128)(2,1)} %bitcast.10, bf16[2048,1024]{1,0:T(8,128)(2,1)} %param.9), kind=kOutput, calls=%fused_computation.36 | convolution fusion | flops 537001984 | bytes 4980740 | tf_op jit(solution)/shard_map/dot_general | solution.py:173
  65.7 8.7 %collective-permute-done.18 = bf16[128,2048]{0,1:T(8,128)(2,1)S(1)} collective-permute-done((bf16[128,2048]{0,1:T(8,128)(2,1)}, bf16[128,2048]{0,1:T(8,128)(2,1)S(1)}, u32[]{:S(2)}, u32[]{:S(2)}) %collective-permute-start.18) | collective-permute-done | bytes 524320 | tf_op jit(solution)/shard_map/ppermute | solution.py:70
  76.6 1.8 %convolution_convert_fusion.6 = bf16[128,1024]{1,0:T(8,128)(2,1)S(1)} fusion(bf16[128,2048]{0,1:T(8,128)(2,1)} %collective-permute-done.16, bf16[2048,1024]{1,0:T(8,128)(2,1)S(1)} %copy-done.1), kind=kOutput, calls=%fused_computation.34 | convolution fusion | flops 537001984 | bytes 4980736 | tf_op jit(solution)/shard_map/dot_general | solution.py:173
  80.3 1.8 %convolution_convert_fusion.3 = bf16[128,1024]{1,0:T(8,128)(2,1)S(1)} fusion(bf16[128,2048]{0,1:T(8,128)(2,1)} %collective-permute-done.22, bf16[2048,1024]{1,0:T(8,128)(2,1)S(1)} %copy-done.1), kind=kOutput, calls=%fused_computation.31 | convolution fusion | flops 537001984 | bytes 4980736 | tf_op jit(solution)/shard_map/dot_general | solution.py:173
  83.3 6.2 %collective-permute-done.27 = bf16[64,2048]{0,1:T(8,128)(2,1)S(1)} collective-permute-done((bf16[64,2048]{0,1:T(8,128)(2,1)S(1)}, bf16[64,2048]{0,1:T(8,128)(2,1)S(1)}, u32[]{:S(2)}, u32[]{:S(2)}) %collective-permute-start.27) | collective-permute-done | bytes 262176 | tf_op jit(solution)/shard_map/ppermute | solution.py:75
  92.2 2.0 %collective-permute-done.19 = bf16[128,1024]{1,0:T(8,128)(2,1)S(1)} collective-permute-done((bf16[128,1024]{1,0:T(8,128)(2,1)S(1)}, bf16[128,1024]{1,0:T(8,128)(2,1)S(1)}, u32[]{:S(2)}, u32[]{:S(2)}) %collective-permute-start.19) | collective-permute-done | bytes 262176 | tf_op jit(solution)/shard_map/ppermute | solution.py:178
  94.2 2.0 %collective-permute-start.28 = (bf16[128,1024]{1,0:T(8,128)(2,1)S(1)}, bf16[128,1024]{1,0:T(8,128)(2,1)S(1)}, u32[]{:S(2)}, u32[]{:S(2)}) collective-permute-start(bf16[128,1024]{1,0:T(8,128)(2,1)S(1)} %convolution_convert_fusion.1), channel_id=1, source_target_pairs={{0,24},{4,28},{8,16},{12,20},{16,8},{20,12},{24,0},{28,4},{1,25},{... | collective-permute-start | bytes 786440 | tf_op jit(solution)/shard_map/ppermute | solution.py:178
  100.9 6.5 %collective-permute-done.21 = bf16[128,1024]{1,0:T(8,128)(2,1)S(1)} collective-permute-done((bf16[128,1024]{1,0:T(8,128)(2,1)S(1)}, bf16[128,1024]{1,0:T(8,128)(2,1)S(1)}, u32[]{:S(2)}, u32[]{:S(2)}) %collective-permute-start.21) | collective-permute-done | bytes 262176 | tf_op jit(solution)/shard_map/ppermute | solution.py:178
  108.2 3.3 %collective-permute-done.30 = bf16[128,1024]{1,0:T(8,128)(2,1)S(1)} collective-permute-done((bf16[128,1024]{1,0:T(8,128)(2,1)S(1)}, bf16[128,1024]{1,0:T(8,128)(2,1)S(1)}, u32[]{:S(2)}, u32[]{:S(2)}) %collective-permute-start.30) | collective-permute-done | bytes 262176 | tf_op jit(solution)/shard_map/ppermute | solution.py:178
  112.9 45.9 %reduce-scatter.2.cloned.1.call-done = bf16[128,2048]{1,0:T(8,128)(2,1)} async-done(((bf16[128,8192]{1,0:T(8,128)(2,1)}), bf16[128,2048]{1,0:T(8,128)(2,1)}) %reduce-scatter.2.cloned.1.call-update) | async-done | bytes 524304 | tf_op jit(solution)/shard_map/reduce_scatter | solution.py:181
  158.8 2.0 %add_convert_fusion = bf16[128,2048]{1,0:T(8,128)(2,1)} fusion(bf16[128,2048]{1,0:T(8,128)(2,1)} %reduce-scatter.2.cloned.1.call-done, bf16[128,2048]{1,0:T(8,128)(2,1)S(1)} %copy-done.3), kind=kLoop, calls=%fused_computation.37 | loop fusion | flops 1048576 | bytes 1572864 | tf_op jit(solution)/shard_map/convert_element_type | solution.py:182
  (109 shorter events, 36.9 us)
Async XLA Ops:
  6.5 152.3 %reduce-scatter.2.cloned.1.call-start = ((), (), s32[]{:S(2)}) async-start(), calls=%async_computation.1 | async-start | bytes 2621440 | tf_op jit(solution)/shard_map/reduce_scatter | solution.py:181
  8.9 16.0 %collective-permute-start.3 = (bf16[16,128,128]{2,1,0:T(8,128)(2,1)}, bf16[16,128,128]{2,1,0:T(8,128)(2,1)}, u32[]{:S(2)}, u32[]{:S(2)}) collective-permute-start(bf16[16,128,128]{2,1,0:T(8,128)(2,1)} %bitcast.2), channel_id=1, source_target_pairs={{0,16},{8,24},{16,0},{24,8},{1,17},{9,25},{17,1},{25,9},{2,18},{10... | collective-permute-start | bytes 1572872 | tf_op jit(solution)/shard_map/ppermute | solution.py:71
  11.9 15.2 %collective-permute-start.1 = (bf16[16,128,128]{2,1,0:T(8,128)(2,1)}, bf16[16,128,128]{2,1,0:T(8,128)(2,1)}, u32[]{:S(2)}, u32[]{:S(2)}) collective-permute-start(bf16[16,128,128]{2,1,0:T(8,128)(2,1)} %bitcast.2), channel_id=1, source_target_pairs={{0,8},{8,0},{16,24},{24,16},{1,9},{9,1},{17,25},{25,17},{2,10},{10... | collective-permute-start | bytes 1572872 | tf_op jit(solution)/shard_map/ppermute | solution.py:70
  13.4 29.6 %collective-permute-start = (bf16[16,128,128]{2,1,0:T(8,128)(2,1)}, bf16[16,128,128]{2,1,0:T(8,128)(2,1)}, u32[]{:S(2)}, u32[]{:S(2)}) collective-permute-start(bf16[16,128,128]{2,1,0:T(8,128)(2,1)} %bitcast.2), channel_id=1, source_target_pairs={{0,4},{4,0},{1,5},{5,1},{2,6},{6,2},{3,7},{7,3},{8,12},{12,8},{9,1... | collective-permute-start | bytes 1572872 | tf_op jit(solution)/shard_map/ppermute | solution.py:82
  14.7 23.5 %collective-permute-start.9 = (bf16[16,128,128]{1,2,0:T(8,128)(2,1)S(1)}, bf16[16,128,128]{1,2,0:T(8,128)(2,1)S(1)}, u32[]{:S(2)}, u32[]{:S(2)}) collective-permute-start(bf16[16,128,128]{1,2,0:T(8,128)(2,1)S(1)} %bitcast.135), channel_id=1, source_target_pairs={{0,8},{8,0},{16,24},{24,16},{1,9},{9,1},{17,25},{25,17},{2,10},{10... | collective-permute-start | bytes 1572872 | tf_op jit(solution)/shard_map/ppermute | solution.py:70
  15.3 20.0 %collective-permute-start.11 = (bf16[16,128,128]{1,2,0:T(8,128)(2,1)S(1)}, bf16[16,128,128]{1,2,0:T(8,128)(2,1)S(1)}, u32[]{:S(2)}, u32[]{:S(2)}) collective-permute-start(bf16[16,128,128]{1,2,0:T(8,128)(2,1)S(1)} %bitcast.136), channel_id=1, source_target_pairs={{0,16},{8,24},{16,0},{24,8},{1,17},{9,25},{17,1},{25,9},{2,18},{10... | collective-permute-start | bytes 1572872 | tf_op jit(solution)/shard_map/ppermute | solution.py:71
  25.0 30.4 %collective-permute-start.8 = (bf16[16,128,128]{1,2,0:T(8,128)(2,1)S(1)}, bf16[16,128,128]{1,2,0:T(8,128)(2,1)S(1)}, u32[]{:S(2)}, u32[]{:S(2)}) collective-permute-start(bf16[16,128,128]{1,2,0:T(8,128)(2,1)S(1)} %bitcast.137), channel_id=1, source_target_pairs={{0,4},{4,0},{1,5},{5,1},{2,6},{6,2},{3,7},{7,3},{8,12},{12,8},{9,1... | collective-permute-start | bytes 1572872 | tf_op jit(solution)/shard_map/ppermute | solution.py:82
  27.1 18.1 %collective-permute-start.5 = (bf16[8,128,128]{2,1,0:T(8,128)(2,1)S(1)}, bf16[8,128,128]{2,1,0:T(8,128)(2,1)S(1)}, u32[]{:S(2)}, u32[]{:S(2)}) collective-permute-start(bf16[8,128,128]{2,1,0:T(8,128)(2,1)S(1)} %slice.24), channel_id=1, source_target_pairs={{0,8},{8,0},{16,24},{24,16},{1,9},{9,1},{17,25},{25,17},{2,10},{10... | collective-permute-start | bytes 786440 | tf_op jit(solution)/shard_map/ppermute | solution.py:74
  35.3 12.7 %collective-permute-start.6 = (bf16[8,128,128]{2,1,0:T(8,128)(2,1)S(1)}, bf16[8,128,128]{2,1,0:T(8,128)(2,1)S(1)}, u32[]{:S(2)}, u32[]{:S(2)}) collective-permute-start(bf16[8,128,128]{2,1,0:T(8,128)(2,1)S(1)} %slice.25), channel_id=1, source_target_pairs={{0,16},{8,24},{16,0},{24,8},{1,17},{9,25},{17,1},{25,9},{2,18},{10... | collective-permute-start | bytes 786440 | tf_op jit(solution)/shard_map/ppermute | solution.py:75
  38.2 9.8 %collective-permute-start.13 = (bf16[8,128,128]{1,2,0:T(8,128)(2,1)S(1)}, bf16[8,128,128]{1,2,0:T(8,128)(2,1)S(1)}, u32[]{:S(2)}, u32[]{:S(2)}) collective-permute-start(bf16[8,128,128]{1,2,0:T(8,128)(2,1)S(1)} %slice.26), channel_id=1, source_target_pairs={{0,8},{8,0},{16,24},{24,16},{1,9},{9,1},{17,25},{25,17},{2,10},{10... | collective-permute-start | bytes 786440 | tf_op jit(solution)/shard_map/ppermute | solution.py:74
  48.0 10.0 %collective-permute-start.10 = (bf16[16,128,128]{1,2,0:T(8,128)(2,1)S(1)}, bf16[16,128,128]{1,2,0:T(8,128)(2,1)S(1)}, u32[]{:S(2)}, u32[]{:S(2)}) collective-permute-start(bf16[16,128,128]{1,2,0:T(8,128)(2,1)S(1)} %collective-permute-done.9), channel_id=1, source_target_pairs={{0,4},{4,0},{1,5},{5,1},{2,6},{6,2},{3,7},{7,3},{8,12},{12,8},{9,1... | collective-permute-start | bytes 1572872 | tf_op jit(solution)/shard_map/ppermute | solution.py:82
  49.4 9.2 %collective-permute-start.12 = (bf16[16,128,128]{1,2,0:T(8,128)(2,1)S(1)}, bf16[16,128,128]{1,2,0:T(8,128)(2,1)S(1)}, u32[]{:S(2)}, u32[]{:S(2)}) collective-permute-start(bf16[16,128,128]{1,2,0:T(8,128)(2,1)S(1)} %collective-permute-done.11), channel_id=1, source_target_pairs={{0,4},{4,0},{1,5},{5,1},{2,6},{6,2},{3,7},{7,3},{8,12},{12,8},{9,1... | collective-permute-start | bytes 1572872 | tf_op jit(solution)/shard_map/ppermute | solution.py:82
  60.0 14.4 %collective-permute-start.18 = (bf16[128,2048]{0,1:T(8,128)(2,1)}, bf16[128,2048]{0,1:T(8,128)(2,1)S(1)}, u32[]{:S(2)}, u32[]{:S(2)}) collective-permute-start(bf16[128,2048]{0,1:T(8,128)(2,1)} %bitcast.10), channel_id=1, source_target_pairs={{0,8},{8,0},{16,24},{24,16},{1,9},{9,1},{17,25},{25,17},{2,10},{10... | collective-permute-start | bytes 1572872 | tf_op jit(solution)/shard_map/ppermute | solution.py:70
  61.5 14.0 %collective-permute-start.22 = (bf16[128,2048]{0,1:T(8,128)(2,1)}, bf16[128,2048]{0,1:T(8,128)(2,1)}, u32[]{:S(2)}, u32[]{:S(2)}) collective-permute-start(bf16[128,2048]{0,1:T(8,128)(2,1)} %bitcast.10), channel_id=1, source_target_pairs={{0,16},{8,24},{16,0},{24,8},{1,17},{9,25},{17,1},{25,9},{2,18},{10... | collective-permute-start | bytes 1572872 | tf_op jit(solution)/shard_map/ppermute | solution.py:71
  62.0 14.5 %collective-permute-start.16 = (bf16[128,2048]{0,1:T(8,128)(2,1)}, bf16[128,2048]{0,1:T(8,128)(2,1)}, u32[]{:S(2)}, u32[]{:S(2)}) collective-permute-start(bf16[128,2048]{0,1:T(8,128)(2,1)} %bitcast.10), channel_id=1, source_target_pairs={{0,4},{4,0},{1,5},{5,1},{2,6},{6,2},{3,7},{7,3},{8,12},{12,8},{9,1... | collective-permute-start | bytes 1572872 | tf_op jit(solution)/shard_map/ppermute | solution.py:82
  74.6 14.9 %collective-permute-start.27 = (bf16[64,2048]{0,1:T(8,128)(2,1)S(1)}, bf16[64,2048]{0,1:T(8,128)(2,1)S(1)}, u32[]{:S(2)}, u32[]{:S(2)}) collective-permute-start(bf16[64,2048]{0,1:T(8,128)(2,1)S(1)} %slice.29), channel_id=1, source_target_pairs={{0,16},{8,24},{16,0},{24,8},{1,17},{9,25},{17,1},{25,9},{2,18},{10... | collective-permute-start | bytes 786440 | tf_op jit(solution)/shard_map/ppermute | solution.py:75
  75.5 15.1 %collective-permute-start.26 = (bf16[64,2048]{0,1:T(8,128)(2,1)}, bf16[64,2048]{0,1:T(8,128)(2,1)S(1)}, u32[]{:S(2)}, u32[]{:S(2)}) collective-permute-start(bf16[64,2048]{0,1:T(8,128)(2,1)} %bitcast.134), channel_id=1, source_target_pairs={{0,8},{8,0},{16,24},{24,16},{1,9},{9,1},{17,25},{25,17},{2,10},{10... | collective-permute-start | bytes 786440 | tf_op jit(solution)/shard_map/ppermute | solution.py:74
  78.4 13.3 %collective-permute-start.17 = (bf16[128,1024]{1,0:T(8,128)(2,1)S(1)}, bf16[128,1024]{1,0:T(8,128)(2,1)S(1)}, u32[]{:S(2)}, u32[]{:S(2)}) collective-permute-start(bf16[128,1024]{1,0:T(8,128)(2,1)S(1)} %convolution_convert_fusion.6), channel_id=1, source_target_pairs={{0,4},{4,0},{8,12},{12,8},{16,20},{20,16},{24,28},{28,24},{1,5},{5... | collective-permute-start | bytes 786440 | tf_op jit(solution)/shard_map/ppermute | solution.py:178
  79.2 15.0 %collective-permute-start.19 = (bf16[128,1024]{1,0:T(8,128)(2,1)S(1)}, bf16[128,1024]{1,0:T(8,128)(2,1)S(1)}, u32[]{:S(2)}, u32[]{:S(2)}) collective-permute-start(bf16[128,1024]{1,0:T(8,128)(2,1)S(1)} %convolution_convert_fusion.5), channel_id=1, source_target_pairs={{0,8},{4,12},{8,0},{12,4},{16,24},{20,28},{24,16},{28,20},{1,9},{5... | collective-permute-start | bytes 786440 | tf_op jit(solution)/shard_map/ppermute | solution.py:178
  82.1 25.3 %collective-permute-start.23 = (bf16[128,1024]{1,0:T(8,128)(2,1)S(1)}, bf16[128,1024]{1,0:T(8,128)(2,1)S(1)}, u32[]{:S(2)}, u32[]{:S(2)}) collective-permute-start(bf16[128,1024]{1,0:T(8,128)(2,1)S(1)} %convolution_convert_fusion.3), channel_id=1, source_target_pairs={{0,16},{4,20},{8,24},{12,28},{16,0},{20,4},{24,8},{28,12},{1,17},{... | collective-permute-start | bytes 786440 | tf_op jit(solution)/shard_map/ppermute | solution.py:178
  94.2 14.0 %collective-permute-start.28 = (bf16[128,1024]{1,0:T(8,128)(2,1)S(1)}, bf16[128,1024]{1,0:T(8,128)(2,1)S(1)}, u32[]{:S(2)}, u32[]{:S(2)}) collective-permute-start(bf16[128,1024]{1,0:T(8,128)(2,1)S(1)} %convolution_convert_fusion.1), channel_id=1, source_target_pairs={{0,24},{4,28},{8,16},{12,20},{16,8},{20,12},{24,0},{28,4},{1,25},{... | collective-permute-start | bytes 786440 | tf_op jit(solution)/shard_map/ppermute | solution.py:178
  97.0 10.4 %collective-permute-start.21 = (bf16[128,1024]{1,0:T(8,128)(2,1)S(1)}, bf16[128,1024]{1,0:T(8,128)(2,1)S(1)}, u32[]{:S(2)}, u32[]{:S(2)}) collective-permute-start(bf16[128,1024]{1,0:T(8,128)(2,1)S(1)} %convolution_convert_fusion.4), channel_id=1, source_target_pairs={{0,12},{4,8},{8,4},{12,0},{16,28},{20,24},{24,20},{28,16},{1,13},{... | collective-permute-start | bytes 786440 | tf_op jit(solution)/shard_map/ppermute | solution.py:178
  97.8 10.3 %collective-permute-start.25 = (bf16[128,1024]{1,0:T(8,128)(2,1)S(1)}, bf16[128,1024]{1,0:T(8,128)(2,1)S(1)}, u32[]{:S(2)}, u32[]{:S(2)}) collective-permute-start(bf16[128,1024]{1,0:T(8,128)(2,1)S(1)} %convolution_convert_fusion.2), channel_id=1, source_target_pairs={{0,20},{4,16},{8,28},{12,24},{16,4},{20,0},{24,12},{28,8},{1,21},{... | collective-permute-start | bytes 786440 | tf_op jit(solution)/shard_map/ppermute | solution.py:178
  99.8 11.7 %collective-permute-start.30 = (bf16[128,1024]{1,0:T(8,128)(2,1)S(1)}, bf16[128,1024]{1,0:T(8,128)(2,1)S(1)}, u32[]{:S(2)}, u32[]{:S(2)}) collective-permute-start(bf16[128,1024]{1,0:T(8,128)(2,1)S(1)} %convolution_convert_fusion), channel_id=1, source_target_pairs={{0,28},{4,24},{8,20},{12,16},{16,12},{20,8},{24,4},{28,0},{1,29},{... | collective-permute-start | bytes 786440 | tf_op jit(solution)/shard_map/ppermute | solution.py:178
  (12 other events, 130.3 us)
Sparse Core Ops, SparseCore 0:
  113.1 45.7 reduce-scatter.1

commit v11 on v7

--- a/solution.py
+++ b/solution.py
@@ -162,6 +162,28 @@
             ratio = numer / row_total[..., None]
         local_context = ratio.transpose(1, 0, 2).reshape(seg_rows, feat_width).astype(jnp.bfloat16)
 
+        if square:
+            chip = lax.axis_index("hi")
+            core = lax.axis_index("lo")
+            blocks = gather_blocks_square(local_context)
+            width = out_weight.shape[1]
+            half = seg_rows // 2
+            reduced = []
+            for h in range(2):
+                by_row = jnp.zeros((half, seq_count * width), jnp.bfloat16)
+                for b, block in enumerate(blocks):
+                    r, t = b // 2, b % 2
+                    partial = jnp.dot(
+                        block[h * half : (h + 1) * half], out_weight, preferred_element_type=jnp.float32
+                    ).astype(jnp.bfloat16)
+                    if b:
+                        pairs = [(i * 2 + l, (i ^ r) * 2 + (l ^ t)) for i in range(4) for l in range(2)]
+                        partial = lax.ppermute(partial, SEQ, pairs)
+                    source = (chip ^ r) * 2 + (core ^ t)
+                    by_row = lax.dynamic_update_slice(by_row, partial, (0, source * width))
+                reduced.append(lax.psum_scatter(by_row, "chan", scatter_dimension=1, tiled=True))
+            ordered = jnp.concatenate(reduced, axis=0)
+            return (residual.astype(jnp.float32) + ordered.astype(jnp.float32)).astype(jnp.bfloat16)
         gathered = gather_seq(local_context)
         group = seq_count // chan_count
         chunks = 2

time: 184 us -> 183 us (level)
  blocking collectives: 36.8 us -> 0 us
  waiting for transfers between devices: 73.4 us -> 90.3 us
  starting transfers between devices: 16 us -> 32.5 us
  matrix products: 20.7 us -> 30 us
  local copies, waits for them, and re-layouts: 17.9 us -> 10.9 us
    all_to_all x2 -> x0, blocking collectives: 36.8 us -> none  [per_device(): lax.all_to_all(partial, SEQ, split_axis=0, concat_axis=1, tiled=True)]
    ppermute x8 -> x14, starting transfers between devices: 4.13 us -> 15.3 us  [per_device(): partial = lax.ppermute(partial, SEQ, pairs)]
    dot_general x2 -> x16, matrix products: 10.5 us -> 19.5 us  [per_device(): jnp.dot(block[h * half:(h + 1) * half], out_weight, preferred_element_typ...]
    ppermute x2 -> x3, waiting for transfers between devices: 3.73 us -> 11.2 us  [gather_blocks_square(): lax.ppermute(from_y[:half], 'hi', swap('hi', 1, 4))]
    ppermute x2 -> x3, waiting for transfers between devices: 2.18 us -> 9.26 us  [gather_blocks_square(): from_x = lax.ppermute(x, 'hi', swap('hi', 1, 4))]
    dynamic_update_slice x7 -> x14, local copies, waits for them, and re-layouts: 6.23 us -> 3.27 us  [per_device(): by_row = lax.dynamic_update_slice(by_row, partial, (0, source * width))]
    reduce_scatter x2, waiting for transfers between devices: 29.5 us -> 32.4 us  [per_device(): lax.psum_scatter(by_row, 'chan', scatter_dimension=1, tiled=True)]
    broadcast_in_dim x1 -> x0, local copies, waits for them, and re-layouts: 2.62 us -> none  [assemble(): out = jnp.zeros((len(pieces) * rows, width), dtype)]
  transfers between devices with their start and end apart: 26 -> 40, of which waited for: 12 -> 17; matrix products, arithmetic and copies ran while one was open for 17% -> 21% of each run, Pallas kernels for 0% -> 0%
where the time goes in v11:
time: 183 us
  waiting for transfers between devices  90.3 us (49%)
  starting transfers between devices  32.5 us (18%)
  matrix products  30 us (16%)
  between operations  14.2 us (8%)
  local copies, waits for them, and re-layouts  10.9 us (6%)
  other arithmetic  5.16 us (3%)
    reduce_scatter x2, waiting for transfers between devices, per_device(): lax.psum_scatter(by_row, 'chan', scatter_dimension=1, tiled=True)  32.4 us
    ppermute x14, waiting for transfers between devices, per_device(): partial = lax.ppermute(partial, SEQ, pairs)  21.7 us
    dot_general x16, matrix products, per_device(): jnp.dot(block[h * half:(h + 1) * half], out_weight, preferred_element_typ...  19.5 us
    ppermute x14, starting transfers between devices, per_device(): partial = lax.ppermute(partial, SEQ, pairs)  15.3 us
    ppermute x3, waiting for transfers between devices, gather_blocks_square(): from_y = lax.ppermute(x, 'hi', swap('hi', 2, 4))  14.4 us
    ppermute x3, waiting for transfers between devices, gather_blocks_square(): lax.ppermute(from_y[:half], 'hi', swap('hi', 1, 4))  11.2 us
    ppermute x3, waiting for transfers between devices, gather_blocks_square(): from_x = lax.ppermute(x, 'hi', swap('hi', 1, 4))  9.26 us
    dot_general x8, matrix products, attention_by_head(): jnp.einsum('hqd,hkd->hqk', queries, keys, preferred_element_type=jnp.floa...  6.47 us
  transfers between devices with their start and end apart: 40, of which 17 were waited for; matrix products, arithmetic and copies ran while one was open for 21% of the time, Pallas kernels for 0%

profile of v11, /device:TPU:0, one launch (start us, length us, event | category | flops | bytes accessed | tf_op | source)
XLA Modules:
  0.0 183.1 jit_solution(12800955605386372798)
XLA Ops:
  8.2 3.0 %collective-permute-start.3 = (bf16[16,128,128]{2,1,0:T(8,128)(2,1)S(1)}, bf16[16,128,128]{2,1,0:T(8,128)(2,1)}, u32[]{:S(2)}, u32[]{:S(2)}) collective-permute-start(bf16[16,128,128]{2,1,0:T(8,128)(2,1)S(1)} %bitcast.153), channel_id=1, source_target_pairs={{0,16},{8,24},{16,0},{24,8},{1,17},{9,25},{17,1},{25,9},{2,18},{10... | collective-permute-start | bytes 1572872 | tf_op jit(solution)/shard_map/ppermute | solution.py:71
  16.5 7.6 %collective-permute-done.3 = bf16[16,128,128]{2,1,0:T(8,128)(2,1)} collective-permute-done((bf16[16,128,128]{2,1,0:T(8,128)(2,1)S(1)}, bf16[16,128,128]{2,1,0:T(8,128)(2,1)}, u32[]{:S(2)}, u32[]{:S(2)}) %collective-permute-start.3) | collective-permute-done | bytes 524320 | tf_op jit(solution)/shard_map/ppermute | solution.py:71
  27.6 6.8 %collective-permute-done.11 = bf16[16,128,128]{2,1,0:T(8,128)(2,1)S(1)} collective-permute-done((bf16[16,128,128]{2,1,0:T(8,128)(2,1)S(1)}, bf16[16,128,128]{2,1,0:T(8,128)(2,1)S(1)}, u32[]{:S(2)}, u32[]{:S(2)}) %collective-permute-start.11) | collective-permute-done | bytes 524320 | tf_op jit(solution)/shard_map/ppermute | solution.py:71
  34.4 1.7 collective-permute-start.6
  38.8 1.6 fusion.107
  41.6 1.6 fusion.111
  43.4 3.7 %collective-permute-done.13 = bf16[8,128,128]{2,1,0:T(8,128)(2,1)S(1)} collective-permute-done((bf16[8,128,128]{2,1,0:T(8,128)(2,1)S(1)}, bf16[8,128,128]{2,1,0:T(8,128)(2,1)S(1)}, u32[]{:S(2)}, u32[]{:S(2)}) %collective-permute-start.13) | collective-permute-done | bytes 262176 | tf_op jit(solution)/shard_map/ppermute | solution.py:74
  52.5 2.1 %fusion.20 = (f32[16,128]{1,0:T(8,128)S(1)}, f32[16,128]{1,0:T(8,128)S(1)}, f32[16,128]{1,0:T(8,128)S(1)}, f32[16,128]{1,0:T(8,128)S(1)}, f32[16,128]{1,0:T(8,128)S(1)}) fusion(f32[16,128,128]{2,1,0:T(8,128)S(1)} %get-tuple-element.38, f32[16,128]{1,0:T(8,128)S(1)} %maximum_maximum_fusion, pred[128,128]{1,0:T(8,128)(4,1)S(1)} %copy.40, ...), kind=kLoop, calls=%fused_computation.57 | loop fusion | flops 3921920 | bytes 5373952 | tf_op jit(solution)/shard_map/reduce_sum | solution.py:106
  61.3 3.0 %fusion.17 = bf16[64,8192]{1,0:T(8,128)(2,1)S(1)} fusion(bf16[64,8192]{1,0:T(8,128)(2,1)S(1)} %broadcast.190.clone.1, s32[]{:T(128)S(6)} %select_n.97, bf16[2048,1024]{1,0:T(8,128)(2,1)} %param.9, bf16[16,8,8,128]{3,2,1,0:T(8,128)(2,1)S(1)} %get-tuple-element.13), kind=kOutput, calls=%fused_computation.45 | convolution fusion | flops 268500992 | bytes 4587524 | tf_op jit(solution)/shard_map/dot_general | solution.py:176
  66.2 7.1 %collective-permute-done.18 = bf16[128,2048]{0,1:T(8,128)(2,1)S(1)} collective-permute-done((bf16[128,2048]{0,1:T(8,128)(2,1)S(1)}, bf16[128,2048]{0,1:T(8,128)(2,1)S(1)}, u32[]{:S(2)}, u32[]{:S(2)}) %collective-permute-start.18) | collective-permute-done | bytes 524320 | tf_op jit(solution)/shard_map/ppermute | solution.py:70
  77.8 1.7 collective-permute-start.28
  84.4 7.4 %collective-permute-done.26 = bf16[64,2048]{0,1:T(8,128)(2,1)S(1)} collective-permute-done((bf16[64,2048]{0,1:T(8,128)(2,1)S(1)}, bf16[64,2048]{0,1:T(8,128)(2,1)S(1)}, u32[]{:S(2)}, u32[]{:S(2)}) %collective-permute-start.26) | collective-permute-done | bytes 262176 | tf_op jit(solution)/shard_map/ppermute | solution.py:74
  97.2 3.0 %collective-permute-done.21 = bf16[64,1024]{1,0:T(8,128)(2,1)S(1)} collective-permute-done((bf16[64,1024]{1,0:T(8,128)(2,1)S(1)}, bf16[64,1024]{1,0:T(8,128)(2,1)S(1)}, u32[]{:S(2)}, u32[]{:S(2)}) %collective-permute-start.21) | collective-permute-done | bytes 131104 | tf_op jit(solution)/shard_map/ppermute | solution.py:181
  101.3 1.9 %collective-permute-start.27 = (bf16[64,1024]{1,0:T(8,128)(2,1)S(1)}, bf16[64,1024]{1,0:T(8,128)(2,1)S(1)}, u32[]{:S(2)}, u32[]{:S(2)}) collective-permute-start(bf16[64,1024]{1,0:T(8,128)(2,1)S(1)} %convolution_convert_fusion.9), channel_id=1, source_target_pairs={{0,24},{4,28},{8,16},{12,20},{16,8},{20,12},{24,0},{28,4},{1,25},{... | collective-permute-start | bytes 393224 | tf_op jit(solution)/shard_map/ppermute | solution.py:181
  104.2 6.7 %collective-permute-done.25 = bf16[64,1024]{1,0:T(8,128)(2,1)S(1)} collective-permute-done((bf16[64,1024]{1,0:T(8,128)(2,1)S(1)}, bf16[64,1024]{1,0:T(8,128)(2,1)S(1)}, u32[]{:S(2)}, u32[]{:S(2)}) %collective-permute-start.25) | collective-permute-done | bytes 131104 | tf_op jit(solution)/shard_map/ppermute | solution.py:181
  112.4 4.6 %collective-permute-done.30 = bf16[64,1024]{1,0:T(8,128)(2,1)S(1)} collective-permute-done((bf16[64,1024]{1,0:T(8,128)(2,1)S(1)}, bf16[64,1024]{1,0:T(8,128)(2,1)S(1)}, u32[]{:S(2)}, u32[]{:S(2)}) %collective-permute-start.30) | collective-permute-done | bytes 131104 | tf_op jit(solution)/shard_map/ppermute | solution.py:181
  120.6 3.1 %convolution_convert_fusion.1 = bf16[64,1024]{1,0:T(8,128)(2,1)S(1)} fusion(bf16[64,2048]{0,1:T(8,128)(2,1)S(1)} %collective-permute-done.28, bf16[2048,1024]{1,0:T(8,128)(2,1)} %param.9), kind=kOutput, calls=%fused_computation.29 | convolution fusion | flops 268500992 | bytes 4587520 | tf_op jit(solution)/shard_map/dot_general | solution.py:176
  123.7 1.9 %collective-permute-start.36 = (bf16[64,1024]{1,0:T(8,128)(2,1)S(1)}, bf16[64,1024]{1,0:T(8,128)(2,1)S(1)}, u32[]{:S(2)}, u32[]{:S(2)}) collective-permute-start(bf16[64,1024]{1,0:T(8,128)(2,1)S(1)} %convolution_convert_fusion.1), channel_id=1, source_target_pairs={{0,24},{4,28},{8,16},{12,20},{16,8},{20,12},{24,0},{28,4},{1,25},{... | collective-permute-start | bytes 393224 | tf_op jit(solution)/shard_map/ppermute | solution.py:181
  129.3 3.3 %collective-permute-done.33 = bf16[64,1024]{1,0:T(8,128)(2,1)S(1)} collective-permute-done((bf16[64,1024]{1,0:T(8,128)(2,1)S(1)}, bf16[64,1024]{1,0:T(8,128)(2,1)S(1)}, u32[]{:S(2)}, u32[]{:S(2)}) %collective-permute-start.33) | collective-permute-done | bytes 131104 | tf_op jit(solution)/shard_map/ppermute | solution.py:181
  134.7 2.0 %collective-permute-start.37 = (bf16[64,1024]{1,0:T(8,128)(2,1)S(1)}, bf16[64,1024]{1,0:T(8,128)(2,1)S(1)}, u32[]{:S(2)}, u32[]{:S(2)}) collective-permute-start(bf16[64,1024]{1,0:T(8,128)(2,1)S(1)} %convolution_convert_fusion), channel_id=1, source_target_pairs={{0,28},{4,24},{8,20},{12,16},{16,12},{20,8},{24,4},{28,0},{1,29},{... | collective-permute-start | bytes 393224 | tf_op jit(solution)/shard_map/ppermute | solution.py:181
  136.7 4.1 %collective-permute-done.37 = bf16[64,1024]{1,0:T(8,128)(2,1)S(1)} collective-permute-done((bf16[64,1024]{1,0:T(8,128)(2,1)S(1)}, bf16[64,1024]{1,0:T(8,128)(2,1)S(1)}, u32[]{:S(2)}, u32[]{:S(2)}) %collective-permute-start.37) | collective-permute-done | bytes 131104 | tf_op jit(solution)/shard_map/ppermute | solution.py:181
  141.9 4.2 %reduce-scatter.3.cloned.1.call-done = bf16[64,2048]{1,0:T(8,128)(2,1)} async-done(((bf16[64,8192]{1,0:T(8,128)(2,1)}), bf16[64,2048]{1,0:T(8,128)(2,1)}) %reduce-scatter.3.cloned.1.call-update) | async-done | bytes 262160 | tf_op jit(solution)/shard_map/reduce_scatter | solution.py:184
  146.1 28.2 %reduce-scatter.5.cloned.1.call-done = bf16[64,2048]{1,0:T(8,128)(2,1)} async-done(((bf16[64,8192]{1,0:T(8,128)(2,1)}), bf16[64,2048]{1,0:T(8,128)(2,1)}) %reduce-scatter.5.cloned.1.call-update) | async-done | bytes 262160 | tf_op jit(solution)/shard_map/reduce_scatter | solution.py:184
  174.3 2.0 %add_convert_fusion = bf16[128,2048]{1,0:T(8,128)(2,1)} fusion(bf16[128,2048]{1,0:T(8,128)(2,1)S(1)} %copy-done.11, bf16[64,2048]{1,0:T(8,128)(2,1)} %reduce-scatter.5.cloned.1.call-done, bf16[64,2048]{1,0:T(8,128)(2,1)} %reduce-scatter.3.cloned.1.call-done), kind=kLoop, calls=%fused_computation.46 | loop fusion | flops 1835008 | bytes 1572864 | tf_op jit(solution)/shard_map/convert_element_type | solution.py:186
  (161 shorter events, 56.4 us)
Async XLA Ops:
  6.5 139.5 %reduce-scatter.3.cloned.1.call-start = ((), (), s32[]{:S(2)}) async-start(), calls=%async_computation.2 | async-start | bytes 1310720 | tf_op jit(solution)/shard_map/reduce_scatter | solution.py:184
  8.2 15.9 %collective-permute-start.3 = (bf16[16,128,128]{2,1,0:T(8,128)(2,1)S(1)}, bf16[16,128,128]{2,1,0:T(8,128)(2,1)}, u32[]{:S(2)}, u32[]{:S(2)}) collective-permute-start(bf16[16,128,128]{2,1,0:T(8,128)(2,1)S(1)} %bitcast.153), channel_id=1, source_target_pairs={{0,16},{8,24},{16,0},{24,8},{1,17},{9,25},{17,1},{25,9},{2,18},{10... | collective-permute-start | bytes 1572872 | tf_op jit(solution)/shard_map/ppermute | solution.py:71
  11.2 14.8 %collective-permute-start.1 = (bf16[16,128,128]{2,1,0:T(8,128)(2,1)S(1)}, bf16[16,128,128]{2,1,0:T(8,128)(2,1)S(1)}, u32[]{:S(2)}, u32[]{:S(2)}) collective-permute-start(bf16[16,128,128]{2,1,0:T(8,128)(2,1)S(1)} %bitcast.154), channel_id=1, source_target_pairs={{0,8},{8,0},{16,24},{24,16},{1,9},{9,1},{17,25},{25,17},{2,10},{10... | collective-permute-start | bytes 1572872 | tf_op jit(solution)/shard_map/ppermute | solution.py:70
  12.7 28.3 %collective-permute-start = (bf16[16,128,128]{2,1,0:T(8,128)(2,1)S(1)}, bf16[16,128,128]{2,1,0:T(8,128)(2,1)}, u32[]{:S(2)}, u32[]{:S(2)}) collective-permute-start(bf16[16,128,128]{2,1,0:T(8,128)(2,1)S(1)} %bitcast.155), channel_id=1, source_target_pairs={{0,4},{4,0},{1,5},{5,1},{2,6},{6,2},{3,7},{7,3},{8,12},{12,8},{9,1... | collective-permute-start | bytes 1572872 | tf_op jit(solution)/shard_map/ppermute | solution.py:82
  14.3 23.0 %collective-permute-start.9 = (bf16[16,128,128]{2,1,0:T(8,128)(2,1)S(1)}, bf16[16,128,128]{2,1,0:T(8,128)(2,1)S(1)}, u32[]{:S(2)}, u32[]{:S(2)}) collective-permute-start(bf16[16,128,128]{2,1,0:T(8,128)(2,1)S(1)} %bitcast.148), channel_id=1, source_target_pairs={{0,8},{8,0},{16,24},{24,16},{1,9},{9,1},{17,25},{25,17},{2,10},{10... | collective-permute-start | bytes 1572872 | tf_op jit(solution)/shard_map/ppermute | solution.py:70
  14.9 19.5 %collective-permute-start.11 = (bf16[16,128,128]{2,1,0:T(8,128)(2,1)S(1)}, bf16[16,128,128]{2,1,0:T(8,128)(2,1)S(1)}, u32[]{:S(2)}, u32[]{:S(2)}) collective-permute-start(bf16[16,128,128]{2,1,0:T(8,128)(2,1)S(1)} %bitcast.149), channel_id=1, source_target_pairs={{0,16},{8,24},{16,0},{24,8},{1,17},{9,25},{17,1},{25,9},{2,18},{10... | collective-permute-start | bytes 1572872 | tf_op jit(solution)/shard_map/ppermute | solution.py:71
  24.1 30.5 %collective-permute-start.8 = (bf16[16,128,128]{2,1,0:T(8,128)(2,1)S(1)}, bf16[16,128,128]{2,1,0:T(8,128)(2,1)S(1)}, u32[]{:S(2)}, u32[]{:S(2)}) collective-permute-start(bf16[16,128,128]{2,1,0:T(8,128)(2,1)S(1)} %bitcast.150), channel_id=1, source_target_pairs={{0,4},{4,0},{1,5},{5,1},{2,6},{6,2},{3,7},{7,3},{8,12},{12,8},{9,1... | collective-permute-start | bytes 1572872 | tf_op jit(solution)/shard_map/ppermute | solution.py:82
  26.1 17.2 %collective-permute-start.5 = (bf16[8,128,128]{2,1,0:T(8,128)(2,1)S(1)}, bf16[8,128,128]{2,1,0:T(8,128)(2,1)S(1)}, u32[]{:S(2)}, u32[]{:S(2)}) collective-permute-start(bf16[8,128,128]{2,1,0:T(8,128)(2,1)S(1)} %slice.82), channel_id=1, source_target_pairs={{0,8},{8,0},{16,24},{24,16},{1,9},{9,1},{17,25},{25,17},{2,10},{10... | collective-permute-start | bytes 786440 | tf_op jit(solution)/shard_map/ppermute | solution.py:74
  34.4 12.7 %collective-permute-start.6 = (bf16[8,128,128]{2,1,0:T(8,128)(2,1)S(1)}, bf16[8,128,128]{2,1,0:T(8,128)(2,1)S(1)}, u32[]{:S(2)}, u32[]{:S(2)}) collective-permute-start(bf16[8,128,128]{2,1,0:T(8,128)(2,1)S(1)} %slice.83), channel_id=1, source_target_pairs={{0,16},{8,24},{16,0},{24,8},{1,17},{9,25},{17,1},{25,9},{2,18},{10... | collective-permute-start | bytes 786440 | tf_op jit(solution)/shard_map/ppermute | solution.py:75
  37.3 9.8 %collective-permute-start.13 = (bf16[8,128,128]{2,1,0:T(8,128)(2,1)S(1)}, bf16[8,128,128]{2,1,0:T(8,128)(2,1)S(1)}, u32[]{:S(2)}, u32[]{:S(2)}) collective-permute-start(bf16[8,128,128]{2,1,0:T(8,128)(2,1)S(1)} %slice.84), channel_id=1, source_target_pairs={{0,8},{8,0},{16,24},{24,16},{1,9},{9,1},{17,25},{25,17},{2,10},{10... | collective-permute-start | bytes 786440 | tf_op jit(solution)/shard_map/ppermute | solution.py:74
  47.1 9.9 %collective-permute-start.10 = (bf16[16,128,128]{2,1,0:T(8,128)(2,1)S(1)}, bf16[16,128,128]{2,1,0:T(8,128)(2,1)S(1)}, u32[]{:S(2)}, u32[]{:S(2)}) collective-permute-start(bf16[16,128,128]{2,1,0:T(8,128)(2,1)S(1)} %collective-permute-done.9), channel_id=1, source_target_pairs={{0,4},{4,0},{1,5},{5,1},{2,6},{6,2},{3,7},{7,3},{8,12},{12,8},{9,1... | collective-permute-start | bytes 1572872 | tf_op jit(solution)/shard_map/ppermute | solution.py:82
  47.7 9.8 %collective-permute-start.12 = (bf16[16,128,128]{2,1,0:T(8,128)(2,1)S(1)}, bf16[16,128,128]{2,1,0:T(8,128)(2,1)S(1)}, u32[]{:S(2)}, u32[]{:S(2)}) collective-permute-start(bf16[16,128,128]{2,1,0:T(8,128)(2,1)S(1)} %collective-permute-done.11), channel_id=1, source_target_pairs={{0,4},{4,0},{1,5},{5,1},{2,6},{6,2},{3,7},{7,3},{8,12},{12,8},{9,1... | collective-permute-start | bytes 1572872 | tf_op jit(solution)/shard_map/ppermute | solution.py:82
  59.1 14.2 %collective-permute-start.18 = (bf16[128,2048]{0,1:T(8,128)(2,1)S(1)}, bf16[128,2048]{0,1:T(8,128)(2,1)S(1)}, u32[]{:S(2)}, u32[]{:S(2)}) collective-permute-start(bf16[128,2048]{0,1:T(8,128)(2,1)S(1)} %bitcast.157), channel_id=1, source_target_pairs={{0,8},{8,0},{16,24},{24,16},{1,9},{9,1},{17,25},{25,17},{2,10},{10... | collective-permute-start | bytes 1572872 | tf_op jit(solution)/shard_map/ppermute | solution.py:70
  60.6 15.1 %collective-permute-start.22 = (bf16[128,2048]{0,1:T(8,128)(2,1)S(1)}, bf16[128,2048]{0,1:T(8,128)(2,1)S(1)}, u32[]{:S(2)}, u32[]{:S(2)}) collective-permute-start(bf16[128,2048]{0,1:T(8,128)(2,1)S(1)} %bitcast.158), channel_id=1, source_target_pairs={{0,16},{8,24},{16,0},{24,8},{1,17},{9,25},{17,1},{25,9},{2,18},{10... | collective-permute-start | bytes 1572872 | tf_op jit(solution)/shard_map/ppermute | solution.py:71
  66.2 16.6 %collective-permute-start.17 = (bf16[64,1024]{1,0:T(8,128)(2,1)S(1)}, bf16[64,1024]{1,0:T(8,128)(2,1)S(1)}, u32[]{:S(2)}, u32[]{:S(2)}) collective-permute-start(bf16[64,1024]{1,0:T(8,128)(2,1)S(1)} %convolution_convert_fusion.14), channel_id=1, source_target_pairs={{0,4},{4,0},{8,12},{12,8},{16,20},{20,16},{24,28},{28,24},{1,5},{5... | collective-permute-start | bytes 393224 | tf_op jit(solution)/shard_map/ppermute | solution.py:181
  76.6 24.7 %collective-permute-start.23 = (bf16[64,1024]{1,0:T(8,128)(2,1)S(1)}, bf16[64,1024]{1,0:T(8,128)(2,1)S(1)}, u32[]{:S(2)}, u32[]{:S(2)}) collective-permute-start(bf16[64,1024]{1,0:T(8,128)(2,1)S(1)} %convolution_convert_fusion.11), channel_id=1, source_target_pairs={{0,16},{4,20},{8,24},{12,28},{16,0},{20,4},{24,8},{28,12},{1,17},{... | collective-permute-start | bytes 393224 | tf_op jit(solution)/shard_map/ppermute | solution.py:181
  77.2 14.7 %collective-permute-start.26 = (bf16[64,2048]{0,1:T(8,128)(2,1)S(1)}, bf16[64,2048]{0,1:T(8,128)(2,1)S(1)}, u32[]{:S(2)}, u32[]{:S(2)}) collective-permute-start(bf16[64,2048]{0,1:T(8,128)(2,1)S(1)} %bitcast.147), channel_id=1, source_target_pairs={{0,8},{8,0},{16,24},{24,16},{1,9},{9,1},{17,25},{25,17},{2,10},{10... | collective-permute-start | bytes 786440 | tf_op jit(solution)/shard_map/ppermute | solution.py:74
  77.8 14.9 %collective-permute-start.28 = (bf16[64,2048]{0,1:T(8,128)(2,1)S(1)}, bf16[64,2048]{0,1:T(8,128)(2,1)S(1)}, u32[]{:S(2)}, u32[]{:S(2)}) collective-permute-start(bf16[64,2048]{0,1:T(8,128)(2,1)S(1)} %slice.92), channel_id=1, source_target_pairs={{0,16},{8,24},{16,0},{24,8},{1,17},{9,25},{17,1},{25,9},{2,18},{10... | collective-permute-start | bytes 786440 | tf_op jit(solution)/shard_map/ppermute | solution.py:75
  82.7 35.6 %collective-permute-start.31 = (bf16[64,1024]{1,0:T(8,128)(2,1)S(1)}, bf16[64,1024]{1,0:T(8,128)(2,1)}, u32[]{:S(2)}, u32[]{:S(2)}) collective-permute-start(bf16[64,1024]{1,0:T(8,128)(2,1)S(1)} %convolution_convert_fusion.6), channel_id=1, source_target_pairs={{0,4},{4,0},{8,12},{12,8},{16,20},{20,16},{24,28},{28,24},{1,5},{5... | collective-permute-start | bytes 393224 | tf_op jit(solution)/shard_map/ppermute | solution.py:181
  82.8 36.6 %collective-permute-start.32 = (bf16[64,1024]{1,0:T(8,128)(2,1)S(1)}, bf16[64,1024]{1,0:T(8,128)(2,1)}, u32[]{:S(2)}, u32[]{:S(2)}) collective-permute-start(bf16[64,1024]{1,0:T(8,128)(2,1)S(1)} %convolution_convert_fusion.5), channel_id=1, source_target_pairs={{0,8},{4,12},{8,0},{12,4},{16,24},{20,28},{24,16},{28,20},{1,9},{5... | collective-permute-start | bytes 393224 | tf_op jit(solution)/shard_map/ppermute | solution.py:181
  100.2 32.5 %collective-permute-start.34 = (bf16[64,1024]{1,0:T(8,128)(2,1)S(1)}, bf16[64,1024]{1,0:T(8,128)(2,1)}, u32[]{:S(2)}, u32[]{:S(2)}) collective-permute-start(bf16[64,1024]{1,0:T(8,128)(2,1)S(1)} %convolution_convert_fusion.3), channel_id=1, source_target_pairs={{0,16},{4,20},{8,24},{12,28},{16,0},{20,4},{24,8},{28,12},{1,17},{... | collective-permute-start | bytes 393224 | tf_op jit(solution)/shard_map/ppermute | solution.py:181
  101.3 11.1 %collective-permute-start.27 = (bf16[64,1024]{1,0:T(8,128)(2,1)S(1)}, bf16[64,1024]{1,0:T(8,128)(2,1)S(1)}, u32[]{:S(2)}, u32[]{:S(2)}) collective-permute-start(bf16[64,1024]{1,0:T(8,128)(2,1)S(1)} %convolution_convert_fusion.9), channel_id=1, source_target_pairs={{0,24},{4,28},{8,16},{12,20},{16,8},{20,12},{24,0},{28,4},{1,25},{... | collective-permute-start | bytes 393224 | tf_op jit(solution)/shard_map/ppermute | solution.py:181
  118.1 56.2 %reduce-scatter.5.cloned.1.call-start = ((), (), s32[]{:S(2)}) async-start(), calls=%async_computation.3 | async-start | bytes 1310720 | tf_op jit(solution)/shard_map/reduce_scatter | solution.py:184
  123.7 13.0 %collective-permute-start.36 = (bf16[64,1024]{1,0:T(8,128)(2,1)S(1)}, bf16[64,1024]{1,0:T(8,128)(2,1)S(1)}, u32[]{:S(2)}, u32[]{:S(2)}) collective-permute-start(bf16[64,1024]{1,0:T(8,128)(2,1)S(1)} %convolution_convert_fusion.1), channel_id=1, source_target_pairs={{0,24},{4,28},{8,16},{12,20},{16,8},{20,12},{24,0},{28,4},{1,25},{... | collective-permute-start | bytes 393224 | tf_op jit(solution)/shard_map/ppermute | solution.py:181
  (28 other events, 208.6 us)
Sparse Core Ops, SparseCore 0:
  118.2 27.8 reduce-scatter.2
  148.5 25.7 reduce-scatter.4

commit v12 on v10

--- a/solution.py
+++ b/solution.py
@@ -132,8 +132,9 @@
             def by_head(x):
                 return x.reshape(seg_rows, heads_here, HEAD_DIM).transpose(1, 0, 2)
 
-            key_blocks = gather_blocks_square(by_head(key_proj))
-            value_blocks = gather_blocks_square(by_head(value_proj))
+            both = gather_blocks_square(jnp.stack([by_head(key_proj), by_head(value_proj)]))
+            key_blocks = [block[0] for block in both]
+            value_blocks = [block[1] for block in both]
             chip = lax.axis_index("hi")
             core = lax.axis_index("lo")
             key_starts = [

time: 168 us -> 176 us (1.048)
  waiting for transfers between devices: 93.8 us -> 109 us
  matrix products: 23.9 us -> 21 us
  starting transfers between devices: 22.6 us -> 19.8 us
  local copies, waits for them, and re-layouts: 8.27 us -> 6.28 us
    ppermute x3 -> x2, waiting for transfers between devices: 13.3 us -> 30 us  [gather_blocks_square(): from_y = lax.ppermute(x, 'hi', swap('hi', 2, 4))]
    ppermute x3 -> x2, waiting for transfers between devices: 3.78 us -> 17.4 us  [gather_blocks_square(): lax.ppermute(from_y[:half], 'hi', swap('hi', 1, 4))]
    ppermute x3 -> x2, waiting for transfers between devices: 11 us -> 0.01 us  [gather_blocks_square(): from_x = lax.ppermute(x, 'hi', swap('hi', 1, 4))]
    ppermute x3 -> x2, waiting for transfers between devices: 6.97 us -> 3.99 us  [gather_blocks_square(): lax.ppermute(from_x[half:], 'hi', swap('hi', 2, 4))]
    dot_general x8, matrix products: 8.56 us -> 6.1 us  [attention_by_head(): jnp.einsum('hqd,hkd->hqk', queries, keys, preferred_element_type=jnp.floa...]
    dot_general x8, matrix products: 10.8 us -> 8.86 us  [per_device(): jnp.dot(block, out_weight, preferred_element_type=jnp.float32)]
    ppermute x3 -> x2, starting transfers between devices: 4.02 us -> 2.33 us  [gather_blocks_square(): lax.ppermute(from_y[:half], 'hi', swap('hi', 1, 4))]
    ppermute x3 -> x2, starting transfers between devices: 3.59 us -> 2.04 us  [gather_blocks_square(): from_x = lax.ppermute(x, 'hi', swap('hi', 1, 4))]
  transfers between devices with their start and end apart: 32 -> 24, of which waited for: 16 -> 10; matrix products, arithmetic and copies ran while one was open for 18% -> 10% of each run, Pallas kernels for 0% -> 0%
where the time goes in v12:
time: 176 us
  waiting for transfers between devices  109 us (62%)
  matrix products  21 us (12%)
  starting transfers between devices  19.8 us (11%)
  between operations  13.9 us (8%)
  local copies, waits for them, and re-layouts  6.28 us (4%)
  other arithmetic  5.89 us (3%)
    reduce_scatter x1, waiting for transfers between devices, per_device(): ordered = lax.psum_scatter(by_row, 'chan', scatter_dimension=1, tiled=True)  44.8 us
    ppermute x2, waiting for transfers between devices, gather_blocks_square(): from_y = lax.ppermute(x, 'hi', swap('hi', 2, 4))  30 us
    ppermute x2, waiting for transfers between devices, gather_blocks_square(): lax.ppermute(from_y[:half], 'hi', swap('hi', 1, 4))  17.4 us
    ppermute x7, waiting for transfers between devices, per_device(): partial = lax.ppermute(partial, SEQ, pairs)  12.7 us
    dot_general x8, matrix products, per_device(): jnp.dot(block, out_weight, preferred_element_type=jnp.float32)  8.86 us
    ppermute x7, starting transfers between devices, per_device(): partial = lax.ppermute(partial, SEQ, pairs)  7.61 us
    dot_general x8, matrix products, attention_by_head(): jnp.einsum('hqd,hkd->hqk', queries, keys, preferred_element_type=jnp.floa...  6.1 us
    dot_general x8, matrix products, attention_by_head(): jnp.einsum('hqk,hkd->hqd', weights.astype(jnp.bfloat16), values, preferre...  6.04 us
  transfers between devices with their start and end apart: 24, of which 10 were waited for; matrix products, arithmetic and copies ran while one was open for 10% of the time, Pallas kernels for 0%

profile of v12, /device:TPU:0, one launch (start us, length us, event | category | flops | bytes accessed | tf_op | source)
XLA Modules:
  0.0 175.7 jit_solution(7275166215013378891)
XLA Ops:
  10.9 3.0 %collective-permute-start.3 = (bf16[2,16,128,128]{3,2,1,0:T(8,128)(2,1)}, bf16[2,16,128,128]{3,2,1,0:T(8,128)(2,1)}, u32[]{:S(2)}, u32[]{:S(2)}) collective-permute-start(bf16[2,16,128,128]{3,2,1,0:T(8,128)(2,1)} %pad_maximum_fusion), channel_id=1, source_target_pairs={{0,16},{8,24},{16,0},{24,8},{1,17},{9,25},{17,1},{25,9},{2,18},{10... | collective-permute-start | bytes 3145736 | tf_op jit(solution)/shard_map/ppermute | solution.py:71
  13.9 1.5 collective-permute-start.1
  16.1 21.2 %collective-permute-done.3 = bf16[2,16,128,128]{3,2,1,0:T(8,128)(2,1)} collective-permute-done((bf16[2,16,128,128]{3,2,1,0:T(8,128)(2,1)}, bf16[2,16,128,128]{3,2,1,0:T(8,128)(2,1)}, u32[]{:S(2)}, u32[]{:S(2)}) %collective-permute-start.3) | collective-permute-done | bytes 1048608 | tf_op jit(solution)/shard_map/ppermute | solution.py:71
  38.4 1.8 %collective-permute-start.5 = (bf16[1,16,128,128]{3,2,1,0:T(8,128)(2,1)S(1)}, bf16[1,16,128,128]{3,2,1,0:T(8,128)(2,1)S(1)}, u32[]{:S(2)}, u32[]{:S(2)}) collective-permute-start(bf16[1,16,128,128]{3,2,1,0:T(8,128)(2,1)S(1)} %slice.61), channel_id=1, source_target_pairs={{0,8},{8,0},{16,24},{24,16},{1,9},{9,1},{17,25},{25,17},{2,10},{10... | collective-permute-start | bytes 1572872 | tf_op jit(solution)/shard_map/ppermute | solution.py:74
  40.3 1.6 collective-permute-start.6
  42.3 1.5 fusion.100
  44.4 7.2 %collective-permute-done.5 = bf16[1,16,128,128]{3,2,1,0:T(8,128)(2,1)S(1)} collective-permute-done((bf16[1,16,128,128]{3,2,1,0:T(8,128)(2,1)S(1)}, bf16[1,16,128,128]{3,2,1,0:T(8,128)(2,1)S(1)}, u32[]{:S(2)}, u32[]{:S(2)}) %collective-permute-start.5) | collective-permute-done | bytes 524320 | tf_op jit(solution)/shard_map/ppermute | solution.py:74
  53.0 1.5 fusion.104
  57.0 2.2 %fusion.24 = (f32[16,128]{1,0:T(8,128)S(1)}, f32[16,128]{1,0:T(8,128)S(1)}, f32[16,128]{1,0:T(8,128)S(1)}, f32[16,128]{1,0:T(8,128)S(1)}, f32[16,128]{1,0:T(8,12...) fusion(f32[16,128,128]{1,2,0:T(8,128)S(1)} %get-tuple-element.36, ...), kind=kLoop, calls=%fused_computation.55 | loop fusion | flops 6275072 | bytes 8593408 | tf_op jit(solution)/shard_map/reduce_sum | solution.py:106
  61.4 1.4 convolution_add_fusion.3
  65.0 1.5 collective-permute-start.14
  67.3 3.5 %fusion.21 = bf16[128,8192]{1,0:T(8,128)(2,1)S(1)} fusion(bf16[128,8192]{1,0:T(8,128)(2,1)S(1)} %broadcast_in_dim.124, s32[]{:T(128)S(6)} %select_n.89, bf16[128,2048]{0,1:T(8,128)(2,1)} %bitcast.31, bf16[2048,1024]{1,0:T(8,128)(2,1)} %param.9), kind=kOutput, calls=%fused_computation.41 | convolution fusion | flops 537001984 | bytes 4980740 | tf_op jit(solution)/shard_map/dot_general | solution.py:174
  70.7 8.8 %collective-permute-done.14 = bf16[128,2048]{0,1:T(8,128)(2,1)S(1)} collective-permute-done((bf16[128,2048]{0,1:T(8,128)(2,1)}, bf16[128,2048]{0,1:T(8,128)(2,1)S(1)}, u32[]{:S(2)}, u32[]{:S(2)}) %collective-permute-start.14) | collective-permute-done | bytes 524320 | tf_op jit(solution)/shard_map/ppermute | solution.py:71
  80.3 1.6 collective-permute-start.15
  83.4 1.5 collective-permute-start.11
  86.5 10.2 %collective-permute-done.18 = bf16[64,2048]{0,1:T(8,128)(2,1)S(1)} collective-permute-done((bf16[64,2048]{0,1:T(8,128)(2,1)S(1)}, bf16[64,2048]{0,1:T(8,128)(2,1)S(1)}, u32[]{:S(2)}, u32[]{:S(2)}) %collective-permute-start.18) | collective-permute-done | bytes 262176 | tf_op jit(solution)/shard_map/ppermute | solution.py:74
  96.7 2.8 %collective-permute-done.19 = bf16[64,2048]{0,1:T(8,128)(2,1)S(1)} collective-permute-done((bf16[64,2048]{0,1:T(8,128)(2,1)S(1)}, bf16[64,2048]{0,1:T(8,128)(2,1)S(1)}, u32[]{:S(2)}, u32[]{:S(2)}) %collective-permute-start.19) | collective-permute-done | bytes 262176 | tf_op jit(solution)/shard_map/ppermute | solution.py:75
  101.1 1.6 collective-permute-start.20
  104.3 1.8 collective-permute-start.13
  107.9 7.2 %collective-permute-done.13 = bf16[128,1024]{1,0:T(8,128)(2,1)S(1)} collective-permute-done((bf16[128,1024]{1,0:T(8,128)(2,1)S(1)}, bf16[128,1024]{1,0:T(8,128)(2,1)S(1)}, u32[]{:S(2)}, u32[]{:S(2)}) %collective-permute-start.13) | collective-permute-done | bytes 262176 | tf_op jit(solution)/shard_map/ppermute | solution.py:179
  115.2 1.7 collective-permute-done.17
  116.9 3.8 %collective-permute-done.22 = bf16[128,1024]{1,0:T(8,128)(2,1)S(1)} collective-permute-done((bf16[128,1024]{1,0:T(8,128)(2,1)S(1)}, bf16[128,1024]{1,0:T(8,128)(2,1)S(1)}, u32[]{:S(2)}, u32[]{:S(2)}) %collective-permute-start.22) | collective-permute-done | bytes 262176 | tf_op jit(solution)/shard_map/ppermute | solution.py:179
  122.1 44.8 %reduce-scatter.2.cloned.1.call-done = bf16[128,2048]{1,0:T(8,128)(2,1)} async-done(((bf16[128,8192]{1,0:T(8,128)(2,1)}), bf16[128,2048]{1,0:T(8,128)(2,1)}) %reduce-scatter.2.cloned.1.call-update) | async-done | bytes 524304 | tf_op jit(solution)/shard_map/reduce_scatter | solution.py:182
  166.8 2.0 %add_convert_fusion = bf16[128,2048]{1,0:T(8,128)(2,1)} fusion(bf16[128,2048]{1,0:T(8,128)(2,1)} %reduce-scatter.2.cloned.1.call-done, bf16[128,2048]{1,0:T(8,128)(2,1)S(1)} %copy-done.3), kind=kLoop, calls=%fused_computation.44 | loop fusion | flops 1048576 | bytes 1572864 | tf_op jit(solution)/shard_map/convert_element_type | solution.py:183
  (84 shorter events, 26.3 us)
Async XLA Ops:
  6.5 160.3 %reduce-scatter.2.cloned.1.call-start = ((), (), s32[]{:S(2)}) async-start(), calls=%async_computation.1 | async-start | bytes 2621440 | tf_op jit(solution)/shard_map/reduce_scatter | solution.py:182
  10.9 26.4 %collective-permute-start.3 = (bf16[2,16,128,128]{3,2,1,0:T(8,128)(2,1)}, bf16[2,16,128,128]{3,2,1,0:T(8,128)(2,1)}, u32[]{:S(2)}, u32[]{:S(2)}) collective-permute-start(bf16[2,16,128,128]{3,2,1,0:T(8,128)(2,1)} %pad_maximum_fusion), channel_id=1, source_target_pairs={{0,16},{8,24},{16,0},{24,8},{1,17},{9,25},{17,1},{25,9},{2,18},{10... | collective-permute-start | bytes 3145736 | tf_op jit(solution)/shard_map/ppermute | solution.py:71
  13.9 26.3 %collective-permute-start.1 = (bf16[2,16,128,128]{3,2,1,0:T(8,128)(2,1)}, bf16[2,16,128,128]{3,2,1,0:T(8,128)(2,1)S(1)}, u32[]{:S(2)}, u32[]{:S(2)}) collective-permute-start(bf16[2,16,128,128]{3,2,1,0:T(8,128)(2,1)} %pad_maximum_fusion), channel_id=1, source_target_pairs={{0,8},{8,0},{16,24},{24,16},{1,9},{9,1},{17,25},{25,17},{2,10},{10... | collective-permute-start | bytes 3145736 | tf_op jit(solution)/shard_map/ppermute | solution.py:70
  15.4 37.7 %collective-permute-start = (bf16[2,16,128,128]{3,2,1,0:T(8,128)(2,1)}, bf16[2,16,128,128]{3,2,1,0:T(8,128)(2,1)}, u32[]{:S(2)}, u32[]{:S(2)}) collective-permute-start(bf16[2,16,128,128]{3,2,1,0:T(8,128)(2,1)} %pad_maximum_fusion), channel_id=1, source_target_pairs={{0,4},{4,0},{1,5},{5,1},{2,6},{6,2},{3,7},{7,3},{8,12},{12,8},{9,1... | collective-permute-start | bytes 3145736 | tf_op jit(solution)/shard_map/ppermute | solution.py:82
  38.4 13.2 %collective-permute-start.5 = (bf16[1,16,128,128]{3,2,1,0:T(8,128)(2,1)S(1)}, bf16[1,16,128,128]{3,2,1,0:T(8,128)(2,1)S(1)}, u32[]{:S(2)}, u32[]{:S(2)}) collective-permute-start(bf16[1,16,128,128]{3,2,1,0:T(8,128)(2,1)S(1)} %slice.61), channel_id=1, source_target_pairs={{0,8},{8,0},{16,24},{24,16},{1,9},{9,1},{17,25},{25,17},{2,10},{10... | collective-permute-start | bytes 1572872 | tf_op jit(solution)/shard_map/ppermute | solution.py:74
  40.3 12.6 %collective-permute-start.6 = (bf16[1,16,128,128]{3,2,1,0:T(8,128)(2,1)S(1)}, bf16[1,16,128,128]{3,2,1,0:T(8,128)(2,1)S(1)}, u32[]{:S(2)}, u32[]{:S(2)}) collective-permute-start(bf16[1,16,128,128]{3,2,1,0:T(8,128)(2,1)S(1)} %slice.63), channel_id=1, source_target_pairs={{0,16},{8,24},{16,0},{24,8},{1,17},{9,25},{17,1},{25,9},{2,18},{10... | collective-permute-start | bytes 1572872 | tf_op jit(solution)/shard_map/ppermute | solution.py:75
  41.8 13.2 %collective-permute-start.4 = (bf16[2,16,128,128]{3,2,1,0:T(8,128)(2,1)}, bf16[2,16,128,128]{3,2,1,0:T(8,128)(2,1)S(1)}, u32[]{:S(2)}, u32[]{:S(2)}) collective-permute-start(bf16[2,16,128,128]{3,2,1,0:T(8,128)(2,1)} %collective-permute-done.3), channel_id=1, source_target_pairs={{0,4},{4,0},{1,5},{5,1},{2,6},{6,2},{3,7},{7,3},{8,12},{12,8},{9,1... | collective-permute-start | bytes 3145736 | tf_op jit(solution)/shard_map/ppermute | solution.py:82
  41.8 13.8 %collective-permute-start.2 = (bf16[2,16,128,128]{3,2,1,0:T(8,128)(2,1)S(1)}, bf16[2,16,128,128]{3,2,1,0:T(8,128)(2,1)S(1)}, u32[]{:S(2)}, u32[]{:S(2)}) collective-permute-start(bf16[2,16,128,128]{3,2,1,0:T(8,128)(2,1)S(1)} %collective-permute-done.1), channel_id=1, source_target_pairs={{0,4},{4,0},{1,5},{5,1},{2,6},{6,2},{3,7},{7,3},{8,12},{12,8},{9,1... | collective-permute-start | bytes 3145736 | tf_op jit(solution)/shard_map/ppermute | solution.py:82
  52.9 3.2 %collective-permute-start.7 = (bf16[2,16,128,128]{3,2,1,0:T(8,128)(2,1)S(1)}, bf16[2,16,128,128]{3,2,1,0:T(8,128)(2,1)S(1)}, u32[]{:S(2)}, u32[]{:S(2)}) collective-permute-start(bf16[2,16,128,128]{3,2,1,0:T(8,128)(2,1)S(1)} %pad_maximum_fusion.1), channel_id=1, source_target_pairs={{0,4},{4,0},{1,5},{5,1},{2,6},{6,2},{3,7},{7,3},{8,12},{12,8},{9,1... | collective-permute-start | bytes 3145736 | tf_op jit(solution)/shard_map/ppermute | solution.py:82
  65.0 14.5 %collective-permute-start.14 = (bf16[128,2048]{0,1:T(8,128)(2,1)}, bf16[128,2048]{0,1:T(8,128)(2,1)S(1)}, u32[]{:S(2)}, u32[]{:S(2)}) collective-permute-start(bf16[128,2048]{0,1:T(8,128)(2,1)} %bitcast.31), channel_id=1, source_target_pairs={{0,16},{8,24},{16,0},{24,8},{1,17},{9,25},{17,1},{25,9},{2,18},{10... | collective-permute-start | bytes 1572872 | tf_op jit(solution)/shard_map/ppermute | solution.py:71
  66.5 15.9 %collective-permute-start.10 = (bf16[128,2048]{0,1:T(8,128)(2,1)}, bf16[128,2048]{0,1:T(8,128)(2,1)S(1)}, u32[]{:S(2)}, u32[]{:S(2)}) collective-permute-start(bf16[128,2048]{0,1:T(8,128)(2,1)} %bitcast.31), channel_id=1, source_target_pairs={{0,8},{8,0},{16,24},{24,16},{1,9},{9,1},{17,25},{25,17},{2,10},{10... | collective-permute-start | bytes 1572872 | tf_op jit(solution)/shard_map/ppermute | solution.py:70
  67.0 18.6 %collective-permute-start.8 = (bf16[128,2048]{0,1:T(8,128)(2,1)}, bf16[128,2048]{0,1:T(8,128)(2,1)S(1)}, u32[]{:S(2)}, u32[]{:S(2)}) collective-permute-start(bf16[128,2048]{0,1:T(8,128)(2,1)} %bitcast.31), channel_id=1, source_target_pairs={{0,4},{4,0},{1,5},{5,1},{2,6},{6,2},{3,7},{7,3},{8,12},{12,8},{9,1... | collective-permute-start | bytes 1572872 | tf_op jit(solution)/shard_map/ppermute | solution.py:82
  80.3 34.9 %collective-permute-start.15 = (bf16[128,1024]{1,0:T(8,128)(2,1)S(1)}, bf16[128,1024]{1,0:T(8,128)(2,1)S(1)}, u32[]{:S(2)}, u32[]{:S(2)}) collective-permute-start(bf16[128,1024]{1,0:T(8,128)(2,1)S(1)} %convolution_convert_fusion.3), channel_id=1, source_target_pairs={{0,16},{4,20},{8,24},{12,28},{16,0},{20,4},{24,8},{28,12},{1,17},{... | collective-permute-start | bytes 786440 | tf_op jit(solution)/shard_map/ppermute | solution.py:179
  81.8 14.9 %collective-permute-start.18 = (bf16[64,2048]{0,1:T(8,128)(2,1)S(1)}, bf16[64,2048]{0,1:T(8,128)(2,1)S(1)}, u32[]{:S(2)}, u32[]{:S(2)}) collective-permute-start(bf16[64,2048]{0,1:T(8,128)(2,1)S(1)} %bitcast.207), channel_id=1, source_target_pairs={{0,8},{8,0},{16,24},{24,16},{1,9},{9,1},{17,25},{25,17},{2,10},{10... | collective-permute-start | bytes 786440 | tf_op jit(solution)/shard_map/ppermute | solution.py:74
  83.4 17.8 %collective-permute-start.11 = (bf16[128,1024]{1,0:T(8,128)(2,1)S(1)}, bf16[128,1024]{1,0:T(8,128)(2,1)S(1)}, u32[]{:S(2)}, u32[]{:S(2)}) collective-permute-start(bf16[128,1024]{1,0:T(8,128)(2,1)S(1)} %convolution_convert_fusion.5), channel_id=1, source_target_pairs={{0,8},{4,12},{8,0},{12,4},{16,24},{20,28},{24,16},{28,20},{1,9},{5... | collective-permute-start | bytes 786440 | tf_op jit(solution)/shard_map/ppermute | solution.py:179
  85.1 14.4 %collective-permute-start.19 = (bf16[64,2048]{0,1:T(8,128)(2,1)S(1)}, bf16[64,2048]{0,1:T(8,128)(2,1)S(1)}, u32[]{:S(2)}, u32[]{:S(2)}) collective-permute-start(bf16[64,2048]{0,1:T(8,128)(2,1)S(1)} %slice.71), channel_id=1, source_target_pairs={{0,16},{8,24},{16,0},{24,8},{1,17},{9,25},{17,1},{25,9},{2,18},{10... | collective-permute-start | bytes 786440 | tf_op jit(solution)/shard_map/ppermute | solution.py:75
  86.4 14.1 %collective-permute-start.9 = (bf16[128,1024]{1,0:T(8,128)(2,1)S(1)}, bf16[128,1024]{1,0:T(8,128)(2,1)S(1)}, u32[]{:S(2)}, u32[]{:S(2)}) collective-permute-start(bf16[128,1024]{1,0:T(8,128)(2,1)S(1)} %convolution_convert_fusion.6), channel_id=1, source_target_pairs={{0,4},{4,0},{8,12},{12,8},{16,20},{20,16},{24,28},{28,24},{1,5},{5... | collective-permute-start | bytes 786440 | tf_op jit(solution)/shard_map/ppermute | solution.py:179
  96.7 6.0 %collective-permute-start.16 = (bf16[128,2048]{0,1:T(8,128)(2,1)S(1)}, bf16[128,2048]{0,1:T(8,128)(2,1)S(1)}, u32[]{:S(2)}, u32[]{:S(2)}) collective-permute-start(bf16[128,2048]{0,1:T(8,128)(2,1)S(1)} %collective-permute-done.14), channel_id=1, source_target_pairs={{0,4},{4,0},{1,5},{5,1},{2,6},{6,2},{3,7},{7,3},{8,12},{12,8},{9,1... | collective-permute-start | bytes 1572872 | tf_op jit(solution)/shard_map/ppermute | solution.py:82
  99.5 4.1 %collective-permute-start.12 = (bf16[128,2048]{0,1:T(8,128)(2,1)S(1)}, bf16[128,2048]{0,1:T(8,128)(2,1)S(1)}, u32[]{:S(2)}, u32[]{:S(2)}) collective-permute-start(bf16[128,2048]{0,1:T(8,128)(2,1)S(1)} %collective-permute-done.10), channel_id=1, source_target_pairs={{0,4},{4,0},{1,5},{5,1},{2,6},{6,2},{3,7},{7,3},{8,12},{12,8},{9,1... | collective-permute-start | bytes 1572872 | tf_op jit(solution)/shard_map/ppermute | solution.py:82
  100.5 5.6 %collective-permute-start.21 = (bf16[128,2048]{0,1:T(8,128)(2,1)S(1)}, bf16[128,2048]{0,1:T(8,128)(2,1)S(1)}, u32[]{:S(2)}, u32[]{:S(2)}) collective-permute-start(bf16[128,2048]{0,1:T(8,128)(2,1)S(1)} %pad_maximum_fusion.2), channel_id=1, source_target_pairs={{0,4},{4,0},{1,5},{5,1},{2,6},{6,2},{3,7},{7,3},{8,12},{12,8},{9,1... | collective-permute-start | bytes 1572872 | tf_op jit(solution)/shard_map/ppermute | solution.py:82
  101.1 15.7 %collective-permute-start.20 = (bf16[128,1024]{1,0:T(8,128)(2,1)S(1)}, bf16[128,1024]{1,0:T(8,128)(2,1)S(1)}, u32[]{:S(2)}, u32[]{:S(2)}) collective-permute-start(bf16[128,1024]{1,0:T(8,128)(2,1)S(1)} %convolution_convert_fusion.1), channel_id=1, source_target_pairs={{0,24},{4,28},{8,16},{12,20},{16,8},{20,12},{24,0},{28,4},{1,25},{... | collective-permute-start | bytes 786440 | tf_op jit(solution)/shard_map/ppermute | solution.py:179
  103.5 13.4 %collective-permute-start.17 = (bf16[128,1024]{1,0:T(8,128)(2,1)S(1)}, bf16[128,1024]{1,0:T(8,128)(2,1)S(1)}, u32[]{:S(2)}, u32[]{:S(2)}) collective-permute-start(bf16[128,1024]{1,0:T(8,128)(2,1)S(1)} %convolution_convert_fusion.2), channel_id=1, source_target_pairs={{0,20},{4,16},{8,28},{12,24},{16,4},{20,0},{24,12},{28,8},{1,21},{... | collective-permute-start | bytes 786440 | tf_op jit(solution)/shard_map/ppermute | solution.py:179
  104.3 10.8 %collective-permute-start.13 = (bf16[128,1024]{1,0:T(8,128)(2,1)S(1)}, bf16[128,1024]{1,0:T(8,128)(2,1)S(1)}, u32[]{:S(2)}, u32[]{:S(2)}) collective-permute-start(bf16[128,1024]{1,0:T(8,128)(2,1)S(1)} %convolution_convert_fusion.4), channel_id=1, source_target_pairs={{0,12},{4,8},{8,4},{12,0},{16,28},{20,24},{24,20},{28,16},{1,13},{... | collective-permute-start | bytes 786440 | tf_op jit(solution)/shard_map/ppermute | solution.py:179
  106.8 13.8 %collective-permute-start.22 = (bf16[128,1024]{1,0:T(8,128)(2,1)S(1)}, bf16[128,1024]{1,0:T(8,128)(2,1)S(1)}, u32[]{:S(2)}, u32[]{:S(2)}) collective-permute-start(bf16[128,1024]{1,0:T(8,128)(2,1)S(1)} %convolution_convert_fusion), channel_id=1, source_target_pairs={{0,28},{4,24},{8,20},{12,16},{16,12},{20,8},{24,4},{28,0},{1,29},{... | collective-permute-start | bytes 786440 | tf_op jit(solution)/shard_map/ppermute | solution.py:179
  (4 other events, 86.0 us)
Sparse Core Ops, SparseCore 0:
  122.2 44.5 reduce-scatter.1

commit v13 on v10

--- a/solution.py
+++ b/solution.py
@@ -85,30 +85,31 @@
 
 def attention_by_head(queries, key_blocks, value_blocks, row_pos, key_starts):
     score_scale = 1.0 / math.sqrt(HEAD_DIM)
-    scores = []
-    masks = []
-    for keys, start in zip(key_blocks, key_starts):
+    row_max = None
+    for keys, values, start in zip(key_blocks, value_blocks, key_starts):
         part = (
             jnp.einsum("hqd,hkd->hqk", queries, keys, preferred_element_type=jnp.float32)
             * score_scale
         )
         key_pos = start + jnp.arange(keys.shape[1], dtype=jnp.int32)
         allowed = (key_pos[None, :] <= row_pos[:, None])[None]
-        scores.append(jnp.where(allowed, part, -1e30))
-        masks.append(allowed)
-    row_max = scores[0].max(axis=-1)
-    for part in scores[1:]:
-        row_max = jnp.maximum(row_max, part.max(axis=-1))
-    row_total = None
-    numer = None
-    for part, allowed, values in zip(scores, masks, value_blocks):
-        weights = jnp.where(allowed, jnp.exp(part - row_max[..., None]), 0.0)
-        total = jnp.sum(weights, axis=-1)
+        part = jnp.where(allowed, part, -1e30)
+        if row_max is None:
+            new_max = jnp.max(part, axis=-1)
+        else:
+            new_max = jnp.maximum(row_max, jnp.max(part, axis=-1))
+        weights = jnp.where(allowed, jnp.exp(part - new_max[..., None]), 0.0)
         term = jnp.einsum(
             "hqk,hkd->hqd", weights.astype(jnp.bfloat16), values, preferred_element_type=jnp.float32
         )
-        row_total = total if row_total is None else row_total + total
-        numer = term if numer is None else numer + term
+        if row_max is None:
+            row_total = jnp.sum(weights, axis=-1)
+            numer = term
+        else:
+            factor = jnp.exp(row_max - new_max)
+            row_total = row_total * factor + jnp.sum(weights, axis=-1)
+            numer = numer * factor[..., None] + term
+        row_max = new_max
     return numer / row_total[..., None]
 
 

time: 168 us -> 169 us (level)
  waiting for transfers between devices: 93.8 us -> 97.5 us
  matrix products: 23.9 us -> 21.7 us
    dot_general x8, matrix products: 8.56 us -> 6.48 us  [attention_by_head(): jnp.einsum('hqd,hkd->hqk', queries, keys, preferred_element_type=jnp.floa...]
    reduce_sum x2 -> x5, other arithmetic: 2.67 us -> 4.17 us  [the longest x4 3.97 us: attention_by_head(): row_total = row_total * factor + jnp.sum(weights, axis=-1)]
  transfers between devices with their start and end apart: 32 -> 32, of which waited for: 16 -> 15; matrix products, arithmetic and copies ran while one was open for 18% -> 17% of each run, Pallas kernels for 0% -> 0%
where the time goes in v13:
time: 169 us
  waiting for transfers between devices  97.5 us (58%)
  starting transfers between devices  22.1 us (13%)
  matrix products  21.7 us (13%)
  between operations  14 us (8%)
  other arithmetic  6.72 us (4%)
  local copies, waits for them, and re-layouts  6.6 us (4%)
    reduce_scatter x1, waiting for transfers between devices, per_device(): ordered = lax.psum_scatter(by_row, 'chan', scatter_dimension=1, tiled=True)  46.3 us
    ppermute x3, waiting for transfers between devices, gather_blocks_square(): from_y = lax.ppermute(x, 'hi', swap('hi', 2, 4))  14 us
    ppermute x7, waiting for transfers between devices, per_device(): partial = lax.ppermute(partial, SEQ, pairs)  12.8 us
    ppermute x3, waiting for transfers between devices, gather_blocks_square(): from_x = lax.ppermute(x, 'hi', swap('hi', 1, 4))  12.1 us
    dot_general x8, matrix products, per_device(): jnp.dot(block, out_weight, preferred_element_type=jnp.float32)  10.6 us
    dot_general x8, matrix products, attention_by_head(): jnp.einsum('hqd,hkd->hqk', queries, keys, preferred_element_type=jnp.floa...  6.48 us
    ppermute x7, starting transfers between devices, per_device(): partial = lax.ppermute(partial, SEQ, pairs)  6.23 us
    ppermute x3, waiting for transfers between devices, gather_blocks_square(): lax.ppermute(from_x[half:], 'hi', swap('hi', 2, 4))  6.19 us
  transfers between devices with their start and end apart: 32, of which 15 were waited for; matrix products, arithmetic and copies ran while one was open for 17% of the time, Pallas kernels for 0%

profile of v13, /device:TPU:0, one launch (start us, length us, event | category | flops | bytes accessed | tf_op | source)
XLA Modules:
  0.0 168.5 jit_solution(6407652867579255159)
XLA Ops:
  8.2 3.0 %collective-permute-start.6 = (bf16[16,128,128]{2,1,0:T(8,128)(2,1)S(1)}, bf16[16,128,128]{2,1,0:T(8,128)(2,1)S(1)}, u32[]{:S(2)}, u32[]{:S(2)}) collective-permute-start(bf16[16,128,128]{2,1,0:T(8,128)(2,1)S(1)} %bitcast.284), channel_id=1, source_target_pairs={{0,16},{8,24},{16,0},{24,8},{1,17},{9,25},{17,1},{25,9},{2,18},{10... | collective-permute-start | bytes 1572872 | tf_op jit(solution)/shard_map/ppermute | solution.py:71
  11.2 1.5 collective-permute-start.2
  16.4 7.6 %collective-permute-done.6 = bf16[16,128,128]{2,1,0:T(8,128)(2,1)S(1)} collective-permute-done((bf16[16,128,128]{2,1,0:T(8,128)(2,1)S(1)}, bf16[16,128,128]{2,1,0:T(8,128)(2,1)S(1)}, u32[]{:S(2)}, u32[]{:S(2)}) %collective-permute-start.6) | collective-permute-done | bytes 524320 | tf_op jit(solution)/shard_map/ppermute | solution.py:71
  24.0 2.2 %collective-permute-done.2 = bf16[16,128,128]{2,1,0:T(8,128)(2,1)} collective-permute-done((bf16[16,128,128]{2,1,0:T(8,128)(2,1)S(1)}, bf16[16,128,128]{2,1,0:T(8,128)(2,1)}, u32[]{:S(2)}, u32[]{:S(2)}) %collective-permute-start.2) | collective-permute-done | bytes 524320 | tf_op jit(solution)/shard_map/ppermute | solution.py:70
  26.2 1.5 collective-permute-start.10
  28.7 5.7 %collective-permute-done.7 = bf16[16,128,128]{1,2,0:T(8,128)(2,1)S(1)} collective-permute-done((bf16[16,128,128]{1,2,0:T(8,128)(2,1)S(1)}, bf16[16,128,128]{1,2,0:T(8,128)(2,1)S(1)}, u32[]{:S(2)}, u32[]{:S(2)}) %collective-permute-start.7) | collective-permute-done | bytes 524320 | tf_op jit(solution)/shard_map/ppermute | solution.py:71
  34.4 1.7 %collective-permute-start.11 = (bf16[8,128,128]{2,1,0:T(8,128)(2,1)S(1)}, bf16[8,128,128]{2,1,0:T(8,128)(2,1)S(1)}, u32[]{:S(2)}, u32[]{:S(2)}) collective-permute-start(bf16[8,128,128]{2,1,0:T(8,128)(2,1)S(1)} %slice.25), channel_id=1, source_target_pairs={{0,16},{8,24},{16,0},{24,8},{1,17},{9,25},{17,1},{25,9},{2,18},{10... | collective-permute-start | bytes 786440 | tf_op jit(solution)/shard_map/ppermute | solution.py:75
  37.3 1.5 collective-permute-start.12
  39.4 1.6 fusion.108
  41.6 1.6 fusion.110
  43.4 3.7 %collective-permute-done.12 = bf16[8,128,128]{1,2,0:T(8,128)(2,1)S(1)} collective-permute-done((bf16[8,128,128]{1,2,0:T(8,128)(2,1)S(1)}, bf16[8,128,128]{1,2,0:T(8,128)(2,1)S(1)}, u32[]{:S(2)}, u32[]{:S(2)}) %collective-permute-start.12) | collective-permute-done | bytes 262176 | tf_op jit(solution)/shard_map/ppermute | solution.py:74
  53.1 1.5 fusion.33
  60.6 1.5 collective-permute-start.18
  62.8 3.2 %fusion.26 = bf16[128,8192]{1,0:T(8,128)(2,1)S(1)} fusion(bf16[128,8192]{1,0:T(8,128)(2,1)S(1)} %broadcast_in_dim.131, s32[]{:T(128)S(6)} %select_n.89, bf16[128,2048]{0,1:T(8,128)(2,1)} %bitcast.32, bf16[2048,1024]{1,0:T(8,128)(2,1)} %param.9), kind=kOutput, calls=%fused_computation.50 | convolution fusion | flops 537001984 | bytes 4980740 | tf_op jit(solution)/shard_map/dot_general | solution.py:174
  66.0 8.7 %collective-permute-done.18 = bf16[128,2048]{0,1:T(8,128)(2,1)S(1)} collective-permute-done((bf16[128,2048]{0,1:T(8,128)(2,1)}, bf16[128,2048]{0,1:T(8,128)(2,1)S(1)}, u32[]{:S(2)}, u32[]{:S(2)}) %collective-permute-start.18) | collective-permute-done | bytes 524320 | tf_op jit(solution)/shard_map/ppermute | solution.py:70
  77.0 1.8 %convolution_convert_fusion.6 = bf16[128,1024]{1,0:T(8,128)(2,1)S(1)} fusion(bf16[128,2048]{0,1:T(8,128)(2,1)} %collective-permute-done.16, bf16[2048,1024]{1,0:T(8,128)(2,1)S(1)} %copy-done.1), kind=kOutput, calls=%fused_computation.48 | convolution fusion | flops 537001984 | bytes 4980736 | tf_op jit(solution)/shard_map/dot_general | solution.py:174
  80.8 1.8 %convolution_convert_fusion.3 = bf16[128,1024]{1,0:T(8,128)(2,1)S(1)} fusion(bf16[128,2048]{0,1:T(8,128)(2,1)} %collective-permute-done.22, bf16[2048,1024]{1,0:T(8,128)(2,1)S(1)} %copy-done.1), kind=kOutput, calls=%fused_computation.45 | convolution fusion | flops 537001984 | bytes 4980736 | tf_op jit(solution)/shard_map/dot_general | solution.py:174
  83.7 6.2 %collective-permute-done.27 = bf16[64,2048]{0,1:T(8,128)(2,1)S(1)} collective-permute-done((bf16[64,2048]{0,1:T(8,128)(2,1)S(1)}, bf16[64,2048]{0,1:T(8,128)(2,1)S(1)}, u32[]{:S(2)}, u32[]{:S(2)}) %collective-permute-start.27) | collective-permute-done | bytes 262176 | tf_op jit(solution)/shard_map/ppermute | solution.py:75
  92.8 1.9 %collective-permute-done.19 = bf16[128,1024]{1,0:T(8,128)(2,1)S(1)} collective-permute-done((bf16[128,1024]{1,0:T(8,128)(2,1)S(1)}, bf16[128,1024]{1,0:T(8,128)(2,1)S(1)}, u32[]{:S(2)}, u32[]{:S(2)}) %collective-permute-start.19) | collective-permute-done | bytes 262176 | tf_op jit(solution)/shard_map/ppermute | solution.py:179
  94.7 2.1 %collective-permute-start.28 = (bf16[128,1024]{1,0:T(8,128)(2,1)S(1)}, bf16[128,1024]{1,0:T(8,128)(2,1)S(1)}, u32[]{:S(2)}, u32[]{:S(2)}) collective-permute-start(bf16[128,1024]{1,0:T(8,128)(2,1)S(1)} %convolution_convert_fusion.1), channel_id=1, source_target_pairs={{0,24},{4,28},{8,16},{12,20},{16,8},{20,12},{24,0},{28,4},{1,25},{... | collective-permute-start | bytes 786440 | tf_op jit(solution)/shard_map/ppermute | solution.py:179
  101.0 7.4 %collective-permute-done.21 = bf16[128,1024]{1,0:T(8,128)(2,1)S(1)} collective-permute-done((bf16[128,1024]{1,0:T(8,128)(2,1)S(1)}, bf16[128,1024]{1,0:T(8,128)(2,1)S(1)}, u32[]{:S(2)}, u32[]{:S(2)}) %collective-permute-start.21) | collective-permute-done | bytes 262176 | tf_op jit(solution)/shard_map/ppermute | solution.py:179
  109.1 2.9 %collective-permute-done.30 = bf16[128,1024]{1,0:T(8,128)(2,1)S(1)} collective-permute-done((bf16[128,1024]{1,0:T(8,128)(2,1)S(1)}, bf16[128,1024]{1,0:T(8,128)(2,1)S(1)}, u32[]{:S(2)}, u32[]{:S(2)}) %collective-permute-start.30) | collective-permute-done | bytes 262176 | tf_op jit(solution)/shard_map/ppermute | solution.py:179
  113.4 46.3 %reduce-scatter.2.cloned.1.call-done = bf16[128,2048]{1,0:T(8,128)(2,1)} async-done(((bf16[128,8192]{1,0:T(8,128)(2,1)}), bf16[128,2048]{1,0:T(8,128)(2,1)}) %reduce-scatter.2.cloned.1.call-update) | async-done | bytes 524304 | tf_op jit(solution)/shard_map/reduce_scatter | solution.py:182
  159.7 2.0 %add_convert_fusion = bf16[128,2048]{1,0:T(8,128)(2,1)} fusion(bf16[128,2048]{1,0:T(8,128)(2,1)} %reduce-scatter.2.cloned.1.call-done, bf16[128,2048]{1,0:T(8,128)(2,1)S(1)} %copy-done.3), kind=kLoop, calls=%fused_computation.51 | loop fusion | flops 1048576 | bytes 1572864 | tf_op jit(solution)/shard_map/convert_element_type | solution.py:183
  (117 shorter events, 35.4 us)
Async XLA Ops:
  6.5 153.2 %reduce-scatter.2.cloned.1.call-start = ((), (), s32[]{:S(2)}) async-start(), calls=%async_computation.1 | async-start | bytes 2621440 | tf_op jit(solution)/shard_map/reduce_scatter | solution.py:182
  8.2 15.8 %collective-permute-start.6 = (bf16[16,128,128]{2,1,0:T(8,128)(2,1)S(1)}, bf16[16,128,128]{2,1,0:T(8,128)(2,1)S(1)}, u32[]{:S(2)}, u32[]{:S(2)}) collective-permute-start(bf16[16,128,128]{2,1,0:T(8,128)(2,1)S(1)} %bitcast.284), channel_id=1, source_target_pairs={{0,16},{8,24},{16,0},{24,8},{1,17},{9,25},{17,1},{25,9},{2,18},{10... | collective-permute-start | bytes 1572872 | tf_op jit(solution)/shard_map/ppermute | solution.py:71
  11.2 15.0 %collective-permute-start.2 = (bf16[16,128,128]{2,1,0:T(8,128)(2,1)S(1)}, bf16[16,128,128]{2,1,0:T(8,128)(2,1)}, u32[]{:S(2)}, u32[]{:S(2)}) collective-permute-start(bf16[16,128,128]{2,1,0:T(8,128)(2,1)S(1)} %bitcast.285), channel_id=1, source_target_pairs={{0,8},{8,0},{16,24},{24,16},{1,9},{9,1},{17,25},{25,17},{2,10},{10... | collective-permute-start | bytes 1572872 | tf_op jit(solution)/shard_map/ppermute | solution.py:70
  12.7 28.3 %collective-permute-start = (bf16[16,128,128]{2,1,0:T(8,128)(2,1)S(1)}, bf16[16,128,128]{2,1,0:T(8,128)(2,1)}, u32[]{:S(2)}, u32[]{:S(2)}) collective-permute-start(bf16[16,128,128]{2,1,0:T(8,128)(2,1)S(1)} %bitcast.286), channel_id=1, source_target_pairs={{0,4},{4,0},{1,5},{5,1},{2,6},{6,2},{3,7},{7,3},{8,12},{12,8},{9,1... | collective-permute-start | bytes 1572872 | tf_op jit(solution)/shard_map/ppermute | solution.py:82
  14.0 23.3 %collective-permute-start.3 = (bf16[16,128,128]{1,2,0:T(8,128)(2,1)S(1)}, bf16[16,128,128]{1,2,0:T(8,128)(2,1)S(1)}, u32[]{:S(2)}, u32[]{:S(2)}) collective-permute-start(bf16[16,128,128]{1,2,0:T(8,128)(2,1)S(1)} %bitcast.280), channel_id=1, source_target_pairs={{0,8},{8,0},{16,24},{24,16},{1,9},{9,1},{17,25},{25,17},{2,10},{10... | collective-permute-start | bytes 1572872 | tf_op jit(solution)/shard_map/ppermute | solution.py:70
  14.6 19.7 %collective-permute-start.7 = (bf16[16,128,128]{1,2,0:T(8,128)(2,1)S(1)}, bf16[16,128,128]{1,2,0:T(8,128)(2,1)S(1)}, u32[]{:S(2)}, u32[]{:S(2)}) collective-permute-start(bf16[16,128,128]{1,2,0:T(8,128)(2,1)S(1)} %bitcast.281), channel_id=1, source_target_pairs={{0,16},{8,24},{16,0},{24,8},{1,17},{9,25},{17,1},{25,9},{2,18},{10... | collective-permute-start | bytes 1572872 | tf_op jit(solution)/shard_map/ppermute | solution.py:71
  24.0 32.1 %collective-permute-start.1 = (bf16[16,128,128]{1,2,0:T(8,128)(2,1)S(1)}, bf16[16,128,128]{1,2,0:T(8,128)(2,1)S(1)}, u32[]{:S(2)}, u32[]{:S(2)}) collective-permute-start(bf16[16,128,128]{1,2,0:T(8,128)(2,1)S(1)} %bitcast.282), channel_id=1, source_target_pairs={{0,4},{4,0},{1,5},{5,1},{2,6},{6,2},{3,7},{7,3},{8,12},{12,8},{9,1... | collective-permute-start | bytes 1572872 | tf_op jit(solution)/shard_map/ppermute | solution.py:82
  26.2 17.1 %collective-permute-start.10 = (bf16[8,128,128]{2,1,0:T(8,128)(2,1)S(1)}, bf16[8,128,128]{2,1,0:T(8,128)(2,1)S(1)}, u32[]{:S(2)}, u32[]{:S(2)}) collective-permute-start(bf16[8,128,128]{2,1,0:T(8,128)(2,1)S(1)} %slice.24), channel_id=1, source_target_pairs={{0,8},{8,0},{16,24},{24,16},{1,9},{9,1},{17,25},{25,17},{2,10},{10... | collective-permute-start | bytes 786440 | tf_op jit(solution)/shard_map/ppermute | solution.py:74
  34.4 12.7 %collective-permute-start.11 = (bf16[8,128,128]{2,1,0:T(8,128)(2,1)S(1)}, bf16[8,128,128]{2,1,0:T(8,128)(2,1)S(1)}, u32[]{:S(2)}, u32[]{:S(2)}) collective-permute-start(bf16[8,128,128]{2,1,0:T(8,128)(2,1)S(1)} %slice.25), channel_id=1, source_target_pairs={{0,16},{8,24},{16,0},{24,8},{1,17},{9,25},{17,1},{25,9},{2,18},{10... | collective-permute-start | bytes 786440 | tf_op jit(solution)/shard_map/ppermute | solution.py:75
  37.3 9.8 %collective-permute-start.12 = (bf16[8,128,128]{1,2,0:T(8,128)(2,1)S(1)}, bf16[8,128,128]{1,2,0:T(8,128)(2,1)S(1)}, u32[]{:S(2)}, u32[]{:S(2)}) collective-permute-start(bf16[8,128,128]{1,2,0:T(8,128)(2,1)S(1)} %slice.26), channel_id=1, source_target_pairs={{0,8},{8,0},{16,24},{24,16},{1,9},{9,1},{17,25},{25,17},{2,10},{10... | collective-permute-start | bytes 786440 | tf_op jit(solution)/shard_map/ppermute | solution.py:74
  47.1 11.4 %collective-permute-start.5 = (bf16[16,128,128]{1,2,0:T(8,128)(2,1)S(1)}, bf16[16,128,128]{1,2,0:T(8,128)(2,1)S(1)}, u32[]{:S(2)}, u32[]{:S(2)}) collective-permute-start(bf16[16,128,128]{1,2,0:T(8,128)(2,1)S(1)} %collective-permute-done.3), channel_id=1, source_target_pairs={{0,4},{4,0},{1,5},{5,1},{2,6},{6,2},{3,7},{7,3},{8,12},{12,8},{9,1... | collective-permute-start | bytes 1572872 | tf_op jit(solution)/shard_map/ppermute | solution.py:82
  48.3 10.8 %collective-permute-start.9 = (bf16[16,128,128]{1,2,0:T(8,128)(2,1)S(1)}, bf16[16,128,128]{1,2,0:T(8,128)(2,1)S(1)}, u32[]{:S(2)}, u32[]{:S(2)}) collective-permute-start(bf16[16,128,128]{1,2,0:T(8,128)(2,1)S(1)} %collective-permute-done.7), channel_id=1, source_target_pairs={{0,4},{4,0},{1,5},{5,1},{2,6},{6,2},{3,7},{7,3},{8,12},{12,8},{9,1... | collective-permute-start | bytes 1572872 | tf_op jit(solution)/shard_map/ppermute | solution.py:82
  60.6 14.2 %collective-permute-start.18 = (bf16[128,2048]{0,1:T(8,128)(2,1)}, bf16[128,2048]{0,1:T(8,128)(2,1)S(1)}, u32[]{:S(2)}, u32[]{:S(2)}) collective-permute-start(bf16[128,2048]{0,1:T(8,128)(2,1)} %bitcast.32), channel_id=1, source_target_pairs={{0,8},{8,0},{16,24},{24,16},{1,9},{9,1},{17,25},{25,17},{2,10},{10... | collective-permute-start | bytes 1572872 | tf_op jit(solution)/shard_map/ppermute | solution.py:70
  62.0 14.0 %collective-permute-start.22 = (bf16[128,2048]{0,1:T(8,128)(2,1)}, bf16[128,2048]{0,1:T(8,128)(2,1)}, u32[]{:S(2)}, u32[]{:S(2)}) collective-permute-start(bf16[128,2048]{0,1:T(8,128)(2,1)} %bitcast.32), channel_id=1, source_target_pairs={{0,16},{8,24},{16,0},{24,8},{1,17},{9,25},{17,1},{25,9},{2,18},{10... | collective-permute-start | bytes 1572872 | tf_op jit(solution)/shard_map/ppermute | solution.py:71
  62.5 14.5 %collective-permute-start.16 = (bf16[128,2048]{0,1:T(8,128)(2,1)}, bf16[128,2048]{0,1:T(8,128)(2,1)}, u32[]{:S(2)}, u32[]{:S(2)}) collective-permute-start(bf16[128,2048]{0,1:T(8,128)(2,1)} %bitcast.32), channel_id=1, source_target_pairs={{0,4},{4,0},{1,5},{5,1},{2,6},{6,2},{3,7},{7,3},{8,12},{12,8},{9,1... | collective-permute-start | bytes 1572872 | tf_op jit(solution)/shard_map/ppermute | solution.py:82
  74.9 14.9 %collective-permute-start.27 = (bf16[64,2048]{0,1:T(8,128)(2,1)S(1)}, bf16[64,2048]{0,1:T(8,128)(2,1)S(1)}, u32[]{:S(2)}, u32[]{:S(2)}) collective-permute-start(bf16[64,2048]{0,1:T(8,128)(2,1)S(1)} %slice.29), channel_id=1, source_target_pairs={{0,16},{8,24},{16,0},{24,8},{1,17},{9,25},{17,1},{25,9},{2,18},{10... | collective-permute-start | bytes 786440 | tf_op jit(solution)/shard_map/ppermute | solution.py:75
  76.0 15.1 %collective-permute-start.26 = (bf16[64,2048]{0,1:T(8,128)(2,1)}, bf16[64,2048]{0,1:T(8,128)(2,1)S(1)}, u32[]{:S(2)}, u32[]{:S(2)}) collective-permute-start(bf16[64,2048]{0,1:T(8,128)(2,1)} %bitcast.278), channel_id=1, source_target_pairs={{0,8},{8,0},{16,24},{24,16},{1,9},{9,1},{17,25},{25,17},{2,10},{10... | collective-permute-start | bytes 786440 | tf_op jit(solution)/shard_map/ppermute | solution.py:74
  78.8 13.3 %collective-permute-start.17 = (bf16[128,1024]{1,0:T(8,128)(2,1)S(1)}, bf16[128,1024]{1,0:T(8,128)(2,1)S(1)}, u32[]{:S(2)}, u32[]{:S(2)}) collective-permute-start(bf16[128,1024]{1,0:T(8,128)(2,1)S(1)} %convolution_convert_fusion.6), channel_id=1, source_target_pairs={{0,4},{4,0},{8,12},{12,8},{16,20},{20,16},{24,28},{28,24},{1,5},{5... | collective-permute-start | bytes 786440 | tf_op jit(solution)/shard_map/ppermute | solution.py:179
  79.7 15.0 %collective-permute-start.19 = (bf16[128,1024]{1,0:T(8,128)(2,1)S(1)}, bf16[128,1024]{1,0:T(8,128)(2,1)S(1)}, u32[]{:S(2)}, u32[]{:S(2)}) collective-permute-start(bf16[128,1024]{1,0:T(8,128)(2,1)S(1)} %convolution_convert_fusion.5), channel_id=1, source_target_pairs={{0,8},{4,12},{8,0},{12,4},{16,24},{20,28},{24,16},{28,20},{1,9},{5... | collective-permute-start | bytes 786440 | tf_op jit(solution)/shard_map/ppermute | solution.py:179
  82.6 25.8 %collective-permute-start.23 = (bf16[128,1024]{1,0:T(8,128)(2,1)S(1)}, bf16[128,1024]{1,0:T(8,128)(2,1)S(1)}, u32[]{:S(2)}, u32[]{:S(2)}) collective-permute-start(bf16[128,1024]{1,0:T(8,128)(2,1)S(1)} %convolution_convert_fusion.3), channel_id=1, source_target_pairs={{0,16},{4,20},{8,24},{12,28},{16,0},{20,4},{24,8},{28,12},{1,17},{... | collective-permute-start | bytes 786440 | tf_op jit(solution)/shard_map/ppermute | solution.py:179
  94.7 14.3 %collective-permute-start.28 = (bf16[128,1024]{1,0:T(8,128)(2,1)S(1)}, bf16[128,1024]{1,0:T(8,128)(2,1)S(1)}, u32[]{:S(2)}, u32[]{:S(2)}) collective-permute-start(bf16[128,1024]{1,0:T(8,128)(2,1)S(1)} %convolution_convert_fusion.1), channel_id=1, source_target_pairs={{0,24},{4,28},{8,16},{12,20},{16,8},{20,12},{24,0},{28,4},{1,25},{... | collective-permute-start | bytes 786440 | tf_op jit(solution)/shard_map/ppermute | solution.py:179
  97.6 10.9 %collective-permute-start.21 = (bf16[128,1024]{1,0:T(8,128)(2,1)S(1)}, bf16[128,1024]{1,0:T(8,128)(2,1)S(1)}, u32[]{:S(2)}, u32[]{:S(2)}) collective-permute-start(bf16[128,1024]{1,0:T(8,128)(2,1)S(1)} %convolution_convert_fusion.4), channel_id=1, source_target_pairs={{0,12},{4,8},{8,4},{12,0},{16,28},{20,24},{24,20},{28,16},{1,13},{... | collective-permute-start | bytes 786440 | tf_op jit(solution)/shard_map/ppermute | solution.py:179
  98.4 10.6 %collective-permute-start.25 = (bf16[128,1024]{1,0:T(8,128)(2,1)S(1)}, bf16[128,1024]{1,0:T(8,128)(2,1)S(1)}, u32[]{:S(2)}, u32[]{:S(2)}) collective-permute-start(bf16[128,1024]{1,0:T(8,128)(2,1)S(1)} %convolution_convert_fusion.2), channel_id=1, source_target_pairs={{0,20},{4,16},{8,28},{12,24},{16,4},{20,0},{24,12},{28,8},{1,21},{... | collective-permute-start | bytes 786440 | tf_op jit(solution)/shard_map/ppermute | solution.py:179
  100.3 11.7 %collective-permute-start.30 = (bf16[128,1024]{1,0:T(8,128)(2,1)S(1)}, bf16[128,1024]{1,0:T(8,128)(2,1)S(1)}, u32[]{:S(2)}, u32[]{:S(2)}) collective-permute-start(bf16[128,1024]{1,0:T(8,128)(2,1)S(1)} %convolution_convert_fusion), channel_id=1, source_target_pairs={{0,28},{4,24},{8,20},{12,16},{16,12},{20,8},{24,4},{28,0},{1,29},{... | collective-permute-start | bytes 786440 | tf_op jit(solution)/shard_map/ppermute | solution.py:179
  (12 other events, 133.4 us)
Sparse Core Ops, SparseCore 0:
  113.5 46.1 reduce-scatter.1

commit v14 on v10

--- a/solution.py
+++ b/solution.py
@@ -132,14 +132,21 @@
             def by_head(x):
                 return x.reshape(seg_rows, heads_here, HEAD_DIM).transpose(1, 0, 2)
 
-            key_blocks = gather_blocks_square(by_head(key_proj))
-            value_blocks = gather_blocks_square(by_head(value_proj))
             chip = lax.axis_index("hi")
             core = lax.axis_index("lo")
-            key_starts = [
-                ((chip ^ (b // 2)) * 2 + (core ^ (b % 2))) * seg_rows for b in range(len(key_blocks))
-            ]
-            ratio = attention_by_head(by_head(query_proj), key_blocks, value_blocks, row_pos, key_starts)
+            key_starts = [((chip ^ (b // 2)) * 2 + (core ^ (b % 2))) * seg_rows for b in range(8)]
+            queries, keys, values = by_head(query_proj), by_head(key_proj), by_head(value_proj)
+            split = heads_here // 2
+            parts = []
+            for lo_head, hi_head in ((0, split), (split, heads_here)):
+                key_blocks = gather_blocks_square(keys[lo_head:hi_head])
+                value_blocks = gather_blocks_square(values[lo_head:hi_head])
+                parts.append(
+                    attention_by_head(
+                        queries[lo_head:hi_head], key_blocks, value_blocks, row_pos, key_starts
+                    )
+                )
+            ratio = jnp.concatenate(parts, axis=0)
         else:
             both = gather_seq(jnp.concatenate([key_proj, value_proj], axis=1))
             total_rows = both.shape[0]

time: 168 us -> 180 us (1.071)
  starting transfers between devices: 22.6 us -> 33.5 us
  waiting for transfers between devices: 93.8 us -> 87.2 us
  matrix products: 23.9 us -> 28.1 us
  local copies, waits for them, and re-layouts: 8.27 us -> 11 us
    ppermute x3 -> x5, waiting for transfers between devices: 13.3 us -> 3.62 us  [gather_blocks_square(): from_y = lax.ppermute(x, 'hi', swap('hi', 2, 4))]
    dot_general x8 -> x16, matrix products: 8.56 us -> 12.1 us  [attention_by_head(): jnp.einsum('hqd,hkd->hqk', queries, keys, preferred_element_type=jnp.floa...]
    ppermute x3 -> x5, starting transfers between devices: 3.52 us -> 6.71 us  [gather_blocks_square(): from_y = lax.ppermute(x, 'hi', swap('hi', 2, 4))]
    ppermute x12 -> x20, starting transfers between devices: 1.88 us -> 4.59 us  [gather_blocks_square(): blocks.append(lax.ppermute(block, 'lo', [(0, 1), (1, 0)]))]
    ppermute x3 -> x5, starting transfers between devices: 2.89 us -> 5.59 us  [gather_blocks_square(): lax.ppermute(from_x[half:], 'hi', swap('hi', 2, 4))]
    ppermute x3 -> x5, waiting for transfers between devices: 3.78 us -> 6.3 us  [gather_blocks_square(): lax.ppermute(from_y[:half], 'hi', swap('hi', 1, 4))]
    ppermute x3 -> x5, waiting for transfers between devices: 11 us -> 9.05 us  [gather_blocks_square(): from_x = lax.ppermute(x, 'hi', swap('hi', 1, 4))]
    ppermute x3 -> x5, starting transfers between devices: 4.02 us -> 5.65 us  [gather_blocks_square(): lax.ppermute(from_y[:half], 'hi', swap('hi', 1, 4))]
  transfers between devices with their start and end apart: 32 -> 48, of which waited for: 16 -> 17; matrix products, arithmetic and copies ran while one was open for 18% -> 21% of each run, Pallas kernels for 0% -> 0%
where the time goes in v14:
time: 180 us
  waiting for transfers between devices  87.2 us (48%)
  starting transfers between devices  33.5 us (19%)
  matrix products  28.1 us (16%)
  between operations  14.3 us (8%)
  local copies, waits for them, and re-layouts  11 us (6%)
  other arithmetic  5.41 us (3%)
    reduce_scatter x1, waiting for transfers between devices, per_device(): ordered = lax.psum_scatter(by_row, 'chan', scatter_dimension=1, tiled=True)  44.7 us
    ppermute x7, waiting for transfers between devices, per_device(): partial = lax.ppermute(partial, SEQ, pairs)  13.9 us
    dot_general x16, matrix products, attention_by_head(): jnp.einsum('hqd,hkd->hqk', queries, keys, preferred_element_type=jnp.floa...  12.1 us
    dot_general x8, matrix products, per_device(): jnp.dot(block, out_weight, preferred_element_type=jnp.float32)  10.4 us
    ppermute x5, waiting for transfers between devices, gather_blocks_square(): from_x = lax.ppermute(x, 'hi', swap('hi', 1, 4))  9.05 us
    ppermute x5, waiting for transfers between devices, gather_blocks_square(): lax.ppermute(from_x[half:], 'hi', swap('hi', 2, 4))  7.94 us
    ppermute x5, starting transfers between devices, gather_blocks_square(): from_y = lax.ppermute(x, 'hi', swap('hi', 2, 4))  6.71 us
    ppermute x7, starting transfers between devices, per_device(): partial = lax.ppermute(partial, SEQ, pairs)  6.54 us
  transfers between devices with their start and end apart: 48, of which 17 were waited for; matrix products, arithmetic and copies ran while one was open for 21% of the time, Pallas kernels for 0%

profile of v14, /device:TPU:0, one launch (start us, length us, event | category | flops | bytes accessed | tf_op | source)
XLA Modules:
  0.0 179.5 jit_solution(15001045145487015027)
XLA Ops:
  8.9 3.0 %collective-permute-start.3 = (bf16[8,128,128]{2,1,0:T(8,128)(2,1)}, bf16[8,128,128]{2,1,0:T(8,128)(2,1)}, u32[]{:S(2)}, u32[]{:S(2)}) collective-permute-start(bf16[8,128,128]{2,1,0:T(8,128)(2,1)} %get-tuple-element.30), channel_id=1, source_target_pairs={{0,16},{8,24},{16,0},{24,8},{1,17},{9,25},{17,1},{25,9},{2,18},{10... | collective-permute-start | bytes 786440 | tf_op jit(solution)/shard_map/ppermute | solution.py:71
  11.9 1.5 collective-permute-start.1
  20.7 3.4 %collective-permute-done.19 = bf16[8,128,128]{2,1,0:T(8,128)(2,1)} collective-permute-done((bf16[8,128,128]{2,1,0:T(8,128)(2,1)S(1)}, bf16[8,128,128]{2,1,0:T(8,128)(2,1)}, u32[]{:S(2)}, u32[]{:S(2)}) %collective-permute-start.19) | collective-permute-done | bytes 262176 | tf_op jit(solution)/shard_map/ppermute | solution.py:71
  24.1 1.7 collective-permute-start.9
  27.2 1.6 collective-permute-start.11
  35.6 1.8 collective-permute-start.21
  37.4 1.5 collective-permute-start.22
  43.4 1.6 collective-permute-start.13
  45.3 3.0 %collective-permute-done.5 = bf16[4,128,128]{2,1,0:T(8,128)(2,1)S(1)} collective-permute-done((bf16[4,128,128]{2,1,0:T(8,128)(2,1)S(1)}, bf16[4,128,128]{2,1,0:T(8,128)(2,1)S(1)}, u32[]{:S(2)}, u32[]{:S(2)}) %collective-permute-start.5) | collective-permute-done | bytes 131104 | tf_op jit(solution)/shard_map/ppermute | solution.py:74
  50.2 1.7 collective-permute-start.30
  51.9 2.2 %collective-permute-done.29 = bf16[4,128,128]{1,2,0:T(8,128)(2,1)S(1)} collective-permute-done((bf16[4,128,128]{1,2,0:T(8,128)(2,1)S(1)}, bf16[4,128,128]{1,2,0:T(8,128)(2,1)S(1)}, u32[]{:S(2)}, u32[]{:S(2)}) %collective-permute-start.29) | collective-permute-done | bytes 131104 | tf_op jit(solution)/shard_map/ppermute | solution.py:74
  54.7 1.4 collective-permute-done.30
  62.3 2.0 %fusion.41 = (f32[8,128]{1,0:T(8,128)S(1)}, f32[8,128]{1,0:T(8,128)S(1)}, f32[8,128]{1,0:T(8,128)S(1)}, f32[8,128]{1,0:T(8,128)S(1)}, f32[8,128]{1,0:T(8,128)S(1...) fusion(f32[8,128,128]{2,1,0:T(8,128)S(1)} %get-tuple-element.61, ...), kind=kLoop, calls=%fused_computation.92 | loop fusion | flops 4314112 | bytes 5918720 | tf_op jit(solution)/shard_map/reduce_sum | solution.py:106
  74.2 3.1 %fusion.30 = bf16[128,8192]{1,0:T(8,128)(2,1)S(1)} fusion(bf16[128,8192]{1,0:T(8,128)(2,1)S(1)} %broadcast_in_dim.221, s32[]{:T(128)S(6)} %select_n.153, bf16[128,2048]{0,1:T(8,128)(2,1)S(1)} %bitcast.125, bf16[2048,1024]{1,0:T(8,128)(2,1)} %param.9), kind=kOutput, calls=%fused_computation.62 | convolution fusion | flops 537001984 | bytes 4980740 | tf_op jit(solution)/shard_map/dot_general | solution.py:180
  77.3 9.0 %collective-permute-done.34 = bf16[128,2048]{0,1:T(8,128)(2,1)S(1)} collective-permute-done((bf16[128,2048]{0,1:T(8,128)(2,1)S(1)}, bf16[128,2048]{0,1:T(8,128)(2,1)S(1)}, u32[]{:S(2)}, u32[]{:S(2)}) %collective-permute-start.34) | collective-permute-done | bytes 524320 | tf_op jit(solution)/shard_map/ppermute | solution.py:70
  88.5 1.8 %convolution_convert_fusion.6 = bf16[128,1024]{1,0:T(8,128)(2,1)S(1)} fusion(bf16[128,2048]{0,1:T(8,128)(2,1)} %collective-permute-done.32, bf16[2048,1024]{1,0:T(8,128)(2,1)S(1)} %copy-done), kind=kOutput, calls=%fused_computation.60 | convolution fusion | flops 537001984 | bytes 4980736 | tf_op jit(solution)/shard_map/dot_general | solution.py:180
  92.1 1.8 %convolution_convert_fusion.3 = bf16[128,1024]{1,0:T(8,128)(2,1)S(1)} fusion(bf16[128,2048]{0,1:T(8,128)(2,1)} %collective-permute-done.38, bf16[2048,1024]{1,0:T(8,128)(2,1)S(1)} %copy-done), kind=kOutput, calls=%fused_computation.57 | convolution fusion | flops 537001984 | bytes 4980736 | tf_op jit(solution)/shard_map/dot_general | solution.py:180
  95.3 6.2 %collective-permute-done.43 = bf16[64,2048]{0,1:T(8,128)(2,1)S(1)} collective-permute-done((bf16[64,2048]{0,1:T(8,128)(2,1)S(1)}, bf16[64,2048]{0,1:T(8,128)(2,1)S(1)}, u32[]{:S(2)}, u32[]{:S(2)}) %collective-permute-start.43) | collective-permute-done | bytes 262176 | tf_op jit(solution)/shard_map/ppermute | solution.py:75
  104.1 2.3 %collective-permute-done.35 = bf16[128,1024]{1,0:T(8,128)(2,1)S(1)} collective-permute-done((bf16[128,1024]{1,0:T(8,128)(2,1)S(1)}, bf16[128,1024]{1,0:T(8,128)(2,1)S(1)}, u32[]{:S(2)}, u32[]{:S(2)}) %collective-permute-start.35) | collective-permute-done | bytes 262176 | tf_op jit(solution)/shard_map/ppermute | solution.py:185
  109.3 2.0 %collective-permute-start.41 = (bf16[128,1024]{1,0:T(8,128)(2,1)S(1)}, bf16[128,1024]{1,0:T(8,128)(2,1)S(1)}, u32[]{:S(2)}, u32[]{:S(2)}) collective-permute-start(bf16[128,1024]{1,0:T(8,128)(2,1)S(1)} %convolution_convert_fusion.2), channel_id=1, source_target_pairs={{0,20},{4,16},{8,28},{12,24},{16,4},{20,0},{24,12},{28,8},{1,21},{... | collective-permute-start | bytes 786440 | tf_op jit(solution)/shard_map/ppermute | solution.py:185
  112.9 5.9 %collective-permute-done.37 = bf16[128,1024]{1,0:T(8,128)(2,1)S(1)} collective-permute-done((bf16[128,1024]{1,0:T(8,128)(2,1)S(1)}, bf16[128,1024]{1,0:T(8,128)(2,1)S(1)}, u32[]{:S(2)}, u32[]{:S(2)}) %collective-permute-start.37) | collective-permute-done | bytes 262176 | tf_op jit(solution)/shard_map/ppermute | solution.py:185
  118.8 5.6 %collective-permute-done.41 = bf16[128,1024]{1,0:T(8,128)(2,1)S(1)} collective-permute-done((bf16[128,1024]{1,0:T(8,128)(2,1)S(1)}, bf16[128,1024]{1,0:T(8,128)(2,1)S(1)}, u32[]{:S(2)}, u32[]{:S(2)}) %collective-permute-start.41) | collective-permute-done | bytes 262176 | tf_op jit(solution)/shard_map/ppermute | solution.py:185
  126.0 44.7 %reduce-scatter.2.cloned.1.call-done = bf16[128,2048]{1,0:T(8,128)(2,1)} async-done(((bf16[128,8192]{1,0:T(8,128)(2,1)}), bf16[128,2048]{1,0:T(8,128)(2,1)}) %reduce-scatter.2.cloned.1.call-update) | async-done | bytes 524304 | tf_op jit(solution)/shard_map/reduce_scatter | solution.py:188
  170.7 2.0 %add_convert_fusion = bf16[128,2048]{1,0:T(8,128)(2,1)} fusion(bf16[128,2048]{1,0:T(8,128)(2,1)} %reduce-scatter.2.cloned.1.call-done, bf16[128,2048]{1,0:T(8,128)(2,1)S(1)} %copy-done.2), kind=kLoop, calls=%fused_computation.63 | loop fusion | flops 1048576 | bytes 1572864 | tf_op jit(solution)/shard_map/convert_element_type | solution.py:189
  (181 shorter events, 54.5 us)
Async XLA Ops:
  6.5 164.2 %reduce-scatter.2.cloned.1.call-start = ((), (), s32[]{:S(2)}) async-start(), calls=%async_computation.1 | async-start | bytes 2621440 | tf_op jit(solution)/shard_map/reduce_scatter | solution.py:188
  8.9 10.4 %collective-permute-start.3 = (bf16[8,128,128]{2,1,0:T(8,128)(2,1)}, bf16[8,128,128]{2,1,0:T(8,128)(2,1)}, u32[]{:S(2)}, u32[]{:S(2)}) collective-permute-start(bf16[8,128,128]{2,1,0:T(8,128)(2,1)} %get-tuple-element.30), channel_id=1, source_target_pairs={{0,16},{8,24},{16,0},{24,8},{1,17},{9,25},{17,1},{25,9},{2,18},{10... | collective-permute-start | bytes 786440 | tf_op jit(solution)/shard_map/ppermute | solution.py:71
  11.9 15.3 %collective-permute-start.1 = (bf16[8,128,128]{2,1,0:T(8,128)(2,1)}, bf16[8,128,128]{2,1,0:T(8,128)(2,1)}, u32[]{:S(2)}, u32[]{:S(2)}) collective-permute-start(bf16[8,128,128]{2,1,0:T(8,128)(2,1)} %get-tuple-element.30), channel_id=1, source_target_pairs={{0,8},{8,0},{16,24},{24,16},{1,9},{9,1},{17,25},{25,17},{2,10},{10... | collective-permute-start | bytes 786440 | tf_op jit(solution)/shard_map/ppermute | solution.py:70
  13.4 18.7 %collective-permute-start = (bf16[8,128,128]{2,1,0:T(8,128)(2,1)}, bf16[8,128,128]{2,1,0:T(8,128)(2,1)}, u32[]{:S(2)}, u32[]{:S(2)}) collective-permute-start(bf16[8,128,128]{2,1,0:T(8,128)(2,1)} %get-tuple-element.30), channel_id=1, source_target_pairs={{0,4},{4,0},{1,5},{5,1},{2,6},{6,2},{3,7},{7,3},{8,12},{12,8},{9,1... | collective-permute-start | bytes 786440 | tf_op jit(solution)/shard_map/ppermute | solution.py:82
  13.4 10.7 %collective-permute-start.19 = (bf16[8,128,128]{2,1,0:T(8,128)(2,1)S(1)}, bf16[8,128,128]{2,1,0:T(8,128)(2,1)}, u32[]{:S(2)}, u32[]{:S(2)}) collective-permute-start(bf16[8,128,128]{2,1,0:T(8,128)(2,1)S(1)} %get-tuple-element.31), channel_id=1, source_target_pairs={{0,16},{8,24},{16,0},{24,8},{1,17},{9,25},{17,1},{25,9},{2,18},{10... | collective-permute-start | bytes 786440 | tf_op jit(solution)/shard_map/ppermute | solution.py:71
  13.9 16.3 %collective-permute-start.17 = (bf16[8,128,128]{2,1,0:T(8,128)(2,1)S(1)}, bf16[8,128,128]{2,1,0:T(8,128)(2,1)}, u32[]{:S(2)}, u32[]{:S(2)}) collective-permute-start(bf16[8,128,128]{2,1,0:T(8,128)(2,1)S(1)} %get-tuple-element.31), channel_id=1, source_target_pairs={{0,8},{8,0},{16,24},{24,16},{1,9},{9,1},{17,25},{25,17},{2,10},{10... | collective-permute-start | bytes 786440 | tf_op jit(solution)/shard_map/ppermute | solution.py:70
  19.3 16.3 %collective-permute-start.16 = (bf16[8,128,128]{2,1,0:T(8,128)(2,1)S(1)}, bf16[8,128,128]{2,1,0:T(8,128)(2,1)S(1)}, u32[]{:S(2)}, u32[]{:S(2)}) collective-permute-start(bf16[8,128,128]{2,1,0:T(8,128)(2,1)S(1)} %get-tuple-element.31), channel_id=1, source_target_pairs={{0,4},{4,0},{1,5},{5,1},{2,6},{6,2},{3,7},{7,3},{8,12},{12,8},{9,1... | collective-permute-start | bytes 786440 | tf_op jit(solution)/shard_map/ppermute | solution.py:82
  24.1 17.1 %collective-permute-start.9 = (bf16[8,128,128]{1,2,0:T(8,128)(2,1)S(1)}, bf16[8,128,128]{1,2,0:T(8,128)(2,1)S(1)}, u32[]{:S(2)}, u32[]{:S(2)}) collective-permute-start(bf16[8,128,128]{1,2,0:T(8,128)(2,1)S(1)} %get-tuple-element.28), channel_id=1, source_target_pairs={{0,8},{8,0},{16,24},{24,16},{1,9},{9,1},{17,25},{25,17},{2,10},{10... | collective-permute-start | bytes 786440 | tf_op jit(solution)/shard_map/ppermute | solution.py:70
  30.1 11.8 %collective-permute-start.25 = (bf16[8,128,128]{1,2,0:T(8,128)(2,1)S(1)}, bf16[8,128,128]{1,2,0:T(8,128)(2,1)S(1)}, u32[]{:S(2)}, u32[]{:S(2)}) collective-permute-start(bf16[8,128,128]{1,2,0:T(8,128)(2,1)S(1)} %get-tuple-element.29), channel_id=1, source_target_pairs={{0,8},{8,0},{16,24},{24,16},{1,9},{9,1},{17,25},{25,17},{2,10},{10... | collective-permute-start | bytes 786440 | tf_op jit(solution)/shard_map/ppermute | solution.py:70
  41.2 23.3 %collective-permute-start.8 = (bf16[8,128,128]{1,2,0:T(8,128)(2,1)S(1)}, bf16[8,128,128]{1,2,0:T(8,128)(2,1)S(1)}, u32[]{:S(2)}, u32[]{:S(2)}) collective-permute-start(bf16[8,128,128]{1,2,0:T(8,128)(2,1)S(1)} %get-tuple-element.28), channel_id=1, source_target_pairs={{0,4},{4,0},{1,5},{5,1},{2,6},{6,2},{3,7},{7,3},{8,12},{12,8},{9,1... | collective-permute-start | bytes 786440 | tf_op jit(solution)/shard_map/ppermute | solution.py:82
  41.3 24.9 %collective-permute-start.24 = (bf16[8,128,128]{1,2,0:T(8,128)(2,1)S(1)}, bf16[8,128,128]{1,2,0:T(8,128)(2,1)S(1)}, u32[]{:S(2)}, u32[]{:S(2)}) collective-permute-start(bf16[8,128,128]{1,2,0:T(8,128)(2,1)S(1)} %get-tuple-element.29), channel_id=1, source_target_pairs={{0,4},{4,0},{1,5},{5,1},{2,6},{6,2},{3,7},{7,3},{8,12},{12,8},{9,1... | collective-permute-start | bytes 786440 | tf_op jit(solution)/shard_map/ppermute | solution.py:82
  57.9 10.4 %collective-permute-start.10 = (bf16[8,128,128]{1,2,0:T(8,128)(2,1)S(1)}, bf16[8,128,128]{1,2,0:T(8,128)(2,1)S(1)}, u32[]{:S(2)}, u32[]{:S(2)}) collective-permute-start(bf16[8,128,128]{1,2,0:T(8,128)(2,1)S(1)} %collective-permute-done.9), channel_id=1, source_target_pairs={{0,4},{4,0},{1,5},{5,1},{2,6},{6,2},{3,7},{7,3},{8,12},{12,8},{9,1... | collective-permute-start | bytes 786440 | tf_op jit(solution)/shard_map/ppermute | solution.py:82
  59.3 11.5 %collective-permute-start.12 = (bf16[8,128,128]{1,2,0:T(8,128)(2,1)S(1)}, bf16[8,128,128]{1,2,0:T(8,128)(2,1)S(1)}, u32[]{:S(2)}, u32[]{:S(2)}) collective-permute-start(bf16[8,128,128]{1,2,0:T(8,128)(2,1)S(1)} %collective-permute-done.11), channel_id=1, source_target_pairs={{0,4},{4,0},{1,5},{5,1},{2,6},{6,2},{3,7},{7,3},{8,12},{12,8},{9,1... | collective-permute-start | bytes 786440 | tf_op jit(solution)/shard_map/ppermute | solution.py:82
  72.1 14.3 %collective-permute-start.34 = (bf16[128,2048]{0,1:T(8,128)(2,1)S(1)}, bf16[128,2048]{0,1:T(8,128)(2,1)S(1)}, u32[]{:S(2)}, u32[]{:S(2)}) collective-permute-start(bf16[128,2048]{0,1:T(8,128)(2,1)S(1)} %bitcast.122), channel_id=1, source_target_pairs={{0,8},{8,0},{16,24},{24,16},{1,9},{9,1},{17,25},{25,17},{2,10},{10... | collective-permute-start | bytes 1572872 | tf_op jit(solution)/shard_map/ppermute | solution.py:70
  72.7 14.7 %collective-permute-start.38 = (bf16[128,2048]{0,1:T(8,128)(2,1)S(1)}, bf16[128,2048]{0,1:T(8,128)(2,1)}, u32[]{:S(2)}, u32[]{:S(2)}) collective-permute-start(bf16[128,2048]{0,1:T(8,128)(2,1)S(1)} %bitcast.123), channel_id=1, source_target_pairs={{0,16},{8,24},{16,0},{24,8},{1,17},{9,25},{17,1},{25,9},{2,18},{10... | collective-permute-start | bytes 1572872 | tf_op jit(solution)/shard_map/ppermute | solution.py:71
  74.0 14.5 %collective-permute-start.32 = (bf16[128,2048]{0,1:T(8,128)(2,1)S(1)}, bf16[128,2048]{0,1:T(8,128)(2,1)}, u32[]{:S(2)}, u32[]{:S(2)}) collective-permute-start(bf16[128,2048]{0,1:T(8,128)(2,1)S(1)} %bitcast.124), channel_id=1, source_target_pairs={{0,4},{4,0},{1,5},{5,1},{2,6},{6,2},{3,7},{7,3},{8,12},{12,8},{9,1... | collective-permute-start | bytes 1572872 | tf_op jit(solution)/shard_map/ppermute | solution.py:82
  86.6 14.9 %collective-permute-start.43 = (bf16[64,2048]{0,1:T(8,128)(2,1)S(1)}, bf16[64,2048]{0,1:T(8,128)(2,1)S(1)}, u32[]{:S(2)}, u32[]{:S(2)}) collective-permute-start(bf16[64,2048]{0,1:T(8,128)(2,1)S(1)} %slice.79), channel_id=1, source_target_pairs={{0,16},{8,24},{16,0},{24,8},{1,17},{9,25},{17,1},{25,9},{2,18},{10... | collective-permute-start | bytes 786440 | tf_op jit(solution)/shard_map/ppermute | solution.py:75
  87.4 15.1 %collective-permute-start.42 = (bf16[64,2048]{0,1:T(8,128)(2,1)}, bf16[64,2048]{0,1:T(8,128)(2,1)S(1)}, u32[]{:S(2)}, u32[]{:S(2)}) collective-permute-start(bf16[64,2048]{0,1:T(8,128)(2,1)} %bitcast.118), channel_id=1, source_target_pairs={{0,8},{8,0},{16,24},{24,16},{1,9},{9,1},{17,25},{25,17},{2,10},{10... | collective-permute-start | bytes 786440 | tf_op jit(solution)/shard_map/ppermute | solution.py:74
  90.3 13.2 %collective-permute-start.33 = (bf16[128,1024]{1,0:T(8,128)(2,1)S(1)}, bf16[128,1024]{1,0:T(8,128)(2,1)S(1)}, u32[]{:S(2)}, u32[]{:S(2)}) collective-permute-start(bf16[128,1024]{1,0:T(8,128)(2,1)S(1)} %convolution_convert_fusion.6), channel_id=1, source_target_pairs={{0,4},{4,0},{8,12},{12,8},{16,20},{20,16},{24,28},{28,24},{1,5},{5... | collective-permute-start | bytes 786440 | tf_op jit(solution)/shard_map/ppermute | solution.py:185
  91.2 15.2 %collective-permute-start.35 = (bf16[128,1024]{1,0:T(8,128)(2,1)S(1)}, bf16[128,1024]{1,0:T(8,128)(2,1)S(1)}, u32[]{:S(2)}, u32[]{:S(2)}) collective-permute-start(bf16[128,1024]{1,0:T(8,128)(2,1)S(1)} %convolution_convert_fusion.5), channel_id=1, source_target_pairs={{0,8},{4,12},{8,0},{12,4},{16,24},{20,28},{24,16},{28,20},{1,9},{5... | collective-permute-start | bytes 786440 | tf_op jit(solution)/shard_map/ppermute | solution.py:185
  93.9 24.8 %collective-permute-start.39 = (bf16[128,1024]{1,0:T(8,128)(2,1)S(1)}, bf16[128,1024]{1,0:T(8,128)(2,1)S(1)}, u32[]{:S(2)}, u32[]{:S(2)}) collective-permute-start(bf16[128,1024]{1,0:T(8,128)(2,1)S(1)} %convolution_convert_fusion.3), channel_id=1, source_target_pairs={{0,16},{4,20},{8,24},{12,28},{16,0},{20,4},{24,8},{28,12},{1,17},{... | collective-permute-start | bytes 786440 | tf_op jit(solution)/shard_map/ppermute | solution.py:185
  106.4 18.1 %collective-permute-start.44 = (bf16[128,1024]{1,0:T(8,128)(2,1)S(1)}, bf16[128,1024]{1,0:T(8,128)(2,1)S(1)}, u32[]{:S(2)}, u32[]{:S(2)}) collective-permute-start(bf16[128,1024]{1,0:T(8,128)(2,1)S(1)} %convolution_convert_fusion.1), channel_id=1, source_target_pairs={{0,24},{4,28},{8,16},{12,20},{16,8},{20,12},{24,0},{28,4},{1,25},{... | collective-permute-start | bytes 786440 | tf_op jit(solution)/shard_map/ppermute | solution.py:185
  109.3 15.2 %collective-permute-start.41 = (bf16[128,1024]{1,0:T(8,128)(2,1)S(1)}, bf16[128,1024]{1,0:T(8,128)(2,1)S(1)}, u32[]{:S(2)}, u32[]{:S(2)}) collective-permute-start(bf16[128,1024]{1,0:T(8,128)(2,1)S(1)} %convolution_convert_fusion.2), channel_id=1, source_target_pairs={{0,20},{4,16},{8,28},{12,24},{16,4},{20,0},{24,12},{28,8},{1,21},{... | collective-permute-start | bytes 786440 | tf_op jit(solution)/shard_map/ppermute | solution.py:185
  112.0 12.5 %collective-permute-start.46 = (bf16[128,1024]{1,0:T(8,128)(2,1)S(1)}, bf16[128,1024]{1,0:T(8,128)(2,1)S(1)}, u32[]{:S(2)}, u32[]{:S(2)}) collective-permute-start(bf16[128,1024]{1,0:T(8,128)(2,1)S(1)} %convolution_convert_fusion), channel_id=1, source_target_pairs={{0,28},{4,24},{8,20},{12,16},{16,12},{20,8},{24,4},{28,0},{1,29},{... | collective-permute-start | bytes 786440 | tf_op jit(solution)/shard_map/ppermute | solution.py:185
  (30 other events, 223.6 us)
Sparse Core Ops, SparseCore 0:
  126.1 44.5 reduce-scatter.1

commit v15 on v10

--- a/solution.py
+++ b/solution.py
@@ -112,6 +112,20 @@
     return numer / row_total[..., None]
 
 
+def gather_same_core(x):
+    half = x.shape[0] // 2
+    from_x = lax.ppermute(x, "hi", swap("hi", 1, 4))
+    from_y = lax.ppermute(x, "hi", swap("hi", 2, 4))
+    diag = jnp.concatenate(
+        [
+            lax.ppermute(from_y[:half], "hi", swap("hi", 1, 4)),
+            lax.ppermute(from_x[half:], "hi", swap("hi", 2, 4)),
+        ],
+        axis=0,
+    )
+    return [x, from_x, from_y, diag]
+
+
 def make_per_device(square):
     def gather_seq(x):
         if square:
@@ -165,19 +179,22 @@
         if square:
             chip = lax.axis_index("hi")
             core = lax.axis_index("lo")
-            blocks = gather_blocks_square(local_context)
             width = out_weight.shape[1]
+            chip_weight = jnp.concatenate(
+                [out_weight, lax.ppermute(out_weight, "lo", [(0, 1), (1, 0)])], axis=1
+            )
+            blocks = gather_same_core(local_context)
             by_row = jnp.zeros((seg_rows, seq_count * width), jnp.bfloat16)
-            for b, block in enumerate(blocks):
-                r, t = b // 2, b % 2
-                partial = jnp.dot(block, out_weight, preferred_element_type=jnp.float32).astype(
+            for r, block in enumerate(blocks):
+                partial = jnp.dot(block, chip_weight, preferred_element_type=jnp.float32).astype(
                     jnp.bfloat16
                 )
-                if b:
-                    pairs = [(h * 2 + l, (h ^ r) * 2 + (l ^ t)) for h in range(4) for l in range(2)]
-                    partial = lax.ppermute(partial, SEQ, pairs)
-                source = (chip ^ r) * 2 + (core ^ t)
-                by_row = lax.dynamic_update_slice(by_row, partial, (0, source * width))
+                if r:
+                    partial = lax.ppermute(partial, "hi", swap("hi", r, 4))
+                mine = (chip ^ r) * 2 + core
+                other = (chip ^ r) * 2 + (1 - core)
+                by_row = lax.dynamic_update_slice(by_row, partial[:, :width], (0, mine * width))
+                by_row = lax.dynamic_update_slice(by_row, partial[:, width:], (0, other * width))
             ordered = lax.psum_scatter(by_row, "chan", scatter_dimension=1, tiled=True)
             return (residual.astype(jnp.float32) + ordered.astype(jnp.float32)).astype(jnp.bfloat16)
         gathered = gather_seq(local_context)

time: 168 us -> 171 us (1.018)
  matrix products: 23.9 us -> 15.6 us
  waiting for transfers between devices: 93.8 us -> 99.4 us
  starting transfers between devices: 22.6 us -> 25.5 us
  local copies, waits for them, and re-layouts: 8.27 us -> 11.1 us
    ppermute x7 -> x8, waiting for transfers between devices: 12.5 us -> 32.5 us  [the longest x3 17.5 us: per_device(): partial = lax.ppermute(partial, 'hi', swap('hi', r, 4))]
    ppermute x3 -> x2, waiting for transfers between devices: 11 us -> 0.01 us  [gather_blocks_square(): from_x = lax.ppermute(x, 'hi', swap('hi', 1, 4))]
    dot_general x8 -> x4, matrix products: 10.8 us -> 5.27 us  [per_device(): jnp.dot(block, chip_weight, preferred_element_type=jnp.float32)]
    ppermute x3 -> x2, waiting for transfers between devices: 6.97 us -> 2.32 us  [gather_blocks_square(): lax.ppermute(from_x[half:], 'hi', swap('hi', 2, 4))]
    ppermute x7 -> x8, starting transfers between devices: 6.69 us -> 10.9 us  [the longest x3 3.68 us: per_device(): partial = lax.ppermute(partial, 'hi', swap('hi', r, 4))]
    concatenate x0 -> x1, local copies, waits for them, and re-layouts: none -> 2.64 us  [per_device(): jnp.concatenate([out_weight, lax.ppermute(out_weight, 'lo', [(0, 1), (1,...]
    ppermute x3 -> x2, waiting for transfers between devices: 13.3 us -> 15.8 us  [gather_blocks_square(): from_y = lax.ppermute(x, 'hi', swap('hi', 2, 4))]
    ppermute x3 -> x2, starting transfers between devices: 4.02 us -> 1.63 us  [gather_blocks_square(): lax.ppermute(from_y[:half], 'hi', swap('hi', 1, 4))]
  transfers between devices with their start and end apart: 32 -> 25, of which waited for: 16 -> 12; matrix products, arithmetic and copies ran while one was open for 18% -> 15% of each run, Pallas kernels for 0% -> 0%
where the time goes in v15:
time: 171 us; the launch traced here: 170 us
  waiting for transfers between devices  99.4 us (58%)
  starting transfers between devices  25.5 us (15%)
  matrix products  15.6 us (9%)
  between operations  13.9 us (8%)
  local copies, waits for them, and re-layouts  11.1 us (6%)
  other arithmetic  4.88 us (3%)
    reduce_scatter x1, waiting for transfers between devices, per_device(): ordered = lax.psum_scatter(by_row, 'chan', scatter_dimension=1, tiled=True)  44.5 us
    ppermute x3, waiting for transfers between devices, per_device(): partial = lax.ppermute(partial, 'hi', swap('hi', r, 4))  17.5 us
    ppermute x2, waiting for transfers between devices, gather_blocks_square(): from_y = lax.ppermute(x, 'hi', swap('hi', 2, 4))  15.8 us
    ppermute x1, waiting for transfers between devices, gather_same_core(): from_x = lax.ppermute(x, 'hi', swap('hi', 1, 4))  7.64 us
    dot_general x8, matrix products, attention_by_head(): jnp.einsum('hqd,hkd->hqk', queries, keys, preferred_element_type=jnp.floa...  6.48 us
    ppermute x1, waiting for transfers between devices, gather_same_core(): lax.ppermute(from_x[half:], 'hi', swap('hi', 2, 4))  5.94 us
    unnamed x13, local copies, waits for them, and re-layouts  5.87 us
    dot_general x4, matrix products, per_device(): jnp.dot(block, chip_weight, preferred_element_type=jnp.float32)  5.27 us
  transfers between devices with their start and end apart: 25, of which 12 were waited for; matrix products, arithmetic and copies ran while one was open for 15% of the time, Pallas kernels for 0%

profile of v15, /device:TPU:0, one launch (start us, length us, event | category | flops | bytes accessed | tf_op | source)
XLA Modules:
  0.0 170.3 jit_solution(17305732234382243689)
XLA Ops:
  8.2 3.0 %collective-permute-start.3 = (bf16[16,128,128]{2,1,0:T(8,128)(2,1)S(1)}, bf16[16,128,128]{2,1,0:T(8,128)(2,1)}, u32[]{:S(2)}, u32[]{:S(2)}) collective-permute-start(bf16[16,128,128]{2,1,0:T(8,128)(2,1)S(1)} %bitcast.135), channel_id=1, source_target_pairs={{0,16},{8,24},{16,0},{24,8},{1,17},{9,25},{17,1},{25,9},{2,18},{10... | collective-permute-start | bytes 1572872 | tf_op jit(solution)/shard_map/ppermute | solution.py:71
  11.3 1.5 collective-permute-start.1
  15.5 8.6 %collective-permute-done.3 = bf16[16,128,128]{2,1,0:T(8,128)(2,1)} collective-permute-done((bf16[16,128,128]{2,1,0:T(8,128)(2,1)S(1)}, bf16[16,128,128]{2,1,0:T(8,128)(2,1)}, u32[]{:S(2)}, u32[]{:S(2)}) %collective-permute-start.3) | collective-permute-done | bytes 524320 | tf_op jit(solution)/shard_map/ppermute | solution.py:71
  24.1 2.0 %collective-permute-start.9 = (bf16[16,128,128]{1,2,0:T(8,128)(2,1)S(1)}, bf16[16,128,128]{1,2,0:T(8,128)(2,1)S(1)}, u32[]{:S(2)}, u32[]{:S(2)}) collective-permute-start(bf16[16,128,128]{1,2,0:T(8,128)(2,1)S(1)} %bitcast.128), channel_id=1, source_target_pairs={{0,8},{8,0},{16,24},{24,16},{1,9},{9,1},{17,25},{25,17},{2,10},{10... | collective-permute-start | bytes 1572872 | tf_op jit(solution)/shard_map/ppermute | solution.py:70
  27.2 7.2 %collective-permute-done.11 = bf16[16,128,128]{1,2,0:T(8,128)(2,1)S(1)} collective-permute-done((bf16[16,128,128]{1,2,0:T(8,128)(2,1)S(1)}, bf16[16,128,128]{1,2,0:T(8,128)(2,1)S(1)}, u32[]{:S(2)}, u32[]{:S(2)}) %collective-permute-start.11) | collective-permute-done | bytes 524320 | tf_op jit(solution)/shard_map/ppermute | solution.py:71
  34.4 1.7 %collective-permute-start.6 = (bf16[8,128,128]{2,1,0:T(8,128)(2,1)S(1)}, bf16[8,128,128]{2,1,0:T(8,128)(2,1)S(1)}, u32[]{:S(2)}, u32[]{:S(2)}) collective-permute-start(bf16[8,128,128]{2,1,0:T(8,128)(2,1)S(1)} %slice.57), channel_id=1, source_target_pairs={{0,16},{8,24},{16,0},{24,8},{1,17},{9,25},{17,1},{25,9},{2,18},{10... | collective-permute-start | bytes 786440 | tf_op jit(solution)/shard_map/ppermute | solution.py:75
  36.2 1.6 fusion.92
  38.4 1.6 collective-permute-start.13
  40.0 1.6 fusion.96
  41.7 2.5 %collective-permute-done.5 = bf16[8,128,128]{2,1,0:T(8,128)(2,1)S(1)} collective-permute-done((bf16[8,128,128]{2,1,0:T(8,128)(2,1)S(1)}, bf16[8,128,128]{2,1,0:T(8,128)(2,1)S(1)}, u32[]{:S(2)}, u32[]{:S(2)}) %collective-permute-start.5) | collective-permute-done | bytes 262176 | tf_op jit(solution)/shard_map/ppermute | solution.py:74
  44.2 2.0 %collective-permute-start.14 = (bf16[8,128,128]{1,2,0:T(8,128)(2,1)S(1)}, bf16[8,128,128]{1,2,0:T(8,128)(2,1)S(1)}, u32[]{:S(2)}, u32[]{:S(2)}) collective-permute-start(bf16[8,128,128]{1,2,0:T(8,128)(2,1)S(1)} %slice.59), channel_id=1, source_target_pairs={{0,16},{8,24},{16,0},{24,8},{1,17},{9,25},{17,1},{25,9},{2,18},{10... | collective-permute-start | bytes 786440 | tf_op jit(solution)/shard_map/ppermute | solution.py:75
  48.3 2.3 %collective-permute-done.14 = bf16[8,128,128]{1,2,0:T(8,128)(2,1)S(1)} collective-permute-done((bf16[8,128,128]{1,2,0:T(8,128)(2,1)S(1)}, bf16[8,128,128]{1,2,0:T(8,128)(2,1)S(1)}, u32[]{:S(2)}, u32[]{:S(2)}) %collective-permute-start.14) | collective-permute-done | bytes 262176 | tf_op jit(solution)/shard_map/ppermute | solution.py:75
  55.9 2.1 %fusion.18 = (f32[16,128]{1,0:T(8,128)S(1)}, f32[16,128]{1,0:T(8,128)S(1)}, f32[16,128]{1,0:T(8,128)S(1)}, f32[16,128]{1,0:T(8,128)S(1)}, f32[16,128]{1,0:T(8,128)S(1)}) fusion(f32[16,128,128]{2,1,0:T(8,128)S(1)} %get-tuple-element.36, f32[16,128]{1,0:T(8,128)S(1)} %maximum_maximum_fusion, pred[128,128]{1,0:T(8,128)(4,1)S(1)} %copy.41, ...), kind=kLoop, calls=%fused_computation.43 | loop fusion | flops 3921920 | bytes 5373952 | tf_op jit(solution)/shard_map/reduce_sum | solution.py:106
  60.8 1.6 collective-permute-start.17
  62.3 2.0 %collective-permute-start.19 = (bf16[128,2048]{0,1:T(8,128)(2,1)S(1)}, bf16[128,2048]{0,1:T(8,128)(2,1)S(1)}, u32[]{:S(2)}, u32[]{:S(2)}) collective-permute-start(bf16[128,2048]{0,1:T(8,128)(2,1)S(1)} %bitcast.133), channel_id=1, source_target_pairs={{0,16},{8,24},{16,0},{24,8},{1,17},{9,25},{17,1},{25,9},{2,18},{10... | collective-permute-start | bytes 1572872 | tf_op jit(solution)/shard_map/ppermute | solution.py:118
  64.3 2.8 %constant_dynamic-update-slice_fusion.5 = bf16[2048,2048]{1,0:T(8,128)(2,1)S(1)} fusion(bf16[2048,1024]{1,0:T(8,128)(2,1)} %param.9), kind=kLoop, calls=%fused_computation.118 | loop fusion | bytes 8388608
  67.2 7.6 %collective-permute-done.17 = bf16[128,2048]{0,1:T(8,128)(2,1)S(1)} collective-permute-done((bf16[128,2048]{0,1:T(8,128)(2,1)S(1)}, bf16[128,2048]{0,1:T(8,128)(2,1)S(1)}, u32[]{:S(2)}, u32[]{:S(2)}) %collective-permute-start.17) | collective-permute-done | bytes 524320 | tf_op jit(solution)/shard_map/ppermute | solution.py:117
  75.0 2.1 %collective-permute-start.22 = (bf16[64,2048]{0,1:T(8,128)(2,1)S(1)}, bf16[64,2048]{0,1:T(8,128)(2,1)S(1)}, u32[]{:S(2)}, u32[]{:S(2)}) collective-permute-start(bf16[64,2048]{0,1:T(8,128)(2,1)S(1)} %slice.67), channel_id=1, source_target_pairs={{0,16},{8,24},{16,0},{24,8},{1,17},{9,25},{17,1},{25,9},{2,18},{10... | collective-permute-start | bytes 786440 | tf_op jit(solution)/shard_map/ppermute | solution.py:122
  77.1 1.5 collective-permute-start.21
  78.6 2.6 %constant_dynamic-update-slice_fusion.4 = bf16[2048,2048]{1,0:T(8,128)(2,1)S(1)} fusion(bf16[2048,2048]{1,0:T(8,128)(2,1)S(1)} %constant_dynamic-update-slice_fusion.5, bf16[2048,1024]{1,0:T(8,128)(2,1)} %collective-permute-done.16), kind=kLoop, calls=%fused_computation.117 | loop fusion | bytes 8388608 | tf_op jit(solution)/shard_map/concatenate | solution.py:183
  82.6 5.9 %collective-permute-done.22 = bf16[64,2048]{0,1:T(8,128)(2,1)S(1)} collective-permute-done((bf16[64,2048]{0,1:T(8,128)(2,1)S(1)}, bf16[64,2048]{0,1:T(8,128)(2,1)S(1)}, u32[]{:S(2)}, u32[]{:S(2)}) %collective-permute-start.22) | collective-permute-done | bytes 262176 | tf_op jit(solution)/shard_map/ppermute | solution.py:122
  97.9 17.0 %collective-permute-done.18 = bf16[128,2048]{1,0:T(8,128)(2,1)S(1)} collective-permute-done((bf16[128,2048]{1,0:T(8,128)(2,1)S(1)}, bf16[128,2048]{1,0:T(8,128)(2,1)S(1)}, u32[]{:S(2)}, u32[]{:S(2)}) %collective-permute-start.18) | collective-permute-done | bytes 524320 | tf_op jit(solution)/shard_map/ppermute | solution.py:193
  117.0 44.5 %reduce-scatter.2.cloned.1.call-done = bf16[128,2048]{1,0:T(8,128)(2,1)} async-done(((bf16[128,8192]{1,0:T(8,128)(2,1)}), bf16[128,2048]{1,0:T(8,128)(2,1)}) %reduce-scatter.2.cloned.1.call-update) | async-done | bytes 524304 | tf_op jit(solution)/shard_map/reduce_scatter | solution.py:198
  161.5 2.0 %add_convert_fusion = bf16[128,2048]{1,0:T(8,128)(2,1)} fusion(bf16[128,2048]{1,0:T(8,128)(2,1)} %reduce-scatter.2.cloned.1.call-done, bf16[128,2048]{1,0:T(8,128)(2,1)S(1)} %copy-done.2), kind=kLoop, calls=%fused_computation.32 | loop fusion | flops 1048576 | bytes 1572864 | tf_op jit(solution)/shard_map/convert_element_type | solution.py:199
  (93 shorter events, 29.0 us)
Async XLA Ops:
  6.5 155.0 %reduce-scatter.2.cloned.1.call-start = ((), (), s32[]{:S(2)}) async-start(), calls=%async_computation.1 | async-start | bytes 2621440 | tf_op jit(solution)/shard_map/reduce_scatter | solution.py:198
  8.2 15.9 %collective-permute-start.3 = (bf16[16,128,128]{2,1,0:T(8,128)(2,1)S(1)}, bf16[16,128,128]{2,1,0:T(8,128)(2,1)}, u32[]{:S(2)}, u32[]{:S(2)}) collective-permute-start(bf16[16,128,128]{2,1,0:T(8,128)(2,1)S(1)} %bitcast.135), channel_id=1, source_target_pairs={{0,16},{8,24},{16,0},{24,8},{1,17},{9,25},{17,1},{25,9},{2,18},{10... | collective-permute-start | bytes 1572872 | tf_op jit(solution)/shard_map/ppermute | solution.py:71
  11.3 15.9 %collective-permute-start.1 = (bf16[16,128,128]{2,1,0:T(8,128)(2,1)S(1)}, bf16[16,128,128]{2,1,0:T(8,128)(2,1)S(1)}, u32[]{:S(2)}, u32[]{:S(2)}) collective-permute-start(bf16[16,128,128]{2,1,0:T(8,128)(2,1)S(1)} %bitcast.136), channel_id=1, source_target_pairs={{0,8},{8,0},{16,24},{24,16},{1,9},{9,1},{17,25},{25,17},{2,10},{10... | collective-permute-start | bytes 1572872 | tf_op jit(solution)/shard_map/ppermute | solution.py:70
  12.8 25.6 %collective-permute-start = (bf16[16,128,128]{2,1,0:T(8,128)(2,1)S(1)}, bf16[16,128,128]{2,1,0:T(8,128)(2,1)}, u32[]{:S(2)}, u32[]{:S(2)}) collective-permute-start(bf16[16,128,128]{2,1,0:T(8,128)(2,1)S(1)} %bitcast.137), channel_id=1, source_target_pairs={{0,4},{4,0},{1,5},{5,1},{2,6},{6,2},{3,7},{7,3},{8,12},{12,8},{9,1... | collective-permute-start | bytes 1572872 | tf_op jit(solution)/shard_map/ppermute | solution.py:82
  13.0 41.8 %collective-permute-start.8 = (bf16[16,128,128]{1,2,0:T(8,128)(2,1)S(1)}, bf16[16,128,128]{1,2,0:T(8,128)(2,1)S(1)}, u32[]{:S(2)}, u32[]{:S(2)}) collective-permute-start(bf16[16,128,128]{1,2,0:T(8,128)(2,1)S(1)} %bitcast.126), channel_id=1, source_target_pairs={{0,4},{4,0},{1,5},{5,1},{2,6},{6,2},{3,7},{7,3},{8,12},{12,8},{9,1... | collective-permute-start | bytes 1572872 | tf_op jit(solution)/shard_map/ppermute | solution.py:82
  13.6 20.8 %collective-permute-start.11 = (bf16[16,128,128]{1,2,0:T(8,128)(2,1)S(1)}, bf16[16,128,128]{1,2,0:T(8,128)(2,1)S(1)}, u32[]{:S(2)}, u32[]{:S(2)}) collective-permute-start(bf16[16,128,128]{1,2,0:T(8,128)(2,1)S(1)} %bitcast.127), channel_id=1, source_target_pairs={{0,16},{8,24},{16,0},{24,8},{1,17},{9,25},{17,1},{25,9},{2,18},{10... | collective-permute-start | bytes 1572872 | tf_op jit(solution)/shard_map/ppermute | solution.py:71
  24.1 17.5 %collective-permute-start.9 = (bf16[16,128,128]{1,2,0:T(8,128)(2,1)S(1)}, bf16[16,128,128]{1,2,0:T(8,128)(2,1)S(1)}, u32[]{:S(2)}, u32[]{:S(2)}) collective-permute-start(bf16[16,128,128]{1,2,0:T(8,128)(2,1)S(1)} %bitcast.128), channel_id=1, source_target_pairs={{0,8},{8,0},{16,24},{24,16},{1,9},{9,1},{17,25},{25,17},{2,10},{10... | collective-permute-start | bytes 1572872 | tf_op jit(solution)/shard_map/ppermute | solution.py:70
  27.1 17.1 %collective-permute-start.5 = (bf16[8,128,128]{2,1,0:T(8,128)(2,1)S(1)}, bf16[8,128,128]{2,1,0:T(8,128)(2,1)S(1)}, u32[]{:S(2)}, u32[]{:S(2)}) collective-permute-start(bf16[8,128,128]{2,1,0:T(8,128)(2,1)S(1)} %slice.56), channel_id=1, source_target_pairs={{0,8},{8,0},{16,24},{24,16},{1,9},{9,1},{17,25},{25,17},{2,10},{10... | collective-permute-start | bytes 786440 | tf_op jit(solution)/shard_map/ppermute | solution.py:74
  34.4 13.2 %collective-permute-start.6 = (bf16[8,128,128]{2,1,0:T(8,128)(2,1)S(1)}, bf16[8,128,128]{2,1,0:T(8,128)(2,1)S(1)}, u32[]{:S(2)}, u32[]{:S(2)}) collective-permute-start(bf16[8,128,128]{2,1,0:T(8,128)(2,1)S(1)} %slice.57), channel_id=1, source_target_pairs={{0,16},{8,24},{16,0},{24,8},{1,17},{9,25},{17,1},{25,9},{2,18},{10... | collective-permute-start | bytes 786440 | tf_op jit(solution)/shard_map/ppermute | solution.py:75
  38.4 9.2 %collective-permute-start.13 = (bf16[8,128,128]{1,2,0:T(8,128)(2,1)S(1)}, bf16[8,128,128]{1,2,0:T(8,128)(2,1)S(1)}, u32[]{:S(2)}, u32[]{:S(2)}) collective-permute-start(bf16[8,128,128]{1,2,0:T(8,128)(2,1)S(1)} %slice.58), channel_id=1, source_target_pairs={{0,8},{8,0},{16,24},{24,16},{1,9},{9,1},{17,25},{25,17},{2,10},{10... | collective-permute-start | bytes 786440 | tf_op jit(solution)/shard_map/ppermute | solution.py:74
  41.6 37.0 %collective-permute-start.16 = (bf16[2048,1024]{1,0:T(8,128)(2,1)}, bf16[2048,1024]{1,0:T(8,128)(2,1)}, u32[]{:S(2)}, u32[]{:S(2)}) collective-permute-start(bf16[2048,1024]{1,0:T(8,128)(2,1)} %param.9), channel_id=1, source_target_pairs={{0,4},{4,0},{1,5},{5,1},{2,6},{6,2},{3,7},{7,3},{8,12},{12,8},{9,1... | collective-permute-start | bytes 12582920 | tf_op jit(solution)/shard_map/ppermute | solution.py:184
  44.2 6.4 %collective-permute-start.14 = (bf16[8,128,128]{1,2,0:T(8,128)(2,1)S(1)}, bf16[8,128,128]{1,2,0:T(8,128)(2,1)S(1)}, u32[]{:S(2)}, u32[]{:S(2)}) collective-permute-start(bf16[8,128,128]{1,2,0:T(8,128)(2,1)S(1)} %slice.59), channel_id=1, source_target_pairs={{0,16},{8,24},{16,0},{24,8},{1,17},{9,25},{17,1},{25,9},{2,18},{10... | collective-permute-start | bytes 786440 | tf_op jit(solution)/shard_map/ppermute | solution.py:75
  47.6 3.5 %collective-permute-start.4 = (bf16[16,128,128]{2,1,0:T(8,128)(2,1)}, bf16[16,128,128]{2,1,0:T(8,128)(2,1)S(1)}, u32[]{:S(2)}, u32[]{:S(2)}) collective-permute-start(bf16[16,128,128]{2,1,0:T(8,128)(2,1)} %collective-permute-done.3), channel_id=1, source_target_pairs={{0,4},{4,0},{1,5},{5,1},{2,6},{6,2},{3,7},{7,3},{8,12},{12,8},{9,1... | collective-permute-start | bytes 1572872 | tf_op jit(solution)/shard_map/ppermute | solution.py:82
  47.7 4.6 %collective-permute-start.2 = (bf16[16,128,128]{2,1,0:T(8,128)(2,1)S(1)}, bf16[16,128,128]{2,1,0:T(8,128)(2,1)S(1)}, u32[]{:S(2)}, u32[]{:S(2)}) collective-permute-start(bf16[16,128,128]{2,1,0:T(8,128)(2,1)S(1)} %collective-permute-done.1), channel_id=1, source_target_pairs={{0,4},{4,0},{1,5},{5,1},{2,6},{6,2},{3,7},{7,3},{8,12},{12,8},{9,1... | collective-permute-start | bytes 1572872 | tf_op jit(solution)/shard_map/ppermute | solution.py:82
  50.6 8.9 %collective-permute-start.10 = (bf16[16,128,128]{1,2,0:T(8,128)(2,1)S(1)}, bf16[16,128,128]{1,2,0:T(8,128)(2,1)S(1)}, u32[]{:S(2)}, u32[]{:S(2)}) collective-permute-start(bf16[16,128,128]{1,2,0:T(8,128)(2,1)S(1)} %collective-permute-done.9), channel_id=1, source_target_pairs={{0,4},{4,0},{1,5},{5,1},{2,6},{6,2},{3,7},{7,3},{8,12},{12,8},{9,1... | collective-permute-start | bytes 1572872 | tf_op jit(solution)/shard_map/ppermute | solution.py:82
  52.3 7.8 %collective-permute-start.12 = (bf16[16,128,128]{1,2,0:T(8,128)(2,1)S(1)}, bf16[16,128,128]{1,2,0:T(8,128)(2,1)S(1)}, u32[]{:S(2)}, u32[]{:S(2)}) collective-permute-start(bf16[16,128,128]{1,2,0:T(8,128)(2,1)S(1)} %collective-permute-done.11), channel_id=1, source_target_pairs={{0,4},{4,0},{1,5},{5,1},{2,6},{6,2},{3,7},{7,3},{8,12},{12,8},{9,1... | collective-permute-start | bytes 1572872 | tf_op jit(solution)/shard_map/ppermute | solution.py:82
  53.3 5.9 %collective-permute-start.15 = (bf16[16,128,128]{1,2,0:T(8,128)(2,1)S(1)}, bf16[16,128,128]{1,2,0:T(8,128)(2,1)S(1)}, u32[]{:S(2)}, u32[]{:S(2)}) collective-permute-start(bf16[16,128,128]{1,2,0:T(8,128)(2,1)S(1)} %constant_dynamic-update-slice_fusion.2), channel_id=1, source_target_pairs={{0,4},{4,0},{1,5},{5,1},{2,6},{6,2},{3,7},{7,3},{8,12},{12,8},{9,1... | collective-permute-start | bytes 1572872 | tf_op jit(solution)/shard_map/ppermute | solution.py:82
  60.8 14.0 %collective-permute-start.17 = (bf16[128,2048]{0,1:T(8,128)(2,1)S(1)}, bf16[128,2048]{0,1:T(8,128)(2,1)S(1)}, u32[]{:S(2)}, u32[]{:S(2)}) collective-permute-start(bf16[128,2048]{0,1:T(8,128)(2,1)S(1)} %bitcast.132), channel_id=1, source_target_pairs={{0,8},{8,0},{16,24},{24,16},{1,9},{9,1},{17,25},{25,17},{2,10},{10... | collective-permute-start | bytes 1572872 | tf_op jit(solution)/shard_map/ppermute | solution.py:117
  62.3 14.8 %collective-permute-start.19 = (bf16[128,2048]{0,1:T(8,128)(2,1)S(1)}, bf16[128,2048]{0,1:T(8,128)(2,1)S(1)}, u32[]{:S(2)}, u32[]{:S(2)}) collective-permute-start(bf16[128,2048]{0,1:T(8,128)(2,1)S(1)} %bitcast.133), channel_id=1, source_target_pairs={{0,16},{8,24},{16,0},{24,8},{1,17},{9,25},{17,1},{25,9},{2,18},{10... | collective-permute-start | bytes 1572872 | tf_op jit(solution)/shard_map/ppermute | solution.py:118
  75.0 13.5 %collective-permute-start.22 = (bf16[64,2048]{0,1:T(8,128)(2,1)S(1)}, bf16[64,2048]{0,1:T(8,128)(2,1)S(1)}, u32[]{:S(2)}, u32[]{:S(2)}) collective-permute-start(bf16[64,2048]{0,1:T(8,128)(2,1)S(1)} %slice.67), channel_id=1, source_target_pairs={{0,16},{8,24},{16,0},{24,8},{1,17},{9,25},{17,1},{25,9},{2,18},{10... | collective-permute-start | bytes 786440 | tf_op jit(solution)/shard_map/ppermute | solution.py:122
  77.1 12.9 %collective-permute-start.21 = (bf16[64,2048]{0,1:T(8,128)(2,1)S(1)}, bf16[64,2048]{0,1:T(8,128)(2,1)S(1)}, u32[]{:S(2)}, u32[]{:S(2)}) collective-permute-start(bf16[64,2048]{0,1:T(8,128)(2,1)S(1)} %bitcast.131), channel_id=1, source_target_pairs={{0,8},{8,0},{16,24},{24,16},{1,9},{9,1},{17,25},{25,17},{2,10},{10... | collective-permute-start | bytes 786440 | tf_op jit(solution)/shard_map/ppermute | solution.py:121
  91.3 24.2 %collective-permute-start.23 = (bf16[128,2048]{1,0:T(8,128)(2,1)S(1)}, bf16[128,2048]{1,0:T(8,128)(2,1)S(1)}, u32[]{:S(2)}, u32[]{:S(2)}) collective-permute-start(bf16[128,2048]{1,0:T(8,128)(2,1)S(1)} %convolution_convert_fusion), channel_id=1, source_target_pairs={{0,24},{8,16},{16,8},{24,0},{1,25},{9,17},{17,9},{25,1},{2,26},{10... | collective-permute-start | bytes 1572872 | tf_op jit(solution)/shard_map/ppermute | solution.py:193
  94.0 20.9 %collective-permute-start.18 = (bf16[128,2048]{1,0:T(8,128)(2,1)S(1)}, bf16[128,2048]{1,0:T(8,128)(2,1)S(1)}, u32[]{:S(2)}, u32[]{:S(2)}) collective-permute-start(bf16[128,2048]{1,0:T(8,128)(2,1)S(1)} %convolution_convert_fusion.2), channel_id=1, source_target_pairs={{0,8},{8,0},{16,24},{24,16},{1,9},{9,1},{17,25},{25,17},{2,10},{10... | collective-permute-start | bytes 1572872 | tf_op jit(solution)/shard_map/ppermute | solution.py:193
  96.4 19.0 %collective-permute-start.20 = (bf16[128,2048]{1,0:T(8,128)(2,1)S(1)}, bf16[128,2048]{1,0:T(8,128)(2,1)S(1)}, u32[]{:S(2)}, u32[]{:S(2)}) collective-permute-start(bf16[128,2048]{1,0:T(8,128)(2,1)S(1)} %convolution_convert_fusion.1), channel_id=1, source_target_pairs={{0,16},{8,24},{16,0},{24,8},{1,17},{9,25},{17,1},{25,9},{2,18},{10... | collective-permute-start | bytes 1572872 | tf_op jit(solution)/shard_map/ppermute | solution.py:193
  (5 other events, 64.7 us)
Sparse Core Ops, SparseCore 0:
  117.1 44.3 reduce-scatter.1

commit v16 on v15

--- a/solution.py
+++ b/solution.py
@@ -189,7 +189,16 @@
                 partial = jnp.dot(block, chip_weight, preferred_element_type=jnp.float32).astype(
                     jnp.bfloat16
                 )
-                if r:
+                if r == 3:
+                    half = partial.shape[0] // 2
+                    first = lax.ppermute(
+                        lax.ppermute(partial[:half], "hi", swap("hi", 1, 4)), "hi", swap("hi", 2, 4)
+                    )
+                    second = lax.ppermute(
+                        lax.ppermute(partial[half:], "hi", swap("hi", 2, 4)), "hi", swap("hi", 1, 4)
+                    )
+                    partial = jnp.concatenate([first, second], axis=0)
+                elif r:
                     partial = lax.ppermute(partial, "hi", swap("hi", r, 4))
                 mine = (chip ^ r) * 2 + core
                 other = (chip ^ r) * 2 + (1 - core)

time: 171 us -> 170 us (level)
  waiting for transfers between devices: 99.4 us -> 97.4 us
  starting transfers between devices: 25.5 us -> 27.3 us
    ppermute x3 -> x2, waiting for transfers between devices: 17.5 us -> 10.4 us  [per_device(): partial = lax.ppermute(partial, 'hi', swap('hi', r, 4))]
    ppermute x0 -> x4, waiting for transfers between devices: none -> 5.87 us  [the longest x1 3.09 us: per_device(): lax.ppermute(lax.ppermute(partial[:half], 'hi', swap('hi', 1, 4)), 'hi',...]
    ppermute x0 -> x4, starting transfers between devices: none -> 3.12 us  [the longest x1 1.53 us: per_device(): lax.ppermute(partial[:half], 'hi', swap('hi', 1, 4))]
    ppermute x3 -> x2, starting transfers between devices: 3.68 us -> 2.35 us  [per_device(): partial = lax.ppermute(partial, 'hi', swap('hi', r, 4))]
    unnamed x13 -> x14, local copies, waits for them, and re-layouts: 5.87 us -> 5.89 us
  transfers between devices with their start and end apart: 25 -> 28, of which waited for: 12 -> 15; matrix products, arithmetic and copies ran while one was open for 15% -> 15% of each run, Pallas kernels for 0% -> 0%
where the time goes in v16:
time: 170 us
  waiting for transfers between devices  97.4 us (57%)
  starting transfers between devices  27.3 us (16%)
  matrix products  15.5 us (9%)
  between operations  13.9 us (8%)
  local copies, waits for them, and re-layouts  11.2 us (7%)
  other arithmetic  4.87 us (3%)
    reduce_scatter x1, waiting for transfers between devices, per_device(): ordered = lax.psum_scatter(by_row, 'chan', scatter_dimension=1, tiled=True)  43.7 us
    ppermute x2, waiting for transfers between devices, gather_blocks_square(): from_y = lax.ppermute(x, 'hi', swap('hi', 2, 4))  15.8 us
    ppermute x2, waiting for transfers between devices, per_device(): partial = lax.ppermute(partial, 'hi', swap('hi', r, 4))  10.4 us
    ppermute x1, waiting for transfers between devices, gather_same_core(): from_x = lax.ppermute(x, 'hi', swap('hi', 1, 4))  7.64 us
    dot_general x8, matrix products, attention_by_head(): jnp.einsum('hqd,hkd->hqk', queries, keys, preferred_element_type=jnp.floa...  6.47 us
    ppermute x1, waiting for transfers between devices, gather_same_core(): lax.ppermute(from_x[half:], 'hi', swap('hi', 2, 4))  5.98 us
    unnamed x14, local copies, waits for them, and re-layouts  5.89 us
    dot_general x4, matrix products, per_device(): jnp.dot(block, chip_weight, preferred_element_type=jnp.float32)  5.26 us
  transfers between devices with their start and end apart: 28, of which 15 were waited for; matrix products, arithmetic and copies ran while one was open for 15% of the time, Pallas kernels for 0%

profile of v16, /device:TPU:0, one launch (start us, length us, event | category | flops | bytes accessed | tf_op | source)
XLA Modules:
  0.0 170.1 jit_solution(16658500029345062637)
XLA Ops:
  8.2 3.0 %collective-permute-start.3 = (bf16[16,128,128]{2,1,0:T(8,128)(2,1)S(1)}, bf16[16,128,128]{2,1,0:T(8,128)(2,1)}, u32[]{:S(2)}, u32[]{:S(2)}) collective-permute-start(bf16[16,128,128]{2,1,0:T(8,128)(2,1)S(1)} %bitcast.135), channel_id=1, source_target_pairs={{0,16},{8,24},{16,0},{24,8},{1,17},{9,25},{17,1},{25,9},{2,18},{10... | collective-permute-start | bytes 1572872 | tf_op jit(solution)/shard_map/ppermute | solution.py:71
  15.5 8.6 %collective-permute-done.3 = bf16[16,128,128]{2,1,0:T(8,128)(2,1)} collective-permute-done((bf16[16,128,128]{2,1,0:T(8,128)(2,1)S(1)}, bf16[16,128,128]{2,1,0:T(8,128)(2,1)}, u32[]{:S(2)}, u32[]{:S(2)}) %collective-permute-start.3) | collective-permute-done | bytes 524320 | tf_op jit(solution)/shard_map/ppermute | solution.py:71
  24.1 2.0 %collective-permute-start.9 = (bf16[16,128,128]{1,2,0:T(8,128)(2,1)S(1)}, bf16[16,128,128]{1,2,0:T(8,128)(2,1)S(1)}, u32[]{:S(2)}, u32[]{:S(2)}) collective-permute-start(bf16[16,128,128]{1,2,0:T(8,128)(2,1)S(1)} %bitcast.128), channel_id=1, source_target_pairs={{0,8},{8,0},{16,24},{24,16},{1,9},{9,1},{17,25},{25,17},{2,10},{10... | collective-permute-start | bytes 1572872 | tf_op jit(solution)/shard_map/ppermute | solution.py:70
  27.2 7.2 %collective-permute-done.11 = bf16[16,128,128]{1,2,0:T(8,128)(2,1)S(1)} collective-permute-done((bf16[16,128,128]{1,2,0:T(8,128)(2,1)S(1)}, bf16[16,128,128]{1,2,0:T(8,128)(2,1)S(1)}, u32[]{:S(2)}, u32[]{:S(2)}) %collective-permute-start.11) | collective-permute-done | bytes 524320 | tf_op jit(solution)/shard_map/ppermute | solution.py:71
  34.4 1.7 %collective-permute-start.6 = (bf16[8,128,128]{2,1,0:T(8,128)(2,1)S(1)}, bf16[8,128,128]{2,1,0:T(8,128)(2,1)S(1)}, u32[]{:S(2)}, u32[]{:S(2)}) collective-permute-start(bf16[8,128,128]{2,1,0:T(8,128)(2,1)S(1)} %slice.65), channel_id=1, source_target_pairs={{0,16},{8,24},{16,0},{24,8},{1,17},{9,25},{17,1},{25,9},{2,18},{10... | collective-permute-start | bytes 786440 | tf_op jit(solution)/shard_map/ppermute | solution.py:75
  36.2 1.6 fusion.93
  38.4 1.6 collective-permute-start.13
  40.0 1.6 fusion.97
  41.7 2.5 %collective-permute-done.5 = bf16[8,128,128]{2,1,0:T(8,128)(2,1)S(1)} collective-permute-done((bf16[8,128,128]{2,1,0:T(8,128)(2,1)S(1)}, bf16[8,128,128]{2,1,0:T(8,128)(2,1)S(1)}, u32[]{:S(2)}, u32[]{:S(2)}) %collective-permute-start.5) | collective-permute-done | bytes 262176 | tf_op jit(solution)/shard_map/ppermute | solution.py:74
  44.2 2.0 %collective-permute-start.14 = (bf16[8,128,128]{1,2,0:T(8,128)(2,1)S(1)}, bf16[8,128,128]{1,2,0:T(8,128)(2,1)S(1)}, u32[]{:S(2)}, u32[]{:S(2)}) collective-permute-start(bf16[8,128,128]{1,2,0:T(8,128)(2,1)S(1)} %slice.67), channel_id=1, source_target_pairs={{0,16},{8,24},{16,0},{24,8},{1,17},{9,25},{17,1},{25,9},{2,18},{10... | collective-permute-start | bytes 786440 | tf_op jit(solution)/shard_map/ppermute | solution.py:75
  48.3 2.3 %collective-permute-done.14 = bf16[8,128,128]{1,2,0:T(8,128)(2,1)S(1)} collective-permute-done((bf16[8,128,128]{1,2,0:T(8,128)(2,1)S(1)}, bf16[8,128,128]{1,2,0:T(8,128)(2,1)S(1)}, u32[]{:S(2)}, u32[]{:S(2)}) %collective-permute-start.14) | collective-permute-done | bytes 262176 | tf_op jit(solution)/shard_map/ppermute | solution.py:75
  55.9 2.1 %fusion.18 = (f32[16,128]{1,0:T(8,128)S(1)}, f32[16,128]{1,0:T(8,128)S(1)}, f32[16,128]{1,0:T(8,128)S(1)}, f32[16,128]{1,0:T(8,128)S(1)}, f32[16,128]{1,0:T(8,128)S(1)}) fusion(f32[16,128,128]{2,1,0:T(8,128)S(1)} %get-tuple-element.38, f32[16,128]{1,0:T(8,128)S(1)} %maximum_maximum_fusion, pred[128,128]{1,0:T(8,128)(4,1)S(1)} %copy.41, ...), kind=kLoop, calls=%fused_computation.43 | loop fusion | flops 3921920 | bytes 5373952 | tf_op jit(solution)/shard_map/reduce_sum | solution.py:106
  60.7 1.6 collective-permute-start.17
  62.3 2.0 %collective-permute-start.19 = (bf16[128,2048]{0,1:T(8,128)(2,1)S(1)}, bf16[128,2048]{0,1:T(8,128)(2,1)S(1)}, u32[]{:S(2)}, u32[]{:S(2)}) collective-permute-start(bf16[128,2048]{0,1:T(8,128)(2,1)S(1)} %bitcast.133), channel_id=1, source_target_pairs={{0,16},{8,24},{16,0},{24,8},{1,17},{9,25},{17,1},{25,9},{2,18},{10... | collective-permute-start | bytes 1572872 | tf_op jit(solution)/shard_map/ppermute | solution.py:118
  64.3 2.8 %constant_dynamic-update-slice_fusion.5 = bf16[2048,2048]{1,0:T(8,128)(2,1)S(1)} fusion(bf16[2048,1024]{1,0:T(8,128)(2,1)} %param.9), kind=kLoop, calls=%fused_computation.118 | loop fusion | bytes 8388608
  67.1 7.6 %collective-permute-done.17 = bf16[128,2048]{0,1:T(8,128)(2,1)S(1)} collective-permute-done((bf16[128,2048]{0,1:T(8,128)(2,1)S(1)}, bf16[128,2048]{0,1:T(8,128)(2,1)S(1)}, u32[]{:S(2)}, u32[]{:S(2)}) %collective-permute-start.17) | collective-permute-done | bytes 524320 | tf_op jit(solution)/shard_map/ppermute | solution.py:117
  75.0 2.1 %collective-permute-start.22 = (bf16[64,2048]{0,1:T(8,128)(2,1)S(1)}, bf16[64,2048]{0,1:T(8,128)(2,1)S(1)}, u32[]{:S(2)}, u32[]{:S(2)}) collective-permute-start(bf16[64,2048]{0,1:T(8,128)(2,1)S(1)} %slice.75), channel_id=1, source_target_pairs={{0,16},{8,24},{16,0},{24,8},{1,17},{9,25},{17,1},{25,9},{2,18},{10... | collective-permute-start | bytes 786440 | tf_op jit(solution)/shard_map/ppermute | solution.py:122
  78.6 2.6 %constant_dynamic-update-slice_fusion.4 = bf16[2048,2048]{1,0:T(8,128)(2,1)S(1)} fusion(bf16[2048,2048]{1,0:T(8,128)(2,1)S(1)} %constant_dynamic-update-slice_fusion.5, bf16[2048,1024]{1,0:T(8,128)(2,1)} %collective-permute-done.16), kind=kLoop, calls=%fused_computation.117 | loop fusion | bytes 8388608 | tf_op jit(solution)/shard_map/concatenate | solution.py:183
  82.5 6.0 %collective-permute-done.22 = bf16[64,2048]{0,1:T(8,128)(2,1)S(1)} collective-permute-done((bf16[64,2048]{0,1:T(8,128)(2,1)S(1)}, bf16[64,2048]{0,1:T(8,128)(2,1)S(1)}, u32[]{:S(2)}, u32[]{:S(2)}) %collective-permute-start.22) | collective-permute-done | bytes 262176 | tf_op jit(solution)/shard_map/ppermute | solution.py:122
  98.5 2.0 %collective-permute-done.23 = bf16[64,2048]{1,0:T(8,128)(2,1)S(1)} collective-permute-done((bf16[64,2048]{1,0:T(8,128)(2,1)S(1)}, bf16[64,2048]{1,0:T(8,128)(2,1)S(1)}, u32[]{:S(2)}, u32[]{:S(2)}) %collective-permute-start.23) | collective-permute-done | bytes 262176 | tf_op jit(solution)/shard_map/ppermute | solution.py:195
  102.5 9.3 %collective-permute-done.18 = bf16[128,2048]{1,0:T(8,128)(2,1)S(1)} collective-permute-done((bf16[128,2048]{1,0:T(8,128)(2,1)S(1)}, bf16[128,2048]{1,0:T(8,128)(2,1)S(1)}, u32[]{:S(2)}, u32[]{:S(2)}) %collective-permute-start.18) | collective-permute-done | bytes 524320 | tf_op jit(solution)/shard_map/ppermute | solution.py:202
  113.0 3.1 %collective-permute-done.24 = bf16[64,2048]{1,0:T(8,128)(2,1)S(1)} collective-permute-done((bf16[64,2048]{1,0:T(8,128)(2,1)S(1)}, bf16[64,2048]{1,0:T(8,128)(2,1)S(1)}, u32[]{:S(2)}, u32[]{:S(2)}) %collective-permute-start.24) | collective-permute-done | bytes 262176 | tf_op jit(solution)/shard_map/ppermute | solution.py:194
  117.6 43.7 %reduce-scatter.2.cloned.1.call-done = bf16[128,2048]{1,0:T(8,128)(2,1)} async-done(((bf16[128,8192]{1,0:T(8,128)(2,1)}), bf16[128,2048]{1,0:T(8,128)(2,1)}) %reduce-scatter.2.cloned.1.call-update) | async-done | bytes 524304 | tf_op jit(solution)/shard_map/reduce_scatter | solution.py:207
  161.3 2.0 %add_convert_fusion = bf16[128,2048]{1,0:T(8,128)(2,1)} fusion(bf16[128,2048]{1,0:T(8,128)(2,1)} %reduce-scatter.2.cloned.1.call-done, bf16[128,2048]{1,0:T(8,128)(2,1)S(1)} %copy-done.2), kind=kLoop, calls=%fused_computation.32 | loop fusion | flops 1048576 | bytes 1572864 | tf_op jit(solution)/shard_map/convert_element_type | solution.py:208
  (102 shorter events, 35.1 us)
Async XLA Ops:
  6.5 154.8 %reduce-scatter.2.cloned.1.call-start = ((), (), s32[]{:S(2)}) async-start(), calls=%async_computation.1 | async-start | bytes 2621440 | tf_op jit(solution)/shard_map/reduce_scatter | solution.py:207
  8.2 15.9 %collective-permute-start.3 = (bf16[16,128,128]{2,1,0:T(8,128)(2,1)S(1)}, bf16[16,128,128]{2,1,0:T(8,128)(2,1)}, u32[]{:S(2)}, u32[]{:S(2)}) collective-permute-start(bf16[16,128,128]{2,1,0:T(8,128)(2,1)S(1)} %bitcast.135), channel_id=1, source_target_pairs={{0,16},{8,24},{16,0},{24,8},{1,17},{9,25},{17,1},{25,9},{2,18},{10... | collective-permute-start | bytes 1572872 | tf_op jit(solution)/shard_map/ppermute | solution.py:71
  11.3 15.9 %collective-permute-start.1 = (bf16[16,128,128]{2,1,0:T(8,128)(2,1)S(1)}, bf16[16,128,128]{2,1,0:T(8,128)(2,1)S(1)}, u32[]{:S(2)}, u32[]{:S(2)}) collective-permute-start(bf16[16,128,128]{2,1,0:T(8,128)(2,1)S(1)} %bitcast.136), channel_id=1, source_target_pairs={{0,8},{8,0},{16,24},{24,16},{1,9},{9,1},{17,25},{25,17},{2,10},{10... | collective-permute-start | bytes 1572872 | tf_op jit(solution)/shard_map/ppermute | solution.py:70
  12.8 25.6 %collective-permute-start = (bf16[16,128,128]{2,1,0:T(8,128)(2,1)S(1)}, bf16[16,128,128]{2,1,0:T(8,128)(2,1)}, u32[]{:S(2)}, u32[]{:S(2)}) collective-permute-start(bf16[16,128,128]{2,1,0:T(8,128)(2,1)S(1)} %bitcast.137), channel_id=1, source_target_pairs={{0,4},{4,0},{1,5},{5,1},{2,6},{6,2},{3,7},{7,3},{8,12},{12,8},{9,1... | collective-permute-start | bytes 1572872 | tf_op jit(solution)/shard_map/ppermute | solution.py:82
  13.0 41.8 %collective-permute-start.8 = (bf16[16,128,128]{1,2,0:T(8,128)(2,1)S(1)}, bf16[16,128,128]{1,2,0:T(8,128)(2,1)S(1)}, u32[]{:S(2)}, u32[]{:S(2)}) collective-permute-start(bf16[16,128,128]{1,2,0:T(8,128)(2,1)S(1)} %bitcast.126), channel_id=1, source_target_pairs={{0,4},{4,0},{1,5},{5,1},{2,6},{6,2},{3,7},{7,3},{8,12},{12,8},{9,1... | collective-permute-start | bytes 1572872 | tf_op jit(solution)/shard_map/ppermute | solution.py:82
  13.6 20.8 %collective-permute-start.11 = (bf16[16,128,128]{1,2,0:T(8,128)(2,1)S(1)}, bf16[16,128,128]{1,2,0:T(8,128)(2,1)S(1)}, u32[]{:S(2)}, u32[]{:S(2)}) collective-permute-start(bf16[16,128,128]{1,2,0:T(8,128)(2,1)S(1)} %bitcast.127), channel_id=1, source_target_pairs={{0,16},{8,24},{16,0},{24,8},{1,17},{9,25},{17,1},{25,9},{2,18},{10... | collective-permute-start | bytes 1572872 | tf_op jit(solution)/shard_map/ppermute | solution.py:71
  24.1 17.5 %collective-permute-start.9 = (bf16[16,128,128]{1,2,0:T(8,128)(2,1)S(1)}, bf16[16,128,128]{1,2,0:T(8,128)(2,1)S(1)}, u32[]{:S(2)}, u32[]{:S(2)}) collective-permute-start(bf16[16,128,128]{1,2,0:T(8,128)(2,1)S(1)} %bitcast.128), channel_id=1, source_target_pairs={{0,8},{8,0},{16,24},{24,16},{1,9},{9,1},{17,25},{25,17},{2,10},{10... | collective-permute-start | bytes 1572872 | tf_op jit(solution)/shard_map/ppermute | solution.py:70
  27.1 17.1 %collective-permute-start.5 = (bf16[8,128,128]{2,1,0:T(8,128)(2,1)S(1)}, bf16[8,128,128]{2,1,0:T(8,128)(2,1)S(1)}, u32[]{:S(2)}, u32[]{:S(2)}) collective-permute-start(bf16[8,128,128]{2,1,0:T(8,128)(2,1)S(1)} %slice.64), channel_id=1, source_target_pairs={{0,8},{8,0},{16,24},{24,16},{1,9},{9,1},{17,25},{25,17},{2,10},{10... | collective-permute-start | bytes 786440 | tf_op jit(solution)/shard_map/ppermute | solution.py:74
  34.4 13.2 %collective-permute-start.6 = (bf16[8,128,128]{2,1,0:T(8,128)(2,1)S(1)}, bf16[8,128,128]{2,1,0:T(8,128)(2,1)S(1)}, u32[]{:S(2)}, u32[]{:S(2)}) collective-permute-start(bf16[8,128,128]{2,1,0:T(8,128)(2,1)S(1)} %slice.65), channel_id=1, source_target_pairs={{0,16},{8,24},{16,0},{24,8},{1,17},{9,25},{17,1},{25,9},{2,18},{10... | collective-permute-start | bytes 786440 | tf_op jit(solution)/shard_map/ppermute | solution.py:75
  38.4 9.2 %collective-permute-start.13 = (bf16[8,128,128]{1,2,0:T(8,128)(2,1)S(1)}, bf16[8,128,128]{1,2,0:T(8,128)(2,1)S(1)}, u32[]{:S(2)}, u32[]{:S(2)}) collective-permute-start(bf16[8,128,128]{1,2,0:T(8,128)(2,1)S(1)} %slice.66), channel_id=1, source_target_pairs={{0,8},{8,0},{16,24},{24,16},{1,9},{9,1},{17,25},{25,17},{2,10},{10... | collective-permute-start | bytes 786440 | tf_op jit(solution)/shard_map/ppermute | solution.py:74
  41.6 37.0 %collective-permute-start.16 = (bf16[2048,1024]{1,0:T(8,128)(2,1)}, bf16[2048,1024]{1,0:T(8,128)(2,1)}, u32[]{:S(2)}, u32[]{:S(2)}) collective-permute-start(bf16[2048,1024]{1,0:T(8,128)(2,1)} %param.9), channel_id=1, source_target_pairs={{0,4},{4,0},{1,5},{5,1},{2,6},{6,2},{3,7},{7,3},{8,12},{12,8},{9,1... | collective-permute-start | bytes 12582920 | tf_op jit(solution)/shard_map/ppermute | solution.py:184
  44.2 6.4 %collective-permute-start.14 = (bf16[8,128,128]{1,2,0:T(8,128)(2,1)S(1)}, bf16[8,128,128]{1,2,0:T(8,128)(2,1)S(1)}, u32[]{:S(2)}, u32[]{:S(2)}) collective-permute-start(bf16[8,128,128]{1,2,0:T(8,128)(2,1)S(1)} %slice.67), channel_id=1, source_target_pairs={{0,16},{8,24},{16,0},{24,8},{1,17},{9,25},{17,1},{25,9},{2,18},{10... | collective-permute-start | bytes 786440 | tf_op jit(solution)/shard_map/ppermute | solution.py:75
  50.6 8.9 %collective-permute-start.10 = (bf16[16,128,128]{1,2,0:T(8,128)(2,1)S(1)}, bf16[16,128,128]{1,2,0:T(8,128)(2,1)S(1)}, u32[]{:S(2)}, u32[]{:S(2)}) collective-permute-start(bf16[16,128,128]{1,2,0:T(8,128)(2,1)S(1)} %collective-permute-done.9), channel_id=1, source_target_pairs={{0,4},{4,0},{1,5},{5,1},{2,6},{6,2},{3,7},{7,3},{8,12},{12,8},{9,1... | collective-permute-start | bytes 1572872 | tf_op jit(solution)/shard_map/ppermute | solution.py:82
  52.3 7.8 %collective-permute-start.12 = (bf16[16,128,128]{1,2,0:T(8,128)(2,1)S(1)}, bf16[16,128,128]{1,2,0:T(8,128)(2,1)S(1)}, u32[]{:S(2)}, u32[]{:S(2)}) collective-permute-start(bf16[16,128,128]{1,2,0:T(8,128)(2,1)S(1)} %collective-permute-done.11), channel_id=1, source_target_pairs={{0,4},{4,0},{1,5},{5,1},{2,6},{6,2},{3,7},{7,3},{8,12},{12,8},{9,1... | collective-permute-start | bytes 1572872 | tf_op jit(solution)/shard_map/ppermute | solution.py:82
  60.7 14.0 %collective-permute-start.17 = (bf16[128,2048]{0,1:T(8,128)(2,1)S(1)}, bf16[128,2048]{0,1:T(8,128)(2,1)S(1)}, u32[]{:S(2)}, u32[]{:S(2)}) collective-permute-start(bf16[128,2048]{0,1:T(8,128)(2,1)S(1)} %bitcast.132), channel_id=1, source_target_pairs={{0,8},{8,0},{16,24},{24,16},{1,9},{9,1},{17,25},{25,17},{2,10},{10... | collective-permute-start | bytes 1572872 | tf_op jit(solution)/shard_map/ppermute | solution.py:117
  62.3 14.8 %collective-permute-start.19 = (bf16[128,2048]{0,1:T(8,128)(2,1)S(1)}, bf16[128,2048]{0,1:T(8,128)(2,1)S(1)}, u32[]{:S(2)}, u32[]{:S(2)}) collective-permute-start(bf16[128,2048]{0,1:T(8,128)(2,1)S(1)} %bitcast.133), channel_id=1, source_target_pairs={{0,16},{8,24},{16,0},{24,8},{1,17},{9,25},{17,1},{25,9},{2,18},{10... | collective-permute-start | bytes 1572872 | tf_op jit(solution)/shard_map/ppermute | solution.py:118
  75.0 13.5 %collective-permute-start.22 = (bf16[64,2048]{0,1:T(8,128)(2,1)S(1)}, bf16[64,2048]{0,1:T(8,128)(2,1)S(1)}, u32[]{:S(2)}, u32[]{:S(2)}) collective-permute-start(bf16[64,2048]{0,1:T(8,128)(2,1)S(1)} %slice.75), channel_id=1, source_target_pairs={{0,16},{8,24},{16,0},{24,8},{1,17},{9,25},{17,1},{25,9},{2,18},{10... | collective-permute-start | bytes 786440 | tf_op jit(solution)/shard_map/ppermute | solution.py:122
  77.1 12.9 %collective-permute-start.21 = (bf16[64,2048]{0,1:T(8,128)(2,1)S(1)}, bf16[64,2048]{0,1:T(8,128)(2,1)S(1)}, u32[]{:S(2)}, u32[]{:S(2)}) collective-permute-start(bf16[64,2048]{0,1:T(8,128)(2,1)S(1)} %bitcast.131), channel_id=1, source_target_pairs={{0,8},{8,0},{16,24},{24,16},{1,9},{9,1},{17,25},{25,17},{2,10},{10... | collective-permute-start | bytes 786440 | tf_op jit(solution)/shard_map/ppermute | solution.py:121
  91.4 9.2 %collective-permute-start.23 = (bf16[64,2048]{1,0:T(8,128)(2,1)S(1)}, bf16[64,2048]{1,0:T(8,128)(2,1)S(1)}, u32[]{:S(2)}, u32[]{:S(2)}) collective-permute-start(bf16[64,2048]{1,0:T(8,128)(2,1)S(1)} %get-tuple-element.14), channel_id=1, source_target_pairs={{0,8},{8,0},{16,24},{24,16},{1,9},{9,1},{17,25},{25,17},{2,10},{10... | collective-permute-start | bytes 786440 | tf_op jit(solution)/shard_map/ppermute | solution.py:195
  92.9 8.8 %collective-permute-start.25 = (bf16[64,2048]{1,0:T(8,128)(2,1)S(1)}, bf16[64,2048]{1,0:T(8,128)(2,1)S(1)}, u32[]{:S(2)}, u32[]{:S(2)}) collective-permute-start(bf16[64,2048]{1,0:T(8,128)(2,1)S(1)} %get-tuple-element.13), channel_id=1, source_target_pairs={{0,16},{8,24},{16,0},{24,8},{1,17},{9,25},{17,1},{25,9},{2,18},{10... | collective-permute-start | bytes 786440 | tf_op jit(solution)/shard_map/ppermute | solution.py:198
  94.6 17.2 %collective-permute-start.18 = (bf16[128,2048]{1,0:T(8,128)(2,1)S(1)}, bf16[128,2048]{1,0:T(8,128)(2,1)S(1)}, u32[]{:S(2)}, u32[]{:S(2)}) collective-permute-start(bf16[128,2048]{1,0:T(8,128)(2,1)S(1)} %convolution_convert_fusion.2), channel_id=1, source_target_pairs={{0,8},{8,0},{16,24},{24,16},{1,9},{9,1},{17,25},{25,17},{2,10},{10... | collective-permute-start | bytes 1572872 | tf_op jit(solution)/shard_map/ppermute | solution.py:202
  97.0 15.9 %collective-permute-start.20 = (bf16[128,2048]{1,0:T(8,128)(2,1)S(1)}, bf16[128,2048]{1,0:T(8,128)(2,1)S(1)}, u32[]{:S(2)}, u32[]{:S(2)}) collective-permute-start(bf16[128,2048]{1,0:T(8,128)(2,1)S(1)} %convolution_convert_fusion.1), channel_id=1, source_target_pairs={{0,16},{8,24},{16,0},{24,8},{1,17},{9,25},{17,1},{25,9},{2,18},{10... | collective-permute-start | bytes 1572872 | tf_op jit(solution)/shard_map/ppermute | solution.py:202
  100.5 15.6 %collective-permute-start.24 = (bf16[64,2048]{1,0:T(8,128)(2,1)S(1)}, bf16[64,2048]{1,0:T(8,128)(2,1)S(1)}, u32[]{:S(2)}, u32[]{:S(2)}) collective-permute-start(bf16[64,2048]{1,0:T(8,128)(2,1)S(1)} %collective-permute-done.23), channel_id=1, source_target_pairs={{0,16},{8,24},{16,0},{24,8},{1,17},{9,25},{17,1},{25,9},{2,18},{10... | collective-permute-start | bytes 786440 | tf_op jit(solution)/shard_map/ppermute | solution.py:194
  101.7 14.4 %collective-permute-start.26 = (bf16[64,2048]{1,0:T(8,128)(2,1)S(1)}, bf16[64,2048]{1,0:T(8,128)(2,1)S(1)}, u32[]{:S(2)}, u32[]{:S(2)}) collective-permute-start(bf16[64,2048]{1,0:T(8,128)(2,1)S(1)} %collective-permute-done.25), channel_id=1, source_target_pairs={{0,8},{8,0},{16,24},{24,16},{1,9},{9,1},{17,25},{25,17},{2,10},{10... | collective-permute-start | bytes 786440 | tf_op jit(solution)/shard_map/ppermute | solution.py:197
  (8 other events, 80.5 us)
Sparse Core Ops, SparseCore 0:
  117.7 43.5 reduce-scatter.1

commit v17 on v10

--- a/solution.py
+++ b/solution.py
@@ -167,7 +167,7 @@
             core = lax.axis_index("lo")
             blocks = gather_blocks_square(local_context)
             width = out_weight.shape[1]
-            by_row = jnp.zeros((seg_rows, seq_count * width), jnp.bfloat16)
+            by_row = jnp.zeros((chan_count, seg_rows, 2 * width), jnp.bfloat16)
             for b, block in enumerate(blocks):
                 r, t = b // 2, b % 2
                 partial = jnp.dot(block, out_weight, preferred_element_type=jnp.float32).astype(
@@ -177,8 +177,10 @@
                     pairs = [(h * 2 + l, (h ^ r) * 2 + (l ^ t)) for h in range(4) for l in range(2)]
                     partial = lax.ppermute(partial, SEQ, pairs)
                 source = (chip ^ r) * 2 + (core ^ t)
-                by_row = lax.dynamic_update_slice(by_row, partial, (0, source * width))
-            ordered = lax.psum_scatter(by_row, "chan", scatter_dimension=1, tiled=True)
+                by_row = lax.dynamic_update_slice(
+                    by_row, partial[None], (source // 2, 0, (source % 2) * width)
+                )
+            ordered = lax.psum_scatter(by_row, "chan", scatter_dimension=0, tiled=True)[0]
             return (residual.astype(jnp.float32) + ordered.astype(jnp.float32)).astype(jnp.bfloat16)
         gathered = gather_seq(local_context)
         group = seq_count // chan_count

time: 168 us -> 167 us (level)
  waiting for transfers between devices: 93.8 us -> 97 us
  matrix products: 23.9 us -> 21.7 us
    dot_general x8, matrix products: 8.56 us -> 6.48 us  [attention_by_head(): jnp.einsum('hqd,hkd->hqk', queries, keys, preferred_element_type=jnp.floa...]
    ppermute x3, waiting for transfers between devices: 13.3 us -> 15.2 us  [gather_blocks_square(): from_y = lax.ppermute(x, 'hi', swap('hi', 2, 4))]
  transfers between devices with their start and end apart: 32 -> 32, of which waited for: 16 -> 15; matrix products, arithmetic and copies ran while one was open for 18% -> 16% of each run, Pallas kernels for 0% -> 0%
where the time goes in v17:
time: 167 us
  waiting for transfers between devices  97 us (58%)
  starting transfers between devices  22.4 us (13%)
  matrix products  21.7 us (13%)
  between operations  14.1 us (8%)
  local copies, waits for them, and re-layouts  6.65 us (4%)
  other arithmetic  5.17 us (3%)
    reduce_scatter x1, waiting for transfers between devices, per_device(): lax.psum_scatter(by_row, 'chan', scatter_dimension=0, tiled=True)[0]  46.1 us
    ppermute x3, waiting for transfers between devices, gather_blocks_square(): from_y = lax.ppermute(x, 'hi', swap('hi', 2, 4))  15.2 us
    ppermute x7, waiting for transfers between devices, per_device(): partial = lax.ppermute(partial, SEQ, pairs)  12.8 us
    dot_general x8, matrix products, per_device(): jnp.dot(block, out_weight, preferred_element_type=jnp.float32)  10.6 us
    ppermute x3, waiting for transfers between devices, gather_blocks_square(): from_x = lax.ppermute(x, 'hi', swap('hi', 1, 4))  10.6 us
    dot_general x8, matrix products, attention_by_head(): jnp.einsum('hqd,hkd->hqk', queries, keys, preferred_element_type=jnp.floa...  6.48 us
    ppermute x7, starting transfers between devices, per_device(): partial = lax.ppermute(partial, SEQ, pairs)  6.29 us
    ppermute x3, waiting for transfers between devices, gather_blocks_square(): lax.ppermute(from_x[half:], 'hi', swap('hi', 2, 4))  6.19 us
  transfers between devices with their start and end apart: 32, of which 15 were waited for; matrix products, arithmetic and copies ran while one was open for 16% of the time, Pallas kernels for 0%

profile of v17, /device:TPU:0, one launch (start us, length us, event | category | flops | bytes accessed | tf_op | source)
XLA Modules:
  0.0 167.0 jit_solution(6188290661574599931)
XLA Ops:
  8.2 3.0 %collective-permute-start.3 = (bf16[16,128,128]{2,1,0:T(8,128)(2,1)S(1)}, bf16[16,128,128]{2,1,0:T(8,128)(2,1)}, u32[]{:S(2)}, u32[]{:S(2)}) collective-permute-start(bf16[16,128,128]{2,1,0:T(8,128)(2,1)S(1)} %bitcast.161), channel_id=1, source_target_pairs={{0,16},{8,24},{16,0},{24,8},{1,17},{9,25},{17,1},{25,9},{2,18},{10... | collective-permute-start | bytes 1572872 | tf_op jit(solution)/shard_map/ppermute | solution.py:71
  11.2 1.5 collective-permute-start.1
  16.1 8.0 %collective-permute-done.3 = bf16[16,128,128]{2,1,0:T(8,128)(2,1)} collective-permute-done((bf16[16,128,128]{2,1,0:T(8,128)(2,1)S(1)}, bf16[16,128,128]{2,1,0:T(8,128)(2,1)}, u32[]{:S(2)}, u32[]{:S(2)}) %collective-permute-start.3) | collective-permute-done | bytes 524320 | tf_op jit(solution)/shard_map/ppermute | solution.py:71
  26.1 1.5 collective-permute-start.5
  27.6 6.8 %collective-permute-done.11 = bf16[16,128,128]{1,2,0:T(8,128)(2,1)S(1)} collective-permute-done((bf16[16,128,128]{1,2,0:T(8,128)(2,1)S(1)}, bf16[16,128,128]{1,2,0:T(8,128)(2,1)S(1)}, u32[]{:S(2)}, u32[]{:S(2)}) %collective-permute-start.11) | collective-permute-done | bytes 524320 | tf_op jit(solution)/shard_map/ppermute | solution.py:71
  34.4 1.7 %collective-permute-start.6 = (bf16[8,128,128]{2,1,0:T(8,128)(2,1)S(1)}, bf16[8,128,128]{2,1,0:T(8,128)(2,1)S(1)}, u32[]{:S(2)}, u32[]{:S(2)}) collective-permute-start(bf16[8,128,128]{2,1,0:T(8,128)(2,1)S(1)} %slice.25), channel_id=1, source_target_pairs={{0,16},{8,24},{16,0},{24,8},{1,17},{9,25},{17,1},{25,9},{2,18},{10... | collective-permute-start | bytes 786440 | tf_op jit(solution)/shard_map/ppermute | solution.py:75
  37.3 1.5 collective-permute-start.13
  38.8 1.6 fusion.91
  41.6 1.6 fusion.95
  43.4 3.7 %collective-permute-done.13 = bf16[8,128,128]{1,2,0:T(8,128)(2,1)S(1)} collective-permute-done((bf16[8,128,128]{1,2,0:T(8,128)(2,1)S(1)}, bf16[8,128,128]{1,2,0:T(8,128)(2,1)S(1)}, u32[]{:S(2)}, u32[]{:S(2)}) %collective-permute-start.13) | collective-permute-done | bytes 262176 | tf_op jit(solution)/shard_map/ppermute | solution.py:74
  52.4 2.1 %fusion.21 = (f32[16,128]{1,0:T(8,128)S(1)}, f32[16,128]{1,0:T(8,128)S(1)}, f32[16,128]{1,0:T(8,128)S(1)}, f32[16,128]{1,0:T(8,128)S(1)}, f32[16,128]{1,0:T(8,128)S(1)}) fusion(f32[16,128,128]{2,1,0:T(8,128)S(1)} %get-tuple-element.36, f32[16,128]{1,0:T(8,128)S(1)} %maximum_maximum_fusion, pred[128,128]{1,0:T(8,128)(4,1)S(1)} %copy.41, ...), kind=kLoop, calls=%fused_computation.50 | loop fusion | flops 3921920 | bytes 5373952 | tf_op jit(solution)/shard_map/reduce_sum | solution.py:106
  57.8 1.4 fusion.15
  59.2 1.5 collective-permute-start.18
  61.6 3.3 %fusion.17 = bf16[4,128,2048]{2,1,0:T(8,128)(2,1)S(1)} fusion(bf16[4,128,2048]{2,1,0:T(8,128)(2,1)S(1)} %broadcast_in_dim.148, s32[]{:T(128)S(6)} %select_n.174, s32[]{:T(128)S(6)} %select_n.176, bf16[128,2048]{0,1:T(8,128)(2,1)} %bitcast.10, bf16[2048,1024]{1,0:T(8,128)(2,1)} %param.9), kind=kOutput, calls=%fused_computation.37 | convolution fusion | flops 537001984 | bytes 4980744 | tf_op jit(solution)/shard_map/dot_general | solution.py:173
  64.9 8.4 %collective-permute-done.18 = bf16[128,2048]{0,1:T(8,128)(2,1)S(1)} collective-permute-done((bf16[128,2048]{0,1:T(8,128)(2,1)}, bf16[128,2048]{0,1:T(8,128)(2,1)S(1)}, u32[]{:S(2)}, u32[]{:S(2)}) %collective-permute-start.18) | collective-permute-done | bytes 524320 | tf_op jit(solution)/shard_map/ppermute | solution.py:70
  75.7 1.8 %convolution_convert_fusion.6 = bf16[128,1024]{1,0:T(8,128)(2,1)S(1)} fusion(bf16[128,2048]{0,1:T(8,128)(2,1)} %collective-permute-done.16, bf16[2048,1024]{1,0:T(8,128)(2,1)S(1)} %copy-done.1), kind=kOutput, calls=%fused_computation.34 | convolution fusion | flops 537001984 | bytes 4980736 | tf_op jit(solution)/shard_map/dot_general | solution.py:173
  79.4 1.8 %convolution_convert_fusion.3 = bf16[128,1024]{1,0:T(8,128)(2,1)S(1)} fusion(bf16[128,2048]{0,1:T(8,128)(2,1)} %collective-permute-done.22, bf16[2048,1024]{1,0:T(8,128)(2,1)S(1)} %copy-done.1), kind=kOutput, calls=%fused_computation.31 | convolution fusion | flops 537001984 | bytes 4980736 | tf_op jit(solution)/shard_map/dot_general | solution.py:173
  82.3 6.2 %collective-permute-done.27 = bf16[64,2048]{0,1:T(8,128)(2,1)S(1)} collective-permute-done((bf16[64,2048]{0,1:T(8,128)(2,1)S(1)}, bf16[64,2048]{0,1:T(8,128)(2,1)S(1)}, u32[]{:S(2)}, u32[]{:S(2)}) %collective-permute-start.27) | collective-permute-done | bytes 262176 | tf_op jit(solution)/shard_map/ppermute | solution.py:75
  91.4 1.9 %collective-permute-done.19 = bf16[128,1024]{1,0:T(8,128)(2,1)S(1)} collective-permute-done((bf16[128,1024]{1,0:T(8,128)(2,1)S(1)}, bf16[128,1024]{1,0:T(8,128)(2,1)S(1)}, u32[]{:S(2)}, u32[]{:S(2)}) %collective-permute-start.19) | collective-permute-done | bytes 262176 | tf_op jit(solution)/shard_map/ppermute | solution.py:178
  93.3 2.1 %collective-permute-start.28 = (bf16[128,1024]{1,0:T(8,128)(2,1)S(1)}, bf16[128,1024]{1,0:T(8,128)(2,1)S(1)}, u32[]{:S(2)}, u32[]{:S(2)}) collective-permute-start(bf16[128,1024]{1,0:T(8,128)(2,1)S(1)} %convolution_convert_fusion.1), channel_id=1, source_target_pairs={{0,24},{4,28},{8,16},{12,20},{16,8},{20,12},{24,0},{28,4},{1,25},{... | collective-permute-start | bytes 786440 | tf_op jit(solution)/shard_map/ppermute | solution.py:178
  99.7 7.3 %collective-permute-done.21 = bf16[128,1024]{1,0:T(8,128)(2,1)S(1)} collective-permute-done((bf16[128,1024]{1,0:T(8,128)(2,1)S(1)}, bf16[128,1024]{1,0:T(8,128)(2,1)S(1)}, u32[]{:S(2)}, u32[]{:S(2)}) %collective-permute-start.21) | collective-permute-done | bytes 262176 | tf_op jit(solution)/shard_map/ppermute | solution.py:178
  107.4 3.3 %collective-permute-done.30 = bf16[128,1024]{1,0:T(8,128)(2,1)S(1)} collective-permute-done((bf16[128,1024]{1,0:T(8,128)(2,1)S(1)}, bf16[128,1024]{1,0:T(8,128)(2,1)S(1)}, u32[]{:S(2)}, u32[]{:S(2)}) %collective-permute-start.30) | collective-permute-done | bytes 262176 | tf_op jit(solution)/shard_map/ppermute | solution.py:178
  112.1 46.1 %reduce-scatter.2.cloned.1.call-done = bf16[1,128,2048]{2,1,0:T(8,128)(2,1)} async-done(((bf16[4,128,2048]{2,1,0:T(8,128)(2,1)}), bf16[1,128,2048]{2,1,0:T(8,128)(2,1)}) %reduce-scatter.2.cloned.1.call-update) | async-done | bytes 524304 | tf_op jit(solution)/shard_map/reduce_scatter | solution.py:183
  158.2 2.0 %fusion.18 = bf16[128,2048]{1,0:T(8,128)(2,1)} fusion(bf16[128,2048]{1,0:T(8,128)(2,1)S(1)} %copy-done.3, bf16[1,128,2048]{2,1,0:T(8,128)(2,1)} %reduce-scatter.2.cloned.1.call-done), kind=kLoop, calls=%fused_computation.39 | loop fusion | flops 1048576 | bytes 1572864 | tf_op jit(solution)/shard_map/convert_element_type | solution.py:184
  (109 shorter events, 32.8 us)
Async XLA Ops:
  6.5 151.6 %reduce-scatter.2.cloned.1.call-start = ((), (), s32[]{:S(2)}) async-start(), calls=%async_computation.1 | async-start | bytes 2621440 | tf_op jit(solution)/shard_map/reduce_scatter | solution.py:183
  8.2 15.9 %collective-permute-start.3 = (bf16[16,128,128]{2,1,0:T(8,128)(2,1)S(1)}, bf16[16,128,128]{2,1,0:T(8,128)(2,1)}, u32[]{:S(2)}, u32[]{:S(2)}) collective-permute-start(bf16[16,128,128]{2,1,0:T(8,128)(2,1)S(1)} %bitcast.161), channel_id=1, source_target_pairs={{0,16},{8,24},{16,0},{24,8},{1,17},{9,25},{17,1},{25,9},{2,18},{10... | collective-permute-start | bytes 1572872 | tf_op jit(solution)/shard_map/ppermute | solution.py:71
  11.2 14.8 %collective-permute-start.1 = (bf16[16,128,128]{2,1,0:T(8,128)(2,1)S(1)}, bf16[16,128,128]{2,1,0:T(8,128)(2,1)S(1)}, u32[]{:S(2)}, u32[]{:S(2)}) collective-permute-start(bf16[16,128,128]{2,1,0:T(8,128)(2,1)S(1)} %bitcast.162), channel_id=1, source_target_pairs={{0,8},{8,0},{16,24},{24,16},{1,9},{9,1},{17,25},{25,17},{2,10},{10... | collective-permute-start | bytes 1572872 | tf_op jit(solution)/shard_map/ppermute | solution.py:70
  12.7 28.3 %collective-permute-start = (bf16[16,128,128]{2,1,0:T(8,128)(2,1)S(1)}, bf16[16,128,128]{2,1,0:T(8,128)(2,1)}, u32[]{:S(2)}, u32[]{:S(2)}) collective-permute-start(bf16[16,128,128]{2,1,0:T(8,128)(2,1)S(1)} %bitcast.163), channel_id=1, source_target_pairs={{0,4},{4,0},{1,5},{5,1},{2,6},{6,2},{3,7},{7,3},{8,12},{12,8},{9,1... | collective-permute-start | bytes 1572872 | tf_op jit(solution)/shard_map/ppermute | solution.py:82
  14.0 23.3 %collective-permute-start.9 = (bf16[16,128,128]{1,2,0:T(8,128)(2,1)S(1)}, bf16[16,128,128]{1,2,0:T(8,128)(2,1)S(1)}, u32[]{:S(2)}, u32[]{:S(2)}) collective-permute-start(bf16[16,128,128]{1,2,0:T(8,128)(2,1)S(1)} %bitcast.156), channel_id=1, source_target_pairs={{0,8},{8,0},{16,24},{24,16},{1,9},{9,1},{17,25},{25,17},{2,10},{10... | collective-permute-start | bytes 1572872 | tf_op jit(solution)/shard_map/ppermute | solution.py:70
  14.6 19.7 %collective-permute-start.11 = (bf16[16,128,128]{1,2,0:T(8,128)(2,1)S(1)}, bf16[16,128,128]{1,2,0:T(8,128)(2,1)S(1)}, u32[]{:S(2)}, u32[]{:S(2)}) collective-permute-start(bf16[16,128,128]{1,2,0:T(8,128)(2,1)S(1)} %bitcast.157), channel_id=1, source_target_pairs={{0,16},{8,24},{16,0},{24,8},{1,17},{9,25},{17,1},{25,9},{2,18},{10... | collective-permute-start | bytes 1572872 | tf_op jit(solution)/shard_map/ppermute | solution.py:71
  24.1 30.4 %collective-permute-start.8 = (bf16[16,128,128]{1,2,0:T(8,128)(2,1)S(1)}, bf16[16,128,128]{1,2,0:T(8,128)(2,1)S(1)}, u32[]{:S(2)}, u32[]{:S(2)}) collective-permute-start(bf16[16,128,128]{1,2,0:T(8,128)(2,1)S(1)} %bitcast.158), channel_id=1, source_target_pairs={{0,4},{4,0},{1,5},{5,1},{2,6},{6,2},{3,7},{7,3},{8,12},{12,8},{9,1... | collective-permute-start | bytes 1572872 | tf_op jit(solution)/shard_map/ppermute | solution.py:82
  26.1 17.2 %collective-permute-start.5 = (bf16[8,128,128]{2,1,0:T(8,128)(2,1)S(1)}, bf16[8,128,128]{2,1,0:T(8,128)(2,1)S(1)}, u32[]{:S(2)}, u32[]{:S(2)}) collective-permute-start(bf16[8,128,128]{2,1,0:T(8,128)(2,1)S(1)} %slice.24), channel_id=1, source_target_pairs={{0,8},{8,0},{16,24},{24,16},{1,9},{9,1},{17,25},{25,17},{2,10},{10... | collective-permute-start | bytes 786440 | tf_op jit(solution)/shard_map/ppermute | solution.py:74
  34.4 12.7 %collective-permute-start.6 = (bf16[8,128,128]{2,1,0:T(8,128)(2,1)S(1)}, bf16[8,128,128]{2,1,0:T(8,128)(2,1)S(1)}, u32[]{:S(2)}, u32[]{:S(2)}) collective-permute-start(bf16[8,128,128]{2,1,0:T(8,128)(2,1)S(1)} %slice.25), channel_id=1, source_target_pairs={{0,16},{8,24},{16,0},{24,8},{1,17},{9,25},{17,1},{25,9},{2,18},{10... | collective-permute-start | bytes 786440 | tf_op jit(solution)/shard_map/ppermute | solution.py:75
  37.3 9.8 %collective-permute-start.13 = (bf16[8,128,128]{1,2,0:T(8,128)(2,1)S(1)}, bf16[8,128,128]{1,2,0:T(8,128)(2,1)S(1)}, u32[]{:S(2)}, u32[]{:S(2)}) collective-permute-start(bf16[8,128,128]{1,2,0:T(8,128)(2,1)S(1)} %slice.26), channel_id=1, source_target_pairs={{0,8},{8,0},{16,24},{24,16},{1,9},{9,1},{17,25},{25,17},{2,10},{10... | collective-permute-start | bytes 786440 | tf_op jit(solution)/shard_map/ppermute | solution.py:74
  47.1 10.0 %collective-permute-start.10 = (bf16[16,128,128]{1,2,0:T(8,128)(2,1)S(1)}, bf16[16,128,128]{1,2,0:T(8,128)(2,1)S(1)}, u32[]{:S(2)}, u32[]{:S(2)}) collective-permute-start(bf16[16,128,128]{1,2,0:T(8,128)(2,1)S(1)} %collective-permute-done.9), channel_id=1, source_target_pairs={{0,4},{4,0},{1,5},{5,1},{2,6},{6,2},{3,7},{7,3},{8,12},{12,8},{9,1... | collective-permute-start | bytes 1572872 | tf_op jit(solution)/shard_map/ppermute | solution.py:82
  47.7 10.0 %collective-permute-start.12 = (bf16[16,128,128]{1,2,0:T(8,128)(2,1)S(1)}, bf16[16,128,128]{1,2,0:T(8,128)(2,1)S(1)}, u32[]{:S(2)}, u32[]{:S(2)}) collective-permute-start(bf16[16,128,128]{1,2,0:T(8,128)(2,1)S(1)} %collective-permute-done.11), channel_id=1, source_target_pairs={{0,4},{4,0},{1,5},{5,1},{2,6},{6,2},{3,7},{7,3},{8,12},{12,8},{9,1... | collective-permute-start | bytes 1572872 | tf_op jit(solution)/shard_map/ppermute | solution.py:82
  59.2 14.2 %collective-permute-start.18 = (bf16[128,2048]{0,1:T(8,128)(2,1)}, bf16[128,2048]{0,1:T(8,128)(2,1)S(1)}, u32[]{:S(2)}, u32[]{:S(2)}) collective-permute-start(bf16[128,2048]{0,1:T(8,128)(2,1)} %bitcast.10), channel_id=1, source_target_pairs={{0,8},{8,0},{16,24},{24,16},{1,9},{9,1},{17,25},{25,17},{2,10},{10... | collective-permute-start | bytes 1572872 | tf_op jit(solution)/shard_map/ppermute | solution.py:70
  60.6 14.0 %collective-permute-start.22 = (bf16[128,2048]{0,1:T(8,128)(2,1)}, bf16[128,2048]{0,1:T(8,128)(2,1)}, u32[]{:S(2)}, u32[]{:S(2)}) collective-permute-start(bf16[128,2048]{0,1:T(8,128)(2,1)} %bitcast.10), channel_id=1, source_target_pairs={{0,16},{8,24},{16,0},{24,8},{1,17},{9,25},{17,1},{25,9},{2,18},{10... | collective-permute-start | bytes 1572872 | tf_op jit(solution)/shard_map/ppermute | solution.py:71
  61.2 14.5 %collective-permute-start.16 = (bf16[128,2048]{0,1:T(8,128)(2,1)}, bf16[128,2048]{0,1:T(8,128)(2,1)}, u32[]{:S(2)}, u32[]{:S(2)}) collective-permute-start(bf16[128,2048]{0,1:T(8,128)(2,1)} %bitcast.10), channel_id=1, source_target_pairs={{0,4},{4,0},{1,5},{5,1},{2,6},{6,2},{3,7},{7,3},{8,12},{12,8},{9,1... | collective-permute-start | bytes 1572872 | tf_op jit(solution)/shard_map/ppermute | solution.py:82
  73.6 14.9 %collective-permute-start.27 = (bf16[64,2048]{0,1:T(8,128)(2,1)S(1)}, bf16[64,2048]{0,1:T(8,128)(2,1)S(1)}, u32[]{:S(2)}, u32[]{:S(2)}) collective-permute-start(bf16[64,2048]{0,1:T(8,128)(2,1)S(1)} %slice.29), channel_id=1, source_target_pairs={{0,16},{8,24},{16,0},{24,8},{1,17},{9,25},{17,1},{25,9},{2,18},{10... | collective-permute-start | bytes 786440 | tf_op jit(solution)/shard_map/ppermute | solution.py:75
  74.7 15.1 %collective-permute-start.26 = (bf16[64,2048]{0,1:T(8,128)(2,1)}, bf16[64,2048]{0,1:T(8,128)(2,1)S(1)}, u32[]{:S(2)}, u32[]{:S(2)}) collective-permute-start(bf16[64,2048]{0,1:T(8,128)(2,1)} %bitcast.155), channel_id=1, source_target_pairs={{0,8},{8,0},{16,24},{24,16},{1,9},{9,1},{17,25},{25,17},{2,10},{10... | collective-permute-start | bytes 786440 | tf_op jit(solution)/shard_map/ppermute | solution.py:74
  77.5 13.3 %collective-permute-start.17 = (bf16[128,1024]{1,0:T(8,128)(2,1)S(1)}, bf16[128,1024]{1,0:T(8,128)(2,1)S(1)}, u32[]{:S(2)}, u32[]{:S(2)}) collective-permute-start(bf16[128,1024]{1,0:T(8,128)(2,1)S(1)} %convolution_convert_fusion.6), channel_id=1, source_target_pairs={{0,4},{4,0},{8,12},{12,8},{16,20},{20,16},{24,28},{28,24},{1,5},{5... | collective-permute-start | bytes 786440 | tf_op jit(solution)/shard_map/ppermute | solution.py:178
  78.4 14.9 %collective-permute-start.19 = (bf16[128,1024]{1,0:T(8,128)(2,1)S(1)}, bf16[128,1024]{1,0:T(8,128)(2,1)S(1)}, u32[]{:S(2)}, u32[]{:S(2)}) collective-permute-start(bf16[128,1024]{1,0:T(8,128)(2,1)S(1)} %convolution_convert_fusion.5), channel_id=1, source_target_pairs={{0,8},{4,12},{8,0},{12,4},{16,24},{20,28},{24,16},{28,20},{1,9},{5... | collective-permute-start | bytes 786440 | tf_op jit(solution)/shard_map/ppermute | solution.py:178
  81.2 25.8 %collective-permute-start.23 = (bf16[128,1024]{1,0:T(8,128)(2,1)S(1)}, bf16[128,1024]{1,0:T(8,128)(2,1)S(1)}, u32[]{:S(2)}, u32[]{:S(2)}) collective-permute-start(bf16[128,1024]{1,0:T(8,128)(2,1)S(1)} %convolution_convert_fusion.3), channel_id=1, source_target_pairs={{0,16},{4,20},{8,24},{12,28},{16,0},{20,4},{24,8},{28,12},{1,17},{... | collective-permute-start | bytes 786440 | tf_op jit(solution)/shard_map/ppermute | solution.py:178
  93.3 14.1 %collective-permute-start.28 = (bf16[128,1024]{1,0:T(8,128)(2,1)S(1)}, bf16[128,1024]{1,0:T(8,128)(2,1)S(1)}, u32[]{:S(2)}, u32[]{:S(2)}) collective-permute-start(bf16[128,1024]{1,0:T(8,128)(2,1)S(1)} %convolution_convert_fusion.1), channel_id=1, source_target_pairs={{0,24},{4,28},{8,16},{12,20},{16,8},{20,12},{24,0},{28,4},{1,25},{... | collective-permute-start | bytes 786440 | tf_op jit(solution)/shard_map/ppermute | solution.py:178
  96.1 10.9 %collective-permute-start.21 = (bf16[128,1024]{1,0:T(8,128)(2,1)S(1)}, bf16[128,1024]{1,0:T(8,128)(2,1)S(1)}, u32[]{:S(2)}, u32[]{:S(2)}) collective-permute-start(bf16[128,1024]{1,0:T(8,128)(2,1)S(1)} %convolution_convert_fusion.4), channel_id=1, source_target_pairs={{0,12},{4,8},{8,4},{12,0},{16,28},{20,24},{24,20},{28,16},{1,13},{... | collective-permute-start | bytes 786440 | tf_op jit(solution)/shard_map/ppermute | solution.py:178
  97.0 10.3 %collective-permute-start.25 = (bf16[128,1024]{1,0:T(8,128)(2,1)S(1)}, bf16[128,1024]{1,0:T(8,128)(2,1)S(1)}, u32[]{:S(2)}, u32[]{:S(2)}) collective-permute-start(bf16[128,1024]{1,0:T(8,128)(2,1)S(1)} %convolution_convert_fusion.2), channel_id=1, source_target_pairs={{0,20},{4,16},{8,28},{12,24},{16,4},{20,0},{24,12},{28,8},{1,21},{... | collective-permute-start | bytes 786440 | tf_op jit(solution)/shard_map/ppermute | solution.py:178
  99.0 11.8 %collective-permute-start.30 = (bf16[128,1024]{1,0:T(8,128)(2,1)S(1)}, bf16[128,1024]{1,0:T(8,128)(2,1)S(1)}, u32[]{:S(2)}, u32[]{:S(2)}) collective-permute-start(bf16[128,1024]{1,0:T(8,128)(2,1)S(1)} %convolution_convert_fusion), channel_id=1, source_target_pairs={{0,28},{4,24},{8,20},{12,16},{16,12},{20,8},{24,4},{28,0},{1,29},{... | collective-permute-start | bytes 786440 | tf_op jit(solution)/shard_map/ppermute | solution.py:178
  (12 other events, 131.4 us)
Sparse Core Ops, SparseCore 0:
  112.2 45.8 reduce-scatter.1

commit v18 on v17

--- a/solution.py
+++ b/solution.py
@@ -173,7 +173,12 @@
                 partial = jnp.dot(block, out_weight, preferred_element_type=jnp.float32).astype(
                     jnp.bfloat16
                 )
-                if b:
+                if r == 3:
+                    first, second = (1, 2) if t == 0 else (2, 1)
+                    partial = lax.ppermute(partial, "hi", swap("hi", first, 4))
+                    pairs = [(h * 2 + l, (h ^ second) * 2 + (l ^ t)) for h in range(4) for l in range(2)]
+                    partial = lax.ppermute(partial, SEQ, pairs)
+                elif b:
                     pairs = [(h * 2 + l, (h ^ r) * 2 + (l ^ t)) for h in range(4) for l in range(2)]
                     partial = lax.ppermute(partial, SEQ, pairs)
                 source = (chip ^ r) * 2 + (core ^ t)

time: 167 us -> 182 us (1.090)
  waiting for transfers between devices: 97 us -> 111 us
    ppermute x0 -> x2, waiting for transfers between devices: none -> 14.9 us  [per_device(): partial = lax.ppermute(partial, 'hi', swap('hi', first, 4))]
    ppermute x0 -> x2, starting transfers between devices: none -> 2.62 us  [per_device(): partial = lax.ppermute(partial, 'hi', swap('hi', first, 4))]
    reduce_scatter x1, waiting for transfers between devices: 46.1 us -> 44.2 us  [per_device(): lax.psum_scatter(by_row, 'chan', scatter_dimension=0, tiled=True)[0]]
  transfers between devices with their start and end apart: 32 -> 34, of which waited for: 15 -> 16; matrix products, arithmetic and copies ran while one was open for 16% -> 15% of each run, Pallas kernels for 0% -> 0%
where the time goes in v18:
time: 182 us; the launch traced here: 181 us
  waiting for transfers between devices  111 us (61%)
  starting transfers between devices  23.2 us (13%)
  matrix products  21.7 us (12%)
  between operations  14.1 us (8%)
  local copies, waits for them, and re-layouts  6.64 us (4%)
  other arithmetic  5.17 us (3%)
    reduce_scatter x1, waiting for transfers between devices, per_device(): lax.psum_scatter(by_row, 'chan', scatter_dimension=0, tiled=True)[0]  44.2 us
    ppermute x3, waiting for transfers between devices, gather_blocks_square(): from_y = lax.ppermute(x, 'hi', swap('hi', 2, 4))  15.2 us
    ppermute x2, waiting for transfers between devices, per_device(): partial = lax.ppermute(partial, 'hi', swap('hi', first, 4))  14.9 us
    ppermute x7, waiting for transfers between devices, per_device(): partial = lax.ppermute(partial, SEQ, pairs)  13.2 us
    dot_general x8, matrix products, per_device(): jnp.dot(block, out_weight, preferred_element_type=jnp.float32)  10.6 us
    ppermute x3, waiting for transfers between devices, gather_blocks_square(): from_x = lax.ppermute(x, 'hi', swap('hi', 1, 4))  10.6 us
    dot_general x8, matrix products, attention_by_head(): jnp.einsum('hqd,hkd->hqk', queries, keys, preferred_element_type=jnp.floa...  6.48 us
    ppermute x3, waiting for transfers between devices, gather_blocks_square(): lax.ppermute(from_x[half:], 'hi', swap('hi', 2, 4))  6.19 us
  transfers between devices with their start and end apart: 34, of which 16 were waited for; matrix products, arithmetic and copies ran while one was open for 15% of the time, Pallas kernels for 0%

profile of v18, /device:TPU:0, one launch (start us, length us, event | category | flops | bytes accessed | tf_op | source)
XLA Modules:
  0.0 181.4 jit_solution(10991198344960415352)
XLA Ops:
  8.2 3.0 %collective-permute-start.3 = (bf16[16,128,128]{2,1,0:T(8,128)(2,1)S(1)}, bf16[16,128,128]{2,1,0:T(8,128)(2,1)}, u32[]{:S(2)}, u32[]{:S(2)}) collective-permute-start(bf16[16,128,128]{2,1,0:T(8,128)(2,1)S(1)} %bitcast.161), channel_id=1, source_target_pairs={{0,16},{8,24},{16,0},{24,8},{1,17},{9,25},{17,1},{25,9},{2,18},{10... | collective-permute-start | bytes 1572872 | tf_op jit(solution)/shard_map/ppermute | solution.py:71
  11.2 1.5 collective-permute-start.1
  16.1 8.0 %collective-permute-done.3 = bf16[16,128,128]{2,1,0:T(8,128)(2,1)} collective-permute-done((bf16[16,128,128]{2,1,0:T(8,128)(2,1)S(1)}, bf16[16,128,128]{2,1,0:T(8,128)(2,1)}, u32[]{:S(2)}, u32[]{:S(2)}) %collective-permute-start.3) | collective-permute-done | bytes 524320 | tf_op jit(solution)/shard_map/ppermute | solution.py:71
  26.1 1.5 collective-permute-start.5
  27.6 6.8 %collective-permute-done.11 = bf16[16,128,128]{1,2,0:T(8,128)(2,1)S(1)} collective-permute-done((bf16[16,128,128]{1,2,0:T(8,128)(2,1)S(1)}, bf16[16,128,128]{1,2,0:T(8,128)(2,1)S(1)}, u32[]{:S(2)}, u32[]{:S(2)}) %collective-permute-start.11) | collective-permute-done | bytes 524320 | tf_op jit(solution)/shard_map/ppermute | solution.py:71
  34.4 1.7 collective-permute-start.6
  37.3 1.5 collective-permute-start.13
  38.8 1.6 fusion.91
  41.6 1.6 fusion.95
  43.4 3.7 %collective-permute-done.13 = bf16[8,128,128]{1,2,0:T(8,128)(2,1)S(1)} collective-permute-done((bf16[8,128,128]{1,2,0:T(8,128)(2,1)S(1)}, bf16[8,128,128]{1,2,0:T(8,128)(2,1)S(1)}, u32[]{:S(2)}, u32[]{:S(2)}) %collective-permute-start.13) | collective-permute-done | bytes 262176 | tf_op jit(solution)/shard_map/ppermute | solution.py:74
  52.4 2.1 %fusion.21 = (f32[16,128]{1,0:T(8,128)S(1)}, f32[16,128]{1,0:T(8,128)S(1)}, f32[16,128]{1,0:T(8,128)S(1)}, f32[16,128]{1,0:T(8,128)S(1)}, f32[16,128]{1,0:T(8,128)S(1)}) fusion(f32[16,128,128]{2,1,0:T(8,128)S(1)} %get-tuple-element.36, f32[16,128]{1,0:T(8,128)S(1)} %maximum_maximum_fusion, pred[128,128]{1,0:T(8,128)(4,1)S(1)} %copy.41, ...), kind=kLoop, calls=%fused_computation.50 | loop fusion | flops 3921920 | bytes 5373952 | tf_op jit(solution)/shard_map/reduce_sum | solution.py:106
  59.2 1.5 collective-permute-start.18
  61.6 3.3 %fusion.17 = bf16[4,128,2048]{2,1,0:T(8,128)(2,1)S(1)} fusion(bf16[4,128,2048]{2,1,0:T(8,128)(2,1)S(1)} %broadcast_in_dim.148, s32[]{:T(128)S(6)} %select_n.174, s32[]{:T(128)S(6)} %select_n.176, bf16[128,2048]{0,1:T(8,128)(2,1)} %bitcast.10, bf16[2048,1024]{1,0:T(8,128)(2,1)} %param.9), kind=kOutput, calls=%fused_computation.37 | convolution fusion | flops 537001984 | bytes 4980744 | tf_op jit(solution)/shard_map/dot_general | solution.py:173
  64.9 8.4 %collective-permute-done.18 = bf16[128,2048]{0,1:T(8,128)(2,1)S(1)} collective-permute-done((bf16[128,2048]{0,1:T(8,128)(2,1)}, bf16[128,2048]{0,1:T(8,128)(2,1)S(1)}, u32[]{:S(2)}, u32[]{:S(2)}) %collective-permute-start.18) | collective-permute-done | bytes 524320 | tf_op jit(solution)/shard_map/ppermute | solution.py:70
  75.7 1.8 %convolution_convert_fusion.6 = bf16[128,1024]{1,0:T(8,128)(2,1)S(1)} fusion(bf16[128,2048]{0,1:T(8,128)(2,1)} %collective-permute-done.16, bf16[2048,1024]{1,0:T(8,128)(2,1)S(1)} %copy-done.1), kind=kOutput, calls=%fused_computation.34 | convolution fusion | flops 537001984 | bytes 4980736 | tf_op jit(solution)/shard_map/dot_general | solution.py:173
  79.4 1.8 convolution_convert_fusion.3
  82.3 6.2 %collective-permute-done.27 = bf16[64,2048]{0,1:T(8,128)(2,1)S(1)} collective-permute-done((bf16[64,2048]{0,1:T(8,128)(2,1)S(1)}, bf16[64,2048]{0,1:T(8,128)(2,1)S(1)}, u32[]{:S(2)}, u32[]{:S(2)}) %collective-permute-start.27) | collective-permute-done | bytes 262176 | tf_op jit(solution)/shard_map/ppermute | solution.py:75
  93.3 6.2 %collective-permute-done.28 = bf16[128,1024]{1,0:T(8,128)(2,1)S(1)} collective-permute-done((bf16[128,1024]{1,0:T(8,128)(2,1)S(1)}, bf16[128,1024]{1,0:T(8,128)(2,1)S(1)}, u32[]{:S(2)}, u32[]{:S(2)}) %collective-permute-start.28) | collective-permute-done | bytes 262176 | tf_op jit(solution)/shard_map/ppermute | solution.py:178
  104.7 1.5 collective-permute-start.31
  106.2 3.7 %collective-permute-done.21 = bf16[128,1024]{1,0:T(8,128)(2,1)S(1)} collective-permute-done((bf16[128,1024]{1,0:T(8,128)(2,1)S(1)}, bf16[128,1024]{1,0:T(8,128)(2,1)S(1)}, u32[]{:S(2)}, u32[]{:S(2)}) %collective-permute-start.21) | collective-permute-done | bytes 262176 | tf_op jit(solution)/shard_map/ppermute | solution.py:183
  110.0 8.7 %collective-permute-done.31 = bf16[128,1024]{1,0:T(8,128)(2,1)S(1)} collective-permute-done((bf16[128,1024]{1,0:T(8,128)(2,1)S(1)}, bf16[128,1024]{1,0:T(8,128)(2,1)S(1)}, u32[]{:S(2)}, u32[]{:S(2)}) %collective-permute-start.31) | collective-permute-done | bytes 262176 | tf_op jit(solution)/shard_map/ppermute | solution.py:178
  118.8 8.1 %collective-permute-done.32 = bf16[128,1024]{1,0:T(8,128)(2,1)S(1)} collective-permute-done((bf16[128,1024]{1,0:T(8,128)(2,1)S(1)}, bf16[128,1024]{1,0:T(8,128)(2,1)S(1)}, u32[]{:S(2)}, u32[]{:S(2)}) %collective-permute-start.32) | collective-permute-done | bytes 262176 | tf_op jit(solution)/shard_map/ppermute | solution.py:180
  128.3 44.2 %reduce-scatter.2.cloned.1.call-done = bf16[1,128,2048]{2,1,0:T(8,128)(2,1)} async-done(((bf16[4,128,2048]{2,1,0:T(8,128)(2,1)}), bf16[1,128,2048]{2,1,0:T(8,128)(2,1)}) %reduce-scatter.2.cloned.1.call-update) | async-done | bytes 524304 | tf_op jit(solution)/shard_map/reduce_scatter | solution.py:188
  172.5 2.0 %fusion.18 = bf16[128,2048]{1,0:T(8,128)(2,1)} fusion(bf16[128,2048]{1,0:T(8,128)(2,1)S(1)} %copy-done.3, bf16[1,128,2048]{2,1,0:T(8,128)(2,1)} %reduce-scatter.2.cloned.1.call-done), kind=kLoop, calls=%fused_computation.39 | loop fusion | flops 1048576 | bytes 1572864 | tf_op jit(solution)/shard_map/convert_element_type | solution.py:189
  (113 shorter events, 36.7 us)
Async XLA Ops:
  6.5 166.0 %reduce-scatter.2.cloned.1.call-start = ((), (), s32[]{:S(2)}) async-start(), calls=%async_computation.1 | async-start | bytes 2621440 | tf_op jit(solution)/shard_map/reduce_scatter | solution.py:188
  8.2 15.9 %collective-permute-start.3 = (bf16[16,128,128]{2,1,0:T(8,128)(2,1)S(1)}, bf16[16,128,128]{2,1,0:T(8,128)(2,1)}, u32[]{:S(2)}, u32[]{:S(2)}) collective-permute-start(bf16[16,128,128]{2,1,0:T(8,128)(2,1)S(1)} %bitcast.161), channel_id=1, source_target_pairs={{0,16},{8,24},{16,0},{24,8},{1,17},{9,25},{17,1},{25,9},{2,18},{10... | collective-permute-start | bytes 1572872 | tf_op jit(solution)/shard_map/ppermute | solution.py:71
  11.2 14.8 %collective-permute-start.1 = (bf16[16,128,128]{2,1,0:T(8,128)(2,1)S(1)}, bf16[16,128,128]{2,1,0:T(8,128)(2,1)S(1)}, u32[]{:S(2)}, u32[]{:S(2)}) collective-permute-start(bf16[16,128,128]{2,1,0:T(8,128)(2,1)S(1)} %bitcast.162), channel_id=1, source_target_pairs={{0,8},{8,0},{16,24},{24,16},{1,9},{9,1},{17,25},{25,17},{2,10},{10... | collective-permute-start | bytes 1572872 | tf_op jit(solution)/shard_map/ppermute | solution.py:70
  12.7 28.3 %collective-permute-start = (bf16[16,128,128]{2,1,0:T(8,128)(2,1)S(1)}, bf16[16,128,128]{2,1,0:T(8,128)(2,1)}, u32[]{:S(2)}, u32[]{:S(2)}) collective-permute-start(bf16[16,128,128]{2,1,0:T(8,128)(2,1)S(1)} %bitcast.163), channel_id=1, source_target_pairs={{0,4},{4,0},{1,5},{5,1},{2,6},{6,2},{3,7},{7,3},{8,12},{12,8},{9,1... | collective-permute-start | bytes 1572872 | tf_op jit(solution)/shard_map/ppermute | solution.py:82
  14.0 23.3 %collective-permute-start.9 = (bf16[16,128,128]{1,2,0:T(8,128)(2,1)S(1)}, bf16[16,128,128]{1,2,0:T(8,128)(2,1)S(1)}, u32[]{:S(2)}, u32[]{:S(2)}) collective-permute-start(bf16[16,128,128]{1,2,0:T(8,128)(2,1)S(1)} %bitcast.156), channel_id=1, source_target_pairs={{0,8},{8,0},{16,24},{24,16},{1,9},{9,1},{17,25},{25,17},{2,10},{10... | collective-permute-start | bytes 1572872 | tf_op jit(solution)/shard_map/ppermute | solution.py:70
  14.6 19.7 %collective-permute-start.11 = (bf16[16,128,128]{1,2,0:T(8,128)(2,1)S(1)}, bf16[16,128,128]{1,2,0:T(8,128)(2,1)S(1)}, u32[]{:S(2)}, u32[]{:S(2)}) collective-permute-start(bf16[16,128,128]{1,2,0:T(8,128)(2,1)S(1)} %bitcast.157), channel_id=1, source_target_pairs={{0,16},{8,24},{16,0},{24,8},{1,17},{9,25},{17,1},{25,9},{2,18},{10... | collective-permute-start | bytes 1572872 | tf_op jit(solution)/shard_map/ppermute | solution.py:71
  24.1 30.4 %collective-permute-start.8 = (bf16[16,128,128]{1,2,0:T(8,128)(2,1)S(1)}, bf16[16,128,128]{1,2,0:T(8,128)(2,1)S(1)}, u32[]{:S(2)}, u32[]{:S(2)}) collective-permute-start(bf16[16,128,128]{1,2,0:T(8,128)(2,1)S(1)} %bitcast.158), channel_id=1, source_target_pairs={{0,4},{4,0},{1,5},{5,1},{2,6},{6,2},{3,7},{7,3},{8,12},{12,8},{9,1... | collective-permute-start | bytes 1572872 | tf_op jit(solution)/shard_map/ppermute | solution.py:82
  26.1 17.2 %collective-permute-start.5 = (bf16[8,128,128]{2,1,0:T(8,128)(2,1)S(1)}, bf16[8,128,128]{2,1,0:T(8,128)(2,1)S(1)}, u32[]{:S(2)}, u32[]{:S(2)}) collective-permute-start(bf16[8,128,128]{2,1,0:T(8,128)(2,1)S(1)} %slice.24), channel_id=1, source_target_pairs={{0,8},{8,0},{16,24},{24,16},{1,9},{9,1},{17,25},{25,17},{2,10},{10... | collective-permute-start | bytes 786440 | tf_op jit(solution)/shard_map/ppermute | solution.py:74
  34.4 12.7 %collective-permute-start.6 = (bf16[8,128,128]{2,1,0:T(8,128)(2,1)S(1)}, bf16[8,128,128]{2,1,0:T(8,128)(2,1)S(1)}, u32[]{:S(2)}, u32[]{:S(2)}) collective-permute-start(bf16[8,128,128]{2,1,0:T(8,128)(2,1)S(1)} %slice.25), channel_id=1, source_target_pairs={{0,16},{8,24},{16,0},{24,8},{1,17},{9,25},{17,1},{25,9},{2,18},{10... | collective-permute-start | bytes 786440 | tf_op jit(solution)/shard_map/ppermute | solution.py:75
  47.1 10.0 %collective-permute-start.10 = (bf16[16,128,128]{1,2,0:T(8,128)(2,1)S(1)}, bf16[16,128,128]{1,2,0:T(8,128)(2,1)S(1)}, u32[]{:S(2)}, u32[]{:S(2)}) collective-permute-start(bf16[16,128,128]{1,2,0:T(8,128)(2,1)S(1)} %collective-permute-done.9), channel_id=1, source_target_pairs={{0,4},{4,0},{1,5},{5,1},{2,6},{6,2},{3,7},{7,3},{8,12},{12,8},{9,1... | collective-permute-start | bytes 1572872 | tf_op jit(solution)/shard_map/ppermute | solution.py:82
  59.2 14.2 %collective-permute-start.18 = (bf16[128,2048]{0,1:T(8,128)(2,1)}, bf16[128,2048]{0,1:T(8,128)(2,1)S(1)}, u32[]{:S(2)}, u32[]{:S(2)}) collective-permute-start(bf16[128,2048]{0,1:T(8,128)(2,1)} %bitcast.10), channel_id=1, source_target_pairs={{0,8},{8,0},{16,24},{24,16},{1,9},{9,1},{17,25},{25,17},{2,10},{10... | collective-permute-start | bytes 1572872 | tf_op jit(solution)/shard_map/ppermute | solution.py:70
  60.6 14.0 %collective-permute-start.22 = (bf16[128,2048]{0,1:T(8,128)(2,1)}, bf16[128,2048]{0,1:T(8,128)(2,1)}, u32[]{:S(2)}, u32[]{:S(2)}) collective-permute-start(bf16[128,2048]{0,1:T(8,128)(2,1)} %bitcast.10), channel_id=1, source_target_pairs={{0,16},{8,24},{16,0},{24,8},{1,17},{9,25},{17,1},{25,9},{2,18},{10... | collective-permute-start | bytes 1572872 | tf_op jit(solution)/shard_map/ppermute | solution.py:71
  61.2 14.5 %collective-permute-start.16 = (bf16[128,2048]{0,1:T(8,128)(2,1)}, bf16[128,2048]{0,1:T(8,128)(2,1)}, u32[]{:S(2)}, u32[]{:S(2)}) collective-permute-start(bf16[128,2048]{0,1:T(8,128)(2,1)} %bitcast.10), channel_id=1, source_target_pairs={{0,4},{4,0},{1,5},{5,1},{2,6},{6,2},{3,7},{7,3},{8,12},{12,8},{9,1... | collective-permute-start | bytes 1572872 | tf_op jit(solution)/shard_map/ppermute | solution.py:82
  73.6 14.9 %collective-permute-start.27 = (bf16[64,2048]{0,1:T(8,128)(2,1)S(1)}, bf16[64,2048]{0,1:T(8,128)(2,1)S(1)}, u32[]{:S(2)}, u32[]{:S(2)}) collective-permute-start(bf16[64,2048]{0,1:T(8,128)(2,1)S(1)} %slice.29), channel_id=1, source_target_pairs={{0,16},{8,24},{16,0},{24,8},{1,17},{9,25},{17,1},{25,9},{2,18},{10... | collective-permute-start | bytes 786440 | tf_op jit(solution)/shard_map/ppermute | solution.py:75
  74.7 15.1 %collective-permute-start.26 = (bf16[64,2048]{0,1:T(8,128)(2,1)}, bf16[64,2048]{0,1:T(8,128)(2,1)S(1)}, u32[]{:S(2)}, u32[]{:S(2)}) collective-permute-start(bf16[64,2048]{0,1:T(8,128)(2,1)} %bitcast.155), channel_id=1, source_target_pairs={{0,8},{8,0},{16,24},{24,16},{1,9},{9,1},{17,25},{25,17},{2,10},{10... | collective-permute-start | bytes 786440 | tf_op jit(solution)/shard_map/ppermute | solution.py:74
  77.5 13.3 %collective-permute-start.17 = (bf16[128,1024]{1,0:T(8,128)(2,1)S(1)}, bf16[128,1024]{1,0:T(8,128)(2,1)S(1)}, u32[]{:S(2)}, u32[]{:S(2)}) collective-permute-start(bf16[128,1024]{1,0:T(8,128)(2,1)S(1)} %convolution_convert_fusion.6), channel_id=1, source_target_pairs={{0,4},{4,0},{8,12},{12,8},{16,20},{20,16},{24,28},{28,24},{1,5},{5... | collective-permute-start | bytes 786440 | tf_op jit(solution)/shard_map/ppermute | solution.py:183
  78.4 14.9 %collective-permute-start.19 = (bf16[128,1024]{1,0:T(8,128)(2,1)S(1)}, bf16[128,1024]{1,0:T(8,128)(2,1)S(1)}, u32[]{:S(2)}, u32[]{:S(2)}) collective-permute-start(bf16[128,1024]{1,0:T(8,128)(2,1)S(1)} %convolution_convert_fusion.5), channel_id=1, source_target_pairs={{0,8},{4,12},{8,0},{12,4},{16,24},{20,28},{24,16},{28,20},{1,9},{5... | collective-permute-start | bytes 786440 | tf_op jit(solution)/shard_map/ppermute | solution.py:183
  81.2 28.7 %collective-permute-start.23 = (bf16[128,1024]{1,0:T(8,128)(2,1)S(1)}, bf16[128,1024]{1,0:T(8,128)(2,1)S(1)}, u32[]{:S(2)}, u32[]{:S(2)}) collective-permute-start(bf16[128,1024]{1,0:T(8,128)(2,1)S(1)} %convolution_convert_fusion.3), channel_id=1, source_target_pairs={{0,16},{4,20},{8,24},{12,28},{16,0},{20,4},{24,8},{28,12},{1,17},{... | collective-permute-start | bytes 786440 | tf_op jit(solution)/shard_map/ppermute | solution.py:183
  88.5 12.1 %collective-permute-start.20 = (bf16[128,2048]{0,1:T(8,128)(2,1)S(1)}, bf16[128,2048]{0,1:T(8,128)(2,1)S(1)}, u32[]{:S(2)}, u32[]{:S(2)}) collective-permute-start(bf16[128,2048]{0,1:T(8,128)(2,1)S(1)} %collective-permute-done.18), channel_id=1, source_target_pairs={{0,4},{4,0},{1,5},{5,1},{2,6},{6,2},{3,7},{7,3},{8,12},{12,8},{9,1... | collective-permute-start | bytes 1572872 | tf_op jit(solution)/shard_map/ppermute | solution.py:82
  89.7 12.2 %collective-permute-start.24 = (bf16[128,2048]{0,1:T(8,128)(2,1)}, bf16[128,2048]{0,1:T(8,128)(2,1)S(1)}, u32[]{:S(2)}, u32[]{:S(2)}) collective-permute-start(bf16[128,2048]{0,1:T(8,128)(2,1)} %collective-permute-done.22), channel_id=1, source_target_pairs={{0,4},{4,0},{1,5},{5,1},{2,6},{6,2},{3,7},{7,3},{8,12},{12,8},{9,1... | collective-permute-start | bytes 1572872 | tf_op jit(solution)/shard_map/ppermute | solution.py:82
  93.3 10.7 %collective-permute-start.30 = (bf16[128,2048]{0,1:T(8,128)(2,1)S(1)}, bf16[128,2048]{0,1:T(8,128)(2,1)S(1)}, u32[]{:S(2)}, u32[]{:S(2)}) collective-permute-start(bf16[128,2048]{0,1:T(8,128)(2,1)S(1)} %pad_maximum_fusion), channel_id=1, source_target_pairs={{0,4},{4,0},{1,5},{5,1},{2,6},{6,2},{3,7},{7,3},{8,12},{12,8},{9,1... | collective-permute-start | bytes 1572872 | tf_op jit(solution)/shard_map/ppermute | solution.py:82
  99.6 19.2 %collective-permute-start.29 = (bf16[128,1024]{1,0:T(8,128)(2,1)S(1)}, bf16[128,1024]{1,0:T(8,128)(2,1)S(1)}, u32[]{:S(2)}, u32[]{:S(2)}) collective-permute-start(bf16[128,1024]{1,0:T(8,128)(2,1)S(1)} %collective-permute-done.28), channel_id=1, source_target_pairs={{0,16},{4,20},{8,24},{12,28},{16,0},{20,4},{24,8},{28,12},{1,17},{... | collective-permute-start | bytes 786440 | tf_op jit(solution)/shard_map/ppermute | solution.py:180
  102.7 16.1 %collective-permute-start.25 = (bf16[128,1024]{1,0:T(8,128)(2,1)S(1)}, bf16[128,1024]{1,0:T(8,128)(2,1)S(1)}, u32[]{:S(2)}, u32[]{:S(2)}) collective-permute-start(bf16[128,1024]{1,0:T(8,128)(2,1)S(1)} %convolution_convert_fusion.2), channel_id=1, source_target_pairs={{0,20},{4,16},{8,28},{12,24},{16,4},{20,0},{24,12},{28,8},{1,21},{... | collective-permute-start | bytes 786440 | tf_op jit(solution)/shard_map/ppermute | solution.py:183
  104.7 14.0 %collective-permute-start.31 = (bf16[128,1024]{1,0:T(8,128)(2,1)S(1)}, bf16[128,1024]{1,0:T(8,128)(2,1)S(1)}, u32[]{:S(2)}, u32[]{:S(2)}) collective-permute-start(bf16[128,1024]{1,0:T(8,128)(2,1)S(1)} %convolution_convert_fusion), channel_id=1, source_target_pairs={{0,16},{8,24},{16,0},{24,8},{1,17},{9,25},{17,1},{25,9},{2,18},{10... | collective-permute-start | bytes 786440 | tf_op jit(solution)/shard_map/ppermute | solution.py:178
  (14 other events, 164.6 us)
Sparse Core Ops, SparseCore 0:
  128.4 44.0 reduce-scatter.1

commit v19 on v17

--- a/solution.py
+++ b/solution.py
@@ -139,7 +139,8 @@
             key_starts = [
                 ((chip ^ (b // 2)) * 2 + (core ^ (b % 2))) * seg_rows for b in range(len(key_blocks))
             ]
-            ratio = attention_by_head(by_head(query_proj), key_blocks, value_blocks, row_pos, key_starts)
+            query_after, _ = lax.optimization_barrier((query_proj, key_blocks[2]))
+            ratio = attention_by_head(by_head(query_after), key_blocks, value_blocks, row_pos, key_starts)
         else:
             both = gather_seq(jnp.concatenate([key_proj, value_proj], axis=1))
             total_rows = both.shape[0]

time: 167 us -> 166 us (level)
  waiting for transfers between devices: 97 us -> 99 us
  matrix products: 21.7 us -> 20 us
    ppermute x3, waiting for transfers between devices: 10.6 us -> 17.7 us  [gather_blocks_square(): from_x = lax.ppermute(x, 'hi', swap('hi', 1, 4))]
    ppermute x3, waiting for transfers between devices: 15.2 us -> 10.7 us  [gather_blocks_square(): from_y = lax.ppermute(x, 'hi', swap('hi', 2, 4))]
    reduce_scatter x1, waiting for transfers between devices: 46.1 us -> 43.4 us  [per_device(): lax.psum_scatter(by_row, 'chan', scatter_dimension=0, tiled=True)[0]]
    ppermute x7, waiting for transfers between devices: 12.8 us -> 15 us  [per_device(): partial = lax.ppermute(partial, SEQ, pairs)]
    ppermute x3, starting transfers between devices: 2.95 us -> 4.72 us  [gather_blocks_square(): lax.ppermute(from_x[half:], 'hi', swap('hi', 2, 4))]
  transfers between devices with their start and end apart: 32 -> 32, of which waited for: 15 -> 13; matrix products, arithmetic and copies ran while one was open for 16% -> 15% of each run, Pallas kernels for 0% -> 0%
where the time goes in v19:
time: 166 us
  waiting for transfers between devices  99 us (60%)
  starting transfers between devices  22.2 us (13%)
  matrix products  20 us (12%)
  between operations  13.9 us (8%)
  local copies, waits for them, and re-layouts  6.05 us (4%)
  other arithmetic  4.7 us (3%)
    reduce_scatter x1, waiting for transfers between devices, per_device(): lax.psum_scatter(by_row, 'chan', scatter_dimension=0, tiled=True)[0]  43.4 us
    ppermute x3, waiting for transfers between devices, gather_blocks_square(): from_x = lax.ppermute(x, 'hi', swap('hi', 1, 4))  17.7 us
    ppermute x7, waiting for transfers between devices, per_device(): partial = lax.ppermute(partial, SEQ, pairs)  15 us
    ppermute x3, waiting for transfers between devices, gather_blocks_square(): from_y = lax.ppermute(x, 'hi', swap('hi', 2, 4))  10.7 us
    dot_general x8, matrix products, per_device(): jnp.dot(block, out_weight, preferred_element_type=jnp.float32)  10.6 us
    dot_general x8, matrix products, attention_by_head(): jnp.einsum('hqd,hkd->hqk', queries, keys, preferred_element_type=jnp.floa...  6.07 us
    ppermute x3, waiting for transfers between devices, gather_blocks_square(): lax.ppermute(from_x[half:], 'hi', swap('hi', 2, 4))  6.01 us
    ppermute x7, starting transfers between devices, per_device(): partial = lax.ppermute(partial, SEQ, pairs)  5.76 us
  transfers between devices with their start and end apart: 32, of which 13 were waited for; matrix products, arithmetic and copies ran while one was open for 15% of the time, Pallas kernels for 0%

profile of v19, /device:TPU:0, one launch (start us, length us, event | category | flops | bytes accessed | tf_op | source)
XLA Modules:
  0.0 165.9 jit_solution(17794150737115736271)
XLA Ops:
  8.2 3.0 %collective-permute-start = (bf16[16,128,128]{2,1,0:T(8,128)(2,1)S(1)}, bf16[16,128,128]{2,1,0:T(8,128)(2,1)}, u32[]{:S(2)}, u32[]{:S(2)}) collective-permute-start(bf16[16,128,128]{2,1,0:T(8,128)(2,1)S(1)} %bitcast.153), channel_id=1, source_target_pairs={{0,8},{8,0},{16,24},{24,16},{1,9},{9,1},{17,25},{25,17},{2,10},{10... | collective-permute-start | bytes 1572872 | tf_op jit(solution)/shard_map/ppermute | solution.py:70
  14.9 9.1 %collective-permute-done = bf16[16,128,128]{2,1,0:T(8,128)(2,1)} collective-permute-done((bf16[16,128,128]{2,1,0:T(8,128)(2,1)S(1)}, bf16[16,128,128]{2,1,0:T(8,128)(2,1)}, u32[]{:S(2)}, u32[]{:S(2)}) %collective-permute-start) | collective-permute-done | bytes 524320 | tf_op jit(solution)/shard_map/ppermute | solution.py:70
  26.1 1.5 collective-permute-start.6
  27.6 9.7 %collective-permute-done.11 = bf16[16,128,128]{1,2,0:T(8,128)(2,1)S(1)} collective-permute-done((bf16[16,128,128]{1,2,0:T(8,128)(2,1)S(1)}, bf16[16,128,128]{1,2,0:T(8,128)(2,1)S(1)}, u32[]{:S(2)}, u32[]{:S(2)}) %collective-permute-start.11) | collective-permute-done | bytes 524320 | tf_op jit(solution)/shard_map/ppermute | solution.py:71
  37.9 2.0 %collective-permute-start.13 = (bf16[8,128,128]{1,2,0:T(8,128)(2,1)S(1)}, bf16[8,128,128]{1,2,0:T(8,128)(2,1)S(1)}, u32[]{:S(2)}, u32[]{:S(2)}) collective-permute-start(bf16[8,128,128]{1,2,0:T(8,128)(2,1)S(1)} %slice.26), channel_id=1, source_target_pairs={{0,8},{8,0},{16,24},{24,16},{1,9},{9,1},{17,25},{25,17},{2,10},{10... | collective-permute-start | bytes 786440 | tf_op jit(solution)/shard_map/ppermute | solution.py:74
  40.0 1.5 fusion.91
  42.0 1.6 collective-permute-start.14
  43.6 1.5 fusion.93
  45.5 2.8 %collective-permute-done.13 = bf16[8,128,128]{1,2,0:T(8,128)(2,1)S(1)} collective-permute-done((bf16[8,128,128]{1,2,0:T(8,128)(2,1)S(1)}, bf16[8,128,128]{1,2,0:T(8,128)(2,1)S(1)}, u32[]{:S(2)}, u32[]{:S(2)}) %collective-permute-start.13) | collective-permute-done | bytes 262176 | tf_op jit(solution)/shard_map/ppermute | solution.py:74
  53.3 2.2 %fusion.19 = (f32[16,128]{1,0:T(8,128)S(1)}, f32[16,128]{1,0:T(8,128)S(1)}, f32[16,128]{1,0:T(8,128)S(1)}, f32[16,128]{1,0:T(8,128)S(1)}, f32[16,128]{1,0:T(8,12...) fusion(f32[16,128,128]{1,2,0:T(8,128)S(1)} %get-tuple-element.38, ...), kind=kLoop, calls=%fused_computation.48 | loop fusion | flops 6275072 | bytes 8593408 | tf_op jit(solution)/shard_map/reduce_sum | solution.py:106
  61.0 3.2 %fusion.15 = bf16[4,128,2048]{2,1,0:T(8,128)(2,1)S(1)} fusion(bf16[4,128,2048]{2,1,0:T(8,128)(2,1)S(1)} %broadcast_in_dim.148, s32[]{:T(128)S(6)} %select_n.174, s32[]{:T(128)S(6)} %select_n.176, bf16[128,2048]{0,1:T(8,128)(2,1)} %bitcast.8, bf16[2048,1024]{1,0:T(8,128)(2,1)} %param.9), kind=kOutput, calls=%fused_computation.35 | convolution fusion | flops 537001984 | bytes 4980744 | tf_op jit(solution)/shard_map/dot_general | solution.py:174
  64.2 8.6 %collective-permute-done.18 = bf16[128,2048]{0,1:T(8,128)(2,1)S(1)} collective-permute-done((bf16[128,2048]{0,1:T(8,128)(2,1)}, bf16[128,2048]{0,1:T(8,128)(2,1)S(1)}, u32[]{:S(2)}, u32[]{:S(2)}) %collective-permute-start.18) | collective-permute-done | bytes 524320 | tf_op jit(solution)/shard_map/ppermute | solution.py:70
  73.1 1.6 collective-permute-start.27
  75.2 1.8 %convolution_convert_fusion.6 = bf16[128,1024]{1,0:T(8,128)(2,1)S(1)} fusion(bf16[128,2048]{0,1:T(8,128)(2,1)} %collective-permute-done.16, bf16[2048,1024]{1,0:T(8,128)(2,1)S(1)} %copy-done.1), kind=kOutput, calls=%fused_computation.32 | convolution fusion | flops 537001984 | bytes 4980736 | tf_op jit(solution)/shard_map/dot_general | solution.py:174
  78.0 1.6 collective-permute-start.19
  79.6 1.8 %convolution_convert_fusion.3 = bf16[128,1024]{1,0:T(8,128)(2,1)S(1)} fusion(bf16[128,2048]{0,1:T(8,128)(2,1)} %collective-permute-done.22, bf16[2048,1024]{1,0:T(8,128)(2,1)S(1)} %copy-done.1), kind=kOutput, calls=%fused_computation.29 | convolution fusion | flops 537001984 | bytes 4980736 | tf_op jit(solution)/shard_map/dot_general | solution.py:174
  82.0 6.0 %collective-permute-done.27 = bf16[64,2048]{0,1:T(8,128)(2,1)S(1)} collective-permute-done((bf16[64,2048]{0,1:T(8,128)(2,1)S(1)}, bf16[64,2048]{0,1:T(8,128)(2,1)S(1)}, u32[]{:S(2)}, u32[]{:S(2)}) %collective-permute-start.27) | collective-permute-done | bytes 262176 | tf_op jit(solution)/shard_map/ppermute | solution.py:75
  88.0 1.8 %collective-permute-done.26 = bf16[64,2048]{0,1:T(8,128)(2,1)S(1)} collective-permute-done((bf16[64,2048]{0,1:T(8,128)(2,1)}, bf16[64,2048]{0,1:T(8,128)(2,1)S(1)}, u32[]{:S(2)}, u32[]{:S(2)}) %collective-permute-start.26) | collective-permute-done | bytes 262176 | tf_op jit(solution)/shard_map/ppermute | solution.py:74
  91.4 2.1 %collective-permute-done.19 = bf16[128,1024]{1,0:T(8,128)(2,1)S(1)} collective-permute-done((bf16[128,1024]{1,0:T(8,128)(2,1)S(1)}, bf16[128,1024]{1,0:T(8,128)(2,1)S(1)}, u32[]{:S(2)}, u32[]{:S(2)}) %collective-permute-start.19) | collective-permute-done | bytes 262176 | tf_op jit(solution)/shard_map/ppermute | solution.py:179
  96.0 2.4 %collective-permute-start.25 = (bf16[128,1024]{1,0:T(8,128)(2,1)S(1)}, bf16[128,1024]{1,0:T(8,128)(2,1)S(1)}, u32[]{:S(2)}, u32[]{:S(2)}) collective-permute-start(bf16[128,1024]{1,0:T(8,128)(2,1)S(1)} %convolution_convert_fusion.2), channel_id=1, source_target_pairs={{0,20},{4,16},{8,28},{12,24},{16,4},{20,0},{24,12},{28,8},{1,21},{... | collective-permute-start | bytes 786440 | tf_op jit(solution)/shard_map/ppermute | solution.py:179
  99.2 6.1 %collective-permute-done.21 = bf16[128,1024]{1,0:T(8,128)(2,1)S(1)} collective-permute-done((bf16[128,1024]{1,0:T(8,128)(2,1)S(1)}, bf16[128,1024]{1,0:T(8,128)(2,1)S(1)}, u32[]{:S(2)}, u32[]{:S(2)}) %collective-permute-start.21) | collective-permute-done | bytes 262176 | tf_op jit(solution)/shard_map/ppermute | solution.py:179
  105.4 6.8 %collective-permute-done.25 = bf16[128,1024]{1,0:T(8,128)(2,1)S(1)} collective-permute-done((bf16[128,1024]{1,0:T(8,128)(2,1)S(1)}, bf16[128,1024]{1,0:T(8,128)(2,1)S(1)}, u32[]{:S(2)}, u32[]{:S(2)}) %collective-permute-start.25) | collective-permute-done | bytes 262176 | tf_op jit(solution)/shard_map/ppermute | solution.py:179
  113.6 43.4 %reduce-scatter.2.cloned.1.call-done = bf16[1,128,2048]{2,1,0:T(8,128)(2,1)} async-done(((bf16[4,128,2048]{2,1,0:T(8,128)(2,1)}), bf16[1,128,2048]{2,1,0:T(8,128)(2,1)}) %reduce-scatter.2.cloned.1.call-update) | async-done | bytes 524304 | tf_op jit(solution)/shard_map/reduce_scatter | solution.py:184
  157.1 2.0 %fusion.16 = bf16[128,2048]{1,0:T(8,128)(2,1)} fusion(bf16[128,2048]{1,0:T(8,128)(2,1)S(1)} %copy-done.3, bf16[1,128,2048]{2,1,0:T(8,128)(2,1)} %reduce-scatter.2.cloned.1.call-done), kind=kLoop, calls=%fused_computation.37 | loop fusion | flops 1048576 | bytes 1572864 | tf_op jit(solution)/shard_map/convert_element_type | solution.py:185
  (103 shorter events, 27.8 us)
Async XLA Ops:
  6.5 150.5 %reduce-scatter.2.cloned.1.call-start = ((), (), s32[]{:S(2)}) async-start(), calls=%async_computation.1 | async-start | bytes 2621440 | tf_op jit(solution)/shard_map/reduce_scatter | solution.py:184
  8.2 15.9 %collective-permute-start = (bf16[16,128,128]{2,1,0:T(8,128)(2,1)S(1)}, bf16[16,128,128]{2,1,0:T(8,128)(2,1)}, u32[]{:S(2)}, u32[]{:S(2)}) collective-permute-start(bf16[16,128,128]{2,1,0:T(8,128)(2,1)S(1)} %bitcast.153), channel_id=1, source_target_pairs={{0,8},{8,0},{16,24},{24,16},{1,9},{9,1},{17,25},{25,17},{2,10},{10... | collective-permute-start | bytes 1572872 | tf_op jit(solution)/shard_map/ppermute | solution.py:70
  11.2 14.8 %collective-permute-start.3 = (bf16[16,128,128]{2,1,0:T(8,128)(2,1)S(1)}, bf16[16,128,128]{2,1,0:T(8,128)(2,1)S(1)}, u32[]{:S(2)}, u32[]{:S(2)}) collective-permute-start(bf16[16,128,128]{2,1,0:T(8,128)(2,1)S(1)} %bitcast.154), channel_id=1, source_target_pairs={{0,16},{8,24},{16,0},{24,8},{1,17},{9,25},{17,1},{25,9},{2,18},{10... | collective-permute-start | bytes 1572872 | tf_op jit(solution)/shard_map/ppermute | solution.py:71
  12.7 29.3 %collective-permute-start.1 = (bf16[16,128,128]{2,1,0:T(8,128)(2,1)S(1)}, bf16[16,128,128]{2,1,0:T(8,128)(2,1)}, u32[]{:S(2)}, u32[]{:S(2)}) collective-permute-start(bf16[16,128,128]{2,1,0:T(8,128)(2,1)S(1)} %bitcast.155), channel_id=1, source_target_pairs={{0,4},{4,0},{1,5},{5,1},{2,6},{6,2},{3,7},{7,3},{8,12},{12,8},{9,1... | collective-permute-start | bytes 1572872 | tf_op jit(solution)/shard_map/ppermute | solution.py:82
  14.0 23.8 %collective-permute-start.9 = (bf16[16,128,128]{1,2,0:T(8,128)(2,1)S(1)}, bf16[16,128,128]{1,2,0:T(8,128)(2,1)S(1)}, u32[]{:S(2)}, u32[]{:S(2)}) collective-permute-start(bf16[16,128,128]{1,2,0:T(8,128)(2,1)S(1)} %bitcast.148), channel_id=1, source_target_pairs={{0,8},{8,0},{16,24},{24,16},{1,9},{9,1},{17,25},{25,17},{2,10},{10... | collective-permute-start | bytes 1572872 | tf_op jit(solution)/shard_map/ppermute | solution.py:70
  14.6 22.6 %collective-permute-start.11 = (bf16[16,128,128]{1,2,0:T(8,128)(2,1)S(1)}, bf16[16,128,128]{1,2,0:T(8,128)(2,1)S(1)}, u32[]{:S(2)}, u32[]{:S(2)}) collective-permute-start(bf16[16,128,128]{1,2,0:T(8,128)(2,1)S(1)} %bitcast.149), channel_id=1, source_target_pairs={{0,16},{8,24},{16,0},{24,8},{1,17},{9,25},{17,1},{25,9},{2,18},{10... | collective-permute-start | bytes 1572872 | tf_op jit(solution)/shard_map/ppermute | solution.py:71
  24.1 31.4 %collective-permute-start.8 = (bf16[16,128,128]{1,2,0:T(8,128)(2,1)S(1)}, bf16[16,128,128]{1,2,0:T(8,128)(2,1)S(1)}, u32[]{:S(2)}, u32[]{:S(2)}) collective-permute-start(bf16[16,128,128]{1,2,0:T(8,128)(2,1)S(1)} %bitcast.150), channel_id=1, source_target_pairs={{0,4},{4,0},{1,5},{5,1},{2,6},{6,2},{3,7},{7,3},{8,12},{12,8},{9,1... | collective-permute-start | bytes 1572872 | tf_op jit(solution)/shard_map/ppermute | solution.py:82
  26.1 22.3 %collective-permute-start.6 = (bf16[8,128,128]{2,1,0:T(8,128)(2,1)S(1)}, bf16[8,128,128]{2,1,0:T(8,128)(2,1)S(1)}, u32[]{:S(2)}, u32[]{:S(2)}) collective-permute-start(bf16[8,128,128]{2,1,0:T(8,128)(2,1)S(1)} %slice.25), channel_id=1, source_target_pairs={{0,16},{8,24},{16,0},{24,8},{1,17},{9,25},{17,1},{25,9},{2,18},{10... | collective-permute-start | bytes 786440 | tf_op jit(solution)/shard_map/ppermute | solution.py:75
  37.3 8.2 %collective-permute-start.5 = (bf16[8,128,128]{2,1,0:T(8,128)(2,1)S(1)}, bf16[8,128,128]{2,1,0:T(8,128)(2,1)S(1)}, u32[]{:S(2)}, u32[]{:S(2)}) collective-permute-start(bf16[8,128,128]{2,1,0:T(8,128)(2,1)S(1)} %slice.24), channel_id=1, source_target_pairs={{0,8},{8,0},{16,24},{24,16},{1,9},{9,1},{17,25},{25,17},{2,10},{10... | collective-permute-start | bytes 786440 | tf_op jit(solution)/shard_map/ppermute | solution.py:74
  37.9 10.4 %collective-permute-start.13 = (bf16[8,128,128]{1,2,0:T(8,128)(2,1)S(1)}, bf16[8,128,128]{1,2,0:T(8,128)(2,1)S(1)}, u32[]{:S(2)}, u32[]{:S(2)}) collective-permute-start(bf16[8,128,128]{1,2,0:T(8,128)(2,1)S(1)} %slice.26), channel_id=1, source_target_pairs={{0,8},{8,0},{16,24},{24,16},{1,9},{9,1},{17,25},{25,17},{2,10},{10... | collective-permute-start | bytes 786440 | tf_op jit(solution)/shard_map/ppermute | solution.py:74
  48.3 8.8 %collective-permute-start.10 = (bf16[16,128,128]{1,2,0:T(8,128)(2,1)S(1)}, bf16[16,128,128]{1,2,0:T(8,128)(2,1)S(1)}, u32[]{:S(2)}, u32[]{:S(2)}) collective-permute-start(bf16[16,128,128]{1,2,0:T(8,128)(2,1)S(1)} %collective-permute-done.9), channel_id=1, source_target_pairs={{0,4},{4,0},{1,5},{5,1},{2,6},{6,2},{3,7},{7,3},{8,12},{12,8},{9,1... | collective-permute-start | bytes 1572872 | tf_op jit(solution)/shard_map/ppermute | solution.py:82
  49.0 8.5 %collective-permute-start.12 = (bf16[16,128,128]{1,2,0:T(8,128)(2,1)S(1)}, bf16[16,128,128]{1,2,0:T(8,128)(2,1)S(1)}, u32[]{:S(2)}, u32[]{:S(2)}) collective-permute-start(bf16[16,128,128]{1,2,0:T(8,128)(2,1)S(1)} %collective-permute-done.11), channel_id=1, source_target_pairs={{0,4},{4,0},{1,5},{5,1},{2,6},{6,2},{3,7},{7,3},{8,12},{12,8},{9,1... | collective-permute-start | bytes 1572872 | tf_op jit(solution)/shard_map/ppermute | solution.py:82
  58.7 14.2 %collective-permute-start.18 = (bf16[128,2048]{0,1:T(8,128)(2,1)}, bf16[128,2048]{0,1:T(8,128)(2,1)S(1)}, u32[]{:S(2)}, u32[]{:S(2)}) collective-permute-start(bf16[128,2048]{0,1:T(8,128)(2,1)} %bitcast.8), channel_id=1, source_target_pairs={{0,8},{8,0},{16,24},{24,16},{1,9},{9,1},{17,25},{25,17},{2,10},{10... | collective-permute-start | bytes 1572872 | tf_op jit(solution)/shard_map/ppermute | solution.py:70
  59.3 15.3 %collective-permute-start.22 = (bf16[128,2048]{0,1:T(8,128)(2,1)}, bf16[128,2048]{0,1:T(8,128)(2,1)}, u32[]{:S(2)}, u32[]{:S(2)}) collective-permute-start(bf16[128,2048]{0,1:T(8,128)(2,1)} %bitcast.8), channel_id=1, source_target_pairs={{0,16},{8,24},{16,0},{24,8},{1,17},{9,25},{17,1},{25,9},{2,18},{10... | collective-permute-start | bytes 1572872 | tf_op jit(solution)/shard_map/ppermute | solution.py:71
  60.7 14.5 %collective-permute-start.16 = (bf16[128,2048]{0,1:T(8,128)(2,1)}, bf16[128,2048]{0,1:T(8,128)(2,1)}, u32[]{:S(2)}, u32[]{:S(2)}) collective-permute-start(bf16[128,2048]{0,1:T(8,128)(2,1)} %bitcast.8), channel_id=1, source_target_pairs={{0,4},{4,0},{1,5},{5,1},{2,6},{6,2},{3,7},{7,3},{8,12},{12,8},{9,1... | collective-permute-start | bytes 1572872 | tf_op jit(solution)/shard_map/ppermute | solution.py:82
  73.1 14.9 %collective-permute-start.27 = (bf16[64,2048]{0,1:T(8,128)(2,1)S(1)}, bf16[64,2048]{0,1:T(8,128)(2,1)S(1)}, u32[]{:S(2)}, u32[]{:S(2)}) collective-permute-start(bf16[64,2048]{0,1:T(8,128)(2,1)S(1)} %slice.29), channel_id=1, source_target_pairs={{0,16},{8,24},{16,0},{24,8},{1,17},{9,25},{17,1},{25,9},{2,18},{10... | collective-permute-start | bytes 786440 | tf_op jit(solution)/shard_map/ppermute | solution.py:75
  74.7 15.1 %collective-permute-start.26 = (bf16[64,2048]{0,1:T(8,128)(2,1)}, bf16[64,2048]{0,1:T(8,128)(2,1)S(1)}, u32[]{:S(2)}, u32[]{:S(2)}) collective-permute-start(bf16[64,2048]{0,1:T(8,128)(2,1)} %bitcast.147), channel_id=1, source_target_pairs={{0,8},{8,0},{16,24},{24,16},{1,9},{9,1},{17,25},{25,17},{2,10},{10... | collective-permute-start | bytes 786440 | tf_op jit(solution)/shard_map/ppermute | solution.py:74
  77.0 13.8 %collective-permute-start.17 = (bf16[128,1024]{1,0:T(8,128)(2,1)S(1)}, bf16[128,1024]{1,0:T(8,128)(2,1)S(1)}, u32[]{:S(2)}, u32[]{:S(2)}) collective-permute-start(bf16[128,1024]{1,0:T(8,128)(2,1)S(1)} %convolution_convert_fusion.6), channel_id=1, source_target_pairs={{0,4},{4,0},{8,12},{12,8},{16,20},{20,16},{24,28},{28,24},{1,5},{5... | collective-permute-start | bytes 786440 | tf_op jit(solution)/shard_map/ppermute | solution.py:179
  78.0 15.4 %collective-permute-start.19 = (bf16[128,1024]{1,0:T(8,128)(2,1)S(1)}, bf16[128,1024]{1,0:T(8,128)(2,1)S(1)}, u32[]{:S(2)}, u32[]{:S(2)}) collective-permute-start(bf16[128,1024]{1,0:T(8,128)(2,1)S(1)} %convolution_convert_fusion.5), channel_id=1, source_target_pairs={{0,8},{4,12},{8,0},{12,4},{16,24},{20,28},{24,16},{28,20},{1,9},{5... | collective-permute-start | bytes 786440 | tf_op jit(solution)/shard_map/ppermute | solution.py:179
  81.4 23.9 %collective-permute-start.23 = (bf16[128,1024]{1,0:T(8,128)(2,1)S(1)}, bf16[128,1024]{1,0:T(8,128)(2,1)S(1)}, u32[]{:S(2)}, u32[]{:S(2)}) collective-permute-start(bf16[128,1024]{1,0:T(8,128)(2,1)S(1)} %convolution_convert_fusion.3), channel_id=1, source_target_pairs={{0,16},{4,20},{8,24},{12,28},{16,0},{20,4},{24,8},{28,12},{1,17},{... | collective-permute-start | bytes 786440 | tf_op jit(solution)/shard_map/ppermute | solution.py:179
  93.5 18.7 %collective-permute-start.28 = (bf16[128,1024]{1,0:T(8,128)(2,1)S(1)}, bf16[128,1024]{1,0:T(8,128)(2,1)S(1)}, u32[]{:S(2)}, u32[]{:S(2)}) collective-permute-start(bf16[128,1024]{1,0:T(8,128)(2,1)S(1)} %convolution_convert_fusion.1), channel_id=1, source_target_pairs={{0,24},{4,28},{8,16},{12,20},{16,8},{20,12},{24,0},{28,4},{1,25},{... | collective-permute-start | bytes 786440 | tf_op jit(solution)/shard_map/ppermute | solution.py:179
  95.1 10.2 %collective-permute-start.21 = (bf16[128,1024]{1,0:T(8,128)(2,1)S(1)}, bf16[128,1024]{1,0:T(8,128)(2,1)S(1)}, u32[]{:S(2)}, u32[]{:S(2)}) collective-permute-start(bf16[128,1024]{1,0:T(8,128)(2,1)S(1)} %convolution_convert_fusion.4), channel_id=1, source_target_pairs={{0,12},{4,8},{8,4},{12,0},{16,28},{20,24},{24,20},{28,16},{1,13},{... | collective-permute-start | bytes 786440 | tf_op jit(solution)/shard_map/ppermute | solution.py:179
  96.0 16.2 %collective-permute-start.25 = (bf16[128,1024]{1,0:T(8,128)(2,1)S(1)}, bf16[128,1024]{1,0:T(8,128)(2,1)S(1)}, u32[]{:S(2)}, u32[]{:S(2)}) collective-permute-start(bf16[128,1024]{1,0:T(8,128)(2,1)S(1)} %convolution_convert_fusion.2), channel_id=1, source_target_pairs={{0,20},{4,16},{8,28},{12,24},{16,4},{20,0},{24,12},{28,8},{1,21},{... | collective-permute-start | bytes 786440 | tf_op jit(solution)/shard_map/ppermute | solution.py:179
  99.1 13.1 %collective-permute-start.30 = (bf16[128,1024]{1,0:T(8,128)(2,1)S(1)}, bf16[128,1024]{1,0:T(8,128)(2,1)S(1)}, u32[]{:S(2)}, u32[]{:S(2)}) collective-permute-start(bf16[128,1024]{1,0:T(8,128)(2,1)S(1)} %convolution_convert_fusion), channel_id=1, source_target_pairs={{0,28},{4,24},{8,20},{12,16},{16,12},{20,8},{24,4},{28,0},{1,29},{... | collective-permute-start | bytes 786440 | tf_op jit(solution)/shard_map/ppermute | solution.py:179
  (12 other events, 149.5 us)
Sparse Core Ops, SparseCore 0:
  113.7 43.2 reduce-scatter.1

commit v20 on v19

--- a/solution.py
+++ b/solution.py
@@ -169,11 +169,18 @@
             blocks = gather_blocks_square(local_context)
             width = out_weight.shape[1]
             by_row = jnp.zeros((chan_count, seg_rows, 2 * width), jnp.bfloat16)
+            own_partial = jnp.dot(blocks[0], out_weight, preferred_element_type=jnp.float32).astype(
+                jnp.bfloat16
+            )
+            own_partial, blocks[2] = lax.optimization_barrier((own_partial, blocks[2]))
             for b, block in enumerate(blocks):
                 r, t = b // 2, b % 2
-                partial = jnp.dot(block, out_weight, preferred_element_type=jnp.float32).astype(
-                    jnp.bfloat16
-                )
+                if b == 0:
+                    partial = own_partial
+                else:
+                    partial = jnp.dot(block, out_weight, preferred_element_type=jnp.float32).astype(
+                        jnp.bfloat16
+                    )
                 if b:
                     pairs = [(h * 2 + l, (h ^ r) * 2 + (l ^ t)) for h in range(4) for l in range(2)]
                     partial = lax.ppermute(partial, SEQ, pairs)

time: 166 us -> 165 us (level)
  matrix products: 20 us -> 18.2 us
    dot_general x8 -> x7, matrix products: 10.6 us -> 6.49 us  [per_device(): jnp.dot(block, out_weight, preferred_element_type=jnp.float32)]
    dot_general x0 -> x1, matrix products: none -> 3.07 us  [per_device(): jnp.dot(blocks[0], out_weight, preferred_element_type=jnp.float32)]
    reduce_scatter x1, waiting for transfers between devices: 43.4 us -> 45.7 us  [per_device(): lax.psum_scatter(by_row, 'chan', scatter_dimension=0, tiled=True)[0]]
    ppermute x7, waiting for transfers between devices: 15 us -> 12.8 us  [per_device(): partial = lax.ppermute(partial, SEQ, pairs)]
  transfers between devices with their start and end apart: 32 -> 32, of which waited for: 13 -> 14; matrix products, arithmetic and copies ran while one was open for 15% -> 14% of each run, Pallas kernels for 0% -> 0%
where the time goes in v20:
time: 165 us
  waiting for transfers between devices  99.9 us (61%)
  starting transfers between devices  22 us (13%)
  matrix products  18.2 us (11%)
  between operations  13.9 us (8%)
  local copies, waits for them, and re-layouts  6.08 us (4%)
  other arithmetic  4.7 us (3%)
    reduce_scatter x1, waiting for transfers between devices, per_device(): lax.psum_scatter(by_row, 'chan', scatter_dimension=0, tiled=True)[0]  45.7 us
    ppermute x3, waiting for transfers between devices, gather_blocks_square(): from_x = lax.ppermute(x, 'hi', swap('hi', 1, 4))  17.9 us
    ppermute x7, waiting for transfers between devices, per_device(): partial = lax.ppermute(partial, SEQ, pairs)  12.8 us
    ppermute x3, waiting for transfers between devices, gather_blocks_square(): from_y = lax.ppermute(x, 'hi', swap('hi', 2, 4))  10.7 us
    ppermute x3, waiting for transfers between devices, gather_blocks_square(): lax.ppermute(from_x[half:], 'hi', swap('hi', 2, 4))  6.77 us
    dot_general x7, matrix products, per_device(): jnp.dot(block, out_weight, preferred_element_type=jnp.float32)  6.49 us
    dot_general x8, matrix products, attention_by_head(): jnp.einsum('hqd,hkd->hqk', queries, keys, preferred_element_type=jnp.floa...  6.09 us
    ppermute x7, starting transfers between devices, per_device(): partial = lax.ppermute(partial, SEQ, pairs)  5.57 us
  transfers between devices with their start and end apart: 32, of which 14 were waited for; matrix products, arithmetic and copies ran while one was open for 14% of the time, Pallas kernels for 0%

profile of v20, /device:TPU:0, one launch (start us, length us, event | category | flops | bytes accessed | tf_op | source)
XLA Modules:
  0.0 164.9 jit_solution(12220772534033618788)
XLA Ops:
  8.2 3.0 %collective-permute-start = (bf16[16,128,128]{2,1,0:T(8,128)(2,1)S(1)}, bf16[16,128,128]{2,1,0:T(8,128)(2,1)}, u32[]{:S(2)}, u32[]{:S(2)}) collective-permute-start(bf16[16,128,128]{2,1,0:T(8,128)(2,1)S(1)} %bitcast.155), channel_id=1, source_target_pairs={{0,8},{8,0},{16,24},{24,16},{1,9},{9,1},{17,25},{25,17},{2,10},{10... | collective-permute-start | bytes 1572872 | tf_op jit(solution)/shard_map/ppermute | solution.py:70
  11.2 1.5 collective-permute-start.3
  14.9 9.1 %collective-permute-done = bf16[16,128,128]{2,1,0:T(8,128)(2,1)} collective-permute-done((bf16[16,128,128]{2,1,0:T(8,128)(2,1)S(1)}, bf16[16,128,128]{2,1,0:T(8,128)(2,1)}, u32[]{:S(2)}, u32[]{:S(2)}) %collective-permute-start) | collective-permute-done | bytes 524320 | tf_op jit(solution)/shard_map/ppermute | solution.py:70
  26.1 1.5 collective-permute-start.6
  27.6 9.7 %collective-permute-done.11 = bf16[16,128,128]{1,2,0:T(8,128)(2,1)S(1)} collective-permute-done((bf16[16,128,128]{1,2,0:T(8,128)(2,1)S(1)}, bf16[16,128,128]{1,2,0:T(8,128)(2,1)S(1)}, u32[]{:S(2)}, u32[]{:S(2)}) %collective-permute-start.11) | collective-permute-done | bytes 524320 | tf_op jit(solution)/shard_map/ppermute | solution.py:71
  37.9 2.1 %collective-permute-start.13 = (bf16[8,128,128]{1,2,0:T(8,128)(2,1)S(1)}, bf16[8,128,128]{1,2,0:T(8,128)(2,1)S(1)}, u32[]{:S(2)}, u32[]{:S(2)}) collective-permute-start(bf16[8,128,128]{1,2,0:T(8,128)(2,1)S(1)} %slice.26), channel_id=1, source_target_pairs={{0,8},{8,0},{16,24},{24,16},{1,9},{9,1},{17,25},{25,17},{2,10},{10... | collective-permute-start | bytes 786440 | tf_op jit(solution)/shard_map/ppermute | solution.py:74
  40.0 1.5 fusion.89
  42.0 1.6 collective-permute-start.14
  43.6 1.5 fusion.91
  45.5 2.8 %collective-permute-done.13 = bf16[8,128,128]{1,2,0:T(8,128)(2,1)S(1)} collective-permute-done((bf16[8,128,128]{1,2,0:T(8,128)(2,1)S(1)}, bf16[8,128,128]{1,2,0:T(8,128)(2,1)S(1)}, u32[]{:S(2)}, u32[]{:S(2)}) %collective-permute-start.13) | collective-permute-done | bytes 262176 | tf_op jit(solution)/shard_map/ppermute | solution.py:74
  53.3 2.2 %fusion.17 = (f32[16,128]{1,0:T(8,128)S(1)}, f32[16,128]{1,0:T(8,128)S(1)}, f32[16,128]{1,0:T(8,128)S(1)}, f32[16,128]{1,0:T(8,128)S(1)}, f32[16,128]{1,0:T(8,12...) fusion(f32[16,128,128]{1,2,0:T(8,128)S(1)} %get-tuple-element.42, ...), kind=kLoop, calls=%fused_computation.46 | loop fusion | flops 6275072 | bytes 8593408 | tf_op jit(solution)/shard_map/reduce_sum | solution.py:106
  60.0 3.1 %convolution_convert_fusion.7 = bf16[128,1024]{1,0:T(8,128)(2,1)S(1)} fusion(bf16[128,2048]{0,1:T(8,128)(2,1)S(1)} %bitcast.154, bf16[2048,1024]{1,0:T(8,128)(2,1)} %param.9), kind=kOutput, calls=%fused_computation.33 | convolution fusion | flops 537001984 | bytes 4980736 | tf_op jit(solution)/shard_map/dot_general | solution.py:172
  63.1 8.8 %collective-permute-done.16 = bf16[128,2048]{0,1:T(8,128)(2,1)S(1)} collective-permute-done((bf16[128,2048]{0,1:T(8,128)(2,1)S(1)}, bf16[128,2048]{0,1:T(8,128)(2,1)S(1)}, u32[]{:S(2)}, u32[]{:S(2)}) %collective-permute-start.16) | collective-permute-done | bytes 524320 | tf_op jit(solution)/shard_map/ppermute | solution.py:70
  72.1 1.6 collective-permute-start.27
  76.1 1.6 collective-permute-start.19
  77.6 1.8 %convolution_convert_fusion.3 = bf16[128,1024]{1,0:T(8,128)(2,1)S(1)} fusion(bf16[128,2048]{0,1:T(8,128)(2,1)} %collective-permute-done.22, bf16[2048,1024]{1,0:T(8,128)(2,1)S(1)} %copy-done.1), kind=kOutput, calls=%fused_computation.29 | convolution fusion | flops 537001984 | bytes 4980736 | tf_op jit(solution)/shard_map/dot_general | solution.py:181
  80.3 6.8 %collective-permute-done.27 = bf16[64,2048]{0,1:T(8,128)(2,1)S(1)} collective-permute-done((bf16[64,2048]{0,1:T(8,128)(2,1)S(1)}, bf16[64,2048]{0,1:T(8,128)(2,1)S(1)}, u32[]{:S(2)}, u32[]{:S(2)}) %collective-permute-start.27) | collective-permute-done | bytes 262176 | tf_op jit(solution)/shard_map/ppermute | solution.py:75
  87.1 1.7 %collective-permute-done.26 = bf16[64,2048]{0,1:T(8,128)(2,1)S(1)} collective-permute-done((bf16[64,2048]{0,1:T(8,128)(2,1)}, bf16[64,2048]{0,1:T(8,128)(2,1)S(1)}, u32[]{:S(2)}, u32[]{:S(2)}) %collective-permute-start.26) | collective-permute-done | bytes 262176 | tf_op jit(solution)/shard_map/ppermute | solution.py:74
  90.5 2.1 %collective-permute-done.19 = bf16[128,1024]{1,0:T(8,128)(2,1)S(1)} collective-permute-done((bf16[128,1024]{1,0:T(8,128)(2,1)S(1)}, bf16[128,1024]{1,0:T(8,128)(2,1)S(1)}, u32[]{:S(2)}, u32[]{:S(2)}) %collective-permute-start.19) | collective-permute-done | bytes 262176 | tf_op jit(solution)/shard_map/ppermute | solution.py:186
  95.0 2.4 %collective-permute-start.25 = (bf16[128,1024]{1,0:T(8,128)(2,1)S(1)}, bf16[128,1024]{1,0:T(8,128)(2,1)S(1)}, u32[]{:S(2)}, u32[]{:S(2)}) collective-permute-start(bf16[128,1024]{1,0:T(8,128)(2,1)S(1)} %convolution_convert_fusion.2), channel_id=1, source_target_pairs={{0,20},{4,16},{8,28},{12,24},{16,4},{20,0},{24,12},{28,8},{1,21},{... | collective-permute-start | bytes 786440 | tf_op jit(solution)/shard_map/ppermute | solution.py:186
  98.2 6.1 %collective-permute-done.21 = bf16[128,1024]{1,0:T(8,128)(2,1)S(1)} collective-permute-done((bf16[128,1024]{1,0:T(8,128)(2,1)S(1)}, bf16[128,1024]{1,0:T(8,128)(2,1)S(1)}, u32[]{:S(2)}, u32[]{:S(2)}) %collective-permute-start.21) | collective-permute-done | bytes 262176 | tf_op jit(solution)/shard_map/ppermute | solution.py:186
  104.4 3.2 %collective-permute-done.25 = bf16[128,1024]{1,0:T(8,128)(2,1)S(1)} collective-permute-done((bf16[128,1024]{1,0:T(8,128)(2,1)S(1)}, bf16[128,1024]{1,0:T(8,128)(2,1)S(1)}, u32[]{:S(2)}, u32[]{:S(2)}) %collective-permute-start.25) | collective-permute-done | bytes 262176 | tf_op jit(solution)/shard_map/ppermute | solution.py:186
  110.5 45.7 %reduce-scatter.2.cloned.1.call-done = bf16[1,128,2048]{2,1,0:T(8,128)(2,1)} async-done(((bf16[4,128,2048]{2,1,0:T(8,128)(2,1)}), bf16[1,128,2048]{2,1,0:T(8,128)(2,1)}) %reduce-scatter.2.cloned.1.call-update) | async-done | bytes 524304 | tf_op jit(solution)/shard_map/reduce_scatter | solution.py:191
  156.1 2.0 %fusion.14 = bf16[128,2048]{1,0:T(8,128)(2,1)} fusion(bf16[128,2048]{1,0:T(8,128)(2,1)S(1)} %copy-done.3, bf16[1,128,2048]{2,1,0:T(8,128)(2,1)} %reduce-scatter.2.cloned.1.call-done), kind=kLoop, calls=%fused_computation.35 | loop fusion | flops 1048576 | bytes 1572864 | tf_op jit(solution)/shard_map/convert_element_type | solution.py:192
  (104 shorter events, 27.7 us)
Async XLA Ops:
  6.5 149.6 %reduce-scatter.2.cloned.1.call-start = ((), (), s32[]{:S(2)}) async-start(), calls=%async_computation.1 | async-start | bytes 2621440 | tf_op jit(solution)/shard_map/reduce_scatter | solution.py:191
  8.2 15.9 %collective-permute-start = (bf16[16,128,128]{2,1,0:T(8,128)(2,1)S(1)}, bf16[16,128,128]{2,1,0:T(8,128)(2,1)}, u32[]{:S(2)}, u32[]{:S(2)}) collective-permute-start(bf16[16,128,128]{2,1,0:T(8,128)(2,1)S(1)} %bitcast.155), channel_id=1, source_target_pairs={{0,8},{8,0},{16,24},{24,16},{1,9},{9,1},{17,25},{25,17},{2,10},{10... | collective-permute-start | bytes 1572872 | tf_op jit(solution)/shard_map/ppermute | solution.py:70
  11.2 14.8 %collective-permute-start.3 = (bf16[16,128,128]{2,1,0:T(8,128)(2,1)S(1)}, bf16[16,128,128]{2,1,0:T(8,128)(2,1)S(1)}, u32[]{:S(2)}, u32[]{:S(2)}) collective-permute-start(bf16[16,128,128]{2,1,0:T(8,128)(2,1)S(1)} %bitcast.156), channel_id=1, source_target_pairs={{0,16},{8,24},{16,0},{24,8},{1,17},{9,25},{17,1},{25,9},{2,18},{10... | collective-permute-start | bytes 1572872 | tf_op jit(solution)/shard_map/ppermute | solution.py:71
  12.7 29.3 %collective-permute-start.1 = (bf16[16,128,128]{2,1,0:T(8,128)(2,1)S(1)}, bf16[16,128,128]{2,1,0:T(8,128)(2,1)}, u32[]{:S(2)}, u32[]{:S(2)}) collective-permute-start(bf16[16,128,128]{2,1,0:T(8,128)(2,1)S(1)} %bitcast.157), channel_id=1, source_target_pairs={{0,4},{4,0},{1,5},{5,1},{2,6},{6,2},{3,7},{7,3},{8,12},{12,8},{9,1... | collective-permute-start | bytes 1572872 | tf_op jit(solution)/shard_map/ppermute | solution.py:82
  14.0 23.8 %collective-permute-start.9 = (bf16[16,128,128]{1,2,0:T(8,128)(2,1)S(1)}, bf16[16,128,128]{1,2,0:T(8,128)(2,1)S(1)}, u32[]{:S(2)}, u32[]{:S(2)}) collective-permute-start(bf16[16,128,128]{1,2,0:T(8,128)(2,1)S(1)} %bitcast.146), channel_id=1, source_target_pairs={{0,8},{8,0},{16,24},{24,16},{1,9},{9,1},{17,25},{25,17},{2,10},{10... | collective-permute-start | bytes 1572872 | tf_op jit(solution)/shard_map/ppermute | solution.py:70
  14.6 22.6 %collective-permute-start.11 = (bf16[16,128,128]{1,2,0:T(8,128)(2,1)S(1)}, bf16[16,128,128]{1,2,0:T(8,128)(2,1)S(1)}, u32[]{:S(2)}, u32[]{:S(2)}) collective-permute-start(bf16[16,128,128]{1,2,0:T(8,128)(2,1)S(1)} %bitcast.147), channel_id=1, source_target_pairs={{0,16},{8,24},{16,0},{24,8},{1,17},{9,25},{17,1},{25,9},{2,18},{10... | collective-permute-start | bytes 1572872 | tf_op jit(solution)/shard_map/ppermute | solution.py:71
  24.1 31.5 %collective-permute-start.8 = (bf16[16,128,128]{1,2,0:T(8,128)(2,1)S(1)}, bf16[16,128,128]{1,2,0:T(8,128)(2,1)S(1)}, u32[]{:S(2)}, u32[]{:S(2)}) collective-permute-start(bf16[16,128,128]{1,2,0:T(8,128)(2,1)S(1)} %bitcast.148), channel_id=1, source_target_pairs={{0,4},{4,0},{1,5},{5,1},{2,6},{6,2},{3,7},{7,3},{8,12},{12,8},{9,1... | collective-permute-start | bytes 1572872 | tf_op jit(solution)/shard_map/ppermute | solution.py:82
  26.1 22.3 %collective-permute-start.6 = (bf16[8,128,128]{2,1,0:T(8,128)(2,1)S(1)}, bf16[8,128,128]{2,1,0:T(8,128)(2,1)S(1)}, u32[]{:S(2)}, u32[]{:S(2)}) collective-permute-start(bf16[8,128,128]{2,1,0:T(8,128)(2,1)S(1)} %slice.25), channel_id=1, source_target_pairs={{0,16},{8,24},{16,0},{24,8},{1,17},{9,25},{17,1},{25,9},{2,18},{10... | collective-permute-start | bytes 786440 | tf_op jit(solution)/shard_map/ppermute | solution.py:75
  37.3 8.2 %collective-permute-start.5 = (bf16[8,128,128]{2,1,0:T(8,128)(2,1)S(1)}, bf16[8,128,128]{2,1,0:T(8,128)(2,1)S(1)}, u32[]{:S(2)}, u32[]{:S(2)}) collective-permute-start(bf16[8,128,128]{2,1,0:T(8,128)(2,1)S(1)} %slice.24), channel_id=1, source_target_pairs={{0,8},{8,0},{16,24},{24,16},{1,9},{9,1},{17,25},{25,17},{2,10},{10... | collective-permute-start | bytes 786440 | tf_op jit(solution)/shard_map/ppermute | solution.py:74
  37.9 10.4 %collective-permute-start.13 = (bf16[8,128,128]{1,2,0:T(8,128)(2,1)S(1)}, bf16[8,128,128]{1,2,0:T(8,128)(2,1)S(1)}, u32[]{:S(2)}, u32[]{:S(2)}) collective-permute-start(bf16[8,128,128]{1,2,0:T(8,128)(2,1)S(1)} %slice.26), channel_id=1, source_target_pairs={{0,8},{8,0},{16,24},{24,16},{1,9},{9,1},{17,25},{25,17},{2,10},{10... | collective-permute-start | bytes 786440 | tf_op jit(solution)/shard_map/ppermute | solution.py:74
  48.3 8.8 %collective-permute-start.10 = (bf16[16,128,128]{1,2,0:T(8,128)(2,1)S(1)}, bf16[16,128,128]{1,2,0:T(8,128)(2,1)S(1)}, u32[]{:S(2)}, u32[]{:S(2)}) collective-permute-start(bf16[16,128,128]{1,2,0:T(8,128)(2,1)S(1)} %collective-permute-done.9), channel_id=1, source_target_pairs={{0,4},{4,0},{1,5},{5,1},{2,6},{6,2},{3,7},{7,3},{8,12},{12,8},{9,1... | collective-permute-start | bytes 1572872 | tf_op jit(solution)/shard_map/ppermute | solution.py:82
  49.0 8.5 %collective-permute-start.12 = (bf16[16,128,128]{1,2,0:T(8,128)(2,1)S(1)}, bf16[16,128,128]{1,2,0:T(8,128)(2,1)S(1)}, u32[]{:S(2)}, u32[]{:S(2)}) collective-permute-start(bf16[16,128,128]{1,2,0:T(8,128)(2,1)S(1)} %collective-permute-done.11), channel_id=1, source_target_pairs={{0,4},{4,0},{1,5},{5,1},{2,6},{6,2},{3,7},{7,3},{8,12},{12,8},{9,1... | collective-permute-start | bytes 1572872 | tf_op jit(solution)/shard_map/ppermute | solution.py:82
  57.9 14.0 %collective-permute-start.16 = (bf16[128,2048]{0,1:T(8,128)(2,1)S(1)}, bf16[128,2048]{0,1:T(8,128)(2,1)S(1)}, u32[]{:S(2)}, u32[]{:S(2)}) collective-permute-start(bf16[128,2048]{0,1:T(8,128)(2,1)S(1)} %bitcast.151), channel_id=1, source_target_pairs={{0,8},{8,0},{16,24},{24,16},{1,9},{9,1},{17,25},{25,17},{2,10},{10... | collective-permute-start | bytes 1572872 | tf_op jit(solution)/shard_map/ppermute | solution.py:70
  58.7 15.1 %collective-permute-start.22 = (bf16[128,2048]{0,1:T(8,128)(2,1)S(1)}, bf16[128,2048]{0,1:T(8,128)(2,1)}, u32[]{:S(2)}, u32[]{:S(2)}) collective-permute-start(bf16[128,2048]{0,1:T(8,128)(2,1)S(1)} %bitcast.152), channel_id=1, source_target_pairs={{0,16},{8,24},{16,0},{24,8},{1,17},{9,25},{17,1},{25,9},{2,18},{10... | collective-permute-start | bytes 1572872 | tf_op jit(solution)/shard_map/ppermute | solution.py:71
  60.0 14.2 %collective-permute-start.17 = (bf16[128,2048]{0,1:T(8,128)(2,1)S(1)}, bf16[128,2048]{0,1:T(8,128)(2,1)S(1)}, u32[]{:S(2)}, u32[]{:S(2)}) collective-permute-start(bf16[128,2048]{0,1:T(8,128)(2,1)S(1)} %bitcast.153), channel_id=1, source_target_pairs={{0,4},{4,0},{1,5},{5,1},{2,6},{6,2},{3,7},{7,3},{8,12},{12,8},{9,1... | collective-permute-start | bytes 1572872 | tf_op jit(solution)/shard_map/ppermute | solution.py:82
  72.1 14.9 %collective-permute-start.27 = (bf16[64,2048]{0,1:T(8,128)(2,1)S(1)}, bf16[64,2048]{0,1:T(8,128)(2,1)S(1)}, u32[]{:S(2)}, u32[]{:S(2)}) collective-permute-start(bf16[64,2048]{0,1:T(8,128)(2,1)S(1)} %slice.29), channel_id=1, source_target_pairs={{0,16},{8,24},{16,0},{24,8},{1,17},{9,25},{17,1},{25,9},{2,18},{10... | collective-permute-start | bytes 786440 | tf_op jit(solution)/shard_map/ppermute | solution.py:75
  73.7 15.1 %collective-permute-start.26 = (bf16[64,2048]{0,1:T(8,128)(2,1)}, bf16[64,2048]{0,1:T(8,128)(2,1)S(1)}, u32[]{:S(2)}, u32[]{:S(2)}) collective-permute-start(bf16[64,2048]{0,1:T(8,128)(2,1)} %bitcast.145), channel_id=1, source_target_pairs={{0,8},{8,0},{16,24},{24,16},{1,9},{9,1},{17,25},{25,17},{2,10},{10... | collective-permute-start | bytes 786440 | tf_op jit(solution)/shard_map/ppermute | solution.py:74
  75.0 14.8 %collective-permute-start.18 = (bf16[128,1024]{1,0:T(8,128)(2,1)S(1)}, bf16[128,1024]{1,0:T(8,128)(2,1)S(1)}, u32[]{:S(2)}, u32[]{:S(2)}) collective-permute-start(bf16[128,1024]{1,0:T(8,128)(2,1)S(1)} %convolution_convert_fusion.6), channel_id=1, source_target_pairs={{0,4},{4,0},{8,12},{12,8},{16,20},{20,16},{24,28},{28,24},{1,5},{5... | collective-permute-start | bytes 786440 | tf_op jit(solution)/shard_map/ppermute | solution.py:186
  76.1 16.5 %collective-permute-start.19 = (bf16[128,1024]{1,0:T(8,128)(2,1)S(1)}, bf16[128,1024]{1,0:T(8,128)(2,1)S(1)}, u32[]{:S(2)}, u32[]{:S(2)}) collective-permute-start(bf16[128,1024]{1,0:T(8,128)(2,1)S(1)} %convolution_convert_fusion.5), channel_id=1, source_target_pairs={{0,8},{4,12},{8,0},{12,4},{16,24},{20,28},{24,16},{28,20},{1,9},{5... | collective-permute-start | bytes 786440 | tf_op jit(solution)/shard_map/ppermute | solution.py:186
  79.5 24.9 %collective-permute-start.23 = (bf16[128,1024]{1,0:T(8,128)(2,1)S(1)}, bf16[128,1024]{1,0:T(8,128)(2,1)S(1)}, u32[]{:S(2)}, u32[]{:S(2)}) collective-permute-start(bf16[128,1024]{1,0:T(8,128)(2,1)S(1)} %convolution_convert_fusion.3), channel_id=1, source_target_pairs={{0,16},{4,20},{8,24},{12,28},{16,0},{20,4},{24,8},{28,12},{1,17},{... | collective-permute-start | bytes 786440 | tf_op jit(solution)/shard_map/ppermute | solution.py:186
  92.5 15.2 %collective-permute-start.28 = (bf16[128,1024]{1,0:T(8,128)(2,1)S(1)}, bf16[128,1024]{1,0:T(8,128)(2,1)S(1)}, u32[]{:S(2)}, u32[]{:S(2)}) collective-permute-start(bf16[128,1024]{1,0:T(8,128)(2,1)S(1)} %convolution_convert_fusion.1), channel_id=1, source_target_pairs={{0,24},{4,28},{8,16},{12,20},{16,8},{20,12},{24,0},{28,4},{1,25},{... | collective-permute-start | bytes 786440 | tf_op jit(solution)/shard_map/ppermute | solution.py:186
  94.2 10.2 %collective-permute-start.21 = (bf16[128,1024]{1,0:T(8,128)(2,1)S(1)}, bf16[128,1024]{1,0:T(8,128)(2,1)S(1)}, u32[]{:S(2)}, u32[]{:S(2)}) collective-permute-start(bf16[128,1024]{1,0:T(8,128)(2,1)S(1)} %convolution_convert_fusion.4), channel_id=1, source_target_pairs={{0,12},{4,8},{8,4},{12,0},{16,28},{20,24},{24,20},{28,16},{1,13},{... | collective-permute-start | bytes 786440 | tf_op jit(solution)/shard_map/ppermute | solution.py:186
  95.0 12.6 %collective-permute-start.25 = (bf16[128,1024]{1,0:T(8,128)(2,1)S(1)}, bf16[128,1024]{1,0:T(8,128)(2,1)S(1)}, u32[]{:S(2)}, u32[]{:S(2)}) collective-permute-start(bf16[128,1024]{1,0:T(8,128)(2,1)S(1)} %convolution_convert_fusion.2), channel_id=1, source_target_pairs={{0,20},{4,16},{8,28},{12,24},{16,4},{20,0},{24,12},{28,8},{1,21},{... | collective-permute-start | bytes 786440 | tf_op jit(solution)/shard_map/ppermute | solution.py:186
  98.2 10.9 %collective-permute-start.30 = (bf16[128,1024]{1,0:T(8,128)(2,1)S(1)}, bf16[128,1024]{1,0:T(8,128)(2,1)S(1)}, u32[]{:S(2)}, u32[]{:S(2)}) collective-permute-start(bf16[128,1024]{1,0:T(8,128)(2,1)S(1)} %convolution_convert_fusion), channel_id=1, source_target_pairs={{0,28},{4,24},{8,20},{12,16},{16,12},{20,8},{24,4},{28,0},{1,29},{... | collective-permute-start | bytes 786440 | tf_op jit(solution)/shard_map/ppermute | solution.py:186
  (12 other events, 149.3 us)
Sparse Core Ops, SparseCore 0:
  110.6 45.4 reduce-scatter.1

commit v21 on v20

--- a/solution.py
+++ b/solution.py
@@ -168,6 +168,7 @@
             core = lax.axis_index("lo")
             blocks = gather_blocks_square(local_context)
             width = out_weight.shape[1]
+            chan_index = lax.axis_index("chan")
             by_row = jnp.zeros((chan_count, seg_rows, 2 * width), jnp.bfloat16)
             own_partial = jnp.dot(blocks[0], out_weight, preferred_element_type=jnp.float32).astype(
                 jnp.bfloat16
@@ -185,11 +186,18 @@
                     pairs = [(h * 2 + l, (h ^ r) * 2 + (l ^ t)) for h in range(4) for l in range(2)]
                     partial = lax.ppermute(partial, SEQ, pairs)
                 source = (chip ^ r) * 2 + (core ^ t)
+                residual_part = lax.dynamic_slice_in_dim(residual, (source % 2) * width, width, 1)
+                partial = jnp.where(
+                    source // 2 == chan_index,
+                    (partial.astype(jnp.float32) + residual_part.astype(jnp.float32)).astype(
+                        jnp.bfloat16
+                    ),
+                    partial,
+                )
                 by_row = lax.dynamic_update_slice(
                     by_row, partial[None], (source // 2, 0, (source % 2) * width)
                 )
-            ordered = lax.psum_scatter(by_row, "chan", scatter_dimension=0, tiled=True)[0]
-            return (residual.astype(jnp.float32) + ordered.astype(jnp.float32)).astype(jnp.bfloat16)
+            return lax.psum_scatter(by_row, "chan", scatter_dimension=0, tiled=True)[0]
         gathered = gather_seq(local_context)
         group = seq_count // chan_count
         chunks = 2

time: 165 us -> 164 us (level)
    reduce_scatter x1, waiting for transfers between devices: 45.7 us -> 43.5 us  [per_device(): return lax.psum_scatter(by_row, 'chan', scatter_dimension=0, tiled=True)[0]]
    convert_element_type x1 -> x0, other arithmetic: 1.96 us -> none  [per_device(): (residual.astype(jnp.float32) + ordered.astype(jnp.float32)).astype(jnp.b...]
    ppermute x7, waiting for transfers between devices: 12.8 us -> 14.7 us  [per_device(): partial = lax.ppermute(partial, SEQ, pairs)]
  transfers between devices with their start and end apart: 32 -> 32, of which waited for: 14 -> 13; matrix products, arithmetic and copies ran while one was open for 14% -> 15% of each run, Pallas kernels for 0% -> 0%
where the time goes in v21:
time: 164 us; the launch traced here: 163 us
  waiting for transfers between devices  99.6 us (61%)
  starting transfers between devices  22.1 us (13%)
  matrix products  18.2 us (11%)
  between operations  14 us (9%)
  local copies, waits for them, and re-layouts  5.88 us (4%)
  other arithmetic  3.45 us (2%)
    reduce_scatter x1, waiting for transfers between devices, per_device(): return lax.psum_scatter(by_row, 'chan', scatter_dimension=0, tiled=True)[0]  43.5 us
    ppermute x3, waiting for transfers between devices, gather_blocks_square(): from_x = lax.ppermute(x, 'hi', swap('hi', 1, 4))  17.9 us
    ppermute x7, waiting for transfers between devices, per_device(): partial = lax.ppermute(partial, SEQ, pairs)  14.7 us
    ppermute x3, waiting for transfers between devices, gather_blocks_square(): from_y = lax.ppermute(x, 'hi', swap('hi', 2, 4))  10.7 us
    ppermute x3, waiting for transfers between devices, gather_blocks_square(): lax.ppermute(from_x[half:], 'hi', swap('hi', 2, 4))  6.66 us
    dot_general x7, matrix products, per_device(): jnp.dot(block, out_weight, preferred_element_type=jnp.float32)  6.47 us
    dot_general x8, matrix products, attention_by_head(): jnp.einsum('hqd,hkd->hqk', queries, keys, preferred_element_type=jnp.floa...  6.09 us
    ppermute x7, starting transfers between devices, per_device(): partial = lax.ppermute(partial, SEQ, pairs)  5.62 us
  transfers between devices with their start and end apart: 32, of which 13 were waited for; matrix products, arithmetic and copies ran while one was open for 15% of the time, Pallas kernels for 0%

profile of v21, /device:TPU:0, one launch (start us, length us, event | category | flops | bytes accessed | tf_op | source)
XLA Modules:
  0.0 163.2 jit_solution(5924231989371017180)
XLA Ops:
  8.2 3.0 %collective-permute-start = (bf16[16,128,128]{2,1,0:T(8,128)(2,1)S(1)}, bf16[16,128,128]{2,1,0:T(8,128)(2,1)}, u32[]{:S(2)}, u32[]{:S(2)}) collective-permute-start(bf16[16,128,128]{2,1,0:T(8,128)(2,1)S(1)} %bitcast.169), channel_id=1, source_target_pairs={{0,8},{8,0},{16,24},{24,16},{1,9},{9,1},{17,25},{25,17},{2,10},{10... | collective-permute-start | bytes 1572872 | tf_op jit(solution)/shard_map/ppermute | solution.py:70
  11.2 1.5 collective-permute-start.3
  14.9 9.1 %collective-permute-done = bf16[16,128,128]{2,1,0:T(8,128)(2,1)} collective-permute-done((bf16[16,128,128]{2,1,0:T(8,128)(2,1)S(1)}, bf16[16,128,128]{2,1,0:T(8,128)(2,1)}, u32[]{:S(2)}, u32[]{:S(2)}) %collective-permute-start) | collective-permute-done | bytes 524320 | tf_op jit(solution)/shard_map/ppermute | solution.py:70
  26.1 1.5 collective-permute-start.6
  27.6 9.7 %collective-permute-done.11 = bf16[16,128,128]{1,2,0:T(8,128)(2,1)S(1)} collective-permute-done((bf16[16,128,128]{1,2,0:T(8,128)(2,1)S(1)}, bf16[16,128,128]{1,2,0:T(8,128)(2,1)S(1)}, u32[]{:S(2)}, u32[]{:S(2)}) %collective-permute-start.11) | collective-permute-done | bytes 524320 | tf_op jit(solution)/shard_map/ppermute | solution.py:71
  37.9 2.1 %collective-permute-start.13 = (bf16[8,128,128]{1,2,0:T(8,128)(2,1)S(1)}, bf16[8,128,128]{1,2,0:T(8,128)(2,1)S(1)}, u32[]{:S(2)}, u32[]{:S(2)}) collective-permute-start(bf16[8,128,128]{1,2,0:T(8,128)(2,1)S(1)} %slice.26), channel_id=1, source_target_pairs={{0,8},{8,0},{16,24},{24,16},{1,9},{9,1},{17,25},{25,17},{2,10},{10... | collective-permute-start | bytes 786440 | tf_op jit(solution)/shard_map/ppermute | solution.py:74
  40.0 1.5 fusion.112
  42.0 1.6 collective-permute-start.14
  43.6 1.5 fusion.114
  45.5 2.8 %collective-permute-done.13 = bf16[8,128,128]{1,2,0:T(8,128)(2,1)S(1)} collective-permute-done((bf16[8,128,128]{1,2,0:T(8,128)(2,1)S(1)}, bf16[8,128,128]{1,2,0:T(8,128)(2,1)S(1)}, u32[]{:S(2)}, u32[]{:S(2)}) %collective-permute-start.13) | collective-permute-done | bytes 262176 | tf_op jit(solution)/shard_map/ppermute | solution.py:74
  53.3 2.2 %fusion.16 = (f32[16,128]{1,0:T(8,128)S(1)}, f32[16,128]{1,0:T(8,128)S(1)}, f32[16,128]{1,0:T(8,128)S(1)}, f32[16,128]{1,0:T(8,128)S(1)}, f32[16,128]{1,0:T(8,12...) fusion(f32[16,128,128]{1,2,0:T(8,128)S(1)} %get-tuple-element.42, ...), kind=kLoop, calls=%fused_computation.44 | loop fusion | flops 6275072 | bytes 8593408 | tf_op jit(solution)/shard_map/reduce_sum | solution.py:106
  58.7 1.4 collective-permute-start.22
  60.0 3.1 %convolution_convert_fusion.7 = bf16[128,1024]{1,0:T(8,128)(2,1)S(1)} fusion(bf16[128,2048]{0,1:T(8,128)(2,1)S(1)} %bitcast.168, bf16[2048,1024]{1,0:T(8,128)(2,1)} %param.9), kind=kOutput, calls=%fused_computation.33 | convolution fusion | flops 537001984 | bytes 4980736 | tf_op jit(solution)/shard_map/dot_general | solution.py:173
  63.1 8.8 %collective-permute-done.16 = bf16[128,2048]{0,1:T(8,128)(2,1)S(1)} collective-permute-done((bf16[128,2048]{0,1:T(8,128)(2,1)S(1)}, bf16[128,2048]{0,1:T(8,128)(2,1)S(1)}, u32[]{:S(2)}, u32[]{:S(2)}) %collective-permute-start.16) | collective-permute-done | bytes 524320 | tf_op jit(solution)/shard_map/ppermute | solution.py:70
  72.1 1.6 collective-permute-start.27
  76.1 1.6 collective-permute-start.19
  77.7 1.8 %convolution_convert_fusion.3 = bf16[128,1024]{1,0:T(8,128)(2,1)S(1)} fusion(bf16[128,2048]{0,1:T(8,128)(2,1)} %collective-permute-done.22, bf16[2048,1024]{1,0:T(8,128)(2,1)S(1)} %copy-done.1), kind=kOutput, calls=%fused_computation.29 | convolution fusion | flops 537001984 | bytes 4980736 | tf_op jit(solution)/shard_map/dot_general | solution.py:182
  80.4 6.7 %collective-permute-done.27 = bf16[64,2048]{0,1:T(8,128)(2,1)S(1)} collective-permute-done((bf16[64,2048]{0,1:T(8,128)(2,1)S(1)}, bf16[64,2048]{0,1:T(8,128)(2,1)S(1)}, u32[]{:S(2)}, u32[]{:S(2)}) %collective-permute-start.27) | collective-permute-done | bytes 262176 | tf_op jit(solution)/shard_map/ppermute | solution.py:75
  87.1 1.7 %collective-permute-done.26 = bf16[64,2048]{0,1:T(8,128)(2,1)S(1)} collective-permute-done((bf16[64,2048]{0,1:T(8,128)(2,1)}, bf16[64,2048]{0,1:T(8,128)(2,1)S(1)}, u32[]{:S(2)}, u32[]{:S(2)}) %collective-permute-start.26) | collective-permute-done | bytes 262176 | tf_op jit(solution)/shard_map/ppermute | solution.py:74
  90.5 2.0 %collective-permute-done.19 = bf16[128,1024]{1,0:T(8,128)(2,1)S(1)} collective-permute-done((bf16[128,1024]{1,0:T(8,128)(2,1)S(1)}, bf16[128,1024]{1,0:T(8,128)(2,1)S(1)}, u32[]{:S(2)}, u32[]{:S(2)}) %collective-permute-start.19) | collective-permute-done | bytes 262176 | tf_op jit(solution)/shard_map/ppermute | solution.py:187
  95.1 2.4 %collective-permute-start.25 = (bf16[128,1024]{1,0:T(8,128)(2,1)S(1)}, bf16[128,1024]{1,0:T(8,128)(2,1)S(1)}, u32[]{:S(2)}, u32[]{:S(2)}) collective-permute-start(bf16[128,1024]{1,0:T(8,128)(2,1)S(1)} %convolution_convert_fusion.2), channel_id=1, source_target_pairs={{0,20},{4,16},{8,28},{12,24},{16,4},{20,0},{24,12},{28,8},{1,21},{... | collective-permute-start | bytes 786440 | tf_op jit(solution)/shard_map/ppermute | solution.py:187
  98.3 6.1 %collective-permute-done.21 = bf16[128,1024]{1,0:T(8,128)(2,1)S(1)} collective-permute-done((bf16[128,1024]{1,0:T(8,128)(2,1)S(1)}, bf16[128,1024]{1,0:T(8,128)(2,1)S(1)}, u32[]{:S(2)}, u32[]{:S(2)}) %collective-permute-start.21) | collective-permute-done | bytes 262176 | tf_op jit(solution)/shard_map/ppermute | solution.py:187
  104.6 6.6 %collective-permute-done.25 = bf16[128,1024]{1,0:T(8,128)(2,1)S(1)} collective-permute-done((bf16[128,1024]{1,0:T(8,128)(2,1)S(1)}, bf16[128,1024]{1,0:T(8,128)(2,1)S(1)}, u32[]{:S(2)}, u32[]{:S(2)}) %collective-permute-start.25) | collective-permute-done | bytes 262176 | tf_op jit(solution)/shard_map/ppermute | solution.py:187
  112.9 43.5 %reduce-scatter.2.cloned.1.call-done = bf16[1,128,2048]{2,1,0:T(8,128)(2,1)} async-done(((bf16[4,128,2048]{2,1,0:T(8,128)(2,1)}), bf16[1,128,2048]{2,1,0:T(8,128)(2,1)}) %reduce-scatter.2.cloned.1.call-update) | async-done | bytes 524304 | tf_op jit(solution)/shard_map/reduce_scatter | solution.py:200
  (103 shorter events, 25.5 us)
Async XLA Ops:
  6.5 149.8 %reduce-scatter.2.cloned.1.call-start = ((), (), s32[]{:S(2)}) async-start(), calls=%async_computation.1 | async-start | bytes 2621440 | tf_op jit(solution)/shard_map/reduce_scatter | solution.py:200
  8.2 15.9 %collective-permute-start = (bf16[16,128,128]{2,1,0:T(8,128)(2,1)S(1)}, bf16[16,128,128]{2,1,0:T(8,128)(2,1)}, u32[]{:S(2)}, u32[]{:S(2)}) collective-permute-start(bf16[16,128,128]{2,1,0:T(8,128)(2,1)S(1)} %bitcast.169), channel_id=1, source_target_pairs={{0,8},{8,0},{16,24},{24,16},{1,9},{9,1},{17,25},{25,17},{2,10},{10... | collective-permute-start | bytes 1572872 | tf_op jit(solution)/shard_map/ppermute | solution.py:70
  11.2 14.8 %collective-permute-start.3 = (bf16[16,128,128]{2,1,0:T(8,128)(2,1)S(1)}, bf16[16,128,128]{2,1,0:T(8,128)(2,1)S(1)}, u32[]{:S(2)}, u32[]{:S(2)}) collective-permute-start(bf16[16,128,128]{2,1,0:T(8,128)(2,1)S(1)} %bitcast.170), channel_id=1, source_target_pairs={{0,16},{8,24},{16,0},{24,8},{1,17},{9,25},{17,1},{25,9},{2,18},{10... | collective-permute-start | bytes 1572872 | tf_op jit(solution)/shard_map/ppermute | solution.py:71
  12.7 29.3 %collective-permute-start.1 = (bf16[16,128,128]{2,1,0:T(8,128)(2,1)S(1)}, bf16[16,128,128]{2,1,0:T(8,128)(2,1)}, u32[]{:S(2)}, u32[]{:S(2)}) collective-permute-start(bf16[16,128,128]{2,1,0:T(8,128)(2,1)S(1)} %bitcast.171), channel_id=1, source_target_pairs={{0,4},{4,0},{1,5},{5,1},{2,6},{6,2},{3,7},{7,3},{8,12},{12,8},{9,1... | collective-permute-start | bytes 1572872 | tf_op jit(solution)/shard_map/ppermute | solution.py:82
  14.0 23.8 %collective-permute-start.9 = (bf16[16,128,128]{1,2,0:T(8,128)(2,1)S(1)}, bf16[16,128,128]{1,2,0:T(8,128)(2,1)S(1)}, u32[]{:S(2)}, u32[]{:S(2)}) collective-permute-start(bf16[16,128,128]{1,2,0:T(8,128)(2,1)S(1)} %bitcast.160), channel_id=1, source_target_pairs={{0,8},{8,0},{16,24},{24,16},{1,9},{9,1},{17,25},{25,17},{2,10},{10... | collective-permute-start | bytes 1572872 | tf_op jit(solution)/shard_map/ppermute | solution.py:70
  14.6 22.6 %collective-permute-start.11 = (bf16[16,128,128]{1,2,0:T(8,128)(2,1)S(1)}, bf16[16,128,128]{1,2,0:T(8,128)(2,1)S(1)}, u32[]{:S(2)}, u32[]{:S(2)}) collective-permute-start(bf16[16,128,128]{1,2,0:T(8,128)(2,1)S(1)} %bitcast.161), channel_id=1, source_target_pairs={{0,16},{8,24},{16,0},{24,8},{1,17},{9,25},{17,1},{25,9},{2,18},{10... | collective-permute-start | bytes 1572872 | tf_op jit(solution)/shard_map/ppermute | solution.py:71
  24.1 31.5 %collective-permute-start.8 = (bf16[16,128,128]{1,2,0:T(8,128)(2,1)S(1)}, bf16[16,128,128]{1,2,0:T(8,128)(2,1)S(1)}, u32[]{:S(2)}, u32[]{:S(2)}) collective-permute-start(bf16[16,128,128]{1,2,0:T(8,128)(2,1)S(1)} %bitcast.162), channel_id=1, source_target_pairs={{0,4},{4,0},{1,5},{5,1},{2,6},{6,2},{3,7},{7,3},{8,12},{12,8},{9,1... | collective-permute-start | bytes 1572872 | tf_op jit(solution)/shard_map/ppermute | solution.py:82
  26.1 22.3 %collective-permute-start.6 = (bf16[8,128,128]{2,1,0:T(8,128)(2,1)S(1)}, bf16[8,128,128]{2,1,0:T(8,128)(2,1)S(1)}, u32[]{:S(2)}, u32[]{:S(2)}) collective-permute-start(bf16[8,128,128]{2,1,0:T(8,128)(2,1)S(1)} %slice.25), channel_id=1, source_target_pairs={{0,16},{8,24},{16,0},{24,8},{1,17},{9,25},{17,1},{25,9},{2,18},{10... | collective-permute-start | bytes 786440 | tf_op jit(solution)/shard_map/ppermute | solution.py:75
  37.3 8.2 %collective-permute-start.5 = (bf16[8,128,128]{2,1,0:T(8,128)(2,1)S(1)}, bf16[8,128,128]{2,1,0:T(8,128)(2,1)S(1)}, u32[]{:S(2)}, u32[]{:S(2)}) collective-permute-start(bf16[8,128,128]{2,1,0:T(8,128)(2,1)S(1)} %slice.24), channel_id=1, source_target_pairs={{0,8},{8,0},{16,24},{24,16},{1,9},{9,1},{17,25},{25,17},{2,10},{10... | collective-permute-start | bytes 786440 | tf_op jit(solution)/shard_map/ppermute | solution.py:74
  37.9 10.4 %collective-permute-start.13 = (bf16[8,128,128]{1,2,0:T(8,128)(2,1)S(1)}, bf16[8,128,128]{1,2,0:T(8,128)(2,1)S(1)}, u32[]{:S(2)}, u32[]{:S(2)}) collective-permute-start(bf16[8,128,128]{1,2,0:T(8,128)(2,1)S(1)} %slice.26), channel_id=1, source_target_pairs={{0,8},{8,0},{16,24},{24,16},{1,9},{9,1},{17,25},{25,17},{2,10},{10... | collective-permute-start | bytes 786440 | tf_op jit(solution)/shard_map/ppermute | solution.py:74
  48.3 8.8 %collective-permute-start.10 = (bf16[16,128,128]{1,2,0:T(8,128)(2,1)S(1)}, bf16[16,128,128]{1,2,0:T(8,128)(2,1)S(1)}, u32[]{:S(2)}, u32[]{:S(2)}) collective-permute-start(bf16[16,128,128]{1,2,0:T(8,128)(2,1)S(1)} %collective-permute-done.9), channel_id=1, source_target_pairs={{0,4},{4,0},{1,5},{5,1},{2,6},{6,2},{3,7},{7,3},{8,12},{12,8},{9,1... | collective-permute-start | bytes 1572872 | tf_op jit(solution)/shard_map/ppermute | solution.py:82
  49.0 8.5 %collective-permute-start.12 = (bf16[16,128,128]{1,2,0:T(8,128)(2,1)S(1)}, bf16[16,128,128]{1,2,0:T(8,128)(2,1)S(1)}, u32[]{:S(2)}, u32[]{:S(2)}) collective-permute-start(bf16[16,128,128]{1,2,0:T(8,128)(2,1)S(1)} %collective-permute-done.11), channel_id=1, source_target_pairs={{0,4},{4,0},{1,5},{5,1},{2,6},{6,2},{3,7},{7,3},{8,12},{12,8},{9,1... | collective-permute-start | bytes 1572872 | tf_op jit(solution)/shard_map/ppermute | solution.py:82
  57.9 14.0 %collective-permute-start.16 = (bf16[128,2048]{0,1:T(8,128)(2,1)S(1)}, bf16[128,2048]{0,1:T(8,128)(2,1)S(1)}, u32[]{:S(2)}, u32[]{:S(2)}) collective-permute-start(bf16[128,2048]{0,1:T(8,128)(2,1)S(1)} %bitcast.165), channel_id=1, source_target_pairs={{0,8},{8,0},{16,24},{24,16},{1,9},{9,1},{17,25},{25,17},{2,10},{10... | collective-permute-start | bytes 1572872 | tf_op jit(solution)/shard_map/ppermute | solution.py:70
  58.7 15.1 %collective-permute-start.22 = (bf16[128,2048]{0,1:T(8,128)(2,1)S(1)}, bf16[128,2048]{0,1:T(8,128)(2,1)}, u32[]{:S(2)}, u32[]{:S(2)}) collective-permute-start(bf16[128,2048]{0,1:T(8,128)(2,1)S(1)} %bitcast.166), channel_id=1, source_target_pairs={{0,16},{8,24},{16,0},{24,8},{1,17},{9,25},{17,1},{25,9},{2,18},{10... | collective-permute-start | bytes 1572872 | tf_op jit(solution)/shard_map/ppermute | solution.py:71
  60.0 14.2 %collective-permute-start.17 = (bf16[128,2048]{0,1:T(8,128)(2,1)S(1)}, bf16[128,2048]{0,1:T(8,128)(2,1)S(1)}, u32[]{:S(2)}, u32[]{:S(2)}) collective-permute-start(bf16[128,2048]{0,1:T(8,128)(2,1)S(1)} %bitcast.167), channel_id=1, source_target_pairs={{0,4},{4,0},{1,5},{5,1},{2,6},{6,2},{3,7},{7,3},{8,12},{12,8},{9,1... | collective-permute-start | bytes 1572872 | tf_op jit(solution)/shard_map/ppermute | solution.py:82
  72.1 14.9 %collective-permute-start.27 = (bf16[64,2048]{0,1:T(8,128)(2,1)S(1)}, bf16[64,2048]{0,1:T(8,128)(2,1)S(1)}, u32[]{:S(2)}, u32[]{:S(2)}) collective-permute-start(bf16[64,2048]{0,1:T(8,128)(2,1)S(1)} %slice.29), channel_id=1, source_target_pairs={{0,16},{8,24},{16,0},{24,8},{1,17},{9,25},{17,1},{25,9},{2,18},{10... | collective-permute-start | bytes 786440 | tf_op jit(solution)/shard_map/ppermute | solution.py:75
  73.7 15.1 %collective-permute-start.26 = (bf16[64,2048]{0,1:T(8,128)(2,1)}, bf16[64,2048]{0,1:T(8,128)(2,1)S(1)}, u32[]{:S(2)}, u32[]{:S(2)}) collective-permute-start(bf16[64,2048]{0,1:T(8,128)(2,1)} %bitcast.159), channel_id=1, source_target_pairs={{0,8},{8,0},{16,24},{24,16},{1,9},{9,1},{17,25},{25,17},{2,10},{10... | collective-permute-start | bytes 786440 | tf_op jit(solution)/shard_map/ppermute | solution.py:74
  75.0 14.8 %collective-permute-start.18 = (bf16[128,1024]{1,0:T(8,128)(2,1)S(1)}, bf16[128,1024]{1,0:T(8,128)(2,1)S(1)}, u32[]{:S(2)}, u32[]{:S(2)}) collective-permute-start(bf16[128,1024]{1,0:T(8,128)(2,1)S(1)} %convolution_convert_fusion.6), channel_id=1, source_target_pairs={{0,4},{4,0},{8,12},{12,8},{16,20},{20,16},{24,28},{28,24},{1,5},{5... | collective-permute-start | bytes 786440 | tf_op jit(solution)/shard_map/ppermute | solution.py:187
  76.1 16.4 %collective-permute-start.19 = (bf16[128,1024]{1,0:T(8,128)(2,1)S(1)}, bf16[128,1024]{1,0:T(8,128)(2,1)S(1)}, u32[]{:S(2)}, u32[]{:S(2)}) collective-permute-start(bf16[128,1024]{1,0:T(8,128)(2,1)S(1)} %convolution_convert_fusion.5), channel_id=1, source_target_pairs={{0,8},{4,12},{8,0},{12,4},{16,24},{20,28},{24,16},{28,20},{1,9},{5... | collective-permute-start | bytes 786440 | tf_op jit(solution)/shard_map/ppermute | solution.py:187
  79.5 25.0 %collective-permute-start.23 = (bf16[128,1024]{1,0:T(8,128)(2,1)S(1)}, bf16[128,1024]{1,0:T(8,128)(2,1)S(1)}, u32[]{:S(2)}, u32[]{:S(2)}) collective-permute-start(bf16[128,1024]{1,0:T(8,128)(2,1)S(1)} %convolution_convert_fusion.3), channel_id=1, source_target_pairs={{0,16},{4,20},{8,24},{12,28},{16,0},{20,4},{24,8},{28,12},{1,17},{... | collective-permute-start | bytes 786440 | tf_op jit(solution)/shard_map/ppermute | solution.py:187
  92.5 18.8 %collective-permute-start.28 = (bf16[128,1024]{1,0:T(8,128)(2,1)S(1)}, bf16[128,1024]{1,0:T(8,128)(2,1)S(1)}, u32[]{:S(2)}, u32[]{:S(2)}) collective-permute-start(bf16[128,1024]{1,0:T(8,128)(2,1)S(1)} %convolution_convert_fusion.1), channel_id=1, source_target_pairs={{0,24},{4,28},{8,16},{12,20},{16,8},{20,12},{24,0},{28,4},{1,25},{... | collective-permute-start | bytes 786440 | tf_op jit(solution)/shard_map/ppermute | solution.py:187
  94.2 10.2 %collective-permute-start.21 = (bf16[128,1024]{1,0:T(8,128)(2,1)S(1)}, bf16[128,1024]{1,0:T(8,128)(2,1)S(1)}, u32[]{:S(2)}, u32[]{:S(2)}) collective-permute-start(bf16[128,1024]{1,0:T(8,128)(2,1)S(1)} %convolution_convert_fusion.4), channel_id=1, source_target_pairs={{0,12},{4,8},{8,4},{12,0},{16,28},{20,24},{24,20},{28,16},{1,13},{... | collective-permute-start | bytes 786440 | tf_op jit(solution)/shard_map/ppermute | solution.py:187
  95.1 16.1 %collective-permute-start.25 = (bf16[128,1024]{1,0:T(8,128)(2,1)S(1)}, bf16[128,1024]{1,0:T(8,128)(2,1)S(1)}, u32[]{:S(2)}, u32[]{:S(2)}) collective-permute-start(bf16[128,1024]{1,0:T(8,128)(2,1)S(1)} %convolution_convert_fusion.2), channel_id=1, source_target_pairs={{0,20},{4,16},{8,28},{12,24},{16,4},{20,0},{24,12},{28,8},{1,21},{... | collective-permute-start | bytes 786440 | tf_op jit(solution)/shard_map/ppermute | solution.py:187
  98.2 13.2 %collective-permute-start.30 = (bf16[128,1024]{1,0:T(8,128)(2,1)S(1)}, bf16[128,1024]{1,0:T(8,128)(2,1)S(1)}, u32[]{:S(2)}, u32[]{:S(2)}) collective-permute-start(bf16[128,1024]{1,0:T(8,128)(2,1)S(1)} %convolution_convert_fusion), channel_id=1, source_target_pairs={{0,28},{4,24},{8,20},{12,16},{16,12},{20,8},{24,4},{28,0},{1,29},{... | collective-permute-start | bytes 786440 | tf_op jit(solution)/shard_map/ppermute | solution.py:187
  (12 other events, 92.5 us)
Sparse Core Ops, SparseCore 0:
  113.0 43.3 reduce-scatter.1

commit v22 on v21

--- a/solution.py
+++ b/solution.py
@@ -174,10 +174,15 @@
                 jnp.bfloat16
             )
             own_partial, blocks[2] = lax.optimization_barrier((own_partial, blocks[2]))
+            diagonal = jnp.dot(
+                jnp.concatenate(blocks[6:], axis=0), out_weight, preferred_element_type=jnp.float32
+            ).astype(jnp.bfloat16)
             for b, block in enumerate(blocks):
                 r, t = b // 2, b % 2
                 if b == 0:
                     partial = own_partial
+                elif b >= 6:
+                    partial = diagonal[(b - 6) * seg_rows : (b - 5) * seg_rows]
                 else:
                     partial = jnp.dot(block, out_weight, preferred_element_type=jnp.float32).astype(
                         jnp.bfloat16

time: 164 us -> 167 us (1.018)
  waiting for transfers between devices: 99.6 us -> 104 us
    ppermute x7, waiting for transfers between devices: 14.7 us -> 16.9 us  [per_device(): partial = lax.ppermute(partial, SEQ, pairs)]
    dot_general x7 -> x5, matrix products: 6.47 us -> 4.99 us  [per_device(): jnp.dot(block, out_weight, preferred_element_type=jnp.float32)]
    unnamed x12 -> x14, local copies, waits for them, and re-layouts: 4.06 us -> 3.24 us
  transfers between devices with their start and end apart: 32 -> 32, of which waited for: 13 -> 13; matrix products, arithmetic and copies ran while one was open for 15% -> 14% of each run, Pallas kernels for 0% -> 0%
where the time goes in v22:
time: 167 us; the launch traced here: 166 us
  waiting for transfers between devices  104 us (62%)
  starting transfers between devices  22.1 us (13%)
  matrix products  18.1 us (11%)
  between operations  13.9 us (8%)
  local copies, waits for them, and re-layouts  5.1 us (3%)
  other arithmetic  3.45 us (2%)
    reduce_scatter x1, waiting for transfers between devices, per_device(): return lax.psum_scatter(by_row, 'chan', scatter_dimension=0, tiled=True)[0]  44.6 us
    ppermute x3, waiting for transfers between devices, gather_blocks_square(): from_x = lax.ppermute(x, 'hi', swap('hi', 1, 4))  19 us
    ppermute x7, waiting for transfers between devices, per_device(): partial = lax.ppermute(partial, SEQ, pairs)  16.9 us
    ppermute x3, waiting for transfers between devices, gather_blocks_square(): from_y = lax.ppermute(x, 'hi', swap('hi', 2, 4))  10.7 us
    ppermute x3, waiting for transfers between devices, gather_blocks_square(): lax.ppermute(from_x[half:], 'hi', swap('hi', 2, 4))  6.48 us
    dot_general x8, matrix products, attention_by_head(): jnp.einsum('hqd,hkd->hqk', queries, keys, preferred_element_type=jnp.floa...  6.04 us
    ppermute x7, starting transfers between devices, per_device(): partial = lax.ppermute(partial, SEQ, pairs)  5.58 us
    dot_general x5, matrix products, per_device(): jnp.dot(block, out_weight, preferred_element_type=jnp.float32)  4.99 us
  transfers between devices with their start and end apart: 32, of which 13 were waited for; matrix products, arithmetic and copies ran while one was open for 14% of the time, Pallas kernels for 0%

profile of v22, /device:TPU:0, one launch (start us, length us, event | category | flops | bytes accessed | tf_op | source)
XLA Modules:
  0.0 166.4 jit_solution(1710090893656124505)
XLA Ops:
  6.5 1.4 copy.16
  8.2 3.0 %collective-permute-start = (bf16[16,128,128]{2,1,0:T(8,128)(2,1)S(1)}, bf16[16,128,128]{2,1,0:T(8,128)(2,1)}, u32[]{:S(2)}, u32[]{:S(2)}) collective-permute-start(bf16[16,128,128]{2,1,0:T(8,128)(2,1)S(1)} %bitcast.166), channel_id=1, source_target_pairs={{0,8},{8,0},{16,24},{24,16},{1,9},{9,1},{17,25},{25,17},{2,10},{10... | collective-permute-start | bytes 1572872 | tf_op jit(solution)/shard_map/ppermute | solution.py:70
  11.2 1.5 collective-permute-start.3
  13.9 10.2 %collective-permute-done = bf16[16,128,128]{2,1,0:T(8,128)(2,1)} collective-permute-done((bf16[16,128,128]{2,1,0:T(8,128)(2,1)S(1)}, bf16[16,128,128]{2,1,0:T(8,128)(2,1)}, u32[]{:S(2)}, u32[]{:S(2)}) %collective-permute-start) | collective-permute-done | bytes 524320 | tf_op jit(solution)/shard_map/ppermute | solution.py:70
  26.1 1.5 collective-permute-start.6
  27.6 9.7 %collective-permute-done.11 = bf16[16,128,128]{1,2,0:T(8,128)(2,1)S(1)} collective-permute-done((bf16[16,128,128]{1,2,0:T(8,128)(2,1)S(1)}, bf16[16,128,128]{1,2,0:T(8,128)(2,1)S(1)}, u32[]{:S(2)}, u32[]{:S(2)}) %collective-permute-start.11) | collective-permute-done | bytes 524320 | tf_op jit(solution)/shard_map/ppermute | solution.py:71
  37.9 2.1 %collective-permute-start.13 = (bf16[8,128,128]{1,2,0:T(8,128)(2,1)S(1)}, bf16[8,128,128]{1,2,0:T(8,128)(2,1)S(1)}, u32[]{:S(2)}, u32[]{:S(2)}) collective-permute-start(bf16[8,128,128]{1,2,0:T(8,128)(2,1)S(1)} %slice.34), channel_id=1, source_target_pairs={{0,8},{8,0},{16,24},{24,16},{1,9},{9,1},{17,25},{25,17},{2,10},{10... | collective-permute-start | bytes 786440 | tf_op jit(solution)/shard_map/ppermute | solution.py:74
  40.0 1.5 fusion.119
  42.0 1.6 collective-permute-start.14
  43.6 1.5 fusion.121
  45.5 2.8 %collective-permute-done.13 = bf16[8,128,128]{1,2,0:T(8,128)(2,1)S(1)} collective-permute-done((bf16[8,128,128]{1,2,0:T(8,128)(2,1)S(1)}, bf16[8,128,128]{1,2,0:T(8,128)(2,1)S(1)}, u32[]{:S(2)}, u32[]{:S(2)}) %collective-permute-start.13) | collective-permute-done | bytes 262176 | tf_op jit(solution)/shard_map/ppermute | solution.py:74
  53.3 2.2 %fusion.21 = (f32[16,128]{1,0:T(8,128)S(1)}, f32[16,128]{1,0:T(8,128)S(1)}, f32[16,128]{1,0:T(8,128)S(1)}, f32[16,128]{1,0:T(8,128)S(1)}, f32[16,128]{1,0:T(8,12...) fusion(f32[16,128,128]{1,2,0:T(8,128)S(1)} %get-tuple-element.44, ...), kind=kLoop, calls=%fused_computation.48 | loop fusion | flops 6275072 | bytes 8593408 | tf_op jit(solution)/shard_map/reduce_sum | solution.py:106
  60.1 3.1 %convolution_convert_fusion.6 = bf16[128,1024]{1,0:T(8,128)(2,1)S(1)} fusion(bf16[128,2048]{0,1:T(8,128)(2,1)S(1)} %bitcast.165, bf16[2048,1024]{1,0:T(8,128)(2,1)} %param.9), kind=kOutput, calls=%fused_computation.32 | convolution fusion | flops 537001984 | bytes 4980736 | tf_op jit(solution)/shard_map/dot_general | solution.py:173
  63.1 8.8 %collective-permute-done.16 = bf16[128,2048]{0,1:T(8,128)(2,1)S(1)} collective-permute-done((bf16[128,2048]{0,1:T(8,128)(2,1)S(1)}, bf16[128,2048]{0,1:T(8,128)(2,1)S(1)}, u32[]{:S(2)}, u32[]{:S(2)}) %collective-permute-start.16) | collective-permute-done | bytes 524320 | tf_op jit(solution)/shard_map/ppermute | solution.py:70
  72.2 1.6 collective-permute-start.27
  76.1 1.5 collective-permute-start.19
  77.7 1.8 %convolution_convert_fusion.2 = bf16[128,1024]{1,0:T(8,128)(2,1)S(1)} fusion(bf16[128,2048]{0,1:T(8,128)(2,1)} %collective-permute-done.22, bf16[2048,1024]{1,0:T(8,128)(2,1)S(1)} %copy-done.1), kind=kOutput, calls=%fused_computation.28 | convolution fusion | flops 537001984 | bytes 4980736 | tf_op jit(solution)/shard_map/dot_general | solution.py:187
  80.6 6.5 %collective-permute-done.27 = bf16[64,2048]{0,1:T(8,128)(2,1)S(1)} collective-permute-done((bf16[64,2048]{0,1:T(8,128)(2,1)S(1)}, bf16[64,2048]{0,1:T(8,128)(2,1)S(1)}, u32[]{:S(2)}, u32[]{:S(2)}) %collective-permute-start.27) | collective-permute-done | bytes 262176 | tf_op jit(solution)/shard_map/ppermute | solution.py:75
  87.1 1.7 %collective-permute-done.26 = bf16[64,2048]{0,1:T(8,128)(2,1)S(1)} collective-permute-done((bf16[64,2048]{0,1:T(8,128)(2,1)}, bf16[64,2048]{0,1:T(8,128)(2,1)S(1)}, u32[]{:S(2)}, u32[]{:S(2)}) %collective-permute-start.26) | collective-permute-done | bytes 262176 | tf_op jit(solution)/shard_map/ppermute | solution.py:74
  89.8 2.7 %collective-permute-done.19 = bf16[128,1024]{1,0:T(8,128)(2,1)S(1)} collective-permute-done((bf16[128,1024]{1,0:T(8,128)(2,1)S(1)}, bf16[128,1024]{1,0:T(8,128)(2,1)S(1)}, u32[]{:S(2)}, u32[]{:S(2)}) %collective-permute-start.19) | collective-permute-done | bytes 262176 | tf_op jit(solution)/shard_map/ppermute | solution.py:192
  96.8 2.1 %collective-permute-start.29 = (bf16[128,1024]{1,0:T(8,128)(2,1)S(1)}, bf16[128,1024]{1,0:T(8,128)(2,1)S(1)}, u32[]{:S(2)}, u32[]{:S(2)}) collective-permute-start(bf16[128,1024]{1,0:T(8,128)(2,1)S(1)} %get-tuple-element.20), channel_id=1, source_target_pairs={{0,24},{4,28},{8,16},{12,20},{16,8},{20,12},{24,0},{28,4},{1,25},{... | collective-permute-start | bytes 786440 | tf_op jit(solution)/shard_map/ppermute | solution.py:192
  99.0 2.3 %collective-permute-done.21 = bf16[128,1024]{1,0:T(8,128)(2,1)S(1)} collective-permute-done((bf16[128,1024]{1,0:T(8,128)(2,1)S(1)}, bf16[128,1024]{1,0:T(8,128)(2,1)S(1)}, u32[]{:S(2)}, u32[]{:S(2)}) %collective-permute-start.21) | collective-permute-done | bytes 262176 | tf_op jit(solution)/shard_map/ppermute | solution.py:192
  101.4 11.9 %collective-permute-done.25 = bf16[128,1024]{1,0:T(8,128)(2,1)S(1)} collective-permute-done((bf16[128,1024]{1,0:T(8,128)(2,1)S(1)}, bf16[128,1024]{1,0:T(8,128)(2,1)S(1)}, u32[]{:S(2)}, u32[]{:S(2)}) %collective-permute-start.25) | collective-permute-done | bytes 262176 | tf_op jit(solution)/shard_map/ppermute | solution.py:192
  115.0 44.6 %reduce-scatter.2.cloned.1.call-done = bf16[1,128,2048]{2,1,0:T(8,128)(2,1)} async-done(((bf16[4,128,2048]{2,1,0:T(8,128)(2,1)}), bf16[1,128,2048]{2,1,0:T(8,128)(2,1)}) %reduce-scatter.2.cloned.1.call-update) | async-done | bytes 524304 | tf_op jit(solution)/shard_map/reduce_scatter | solution.py:205
  (105 shorter events, 24.9 us)
Async XLA Ops:
  6.5 153.0 %reduce-scatter.2.cloned.1.call-start = ((), (), s32[]{:S(2)}) async-start(), calls=%async_computation.1 | async-start | bytes 2621440 | tf_op jit(solution)/shard_map/reduce_scatter | solution.py:205
  8.2 15.9 %collective-permute-start = (bf16[16,128,128]{2,1,0:T(8,128)(2,1)S(1)}, bf16[16,128,128]{2,1,0:T(8,128)(2,1)}, u32[]{:S(2)}, u32[]{:S(2)}) collective-permute-start(bf16[16,128,128]{2,1,0:T(8,128)(2,1)S(1)} %bitcast.166), channel_id=1, source_target_pairs={{0,8},{8,0},{16,24},{24,16},{1,9},{9,1},{17,25},{25,17},{2,10},{10... | collective-permute-start | bytes 1572872 | tf_op jit(solution)/shard_map/ppermute | solution.py:70
  11.2 14.8 %collective-permute-start.3 = (bf16[16,128,128]{2,1,0:T(8,128)(2,1)S(1)}, bf16[16,128,128]{2,1,0:T(8,128)(2,1)S(1)}, u32[]{:S(2)}, u32[]{:S(2)}) collective-permute-start(bf16[16,128,128]{2,1,0:T(8,128)(2,1)S(1)} %bitcast.167), channel_id=1, source_target_pairs={{0,16},{8,24},{16,0},{24,8},{1,17},{9,25},{17,1},{25,9},{2,18},{10... | collective-permute-start | bytes 1572872 | tf_op jit(solution)/shard_map/ppermute | solution.py:71
  12.8 29.3 %collective-permute-start.1 = (bf16[16,128,128]{2,1,0:T(8,128)(2,1)S(1)}, bf16[16,128,128]{2,1,0:T(8,128)(2,1)}, u32[]{:S(2)}, u32[]{:S(2)}) collective-permute-start(bf16[16,128,128]{2,1,0:T(8,128)(2,1)S(1)} %bitcast.168), channel_id=1, source_target_pairs={{0,4},{4,0},{1,5},{5,1},{2,6},{6,2},{3,7},{7,3},{8,12},{12,8},{9,1... | collective-permute-start | bytes 1572872 | tf_op jit(solution)/shard_map/ppermute | solution.py:82
  13.0 24.9 %collective-permute-start.9 = (bf16[16,128,128]{1,2,0:T(8,128)(2,1)S(1)}, bf16[16,128,128]{1,2,0:T(8,128)(2,1)S(1)}, u32[]{:S(2)}, u32[]{:S(2)}) collective-permute-start(bf16[16,128,128]{1,2,0:T(8,128)(2,1)S(1)} %bitcast.157), channel_id=1, source_target_pairs={{0,8},{8,0},{16,24},{24,16},{1,9},{9,1},{17,25},{25,17},{2,10},{10... | collective-permute-start | bytes 1572872 | tf_op jit(solution)/shard_map/ppermute | solution.py:70
  13.6 23.7 %collective-permute-start.11 = (bf16[16,128,128]{1,2,0:T(8,128)(2,1)S(1)}, bf16[16,128,128]{1,2,0:T(8,128)(2,1)S(1)}, u32[]{:S(2)}, u32[]{:S(2)}) collective-permute-start(bf16[16,128,128]{1,2,0:T(8,128)(2,1)S(1)} %bitcast.158), channel_id=1, source_target_pairs={{0,16},{8,24},{16,0},{24,8},{1,17},{9,25},{17,1},{25,9},{2,18},{10... | collective-permute-start | bytes 1572872 | tf_op jit(solution)/shard_map/ppermute | solution.py:71
  24.1 31.4 %collective-permute-start.8 = (bf16[16,128,128]{1,2,0:T(8,128)(2,1)S(1)}, bf16[16,128,128]{1,2,0:T(8,128)(2,1)S(1)}, u32[]{:S(2)}, u32[]{:S(2)}) collective-permute-start(bf16[16,128,128]{1,2,0:T(8,128)(2,1)S(1)} %bitcast.159), channel_id=1, source_target_pairs={{0,4},{4,0},{1,5},{5,1},{2,6},{6,2},{3,7},{7,3},{8,12},{12,8},{9,1... | collective-permute-start | bytes 1572872 | tf_op jit(solution)/shard_map/ppermute | solution.py:82
  26.1 22.3 %collective-permute-start.6 = (bf16[8,128,128]{2,1,0:T(8,128)(2,1)S(1)}, bf16[8,128,128]{2,1,0:T(8,128)(2,1)S(1)}, u32[]{:S(2)}, u32[]{:S(2)}) collective-permute-start(bf16[8,128,128]{2,1,0:T(8,128)(2,1)S(1)} %slice.33), channel_id=1, source_target_pairs={{0,16},{8,24},{16,0},{24,8},{1,17},{9,25},{17,1},{25,9},{2,18},{10... | collective-permute-start | bytes 786440 | tf_op jit(solution)/shard_map/ppermute | solution.py:75
  37.3 8.2 %collective-permute-start.5 = (bf16[8,128,128]{2,1,0:T(8,128)(2,1)S(1)}, bf16[8,128,128]{2,1,0:T(8,128)(2,1)S(1)}, u32[]{:S(2)}, u32[]{:S(2)}) collective-permute-start(bf16[8,128,128]{2,1,0:T(8,128)(2,1)S(1)} %slice.32), channel_id=1, source_target_pairs={{0,8},{8,0},{16,24},{24,16},{1,9},{9,1},{17,25},{25,17},{2,10},{10... | collective-permute-start | bytes 786440 | tf_op jit(solution)/shard_map/ppermute | solution.py:74
  37.9 10.4 %collective-permute-start.13 = (bf16[8,128,128]{1,2,0:T(8,128)(2,1)S(1)}, bf16[8,128,128]{1,2,0:T(8,128)(2,1)S(1)}, u32[]{:S(2)}, u32[]{:S(2)}) collective-permute-start(bf16[8,128,128]{1,2,0:T(8,128)(2,1)S(1)} %slice.34), channel_id=1, source_target_pairs={{0,8},{8,0},{16,24},{24,16},{1,9},{9,1},{17,25},{25,17},{2,10},{10... | collective-permute-start | bytes 786440 | tf_op jit(solution)/shard_map/ppermute | solution.py:74
  48.4 8.8 %collective-permute-start.10 = (bf16[16,128,128]{1,2,0:T(8,128)(2,1)S(1)}, bf16[16,128,128]{1,2,0:T(8,128)(2,1)S(1)}, u32[]{:S(2)}, u32[]{:S(2)}) collective-permute-start(bf16[16,128,128]{1,2,0:T(8,128)(2,1)S(1)} %collective-permute-done.9), channel_id=1, source_target_pairs={{0,4},{4,0},{1,5},{5,1},{2,6},{6,2},{3,7},{7,3},{8,12},{12,8},{9,1... | collective-permute-start | bytes 1572872 | tf_op jit(solution)/shard_map/ppermute | solution.py:82
  49.0 8.5 %collective-permute-start.12 = (bf16[16,128,128]{1,2,0:T(8,128)(2,1)S(1)}, bf16[16,128,128]{1,2,0:T(8,128)(2,1)S(1)}, u32[]{:S(2)}, u32[]{:S(2)}) collective-permute-start(bf16[16,128,128]{1,2,0:T(8,128)(2,1)S(1)} %collective-permute-done.11), channel_id=1, source_target_pairs={{0,4},{4,0},{1,5},{5,1},{2,6},{6,2},{3,7},{7,3},{8,12},{12,8},{9,1... | collective-permute-start | bytes 1572872 | tf_op jit(solution)/shard_map/ppermute | solution.py:82
  57.9 14.0 %collective-permute-start.16 = (bf16[128,2048]{0,1:T(8,128)(2,1)S(1)}, bf16[128,2048]{0,1:T(8,128)(2,1)S(1)}, u32[]{:S(2)}, u32[]{:S(2)}) collective-permute-start(bf16[128,2048]{0,1:T(8,128)(2,1)S(1)} %bitcast.162), channel_id=1, source_target_pairs={{0,8},{8,0},{16,24},{24,16},{1,9},{9,1},{17,25},{25,17},{2,10},{10... | collective-permute-start | bytes 1572872 | tf_op jit(solution)/shard_map/ppermute | solution.py:70
  58.7 15.1 %collective-permute-start.22 = (bf16[128,2048]{0,1:T(8,128)(2,1)S(1)}, bf16[128,2048]{0,1:T(8,128)(2,1)}, u32[]{:S(2)}, u32[]{:S(2)}) collective-permute-start(bf16[128,2048]{0,1:T(8,128)(2,1)S(1)} %bitcast.163), channel_id=1, source_target_pairs={{0,16},{8,24},{16,0},{24,8},{1,17},{9,25},{17,1},{25,9},{2,18},{10... | collective-permute-start | bytes 1572872 | tf_op jit(solution)/shard_map/ppermute | solution.py:71
  60.0 14.3 %collective-permute-start.17 = (bf16[128,2048]{0,1:T(8,128)(2,1)S(1)}, bf16[128,2048]{0,1:T(8,128)(2,1)S(1)}, u32[]{:S(2)}, u32[]{:S(2)}) collective-permute-start(bf16[128,2048]{0,1:T(8,128)(2,1)S(1)} %bitcast.164), channel_id=1, source_target_pairs={{0,4},{4,0},{1,5},{5,1},{2,6},{6,2},{3,7},{7,3},{8,12},{12,8},{9,1... | collective-permute-start | bytes 1572872 | tf_op jit(solution)/shard_map/ppermute | solution.py:82
  72.2 14.9 %collective-permute-start.27 = (bf16[64,2048]{0,1:T(8,128)(2,1)S(1)}, bf16[64,2048]{0,1:T(8,128)(2,1)S(1)}, u32[]{:S(2)}, u32[]{:S(2)}) collective-permute-start(bf16[64,2048]{0,1:T(8,128)(2,1)S(1)} %slice.37), channel_id=1, source_target_pairs={{0,16},{8,24},{16,0},{24,8},{1,17},{9,25},{17,1},{25,9},{2,18},{10... | collective-permute-start | bytes 786440 | tf_op jit(solution)/shard_map/ppermute | solution.py:75
  73.8 15.1 %collective-permute-start.26 = (bf16[64,2048]{0,1:T(8,128)(2,1)}, bf16[64,2048]{0,1:T(8,128)(2,1)S(1)}, u32[]{:S(2)}, u32[]{:S(2)}) collective-permute-start(bf16[64,2048]{0,1:T(8,128)(2,1)} %bitcast.156), channel_id=1, source_target_pairs={{0,8},{8,0},{16,24},{24,16},{1,9},{9,1},{17,25},{25,17},{2,10},{10... | collective-permute-start | bytes 786440 | tf_op jit(solution)/shard_map/ppermute | solution.py:74
  75.1 14.1 %collective-permute-start.18 = (bf16[128,1024]{1,0:T(8,128)(2,1)S(1)}, bf16[128,1024]{1,0:T(8,128)(2,1)S(1)}, u32[]{:S(2)}, u32[]{:S(2)}) collective-permute-start(bf16[128,1024]{1,0:T(8,128)(2,1)S(1)} %convolution_convert_fusion.5), channel_id=1, source_target_pairs={{0,4},{4,0},{8,12},{12,8},{16,20},{20,16},{24,28},{28,24},{1,5},{5... | collective-permute-start | bytes 786440 | tf_op jit(solution)/shard_map/ppermute | solution.py:192
  76.1 16.4 %collective-permute-start.19 = (bf16[128,1024]{1,0:T(8,128)(2,1)S(1)}, bf16[128,1024]{1,0:T(8,128)(2,1)S(1)}, u32[]{:S(2)}, u32[]{:S(2)}) collective-permute-start(bf16[128,1024]{1,0:T(8,128)(2,1)S(1)} %convolution_convert_fusion.4), channel_id=1, source_target_pairs={{0,8},{4,12},{8,0},{12,4},{16,24},{20,28},{24,16},{28,20},{1,9},{5... | collective-permute-start | bytes 786440 | tf_op jit(solution)/shard_map/ppermute | solution.py:192
  79.5 21.8 %collective-permute-start.23 = (bf16[128,1024]{1,0:T(8,128)(2,1)S(1)}, bf16[128,1024]{1,0:T(8,128)(2,1)S(1)}, u32[]{:S(2)}, u32[]{:S(2)}) collective-permute-start(bf16[128,1024]{1,0:T(8,128)(2,1)S(1)} %convolution_convert_fusion.2), channel_id=1, source_target_pairs={{0,16},{4,20},{8,24},{12,28},{16,0},{20,4},{24,8},{28,12},{1,17},{... | collective-permute-start | bytes 786440 | tf_op jit(solution)/shard_map/ppermute | solution.py:192
  93.4 7.8 %collective-permute-start.21 = (bf16[128,1024]{1,0:T(8,128)(2,1)S(1)}, bf16[128,1024]{1,0:T(8,128)(2,1)S(1)}, u32[]{:S(2)}, u32[]{:S(2)}) collective-permute-start(bf16[128,1024]{1,0:T(8,128)(2,1)S(1)} %convolution_convert_fusion.3), channel_id=1, source_target_pairs={{0,12},{4,8},{8,4},{12,0},{16,28},{20,24},{24,20},{28,16},{1,13},{... | collective-permute-start | bytes 786440 | tf_op jit(solution)/shard_map/ppermute | solution.py:192
  94.2 19.1 %collective-permute-start.25 = (bf16[128,1024]{1,0:T(8,128)(2,1)S(1)}, bf16[128,1024]{1,0:T(8,128)(2,1)S(1)}, u32[]{:S(2)}, u32[]{:S(2)}) collective-permute-start(bf16[128,1024]{1,0:T(8,128)(2,1)S(1)} %convolution_convert_fusion.1), channel_id=1, source_target_pairs={{0,20},{4,16},{8,28},{12,24},{16,4},{20,0},{24,12},{28,8},{1,21},{... | collective-permute-start | bytes 786440 | tf_op jit(solution)/shard_map/ppermute | solution.py:192
  96.8 16.6 %collective-permute-start.29 = (bf16[128,1024]{1,0:T(8,128)(2,1)S(1)}, bf16[128,1024]{1,0:T(8,128)(2,1)S(1)}, u32[]{:S(2)}, u32[]{:S(2)}) collective-permute-start(bf16[128,1024]{1,0:T(8,128)(2,1)S(1)} %get-tuple-element.20), channel_id=1, source_target_pairs={{0,24},{4,28},{8,16},{12,20},{16,8},{20,12},{24,0},{28,4},{1,25},{... | collective-permute-start | bytes 786440 | tf_op jit(solution)/shard_map/ppermute | solution.py:192
  99.0 14.6 %collective-permute-start.30 = (bf16[128,1024]{1,0:T(8,128)(2,1)S(1)}, bf16[128,1024]{1,0:T(8,128)(2,1)S(1)}, u32[]{:S(2)}, u32[]{:S(2)}) collective-permute-start(bf16[128,1024]{1,0:T(8,128)(2,1)S(1)} %get-tuple-element.19), channel_id=1, source_target_pairs={{0,28},{4,24},{8,20},{12,16},{16,12},{20,8},{24,4},{28,0},{1,29},{... | collective-permute-start | bytes 786440 | tf_op jit(solution)/shard_map/ppermute | solution.py:192
  (13 other events, 92.6 us)
Sparse Core Ops, SparseCore 0:
  115.1 44.4 reduce-scatter.1

commit v23 on v21

--- a/solution.py
+++ b/solution.py
@@ -87,11 +87,19 @@
     score_scale = 1.0 / math.sqrt(HEAD_DIM)
     scores = []
     masks = []
-    for keys, start in zip(key_blocks, key_starts):
-        part = (
-            jnp.einsum("hqd,hkd->hqk", queries, keys, preferred_element_type=jnp.float32)
-            * score_scale
-        )
+    raw = [
+        jnp.einsum("hqd,hkd->hqk", queries, keys, preferred_element_type=jnp.float32)
+        for keys in key_blocks[:2]
+    ]
+    raw[0], raw[1], _ = lax.optimization_barrier((raw[0], raw[1], key_blocks[2]))
+    for i, (keys, start) in enumerate(zip(key_blocks, key_starts)):
+        if i < 2:
+            part = raw[i] * score_scale
+        else:
+            part = (
+                jnp.einsum("hqd,hkd->hqk", queries, keys, preferred_element_type=jnp.float32)
+                * score_scale
+            )
         key_pos = start + jnp.arange(keys.shape[1], dtype=jnp.int32)
         allowed = (key_pos[None, :] <= row_pos[:, None])[None]
         scores.append(jnp.where(allowed, part, -1e30))

time: 164 us -> 168 us (1.024)
  matrix products: 18.2 us -> 20.5 us
    reduce_scatter x1, waiting for transfers between devices: 43.5 us -> 45.7 us  [per_device(): return lax.psum_scatter(by_row, 'chan', scatter_dimension=0, tiled=True)[0]]
    ppermute x7, waiting for transfers between devices: 14.7 us -> 12.5 us  [per_device(): partial = lax.ppermute(partial, SEQ, pairs)]
    dot_general x8, matrix products: 2.59 us -> 4.59 us  [attention_by_head(): jnp.einsum('hqk,hkd->hqd', weights.astype(jnp.bfloat16), values, preferre...]
  transfers between devices with their start and end apart: 32 -> 32, of which waited for: 13 -> 14; matrix products, arithmetic and copies ran while one was open for 15% -> 17% of each run, Pallas kernels for 0% -> 0%
where the time goes in v23:
time: 168 us
  waiting for transfers between devices  99.9 us (59%)
  starting transfers between devices  22.2 us (13%)
  matrix products  20.5 us (12%)
  between operations  13.9 us (8%)
  local copies, waits for them, and re-layouts  6.84 us (4%)
  other arithmetic  4.77 us (3%)
    reduce_scatter x1, waiting for transfers between devices, per_device(): return lax.psum_scatter(by_row, 'chan', scatter_dimension=0, tiled=True)[0]  45.7 us
    ppermute x3, waiting for transfers between devices, gather_blocks_square(): from_x = lax.ppermute(x, 'hi', swap('hi', 1, 4))  17.9 us
    ppermute x7, waiting for transfers between devices, per_device(): partial = lax.ppermute(partial, SEQ, pairs)  12.5 us
    ppermute x3, waiting for transfers between devices, gather_blocks_square(): from_y = lax.ppermute(x, 'hi', swap('hi', 2, 4))  9.64 us
    ppermute x3, waiting for transfers between devices, gather_blocks_square(): lax.ppermute(from_x[half:], 'hi', swap('hi', 2, 4))  6.88 us
    dot_general x8, matrix products, attention_by_head(): jnp.einsum('hqd,hkd->hqk', queries, keys, preferred_element_type=jnp.floa...  6.55 us
    ppermute x3, waiting for transfers between devices, gather_blocks_square(): lax.ppermute(from_y[:half], 'hi', swap('hi', 1, 4))  6.29 us
    dot_general x7, matrix products, per_device(): jnp.dot(block, out_weight, preferred_element_type=jnp.float32)  6.27 us
  transfers between devices with their start and end apart: 32, of which 14 were waited for; matrix products, arithmetic and copies ran while one was open for 17% of the time, Pallas kernels for 0%

profile of v23, /device:TPU:0, one launch (start us, length us, event | category | flops | bytes accessed | tf_op | source)
XLA Modules:
  0.0 168.1 jit_solution(17794009676289308148)
XLA Ops:
  8.2 3.0 %collective-permute-start = (bf16[16,128,128]{2,1,0:T(8,128)(2,1)S(1)}, bf16[16,128,128]{2,1,0:T(8,128)(2,1)}, u32[]{:S(2)}, u32[]{:S(2)}) collective-permute-start(bf16[16,128,128]{2,1,0:T(8,128)(2,1)S(1)} %bitcast.155), channel_id=1, source_target_pairs={{0,8},{8,0},{16,24},{24,16},{1,9},{9,1},{17,25},{25,17},{2,10},{10... | collective-permute-start | bytes 1572872 | tf_op jit(solution)/shard_map/ppermute | solution.py:70
  11.2 1.5 collective-permute-start.3
  15.0 9.0 %collective-permute-done = bf16[16,128,128]{2,1,0:T(8,128)(2,1)} collective-permute-done((bf16[16,128,128]{2,1,0:T(8,128)(2,1)S(1)}, bf16[16,128,128]{2,1,0:T(8,128)(2,1)}, u32[]{:S(2)}, u32[]{:S(2)}) %collective-permute-start) | collective-permute-done | bytes 524320 | tf_op jit(solution)/shard_map/ppermute | solution.py:70
  26.0 1.5 collective-permute-start.6
  28.5 8.6 %collective-permute-done.11 = bf16[16,128,128]{1,2,0:T(8,128)(2,1)S(1)} collective-permute-done((bf16[16,128,128]{1,2,0:T(8,128)(2,1)S(1)}, bf16[16,128,128]{1,2,0:T(8,128)(2,1)S(1)}, u32[]{:S(2)}, u32[]{:S(2)}) %collective-permute-start.11) | collective-permute-done | bytes 524320 | tf_op jit(solution)/shard_map/ppermute | solution.py:71
  37.4 1.9 %collective-permute-start.13 = (bf16[8,128,128]{1,2,0:T(8,128)(2,1)S(1)}, bf16[8,128,128]{1,2,0:T(8,128)(2,1)S(1)}, u32[]{:S(2)}, u32[]{:S(2)}) collective-permute-start(bf16[8,128,128]{1,2,0:T(8,128)(2,1)S(1)} %slice.26), channel_id=1, source_target_pairs={{0,8},{8,0},{16,24},{24,16},{1,9},{9,1},{17,25},{25,17},{2,10},{10... | collective-permute-start | bytes 786440 | tf_op jit(solution)/shard_map/ppermute | solution.py:74
  39.3 1.6 fusion.122
  41.4 1.6 fusion.120
  43.1 1.6 collective-permute-start.14
  46.4 3.9 %collective-permute-done.13 = bf16[8,128,128]{1,2,0:T(8,128)(2,1)S(1)} collective-permute-done((bf16[8,128,128]{1,2,0:T(8,128)(2,1)S(1)}, bf16[8,128,128]{1,2,0:T(8,128)(2,1)S(1)}, u32[]{:S(2)}, u32[]{:S(2)}) %collective-permute-start.13) | collective-permute-done | bytes 262176 | tf_op jit(solution)/shard_map/ppermute | solution.py:74
  55.7 3.0 %fusion.28 = (f32[16,128]{1,0:T(8,128)S(1)}, f32[16,128]{1,0:T(8,128)S(1)}, f32[16,128]{1,0:T(8,128)S(1)}, f32[16,128]{1,0:T(8,128)S(1)}, f32[16,128]{1,0:T(8,12...) fusion(f32[16,128,128]{2,1,0:T(8,128)S(1)} %fusion.42, ...), kind=kLoop, calls=%fused_computation.56 | loop fusion | flops 7323648 | bytes 8593408 | tf_op jit(solution)/shard_map/reduce_sum | solution.py:114
  63.2 1.7 collective-permute-start.22
  64.9 3.1 %convolution_convert_fusion.7 = bf16[128,1024]{1,0:T(8,128)(2,1)S(1)} fusion(bf16[128,2048]{0,1:T(8,128)(2,1)S(1)} %bitcast.161, bf16[2048,1024]{1,0:T(8,128)(2,1)} %param.9), kind=kOutput, calls=%fused_computation.29 | convolution fusion | flops 537001984 | bytes 4980736 | tf_op jit(solution)/shard_map/dot_general | solution.py:181
  68.0 8.8 %collective-permute-done.16 = bf16[128,2048]{0,1:T(8,128)(2,1)S(1)} collective-permute-done((bf16[128,2048]{0,1:T(8,128)(2,1)S(1)}, bf16[128,2048]{0,1:T(8,128)(2,1)S(1)}, u32[]{:S(2)}, u32[]{:S(2)}) %collective-permute-start.16) | collective-permute-done | bytes 524320 | tf_op jit(solution)/shard_map/ppermute | solution.py:70
  77.0 1.6 collective-permute-start.27
  80.7 1.6 collective-permute-start.19
  82.3 1.8 %convolution_convert_fusion.3 = bf16[128,1024]{1,0:T(8,128)(2,1)S(1)} fusion(bf16[128,2048]{0,1:T(8,128)(2,1)} %collective-permute-done.22, bf16[2048,1024]{1,0:T(8,128)(2,1)S(1)} %copy-done.1), kind=kOutput, calls=%fused_computation.25 | convolution fusion | flops 537001984 | bytes 4980736 | tf_op jit(solution)/shard_map/dot_general | solution.py:190
  85.1 6.9 %collective-permute-done.27 = bf16[64,2048]{0,1:T(8,128)(2,1)S(1)} collective-permute-done((bf16[64,2048]{0,1:T(8,128)(2,1)S(1)}, bf16[64,2048]{0,1:T(8,128)(2,1)S(1)}, u32[]{:S(2)}, u32[]{:S(2)}) %collective-permute-start.27) | collective-permute-done | bytes 262176 | tf_op jit(solution)/shard_map/ppermute | solution.py:75
  91.9 1.7 %collective-permute-done.26 = bf16[64,2048]{0,1:T(8,128)(2,1)S(1)} collective-permute-done((bf16[64,2048]{0,1:T(8,128)(2,1)}, bf16[64,2048]{0,1:T(8,128)(2,1)S(1)}, u32[]{:S(2)}, u32[]{:S(2)}) %collective-permute-start.26) | collective-permute-done | bytes 262176 | tf_op jit(solution)/shard_map/ppermute | solution.py:74
  95.4 2.0 %collective-permute-done.19 = bf16[128,1024]{1,0:T(8,128)(2,1)S(1)} collective-permute-done((bf16[128,1024]{1,0:T(8,128)(2,1)S(1)}, bf16[128,1024]{1,0:T(8,128)(2,1)S(1)}, u32[]{:S(2)}, u32[]{:S(2)}) %collective-permute-start.19) | collective-permute-done | bytes 262176 | tf_op jit(solution)/shard_map/ppermute | solution.py:195
  99.9 2.4 %collective-permute-start.25 = (bf16[128,1024]{1,0:T(8,128)(2,1)S(1)}, bf16[128,1024]{1,0:T(8,128)(2,1)S(1)}, u32[]{:S(2)}, u32[]{:S(2)}) collective-permute-start(bf16[128,1024]{1,0:T(8,128)(2,1)S(1)} %convolution_convert_fusion.2), channel_id=1, source_target_pairs={{0,20},{4,16},{8,28},{12,24},{16,4},{20,0},{24,12},{28,8},{1,21},{... | collective-permute-start | bytes 786440 | tf_op jit(solution)/shard_map/ppermute | solution.py:195
  103.1 6.1 %collective-permute-done.21 = bf16[128,1024]{1,0:T(8,128)(2,1)S(1)} collective-permute-done((bf16[128,1024]{1,0:T(8,128)(2,1)S(1)}, bf16[128,1024]{1,0:T(8,128)(2,1)S(1)}, u32[]{:S(2)}, u32[]{:S(2)}) %collective-permute-start.21) | collective-permute-done | bytes 262176 | tf_op jit(solution)/shard_map/ppermute | solution.py:195
  109.4 2.9 %collective-permute-done.25 = bf16[128,1024]{1,0:T(8,128)(2,1)S(1)} collective-permute-done((bf16[128,1024]{1,0:T(8,128)(2,1)S(1)}, bf16[128,1024]{1,0:T(8,128)(2,1)S(1)}, u32[]{:S(2)}, u32[]{:S(2)}) %collective-permute-start.25) | collective-permute-done | bytes 262176 | tf_op jit(solution)/shard_map/ppermute | solution.py:195
  115.5 45.7 %reduce-scatter.2.cloned.1.call-done = bf16[1,128,2048]{2,1,0:T(8,128)(2,1)} async-done(((bf16[4,128,2048]{2,1,0:T(8,128)(2,1)}), bf16[1,128,2048]{2,1,0:T(8,128)(2,1)}) %reduce-scatter.2.cloned.1.call-update) | async-done | bytes 524304 | tf_op jit(solution)/shard_map/reduce_scatter | solution.py:208
  (108 shorter events, 30.7 us)
Async XLA Ops:
  6.5 154.7 %reduce-scatter.2.cloned.1.call-start = ((), (), s32[]{:S(2)}) async-start(), calls=%async_computation.1 | async-start | bytes 2621440 | tf_op jit(solution)/shard_map/reduce_scatter | solution.py:208
  8.2 15.9 %collective-permute-start = (bf16[16,128,128]{2,1,0:T(8,128)(2,1)S(1)}, bf16[16,128,128]{2,1,0:T(8,128)(2,1)}, u32[]{:S(2)}, u32[]{:S(2)}) collective-permute-start(bf16[16,128,128]{2,1,0:T(8,128)(2,1)S(1)} %bitcast.155), channel_id=1, source_target_pairs={{0,8},{8,0},{16,24},{24,16},{1,9},{9,1},{17,25},{25,17},{2,10},{10... | collective-permute-start | bytes 1572872 | tf_op jit(solution)/shard_map/ppermute | solution.py:70
  11.2 31.9 %collective-permute-start.1 = (bf16[16,128,128]{2,1,0:T(8,128)(2,1)S(1)}, bf16[16,128,128]{2,1,0:T(8,128)(2,1)S(1)}, u32[]{:S(2)}, u32[]{:S(2)}) collective-permute-start(bf16[16,128,128]{2,1,0:T(8,128)(2,1)S(1)} %bitcast.156), channel_id=1, source_target_pairs={{0,4},{4,0},{1,5},{5,1},{2,6},{6,2},{3,7},{7,3},{8,12},{12,8},{9,1... | collective-permute-start | bytes 1572872 | tf_op jit(solution)/shard_map/ppermute | solution.py:82
  11.2 14.8 %collective-permute-start.3 = (bf16[16,128,128]{2,1,0:T(8,128)(2,1)S(1)}, bf16[16,128,128]{2,1,0:T(8,128)(2,1)}, u32[]{:S(2)}, u32[]{:S(2)}) collective-permute-start(bf16[16,128,128]{2,1,0:T(8,128)(2,1)S(1)} %bitcast.157), channel_id=1, source_target_pairs={{0,16},{8,24},{16,0},{24,8},{1,17},{9,25},{17,1},{25,9},{2,18},{10... | collective-permute-start | bytes 1572872 | tf_op jit(solution)/shard_map/ppermute | solution.py:71
  14.0 23.4 %collective-permute-start.9 = (bf16[16,128,128]{1,2,0:T(8,128)(2,1)S(1)}, bf16[16,128,128]{1,2,0:T(8,128)(2,1)S(1)}, u32[]{:S(2)}, u32[]{:S(2)}) collective-permute-start(bf16[16,128,128]{1,2,0:T(8,128)(2,1)S(1)} %bitcast.150), channel_id=1, source_target_pairs={{0,8},{8,0},{16,24},{24,16},{1,9},{9,1},{17,25},{25,17},{2,10},{10... | collective-permute-start | bytes 1572872 | tf_op jit(solution)/shard_map/ppermute | solution.py:70
  14.6 22.5 %collective-permute-start.11 = (bf16[16,128,128]{1,2,0:T(8,128)(2,1)S(1)}, bf16[16,128,128]{1,2,0:T(8,128)(2,1)S(1)}, u32[]{:S(2)}, u32[]{:S(2)}) collective-permute-start(bf16[16,128,128]{1,2,0:T(8,128)(2,1)S(1)} %bitcast.151), channel_id=1, source_target_pairs={{0,16},{8,24},{16,0},{24,8},{1,17},{9,25},{17,1},{25,9},{2,18},{10... | collective-permute-start | bytes 1572872 | tf_op jit(solution)/shard_map/ppermute | solution.py:71
  24.1 34.6 %collective-permute-start.8 = (bf16[16,128,128]{1,2,0:T(8,128)(2,1)S(1)}, bf16[16,128,128]{1,2,0:T(8,128)(2,1)S(1)}, u32[]{:S(2)}, u32[]{:S(2)}) collective-permute-start(bf16[16,128,128]{1,2,0:T(8,128)(2,1)S(1)} %bitcast.152), channel_id=1, source_target_pairs={{0,4},{4,0},{1,5},{5,1},{2,6},{6,2},{3,7},{7,3},{8,12},{12,8},{9,1... | collective-permute-start | bytes 1572872 | tf_op jit(solution)/shard_map/ppermute | solution.py:82
  26.0 24.3 %collective-permute-start.6 = (bf16[8,128,128]{2,1,0:T(8,128)(2,1)S(1)}, bf16[8,128,128]{2,1,0:T(8,128)(2,1)S(1)}, u32[]{:S(2)}, u32[]{:S(2)}) collective-permute-start(bf16[8,128,128]{2,1,0:T(8,128)(2,1)S(1)} %slice.25), channel_id=1, source_target_pairs={{0,16},{8,24},{16,0},{24,8},{1,17},{9,25},{17,1},{25,9},{2,18},{10... | collective-permute-start | bytes 786440 | tf_op jit(solution)/shard_map/ppermute | solution.py:75
  37.2 9.2 %collective-permute-start.5 = (bf16[8,128,128]{2,1,0:T(8,128)(2,1)S(1)}, bf16[8,128,128]{2,1,0:T(8,128)(2,1)S(1)}, u32[]{:S(2)}, u32[]{:S(2)}) collective-permute-start(bf16[8,128,128]{2,1,0:T(8,128)(2,1)S(1)} %slice.24), channel_id=1, source_target_pairs={{0,8},{8,0},{16,24},{24,16},{1,9},{9,1},{17,25},{25,17},{2,10},{10... | collective-permute-start | bytes 786440 | tf_op jit(solution)/shard_map/ppermute | solution.py:74
  37.4 12.9 %collective-permute-start.13 = (bf16[8,128,128]{1,2,0:T(8,128)(2,1)S(1)}, bf16[8,128,128]{1,2,0:T(8,128)(2,1)S(1)}, u32[]{:S(2)}, u32[]{:S(2)}) collective-permute-start(bf16[8,128,128]{1,2,0:T(8,128)(2,1)S(1)} %slice.26), channel_id=1, source_target_pairs={{0,8},{8,0},{16,24},{24,16},{1,9},{9,1},{17,25},{25,17},{2,10},{10... | collective-permute-start | bytes 786440 | tf_op jit(solution)/shard_map/ppermute | solution.py:74
  50.4 11.2 %collective-permute-start.10 = (bf16[16,128,128]{1,2,0:T(8,128)(2,1)S(1)}, bf16[16,128,128]{1,2,0:T(8,128)(2,1)S(1)}, u32[]{:S(2)}, u32[]{:S(2)}) collective-permute-start(bf16[16,128,128]{1,2,0:T(8,128)(2,1)S(1)} %collective-permute-done.9), channel_id=1, source_target_pairs={{0,4},{4,0},{1,5},{5,1},{2,6},{6,2},{3,7},{7,3},{8,12},{12,8},{9,1... | collective-permute-start | bytes 1572872 | tf_op jit(solution)/shard_map/ppermute | solution.py:82
  51.0 11.1 %collective-permute-start.12 = (bf16[16,128,128]{1,2,0:T(8,128)(2,1)S(1)}, bf16[16,128,128]{1,2,0:T(8,128)(2,1)S(1)}, u32[]{:S(2)}, u32[]{:S(2)}) collective-permute-start(bf16[16,128,128]{1,2,0:T(8,128)(2,1)S(1)} %collective-permute-done.11), channel_id=1, source_target_pairs={{0,4},{4,0},{1,5},{5,1},{2,6},{6,2},{3,7},{7,3},{8,12},{12,8},{9,1... | collective-permute-start | bytes 1572872 | tf_op jit(solution)/shard_map/ppermute | solution.py:82
  62.8 14.0 %collective-permute-start.16 = (bf16[128,2048]{0,1:T(8,128)(2,1)S(1)}, bf16[128,2048]{0,1:T(8,128)(2,1)S(1)}, u32[]{:S(2)}, u32[]{:S(2)}) collective-permute-start(bf16[128,2048]{0,1:T(8,128)(2,1)S(1)} %bitcast.158), channel_id=1, source_target_pairs={{0,8},{8,0},{16,24},{24,16},{1,9},{9,1},{17,25},{25,17},{2,10},{10... | collective-permute-start | bytes 1572872 | tf_op jit(solution)/shard_map/ppermute | solution.py:70
  63.2 15.4 %collective-permute-start.22 = (bf16[128,2048]{0,1:T(8,128)(2,1)S(1)}, bf16[128,2048]{0,1:T(8,128)(2,1)}, u32[]{:S(2)}, u32[]{:S(2)}) collective-permute-start(bf16[128,2048]{0,1:T(8,128)(2,1)S(1)} %bitcast.159), channel_id=1, source_target_pairs={{0,16},{8,24},{16,0},{24,8},{1,17},{9,25},{17,1},{25,9},{2,18},{10... | collective-permute-start | bytes 1572872 | tf_op jit(solution)/shard_map/ppermute | solution.py:71
  64.9 14.2 %collective-permute-start.17 = (bf16[128,2048]{0,1:T(8,128)(2,1)S(1)}, bf16[128,2048]{0,1:T(8,128)(2,1)S(1)}, u32[]{:S(2)}, u32[]{:S(2)}) collective-permute-start(bf16[128,2048]{0,1:T(8,128)(2,1)S(1)} %bitcast.160), channel_id=1, source_target_pairs={{0,4},{4,0},{1,5},{5,1},{2,6},{6,2},{3,7},{7,3},{8,12},{12,8},{9,1... | collective-permute-start | bytes 1572872 | tf_op jit(solution)/shard_map/ppermute | solution.py:82
  77.0 14.9 %collective-permute-start.27 = (bf16[64,2048]{0,1:T(8,128)(2,1)S(1)}, bf16[64,2048]{0,1:T(8,128)(2,1)S(1)}, u32[]{:S(2)}, u32[]{:S(2)}) collective-permute-start(bf16[64,2048]{0,1:T(8,128)(2,1)S(1)} %slice.29), channel_id=1, source_target_pairs={{0,16},{8,24},{16,0},{24,8},{1,17},{9,25},{17,1},{25,9},{2,18},{10... | collective-permute-start | bytes 786440 | tf_op jit(solution)/shard_map/ppermute | solution.py:75
  78.6 15.1 %collective-permute-start.26 = (bf16[64,2048]{0,1:T(8,128)(2,1)}, bf16[64,2048]{0,1:T(8,128)(2,1)S(1)}, u32[]{:S(2)}, u32[]{:S(2)}) collective-permute-start(bf16[64,2048]{0,1:T(8,128)(2,1)} %bitcast.149), channel_id=1, source_target_pairs={{0,8},{8,0},{16,24},{24,16},{1,9},{9,1},{17,25},{25,17},{2,10},{10... | collective-permute-start | bytes 786440 | tf_op jit(solution)/shard_map/ppermute | solution.py:74
  79.9 14.8 %collective-permute-start.18 = (bf16[128,1024]{1,0:T(8,128)(2,1)S(1)}, bf16[128,1024]{1,0:T(8,128)(2,1)S(1)}, u32[]{:S(2)}, u32[]{:S(2)}) collective-permute-start(bf16[128,1024]{1,0:T(8,128)(2,1)S(1)} %convolution_convert_fusion.6), channel_id=1, source_target_pairs={{0,4},{4,0},{8,12},{12,8},{16,20},{20,16},{24,28},{28,24},{1,5},{5... | collective-permute-start | bytes 786440 | tf_op jit(solution)/shard_map/ppermute | solution.py:195
  80.7 16.6 %collective-permute-start.19 = (bf16[128,1024]{1,0:T(8,128)(2,1)S(1)}, bf16[128,1024]{1,0:T(8,128)(2,1)S(1)}, u32[]{:S(2)}, u32[]{:S(2)}) collective-permute-start(bf16[128,1024]{1,0:T(8,128)(2,1)S(1)} %convolution_convert_fusion.5), channel_id=1, source_target_pairs={{0,8},{4,12},{8,0},{12,4},{16,24},{20,28},{24,16},{28,20},{1,9},{5... | collective-permute-start | bytes 786440 | tf_op jit(solution)/shard_map/ppermute | solution.py:195
  84.1 25.2 %collective-permute-start.23 = (bf16[128,1024]{1,0:T(8,128)(2,1)S(1)}, bf16[128,1024]{1,0:T(8,128)(2,1)S(1)}, u32[]{:S(2)}, u32[]{:S(2)}) collective-permute-start(bf16[128,1024]{1,0:T(8,128)(2,1)S(1)} %convolution_convert_fusion.3), channel_id=1, source_target_pairs={{0,16},{4,20},{8,24},{12,28},{16,0},{20,4},{24,8},{28,12},{1,17},{... | collective-permute-start | bytes 786440 | tf_op jit(solution)/shard_map/ppermute | solution.py:195
  97.4 15.1 %collective-permute-start.28 = (bf16[128,1024]{1,0:T(8,128)(2,1)S(1)}, bf16[128,1024]{1,0:T(8,128)(2,1)S(1)}, u32[]{:S(2)}, u32[]{:S(2)}) collective-permute-start(bf16[128,1024]{1,0:T(8,128)(2,1)S(1)} %convolution_convert_fusion.1), channel_id=1, source_target_pairs={{0,24},{4,28},{8,16},{12,20},{16,8},{20,12},{24,0},{28,4},{1,25},{... | collective-permute-start | bytes 786440 | tf_op jit(solution)/shard_map/ppermute | solution.py:195
  99.1 10.1 %collective-permute-start.21 = (bf16[128,1024]{1,0:T(8,128)(2,1)S(1)}, bf16[128,1024]{1,0:T(8,128)(2,1)S(1)}, u32[]{:S(2)}, u32[]{:S(2)}) collective-permute-start(bf16[128,1024]{1,0:T(8,128)(2,1)S(1)} %convolution_convert_fusion.4), channel_id=1, source_target_pairs={{0,12},{4,8},{8,4},{12,0},{16,28},{20,24},{24,20},{28,16},{1,13},{... | collective-permute-start | bytes 786440 | tf_op jit(solution)/shard_map/ppermute | solution.py:195
  99.9 12.4 %collective-permute-start.25 = (bf16[128,1024]{1,0:T(8,128)(2,1)S(1)}, bf16[128,1024]{1,0:T(8,128)(2,1)S(1)}, u32[]{:S(2)}, u32[]{:S(2)}) collective-permute-start(bf16[128,1024]{1,0:T(8,128)(2,1)S(1)} %convolution_convert_fusion.2), channel_id=1, source_target_pairs={{0,20},{4,16},{8,28},{12,24},{16,4},{20,0},{24,12},{28,8},{1,21},{... | collective-permute-start | bytes 786440 | tf_op jit(solution)/shard_map/ppermute | solution.py:195
  103.1 11.0 %collective-permute-start.30 = (bf16[128,1024]{1,0:T(8,128)(2,1)S(1)}, bf16[128,1024]{1,0:T(8,128)(2,1)S(1)}, u32[]{:S(2)}, u32[]{:S(2)}) collective-permute-start(bf16[128,1024]{1,0:T(8,128)(2,1)S(1)} %convolution_convert_fusion), channel_id=1, source_target_pairs={{0,28},{4,24},{8,20},{12,16},{16,12},{20,8},{24,4},{28,0},{1,29},{... | collective-permute-start | bytes 786440 | tf_op jit(solution)/shard_map/ppermute | solution.py:195
  (12 other events, 98.7 us)
Sparse Core Ops, SparseCore 0:
  115.6 45.5 reduce-scatter.1
